TPU v7x, 128 devices: a whole 4x4x4 slice. The times are simulated.
128 devices in a mesh: req: 16 (over z, y), cuts: 8 (over x, core).
Axes of the slice: x: 4, y: 4, z: 4, core: 2. Of those that a mesh axis runs over, the one named last changes fastest.
Arguments:
- tokens: bfloat16 [16384, 1024], P(('req', 'cuts')), may hold values from -6 to 6
- qkv_weight: bfloat16 [1024, 2048], replicated, may hold values from -0.1875 to 0.1875
- out_weight: bfloat16 [1024, 1024], replicated, may hold values from -0.1875 to 0.1875
- norm_attn: float32 [1024], replicated, may hold values from 0.4 to 1.6
- norm_expert: float32 [1024], replicated, may hold values from 0.4 to 1.6
- keys_cache: bfloat16 [128, 2048, 512], P(('req', 'cuts')), may hold values from -4000 to 4000
- values_cache: bfloat16 [128, 2048, 512], P(('req', 'cuts')), may hold values from -6 to 6
- lengths: int32 [128], P(('req', 'cuts')), may hold values from 1 to 2048, 131072 in all
- routes: int32 [16384, 8], P(('req', 'cuts')), may hold values from 0 to 31, all different within a row; in each aligned block of 128 rows (0 to 127, 128 to 255, ...) at most 40 rows name the same one
- gates: float32 [16384, 8], P(('req', 'cuts')), may hold values from 0.05 to 0.25
- gate_up: bfloat16 [128, 1024, 256], P(('req', 'cuts')), may hold values from -0.1875 to 0.1875
- down_weight: bfloat16 [128, 128, 1024], P(('req', 'cuts')), may hold values from -0.25 to 0.25
Outputs:
- attn_branch: bfloat16 [16384, 1024], P(('req', 'cuts'))
- expert_mix: bfloat16 [16384, 1024], P(('req', 'cuts'))
Inputs may be any that keep to these rules, and one draw needn't show every extreme that they name: `routes`: each row names 8 different experts; within the 128 rows of one request no expert is named by more than 40 rows, a bound that some block reaches. `lengths`: one request has exactly 2048 live cache slots.
All inputs are finite; a program needn't handle non-finite values. No bound on the sum of `lengths` on one device may be relied on, other than what follows from the above.
Results may differ from a plain program's by a relative error of at most 0.012.
The roundings to bfloat16 on the way count: a program that leaves them out, or rounds other values in their place, can miss the bound.
Values may be sent and summed in bfloat16 or wider, within the bound.
No kernel may reach another device: no remote copies, remote signals or barrier semaphores. Data moves between devices by JAX's collectives and lax.ppermute only.
A program may use at most 128 MiB of HBM per device.

v0:
```python
import jax
import jax.numpy as jnp
from jax import lax
from jax.sharding import PartitionSpec as P

HEADS = 16
KV_HEADS = 8
HEAD = 64
EXPERTS = 32
TOP = 8
CAPACITY = 40


def rms_scale(values, gain):
    wide = values.astype(jnp.float32)
    power = jnp.mean(wide * wide, axis=-1, keepdims=True)
    return wide * lax.rsqrt(power + 1e-06) * gain


def rotate(vectors, places):
    half = vectors.shape[-1] // 2
    freq = 10000.0 ** (-jnp.arange(half, dtype=jnp.float32) / half)
    angle = places[:, None] * freq[None, :]
    cosine = jnp.cos(angle)[:, None, :]
    sine = jnp.sin(angle)[:, None, :]
    first = vectors[..., :half]
    second = vectors[..., half:]
    return jnp.concatenate(
        [first * cosine - second * sine, second * cosine + first * sine], axis=-1
    )


def attend(tokens, qkv_weight, out_weight, norm_attn, keys_cache, values_cache, length):
    rows = tokens.shape[0]
    span = keys_cache.shape[0]
    qwidth = HEADS * HEAD
    kvwidth = KV_HEADS * HEAD
    normed = rms_scale(tokens, norm_attn).astype(jnp.bfloat16)
    mixed = jnp.dot(normed, qkv_weight, preferred_element_type=jnp.float32)
    places = (length + jnp.arange(rows, dtype=jnp.int32)).astype(jnp.float32)
    query = rotate(mixed[:, :qwidth].reshape(rows, HEADS, HEAD), places).astype(jnp.bfloat16)
    key_new = rotate(
        mixed[:, qwidth : qwidth + kvwidth].reshape(rows, KV_HEADS, HEAD), places
    ).astype(jnp.bfloat16)
    value_new = mixed[:, qwidth + kvwidth :].astype(jnp.bfloat16)
    keys = jnp.concatenate([keys_cache, key_new.reshape(rows, kvwidth)], axis=0).reshape(
        span + rows, KV_HEADS, HEAD
    )
    values = jnp.concatenate([values_cache, value_new], axis=0).reshape(span + rows, KV_HEADS, HEAD)
    query = query.reshape(rows, KV_HEADS, HEADS // KV_HEADS, HEAD)
    scores = (
        jnp.einsum("tkgd,skd->kgts", query, keys, preferred_element_type=jnp.float32) * 0.015625
    )
    column = jnp.arange(span + rows, dtype=jnp.int32)[None, :]
    row_index = jnp.arange(rows, dtype=jnp.int32)[:, None]
    valid = jnp.where(column < span, column < length, column - span <= row_index)
    scores = jnp.where(valid[None, None], scores, -1e30)
    top = jnp.max(scores, axis=-1, keepdims=True)
    weights = jnp.exp(scores - top)
    weights = (weights / jnp.sum(weights, axis=-1, keepdims=True)).astype(jnp.bfloat16)
    heads_out = jnp.einsum("kgts,skd->tkgd", weights, values, preferred_element_type=jnp.float32)
    heads_out = heads_out.astype(jnp.bfloat16).reshape(rows, qwidth)
    return jnp.dot(heads_out, out_weight, preferred_element_type=jnp.float32)


def expert_rows(batch, gate_up, down_weight):
    shape = batch.shape
    flat = batch.reshape(-1, shape[-1])
    width = down_weight.shape[0]
    both = jnp.dot(flat, gate_up, preferred_element_type=jnp.float32)
    hidden = (jax.nn.silu(both[:, :width]) * both[:, width:]).astype(jnp.bfloat16)
    part = jnp.dot(hidden, down_weight, preferred_element_type=jnp.float32)
    return part.reshape(shape)


def on_device(
    tokens,
    qkv_weight,
    out_weight,
    norm_attn,
    norm_expert,
    keys_cache,
    values_cache,
    lengths,
    routes,
    gates,
    gate_up,
    down_weight,
):
    branch = attend(
        tokens, qkv_weight, out_weight, norm_attn, keys_cache[0], values_cache[0], lengths[0]
    )
    carried = tokens.astype(jnp.float32) + 0.22 * branch
    normed = rms_scale(carried, norm_expert).astype(jnp.bfloat16)
    rows = tokens.shape[0]
    width = tokens.shape[1]
    capacity = CAPACITY
    groups = lax.axis_size("req")
    slices = groups * lax.axis_size("cuts") // EXPERTS
    chosen = routes.reshape(-1)
    marks = (chosen[:, None] == jnp.arange(EXPERTS, dtype=jnp.int32)[None, :]).astype(jnp.int32)
    before = jnp.cumsum(marks, axis=0) - marks
    slot = jnp.sum(before * marks, axis=1)
    owner = jnp.arange(rows * TOP, dtype=jnp.int32) // TOP
    padded = jnp.concatenate([normed, jnp.zeros((1, width), jnp.bfloat16)], axis=0)
    place = chosen * capacity + slot
    table = jnp.full((EXPERTS * capacity,), rows, jnp.int32).at[place].set(owner)
    outgoing = padded[table]
    outgoing = jnp.repeat(outgoing.reshape(EXPERTS, capacity, width), slices, axis=0)
    part = expert_rows(
        lax.all_to_all(outgoing, ("req", "cuts"), split_axis=0, concat_axis=0, tiled=True),
        gate_up[0],
        down_weight[0],
    )
    partial_value = lax.all_to_all(
        part.astype(jnp.bfloat16), ("req", "cuts"), split_axis=0, concat_axis=0, tiled=True
    ).astype(part.dtype)
    produced = jnp.sum(partial_value.reshape(EXPERTS, slices, capacity, width), axis=1).astype(
        jnp.bfloat16
    )
    results = produced.reshape(EXPERTS * capacity, width)[place]
    weighted = results.astype(jnp.float32) * gates.reshape(-1, 1)
    mix = jnp.sum(weighted.reshape(rows, TOP, width), axis=1)
    return (branch.astype(jnp.bfloat16), mix.astype(jnp.bfloat16))


def solution(mesh):
    placed = (
        P(("req", "cuts"), None),
        P(),
        P(),
        P(),
        P(),
        P(("req", "cuts"), None, None),
        P(("req", "cuts"), None, None),
        P(("req", "cuts")),
        P(("req", "cuts"), None),
        P(("req", "cuts"), None),
        P(("req", "cuts"), None, None),
        P(("req", "cuts"), None, None),
    )
    return jax.shard_map(
        on_device,
        mesh=mesh,
        in_specs=placed,
        out_specs=(P(("req", "cuts"), None), P(("req", "cuts"), None)),
        check_vma=False,
    )
```

profile of v0, /device:TPU:0, one launch (start us, length us, event | category | flops | bytes accessed | tf_op | source)
XLA Modules:
  0.0 393.9 jit_solution(6894874991148504739)
XLA Ops:
  0.7 0.5 multiply_power_fusion
  1.2 1.1 fusion.18
  2.3 3.1 fusion.23
  5.6 0.7 eq.29
  6.4 0.6 broadcast_multiply_fusion
  7.0 0.6 add_select_fusion
  8.2 0.5 add_convert_fusion.2
  8.8 0.2 copy.43
  9.1 0.8 multiply_cosine_fusion
  10.0 4.0 %copy.41 = bf16[1,2048,512]{1,2,0:T(8,128)(2,1)} copy(bf16[1,2048,512]{2,1,0:T(8,128)(2,1)} %param.17) | data formatting | bytes 4194304 | tf_op args[5]
  14.1 4.0 %copy.39 = bf16[1,2048,512]{1,2,0:T(8,128)(2,1)} copy(bf16[1,2048,512]{2,1,0:T(8,128)(2,1)} %param.18) | data formatting | bytes 4194304 | tf_op args[6]
  18.1 1.8 fusion.17
  19.8 10.2 %fusion.10 = f32[8,2176,128,2]{2,1,3,0:T(8,128)} fusion(bf16[128,8,32]{0,2,1:T(8,128)(2,1)S(1)} %get-tuple-element.7, bf16[128,8,32]{0,2,1:T(8,128)(2,1)S(1)} %get-tuple-element.6, bf16[2048,8,64]{0,2,1:T(8,128)(2,1)} %bitcast.81, bf16[128,8,2,32]{0,3,2,1:T(8,128)(2,1)S(1)} %bitcast.87, bf16[128,8,2,32]{0,3,2,1:T(8,128)(2,1)S(1)} %bitcast.86), kind=kOutput, calls=%fused_computation.22 | convolution fusion | flops 577634304 | bytes 20316160 | tf_op jit(solution)/shard_map/tkgd,skd->kgts/dot_general | solution.py:52
  30.1 22.1 %fusion.44 = (f32[8,2,128]{2,1,0:T(2,128)S(1)}, f32[8,2,128,2176]{2,3,1,0:T(8,128)}) fusion(f32[8,2176,128,2]{2,1,3,0:T(8,128)} %fusion.10, pred[128,2176]{0,1:T(8,128)(4,1)S(1)} %fusion.17), kind=kOutput, calls=%fused_computation.88 | output fusion | flops 26740864 | bytes 35938304 | tf_op jit(solution)/shard_map/sub | solution.py:59
  52.1 8.4 %fusion.16 = bf16[8,64,2,128]{3,1,2,0:T(8,128)(2,1)S(1)} fusion(f32[8,2,128,2176]{2,3,1,0:T(8,128)} %get-tuple-element.11, f32[8,2,128]{2,1,0:T(2,128)S(1)} %get-tuple-element.10, bf16[128,8,64]{0,2,1:T(8,128)(2,1)S(1)} %bitcast.90, bf16[2048,8,64]{0,2,1:T(8,128)(2,1)} %bitcast.83), kind=kOutput, calls=%fused_computation.28 | convolution fusion | flops 583925760 | bytes 20324352 | tf_op jit(solution)/shard_map/kgts,skd->tkgd/dot_general | solution.py:61
  60.6 0.6 multiply_reduce_fusion
  61.2 9.0 %reduce-window.6 = s32[32,8,128]{2,1,0:T(8,128)S(1)} reduce-window(s32[32,8,128]{2,1,0:T(8,128)S(1)} %fusion.34, s32[]{:T(128)} %constant.55.clone.1), window={size=1x1x128 pad=0_0x0_0x127_0}, to_apply=%region_4.5 | reduce-window | flops 4161536 | bytes 262148 | tf_op jit(solution)/shard_map/reduce-window
  71.0 4.5 %scatter_custom_fusion = s32[1280]{0:T(1024)S(1)} fusion(s32[1024]{0:T(1024)S(1)} %bitcast.93, s32[1024]{0:T(1024)} %add_select_fusion, s32[]{:T(128)} %constant.53.clone.1), kind=kCustom, calls=%fused_computation.75 | custom fusion | bytes 5632 | tf_op jit(solution)/shard_map/scatter | solution.py:107
  75.5 0.8 multiply_convert_fusion
  76.3 5.3 %gather_fusion = bf16[1280,1024]{1,0:T(8,128)(2,1)} fusion(bf16[129,1024]{1,0:T(8,128)(2,1)S(1)} %concatenate.39, s32[2048]{0:T(1024)S(1)} %pad_clamp_fusion), kind=kCustom, calls=%fused_computation | custom fusion | bytes 5248000 | tf_op jit(solution)/shard_map/gather | solution.py:108
  81.6 7.2 %broadcast_in_dim.40 = bf16[32,4,40,1024]{3,2,1,0:T(8,128)(2,1)} broadcast(bf16[32,40,1024]{2,1,0:T(8,128)(2,1)} %bitcast.80), dimensions={0,2,3} | broadcast | bytes 13107200 | tf_op jit(solution)/shard_map/broadcast_in_dim | solution.py:109
  88.8 131.4 %all_to_all.10 = bf16[128,40,1024]{2,1,0:T(8,128)(2,1)S(1)} all-to-all(bf16[128,40,1024]{2,1,0:T(8,128)(2,1)} %bitcast.78), channel_id=1, replica_groups=mesh['req'=16,'cuts'=8] {'req','cuts'}, dimensions={0} | all-to-all | bytes 20971520 | tf_op jit(solution)/shard_map/all_to_all | solution.py:111
  220.2 2.9 fusion.21
  223.1 0.7 fusion.7
  223.8 0.2 copy-done.3
  224.1 5.4 %convolution_convert_fusion = bf16[128,40,1024]{2,0,1:T(8,128)(2,1)} fusion(bf16[128,40,128]{2,1,0:T(8,128)(2,1)S(1)} %bitcast.82, bf16[1,128,1024]{2,1,0:T(8,128)(2,1)S(1)} %copy-done.3), kind=kOutput, calls=%fused_computation.13 | convolution fusion | flops 1347420160 | bytes 12058624 | tf_op jit(solution)/shard_map/dot_general | solution.py:72
  229.5 13.7 %copy.51 = bf16[128,40,1024]{2,1,0:T(8,128)(2,1)} copy(bf16[128,40,1024]{2,0,1:T(8,128)(2,1)} %convolution_convert_fusion) | data formatting | bytes 20971520 | tf_op jit(solution)/shard_map/convert_element_type | solution.py:116
  243.2 6.3 %all-to-all-start.1 = ((bf16[128,40,1024]{2,1,0:T(8,128)(2,1)}), bf16[128,40,1024]{2,1,0:T(8,128)(2,1)}, u32[]{:S(2)}, u32[]{:S(2)}) async-start(bf16[128,40,1024]{2,1,0:T(8,128)(2,1)} %copy.51), calls=%async_computation.1 | async-start | bytes 20971520 | tf_op jit(solution)/shard_map/all_to_all | solution.py:115
  249.6 123.2 %all-to-all-done.1 = bf16[128,40,1024]{2,1,0:T(8,128)(2,1)} async-done(((bf16[128,40,1024]{2,1,0:T(8,128)(2,1)}), bf16[128,40,1024]{2,1,0:T(8,128)(2,1)}, u32[]{:S(2)}, u32[]{:S(2)}) %all-to-all-start.1) | async-done | bytes 10485792 | tf_op jit(solution)/shard_map/all_to_all | solution.py:115
  372.8 9.1 %bitcast_reduce_fusion = bf16[32,40,1024]{2,1,0:T(8,128)(2,1)} fusion(bf16[128,40,1024]{2,1,0:T(8,128)(2,1)} %all-to-all-done.1), kind=kLoop, calls=%fused_computation.8 | loop fusion | flops 3932160 | bytes 13107200 | tf_op jit(solution)/shard_map/reduce_sum | solution.py:118
  381.9 8.3 %gather_fusion.1 = bf16[1024,1024]{1,0:T(8,128)(2,1)} fusion(bf16[1280,1024]{1,0:T(8,128)(2,1)} %bitcast.77, s32[1024]{0:T(1024)S(1)} %broadcast_clamp_fusion), kind=kCustom, calls=%fused_computation.1 | custom fusion | bytes 4198400 | tf_op jit(solution)/shard_map/gather | solution.py:121
  390.2 3.7 fusion.6
  (48 shorter events, 1.5 us)
Async XLA Ops:
  0.6 60.0 %copy-start = (bf16[1024,1024]{1,0:T(8,128)(2,1)S(1)}, bf16[1024,1024]{1,0:T(8,128)(2,1)}, u32[]{:S(2)}) copy-start(bf16[1024,1024]{1,0:T(8,128)(2,1)} %param.14) | copy-start | bytes 6291460
  0.6 4.8 %copy-start.5 = (s32[128,8]{0,1:T(8,128)S(1)}, s32[128,8]{0,1:T(8,128)}, u32[]{:S(2)}) copy-start(s32[128,8]{0,1:T(8,128)} %param.20) | copy-start | bytes 12292
  52.1 8.5 %copy-start.2 = (bf16[128,1024]{1,0:T(8,128)(2,1)S(1)}, bf16[128,1024]{1,0:T(8,128)(2,1)}, u32[]{:S(2)}) copy-start(bf16[128,1024]{1,0:T(8,128)(2,1)} %param.12) | copy-start | bytes 786436
  52.1 9.1 %copy-start.4 = (s32[8,128]{1,0:T(8,128)S(1)}, s32[8,128]{1,0:T(8,128)}, u32[]{:S(2)}) copy-start(s32[8,128]{1,0:T(8,128)} %eq.29) | copy-start | bytes 12292
  60.6 10.1 %copy-start.6 = (s32[128,8]{0,1:T(8,128)S(1)}, s32[128,8]{0,1:T(8,128)}, u32[]{:S(2)}) copy-start(s32[128,8]{0,1:T(8,128)} %broadcast_multiply_fusion) | copy-start | bytes 12292
  60.6 14.9 %copy-start.7 = (f32[1024]{0:T(1024)S(1)}, f32[1024]{0:T(1024)}, u32[]{:S(2)}) copy-start(f32[1024]{0:T(1024)} %param.16) | copy-start | bytes 12292
  88.8 131.4 %copy-start.9 = (bf16[1,1024,256]{2,1,0:T(8,128)(2,1)S(1)}, bf16[1,1024,256]{2,1,0:T(8,128)(2,1)}, u32[]{:S(2)}) copy-start(bf16[1,1024,256]{2,1,0:T(8,128)(2,1)} %param.22) | copy-start | bytes 1572868
  223.1 1.0 copy-start.3
  243.2 6.3 %copy-start.8 = (f32[128,8]{0,1:T(8,128)S(1)}, f32[128,8]{0,1:T(8,128)}, u32[]{:S(2)}) copy-start(f32[128,8]{0,1:T(8,128)} %param.21) | copy-start | bytes 12292
  243.2 129.6 %all-to-all-start.1 = ((bf16[128,40,1024]{2,1,0:T(8,128)(2,1)}), bf16[128,40,1024]{2,1,0:T(8,128)(2,1)}, u32[]{:S(2)}, u32[]{:S(2)}) async-start(bf16[128,40,1024]{2,1,0:T(8,128)(2,1)} %copy.51), calls=%async_computation.1 | async-start | bytes 20971520 | tf_op jit(solution)/shard_map/all_to_all | solution.py:115
  381.9 11.9 %copy-start.1 = (bf16[1024,1024]{1,0:T(8,128)(2,1)S(1)}, bf16[1024,1024]{1,0:T(8,128)(2,1)}, u32[]{:S(2)}) copy-start(bf16[1024,1024]{1,0:T(8,128)(2,1)} %param.14) | copy-start | bytes 6291460
where the time goes:
time: 401 us; the launch traced here: 394 us
  blocking collectives  131 us (33%)
  waiting for transfers between devices  123 us (31%)
  other arithmetic  51.5 us (13%)
  local copies, waits for them, and re-layouts  49.2 us (12%)
  matrix products  30.6 us (8%)
  starting transfers between devices  6.26 us (2%)
    all_to_all x1, blocking collectives, on_device(): lax.all_to_all(outgoing, ('req', 'cuts'), split_axis=0, concat_axis=0, ti...  131 us
    all_to_all x1, waiting for transfers between devices, on_device(): lax.all_to_all(part.astype(jnp.bfloat16), ('req', 'cuts'), split_axis=0,...  123 us
    sub x1, other arithmetic, attend(): weights = jnp.exp(scores - top)  22.1 us
    convert_element_type x1, local copies, waits for them, and re-layouts, on_device(): part.astype(jnp.bfloat16)  13.7 us
    dot_general x1, matrix products, attend(): jnp.einsum('tkgd,skd->kgts', query, keys, preferred_element_type=jnp.floa...  10.2 us
    another operation x5, other arithmetic  9.26 us
    reduce_sum x1, other arithmetic, on_device(): jnp.sum(partial_value.reshape(EXPERTS, slices, capacity, width), axis=1)  9.09 us
    dot_general x1, matrix products, attend(): jnp.einsum('kgts,skd->tkgd', weights, values, preferred_element_type=jnp....  8.42 us
  transfers between devices with their start and end apart: 1, of which 1 were waited for; matrix products, arithmetic and copies ran while one was open for 0% of the time, Pallas kernels for 0%

commit v1 on v0

--- a/solution.py
+++ b/solution.py
@@ -63,14 +63,13 @@
     return jnp.dot(heads_out, out_weight, preferred_element_type=jnp.float32)
 
 
-def expert_rows(batch, gate_up, down_weight):
-    shape = batch.shape
-    flat = batch.reshape(-1, shape[-1])
-    width = down_weight.shape[0]
-    both = jnp.dot(flat, gate_up, preferred_element_type=jnp.float32)
-    hidden = (jax.nn.silu(both[:, :width]) * both[:, width:]).astype(jnp.bfloat16)
-    part = jnp.dot(hidden, down_weight, preferred_element_type=jnp.float32)
-    return part.reshape(shape)
+def gather_expert(piece, slices):
+    cuts = lax.axis_size("cuts")
+    pieces = [piece]
+    for shift in range(1, slices):
+        pairs = [(i, (i // slices) * slices + (i % slices + shift) % slices) for i in range(cuts)]
+        pieces.append(lax.ppermute(piece, "cuts", pairs))
+    return pieces
 
 
 def on_device(
@@ -87,6 +86,11 @@
     gate_up,
     down_weight,
 ):
+    groups = lax.axis_size("req")
+    slices = groups * lax.axis_size("cuts") // EXPERTS
+    width_dev = down_weight.shape[1]
+    gate_up_all = jnp.concatenate(gather_expert(gate_up[0], slices), axis=1)
+    down_all = jnp.concatenate(gather_expert(down_weight[0], slices), axis=0)
     branch = attend(
         tokens, qkv_weight, out_weight, norm_attn, keys_cache[0], values_cache[0], lengths[0]
     )
@@ -95,32 +99,48 @@
     rows = tokens.shape[0]
     width = tokens.shape[1]
     capacity = CAPACITY
-    groups = lax.axis_size("req")
-    slices = groups * lax.axis_size("cuts") // EXPERTS
-    chosen = routes.reshape(-1)
-    marks = (chosen[:, None] == jnp.arange(EXPERTS, dtype=jnp.int32)[None, :]).astype(jnp.int32)
-    before = jnp.cumsum(marks, axis=0) - marks
-    slot = jnp.sum(before * marks, axis=1)
-    owner = jnp.arange(rows * TOP, dtype=jnp.int32) // TOP
-    padded = jnp.concatenate([normed, jnp.zeros((1, width), jnp.bfloat16)], axis=0)
-    place = chosen * capacity + slot
-    table = jnp.full((EXPERTS * capacity,), rows, jnp.int32).at[place].set(owner)
-    outgoing = padded[table]
-    outgoing = jnp.repeat(outgoing.reshape(EXPERTS, capacity, width), slices, axis=0)
-    part = expert_rows(
-        lax.all_to_all(outgoing, ("req", "cuts"), split_axis=0, concat_axis=0, tiled=True),
-        gate_up[0],
-        down_weight[0],
+    hits = routes[:, :, None] == jnp.arange(EXPERTS, dtype=jnp.int32)[None, None, :]
+    marks = jnp.any(hits, axis=1)
+    weight = jnp.sum(jnp.where(hits, gates[:, :, None], 0.0), axis=1)
+    lower = (
+        jnp.arange(rows, dtype=jnp.int32)[:, None] > jnp.arange(rows, dtype=jnp.int32)[None, :]
+    ).astype(jnp.bfloat16)
+    before = jnp.dot(lower, marks.astype(jnp.bfloat16), preferred_element_type=jnp.float32)
+    slot = before.astype(jnp.int32)
+    taken = marks[:, :, None] & (
+        slot[:, :, None] == jnp.arange(capacity, dtype=jnp.int32)[None, None, :]
     )
-    partial_value = lax.all_to_all(
-        part.astype(jnp.bfloat16), ("req", "cuts"), split_axis=0, concat_axis=0, tiled=True
-    ).astype(part.dtype)
-    produced = jnp.sum(partial_value.reshape(EXPERTS, slices, capacity, width), axis=1).astype(
-        jnp.bfloat16
+    pick = taken.reshape(rows, EXPERTS * capacity)
+    outgoing = jnp.dot(
+        pick.astype(jnp.bfloat16).T, normed, preferred_element_type=jnp.float32
+    ).astype(jnp.bfloat16)
+    received = lax.all_to_all(
+        outgoing.reshape(EXPERTS * slices, capacity // slices, width),
+        ("req", "cuts"),
+        split_axis=0,
+        concat_axis=0,
+        tiled=True,
+    ).reshape(-1, width)
+    both = jnp.dot(received, gate_up_all, preferred_element_type=jnp.float32)
+    both = both.reshape(-1, slices, 2 * width_dev)
+    hidden = (jax.nn.silu(both[..., :width_dev]) * both[..., width_dev:]).astype(jnp.bfloat16)
+    produced = jnp.dot(
+        hidden.reshape(-1, slices * width_dev), down_all, preferred_element_type=jnp.float32
+    ).astype(jnp.bfloat16)
+    results = lax.all_to_all(
+        produced.reshape(EXPERTS * slices, capacity // slices, width),
+        ("req", "cuts"),
+        split_axis=0,
+        concat_axis=0,
+        tiled=True,
+    ).reshape(EXPERTS * capacity, width)
+    scale = jnp.where(pick, jnp.repeat(weight, capacity, axis=1), 0.0)
+    mix = jnp.dot(
+        scale,
+        results.astype(jnp.float32),
+        precision=lax.Precision.HIGHEST,
+        preferred_element_type=jnp.float32,
     )
-    results = produced.reshape(EXPERTS * capacity, width)[place]
-    weighted = results.astype(jnp.float32) * gates.reshape(-1, 1)
-    mix = jnp.sum(weighted.reshape(rows, TOP, width), axis=1)
     return (branch.astype(jnp.bfloat16), mix.astype(jnp.bfloat16))
 
 

time: 401 us -> 251 us (0.63); the launches traced: 394 us -> 249 us
  blocking collectives: 131 us -> 0 us
  other arithmetic: 51.5 us -> 29.4 us
  starting transfers between devices: 6.26 us -> 27.1 us
  local copies, waits for them, and re-layouts: 49.2 us -> 36.8 us
  matrix products: 30.6 us -> 38.5 us
  waiting for transfers between devices: 123 us -> 116 us
    all_to_all x1 -> x0, blocking collectives: 131 us -> none  [on_device(): lax.all_to_all(outgoing, ('req', 'cuts'), split_axis=0, concat_axis=0, ti...]
    all_to_all x1 -> x2, waiting for transfers between devices: 123 us -> 52.2 us  [the longest x1 52.2 us: on_device(): lax.all_to_all(produced.reshape(EXPERTS * slices, capacity // slices, wid...]
    ppermute x0 -> x6, waiting for transfers between devices: none -> 63.6 us  [gather_expert(): pieces.append(lax.ppermute(piece, 'cuts', pairs))]
    reshape x0 -> x4, local copies, waits for them, and re-layouts: none -> 24.3 us  [the longest x1 6.14 us: on_device(): received = lax.all_to_all(outgoing.reshape(EXPERTS * slices, capacity //...]
    all_to_all x1 -> x2, starting transfers between devices: 6.26 us -> 23.5 us  [the longest x1 11.8 us: on_device(): lax.all_to_all(produced.reshape(EXPERTS * slices, capacity // slices, wid...]
    convert_element_type x1 -> x0, local copies, waits for them, and re-layouts: 13.7 us -> none  [on_device(): part.astype(jnp.bfloat16)]
    gather x2 -> x0, local copies, waits for them, and re-layouts: 13.6 us -> none  [the longest x1 8.26 us: on_device(): results = produced.reshape(EXPERTS * capacity, width)[place]]
    reduce_sum x3 -> x1, other arithmetic: 12.8 us -> 0.02 us  [on_device(): weight = jnp.sum(jnp.where(hits, gates[:, :, None], 0.0), axis=1)]
  transfers between devices with their start and end apart: 1 -> 8, of which waited for: 1 -> 4; matrix products, arithmetic and copies ran while one was open for 0% -> 7% of each run, Pallas kernels for 0% -> 0%
where the time goes in v1:
time: 251 us; the launch traced here: 249 us
  waiting for transfers between devices  116 us (46%)
  matrix products  38.5 us (15%)
  local copies, waits for them, and re-layouts  36.8 us (15%)
  other arithmetic  29.4 us (12%)
  starting transfers between devices  27.1 us (11%)
    ppermute x6, waiting for transfers between devices, gather_expert(): pieces.append(lax.ppermute(piece, 'cuts', pairs))  63.6 us
    all_to_all x1, waiting for transfers between devices, on_device(): lax.all_to_all(produced.reshape(EXPERTS * slices, capacity // slices, wid...  52.2 us
    sub x1, other arithmetic, attend(): weights = jnp.exp(scores - top)  22.1 us
    all_to_all x1, starting transfers between devices, on_device(): lax.all_to_all(produced.reshape(EXPERTS * slices, capacity // slices, wid...  11.8 us
    all_to_all x1, starting transfers between devices, on_device(): lax.all_to_all(outgoing.reshape(EXPERTS * slices, capacity // slices, wid...  11.7 us
    dot_general x1, matrix products, attend(): jnp.einsum('tkgd,skd->kgts', query, keys, preferred_element_type=jnp.floa...  10.2 us
    dot_general x1, matrix products, attend(): jnp.einsum('kgts,skd->tkgd', weights, values, preferred_element_type=jnp....  8.42 us
    unnamed x16, local copies, waits for them, and re-layouts  7.96 us
  transfers between devices with their start and end apart: 8, of which 4 were waited for; matrix products, arithmetic and copies ran while one was open for 7% of the time, Pallas kernels for 0%

profile of v1, /device:TPU:0, one launch (start us, length us, event | category | flops | bytes accessed | tf_op | source)
XLA Modules:
  0.0 249.1 jit_solution(6828179019275281886)
XLA Ops:
  0.7 1.2 fusion.26
  1.9 3.1 %fusion.29 = f32[128,2048]{1,0:T(8,128)S(1)} fusion(bf16[1024,2048]{1,0:T(8,128)(2,1)} %param.13, bf16[128,1024]{1,0:T(8,128)(2,1)} %param.12, f32[1024]{0:T(1024)} %param.15, f32[128]{0:T(128)S(1)} %add_rsqrt_fusion.1), kind=kOutput, calls=%fused_computation.48 | convolution fusion | flops 537395200 | bytes 5509632 | tf_op jit(solution)/shard_map/dot_general | solution.py:39
  5.7 0.5 add_convert_fusion.2
  6.6 0.8 multiply_cosine_fusion
  7.5 4.0 %copy.39 = bf16[1,2048,512]{1,2,0:T(8,128)(2,1)} copy(bf16[1,2048,512]{2,1,0:T(8,128)(2,1)} %param.17) | data formatting | bytes 4194304 | tf_op args[5]
  11.6 4.0 %copy.37 = bf16[1,2048,512]{1,2,0:T(8,128)(2,1)} copy(bf16[1,2048,512]{2,1,0:T(8,128)(2,1)} %param.18) | data formatting | bytes 4194304 | tf_op args[6]
  15.6 1.8 fusion.15
  17.3 10.2 %fusion.9 = f32[8,2176,128,2]{2,1,3,0:T(8,128)} fusion(bf16[128,8,32]{0,2,1:T(8,128)(2,1)S(1)} %get-tuple-element.7, bf16[128,8,32]{0,2,1:T(8,128)(2,1)S(1)} %get-tuple-element.6, bf16[2048,8,64]{0,2,1:T(8,128)(2,1)} %bitcast.59, bf16[128,8,2,32]{0,3,2,1:T(8,128)(2,1)S(1)} %bitcast.67, bf16[128,8,2,32]{0,3,2,1:T(8,128)(2,1)S(1)} %bitcast.66), kind=kOutput, calls=%fused_computation.17 | convolution fusion | flops 577634304 | bytes 20316160 | tf_op jit(solution)/shard_map/tkgd,skd->kgts/dot_general | solution.py:52
  27.5 22.1 %fusion.46 = (f32[8,2,128]{2,1,0:T(2,128)S(1)}, f32[8,2,128,2176]{2,3,1,0:T(8,128)}) fusion(f32[8,2176,128,2]{2,1,3,0:T(8,128)} %fusion.9, pred[128,2176]{0,1:T(8,128)(4,1)S(1)} %fusion.15), kind=kOutput, calls=%fused_computation.81 | output fusion | flops 26740864 | bytes 35938304 | tf_op jit(solution)/shard_map/sub | solution.py:59
  49.7 8.4 %fusion.14 = bf16[8,64,2,128]{3,1,2,0:T(8,128)(2,1)S(1)} fusion(f32[8,2,128,2176]{2,3,1,0:T(8,128)} %get-tuple-element.11, f32[8,2,128]{2,1,0:T(2,128)S(1)} %get-tuple-element.10, bf16[128,8,64]{0,2,1:T(8,128)(2,1)S(1)} %bitcast.73, bf16[2048,8,64]{0,2,1:T(8,128)(2,1)} %bitcast.61), kind=kOutput, calls=%fused_computation.24 | convolution fusion | flops 583925760 | bytes 20324352 | tf_op jit(solution)/shard_map/kgts,skd->tkgd/dot_general | solution.py:61
  58.1 1.2 multiply_reduce_fusion
  59.6 0.2 fusion.25
  59.9 2.4 convolution_convert_fusion.1
  62.3 6.0 %reshape.235 = bf16[128,10,1024]{2,1,0:T(8,128)(2,1)} reshape(bf16[1280,1024]{1,0:T(8,128)(2,1)} %convolution_convert_fusion.1) | data formatting | bytes 5242880 | tf_op jit(solution)/shard_map/reshape | solution.py:118
  68.3 11.7 %all-to-all-start = ((bf16[128,10,1024]{2,1,0:T(8,128)(2,1)}), bf16[128,10,1024]{2,1,0:T(8,128)(2,1)}, u32[]{:S(2)}, u32[]{:S(2)}) async-start(bf16[128,10,1024]{2,1,0:T(8,128)(2,1)} %reshape.235), calls=%async_computation | async-start | bytes 8388608 | tf_op jit(solution)/shard_map/all_to_all | solution.py:117
  80.1 1.1 collective-permute-start.1
  81.3 1.2 collective-permute-start.2
  82.5 1.1 collective-permute-start.4
  83.6 52.7 %collective-permute-done = bf16[1024,256]{1,0:T(8,128)(2,1)S(1)} collective-permute-done((bf16[1024,256]{1,0:T(8,128)(2,1)S(1)}, bf16[1024,256]{1,0:T(8,128)(2,1)S(1)}, u32[]{:S(2)}, u32[]{:S(2)}) %collective-permute-start) | collective-permute-done | bytes 524320 | tf_op jit(solution)/shard_map/ppermute | solution.py:71
  136.4 1.1 collective-permute-done.1
  137.5 9.7 %collective-permute-done.2 = bf16[1024,256]{1,0:T(8,128)(2,1)S(1)} collective-permute-done((bf16[1024,256]{1,0:T(8,128)(2,1)S(1)}, bf16[1024,256]{1,0:T(8,128)(2,1)S(1)}, u32[]{:S(2)}, u32[]{:S(2)}) %collective-permute-start.2) | collective-permute-done | bytes 524320 | tf_op jit(solution)/shard_map/ppermute | solution.py:71
  147.2 1.6 maximum_bitcast_fusion.4
  148.8 3.9 %copy.43 = bf16[1024,1024]{1,0:T(8,128)(2,1)} copy(bf16[1024,1024]{0,1:T(8,128)(2,1)} %maximum_bitcast_fusion.4) | data formatting | bytes 4194304 | tf_op jit(solution)/shard_map/dot_general | solution.py:124
  152.7 6.1 %reshape.242 = bf16[1280,1024,1]{1,0,2:T(8,128)(2,1)} reshape(bf16[128,10,1024]{2,1,0:T(8,128)(2,1)} %all-to-all-done) | data formatting | bytes 5242880 | tf_op jit(solution)/shard_map/reshape | solution.py:123
  158.9 5.3 %fusion.47 = f32[1280,4,256]{0,2,1:T(8,128)S(1)} fusion(bf16[1280,1024,1]{1,0,2:T(8,128)(2,1)} %reshape.242, bf16[4,256,1024]{2,1,0:T(8,128)(2,1)} %bitcast.62), kind=kOutput, calls=%fused_computation.82 | convolution fusion | flops 2684354560 | bytes 9961472 | tf_op jit(solution)/shard_map/dot_general | solution.py:124
  164.2 0.8 fusion.6
  165.0 4.0 %convolution_convert_fusion = bf16[1280,1024]{1,0:T(8,128)(2,1)} fusion(bf16[1280,512]{0,1:T(8,128)(2,1)S(1)} %bitcast.64, bf16[128,1024]{1,0:T(8,128)(2,1)} %collective-permute-done.5, bf16[128,1024]{1,0:T(8,128)(2,1)S(1)} %collective-permute-done.4, bf16[128,1024]{1,0:T(8,128)(2,1)S(1)} %collective-permute-done.3, bf16[128,1024]{1,0:T(8,128)(2,1)S(1)} %bitcast.77), kind=kOutput, calls=%fused_computation.9 | convolution fusion | flops 1347682304 | bytes 4980736 | tf_op jit(solution)/shard_map/dot_general | solution.py:127
  169.0 6.0 %reshape.238 = bf16[128,10,1024]{2,1,0:T(8,128)(2,1)} reshape(bf16[1280,1024]{1,0:T(8,128)(2,1)} %convolution_convert_fusion) | data formatting | bytes 5242880 | tf_op jit(solution)/shard_map/reshape | solution.py:131
  175.0 11.8 %all-to-all-start.1 = ((bf16[128,10,1024]{2,1,0:T(8,128)(2,1)}), bf16[128,10,1024]{2,1,0:T(8,128)(2,1)}, u32[]{:S(2)}, u32[]{:S(2)}) async-start(bf16[128,10,1024]{2,1,0:T(8,128)(2,1)} %reshape.238), calls=%async_computation.1 | async-start | bytes 8388608 | tf_op jit(solution)/shard_map/all_to_all | solution.py:130
  187.0 52.2 %all-to-all-done.1 = bf16[128,10,1024]{2,1,0:T(8,128)(2,1)} async-done(((bf16[128,10,1024]{2,1,0:T(8,128)(2,1)}), bf16[128,10,1024]{2,1,0:T(8,128)(2,1)}, u32[]{:S(2)}, u32[]{:S(2)}) %all-to-all-start.1) | async-done | bytes 2621472 | tf_op jit(solution)/shard_map/all_to_all | solution.py:130
  239.2 6.1 %reshape.239 = bf16[1280,1024]{1,0:T(8,128)(2,1)} reshape(bf16[128,10,1024]{2,1,0:T(8,128)(2,1)} %all-to-all-done.1) | data formatting | bytes 5242880 | tf_op jit(solution)/shard_map/reshape | solution.py:136
  245.3 3.8 %convolution_convert_fusion.2 = bf16[128,1024]{1,0:T(8,128)(2,1)} fusion(f32[128,1280]{0,1:T(8,128)S(1)} %bitcast.60, bf16[1280,1024]{1,0:T(8,128)(2,1)} %reshape.239), kind=kOutput, calls=%fused_computation.23 | convolution fusion | flops 2013396992 | bytes 3538944 | tf_op jit(solution)/shard_map/dot_general | solution.py:138
  (40 shorter events, 1.2 us)
Async XLA Ops:
  0.6 57.5 %copy-start = (bf16[1024,1024]{1,0:T(8,128)(2,1)S(1)}, bf16[1024,1024]{1,0:T(8,128)(2,1)}, u32[]{:S(2)}) copy-start(bf16[1024,1024]{1,0:T(8,128)(2,1)} %param.14) | copy-start | bytes 6291460
  49.7 8.5 %copy-start.1 = (bf16[128,1024]{1,0:T(8,128)(2,1)S(1)}, bf16[128,1024]{1,0:T(8,128)(2,1)}, u32[]{:S(2)}) copy-start(bf16[128,1024]{1,0:T(8,128)(2,1)} %param.12) | copy-start | bytes 786436
  58.1 1.3 copy-start.3
  58.1 1.8 copy-start.4
  68.3 11.7 %copy-start.2 = (bf16[1,1024,256]{2,1,0:T(8,128)(2,1)S(1)}, bf16[1,1024,256]{2,1,0:T(8,128)(2,1)}, u32[]{:S(2)}) copy-start(bf16[1,1024,256]{2,1,0:T(8,128)(2,1)} %param.22) | copy-start | bytes 1572868
  68.3 14.2 %copy-start.6 = (bf16[1,128,1024]{2,1,0:T(8,128)(2,1)S(1)}, bf16[1,128,1024]{2,1,0:T(8,128)(2,1)}, u32[]{:S(2)}) copy-start(bf16[1,128,1024]{2,1,0:T(8,128)(2,1)} %param.23) | copy-start | bytes 786436
  68.3 84.4 %all-to-all-start = ((bf16[128,10,1024]{2,1,0:T(8,128)(2,1)}), bf16[128,10,1024]{2,1,0:T(8,128)(2,1)}, u32[]{:S(2)}, u32[]{:S(2)}) async-start(bf16[128,10,1024]{2,1,0:T(8,128)(2,1)} %reshape.235), calls=%async_computation | async-start | bytes 8388608 | tf_op jit(solution)/shard_map/all_to_all | solution.py:117
  80.0 56.3 %collective-permute-start = (bf16[1024,256]{1,0:T(8,128)(2,1)S(1)}, bf16[1024,256]{1,0:T(8,128)(2,1)S(1)}, u32[]{:S(2)}, u32[]{:S(2)}) collective-permute-start(bf16[1024,256]{1,0:T(8,128)(2,1)S(1)} %bitcast.68), channel_id=1, source_target_pairs={{0,1},{1,2},{2,3},{3,0},{4,5},{5,6},{6,7},{7,4},{8,9},{9,10},{10,1... | collective-permute-start | bytes 1572872 | tf_op jit(solution)/shard_map/ppermute | solution.py:71
  80.1 57.4 %collective-permute-start.1 = (bf16[1024,256]{1,0:T(8,128)(2,1)S(1)}, bf16[1024,256]{1,0:T(8,128)(2,1)S(1)}, u32[]{:S(2)}, u32[]{:S(2)}) collective-permute-start(bf16[1024,256]{1,0:T(8,128)(2,1)S(1)} %bitcast.69), channel_id=1, source_target_pairs={{0,2},{1,3},{2,0},{3,1},{4,6},{5,7},{6,4},{7,5},{8,10},{9,11},{10,... | collective-permute-start | bytes 1572872 | tf_op jit(solution)/shard_map/ppermute | solution.py:71
  81.3 65.9 %collective-permute-start.2 = (bf16[1024,256]{1,0:T(8,128)(2,1)S(1)}, bf16[1024,256]{1,0:T(8,128)(2,1)S(1)}, u32[]{:S(2)}, u32[]{:S(2)}) collective-permute-start(bf16[1024,256]{1,0:T(8,128)(2,1)S(1)} %bitcast.70), channel_id=1, source_target_pairs={{0,3},{1,0},{2,1},{3,2},{4,7},{5,4},{6,5},{7,6},{8,11},{9,8},{10,9... | collective-permute-start | bytes 1572872 | tf_op jit(solution)/shard_map/ppermute | solution.py:71
  82.5 82.5 %collective-permute-start.3 = (bf16[128,1024]{1,0:T(8,128)(2,1)S(1)}, bf16[128,1024]{1,0:T(8,128)(2,1)S(1)}, u32[]{:S(2)}, u32[]{:S(2)}) collective-permute-start(bf16[128,1024]{1,0:T(8,128)(2,1)S(1)} %bitcast.74), channel_id=1, source_target_pairs={{0,1},{1,2},{2,3},{3,0},{4,5},{5,6},{6,7},{7,4},{8,9},{9,10},{10,1... | collective-permute-start | bytes 786440 | tf_op jit(solution)/shard_map/ppermute | solution.py:71
  82.5 82.5 %collective-permute-start.4 = (bf16[128,1024]{1,0:T(8,128)(2,1)S(1)}, bf16[128,1024]{1,0:T(8,128)(2,1)S(1)}, u32[]{:S(2)}, u32[]{:S(2)}) collective-permute-start(bf16[128,1024]{1,0:T(8,128)(2,1)S(1)} %bitcast.75), channel_id=1, source_target_pairs={{0,2},{1,3},{2,0},{3,1},{4,6},{5,7},{6,4},{7,5},{8,10},{9,11},{10,... | collective-permute-start | bytes 786440 | tf_op jit(solution)/shard_map/ppermute | solution.py:71
  136.4 28.6 %collective-permute-start.5 = (bf16[128,1024]{1,0:T(8,128)(2,1)S(1)}, bf16[128,1024]{1,0:T(8,128)(2,1)}, u32[]{:S(2)}, u32[]{:S(2)}) collective-permute-start(bf16[128,1024]{1,0:T(8,128)(2,1)S(1)} %bitcast.76), channel_id=1, source_target_pairs={{0,3},{1,0},{2,1},{3,2},{4,7},{5,4},{6,5},{7,6},{8,11},{9,8},{10,9... | collective-permute-start | bytes 786440 | tf_op jit(solution)/shard_map/ppermute | solution.py:71
  175.0 11.8 %copy-start.5 = (f32[128,8]{0,1:T(8,128)S(1)}, f32[128,8]{0,1:T(8,128)}, u32[]{:S(2)}) copy-start(f32[128,8]{0,1:T(8,128)} %param.21) | copy-start | bytes 12292
  175.0 64.2 %all-to-all-start.1 = ((bf16[128,10,1024]{2,1,0:T(8,128)(2,1)}), bf16[128,10,1024]{2,1,0:T(8,128)(2,1)}, u32[]{:S(2)}, u32[]{:S(2)}) async-start(bf16[128,10,1024]{2,1,0:T(8,128)(2,1)} %reshape.238), calls=%async_computation.1 | async-start | bytes 8388608 | tf_op jit(solution)/shard_map/all_to_all | solution.py:130

commit v2 on v1

--- a/solution.py
+++ b/solution.py
@@ -63,15 +63,6 @@
     return jnp.dot(heads_out, out_weight, preferred_element_type=jnp.float32)
 
 
-def gather_expert(piece, slices):
-    cuts = lax.axis_size("cuts")
-    pieces = [piece]
-    for shift in range(1, slices):
-        pairs = [(i, (i // slices) * slices + (i % slices + shift) % slices) for i in range(cuts)]
-        pieces.append(lax.ppermute(piece, "cuts", pairs))
-    return pieces
-
-
 def on_device(
     tokens,
     qkv_weight,
@@ -86,18 +77,16 @@
     gate_up,
     down_weight,
 ):
-    groups = lax.axis_size("req")
-    slices = groups * lax.axis_size("cuts") // EXPERTS
+    slices = lax.axis_size("q")
     width_dev = down_weight.shape[1]
-    gate_up_all = jnp.concatenate(gather_expert(gate_up[0], slices), axis=1)
-    down_all = jnp.concatenate(gather_expert(down_weight[0], slices), axis=0)
+    gate_up_all = lax.all_gather(gate_up[0], "q", axis=1, tiled=True)
+    down_all = lax.all_gather(down_weight[0], "q", axis=0, tiled=True)
     branch = attend(
         tokens, qkv_weight, out_weight, norm_attn, keys_cache[0], values_cache[0], lengths[0]
     )
     carried = tokens.astype(jnp.float32) + 0.22 * branch
     normed = rms_scale(carried, norm_expert).astype(jnp.bfloat16)
     rows = tokens.shape[0]
-    width = tokens.shape[1]
     capacity = CAPACITY
     hits = routes[:, :, None] == jnp.arange(EXPERTS, dtype=jnp.int32)[None, None, :]
     marks = jnp.any(hits, axis=1)
@@ -107,35 +96,24 @@
     ).astype(jnp.bfloat16)
     before = jnp.dot(lower, marks.astype(jnp.bfloat16), preferred_element_type=jnp.float32)
     slot = before.astype(jnp.int32)
-    taken = marks[:, :, None] & (
+    pick = marks[:, :, None] & (
         slot[:, :, None] == jnp.arange(capacity, dtype=jnp.int32)[None, None, :]
     )
-    pick = taken.reshape(rows, EXPERTS * capacity)
-    outgoing = jnp.dot(
-        pick.astype(jnp.bfloat16).T, normed, preferred_element_type=jnp.float32
+    outgoing = jnp.einsum(
+        "tec,tw->ecw", pick.astype(jnp.bfloat16), normed, preferred_element_type=jnp.float32
     ).astype(jnp.bfloat16)
-    received = lax.all_to_all(
-        outgoing.reshape(EXPERTS * slices, capacity // slices, width),
-        ("req", "cuts"),
-        split_axis=0,
-        concat_axis=0,
-        tiled=True,
-    ).reshape(-1, width)
-    both = jnp.dot(received, gate_up_all, preferred_element_type=jnp.float32)
-    both = both.reshape(-1, slices, 2 * width_dev)
+    received = lax.all_to_all(outgoing, ("req", "h"), split_axis=0, concat_axis=0, tiled=True)
+    both = jnp.einsum("scw,wh->sch", received, gate_up_all, preferred_element_type=jnp.float32)
+    both = both.reshape(both.shape[0], both.shape[1], slices, 2 * width_dev)
     hidden = (jax.nn.silu(both[..., :width_dev]) * both[..., width_dev:]).astype(jnp.bfloat16)
-    produced = jnp.dot(
-        hidden.reshape(-1, slices * width_dev), down_all, preferred_element_type=jnp.float32
+    hidden = hidden.reshape(both.shape[0], both.shape[1], slices * width_dev)
+    produced = jnp.einsum(
+        "sch,hw->scw", hidden, down_all, preferred_element_type=jnp.float32
     ).astype(jnp.bfloat16)
-    results = lax.all_to_all(
-        produced.reshape(EXPERTS * slices, capacity // slices, width),
-        ("req", "cuts"),
-        split_axis=0,
-        concat_axis=0,
-        tiled=True,
-    ).reshape(EXPERTS * capacity, width)
-    scale = jnp.where(pick, jnp.repeat(weight, capacity, axis=1), 0.0)
-    mix = jnp.dot(
+    results = lax.all_to_all(produced, ("req", "h"), split_axis=0, concat_axis=0, tiled=True)
+    scale = jnp.where(pick, weight[:, :, None], 0.0)
+    mix = jnp.einsum(
+        "tec,ecw->tw",
         scale,
         results.astype(jnp.float32),
         precision=lax.Precision.HIGHEST,
@@ -145,24 +123,30 @@
 
 
 def solution(mesh):
+    groups = mesh.shape["req"]
+    slices = groups * mesh.shape["cuts"] // EXPERTS
+    split = jax.sharding.Mesh(
+        mesh.devices.reshape(groups, mesh.shape["cuts"] // slices, slices), ("req", "h", "q")
+    )
+    rows = ("req", "h", "q")
     placed = (
-        P(("req", "cuts"), None),
+        P(rows, None),
         P(),
         P(),
         P(),
         P(),
-        P(("req", "cuts"), None, None),
-        P(("req", "cuts"), None, None),
-        P(("req", "cuts")),
-        P(("req", "cuts"), None),
-        P(("req", "cuts"), None),
-        P(("req", "cuts"), None, None),
-        P(("req", "cuts"), None, None),
+        P(rows, None, None),
+        P(rows, None, None),
+        P(rows),
+        P(rows, None),
+        P(rows, None),
+        P(rows, None, None),
+        P(rows, None, None),
     )
     return jax.shard_map(
         on_device,
-        mesh=mesh,
+        mesh=split,
         in_specs=placed,
-        out_specs=(P(("req", "cuts"), None), P(("req", "cuts"), None)),
+        out_specs=(P(rows, None), P(rows, None)),
         check_vma=False,
     )

time: 251 us -> 201 us (0.80)
  waiting for transfers between devices: 116 us -> 80.3 us
  local copies, waits for them, and re-layouts: 36.8 us -> 17.4 us
  between operations: 1.55 us -> 14.9 us
  starting transfers between devices: 27.1 us -> 16.3 us
  matrix products: 38.5 us -> 41.6 us
    ppermute x6 -> x0, waiting for transfers between devices: 63.6 us -> none  [gather_expert(): pieces.append(lax.ppermute(piece, 'cuts', pairs))]
    all_to_all x2, waiting for transfers between devices: 52.2 us -> 78.9 us  [the longest x1 43.9 us: on_device(): lax.all_to_all(outgoing, ('req', 'h'), split_axis=0, concat_axis=0, tiled...]
    reshape x4 -> x2, local copies, waits for them, and re-layouts: 24.3 us -> 8.94 us  [the longest x1 7.57 us: on_device(): both = both.reshape(both.shape[0], both.shape[1], slices, 2 * width_dev)]
    all_to_all x2, starting transfers between devices: 23.5 us -> 16.2 us  [the longest x1 11.3 us: on_device(): lax.all_to_all(outgoing, ('req', 'h'), split_axis=0, concat_axis=0, tiled...]
    dot_general x1 -> x0, local copies, waits for them, and re-layouts: 3.92 us -> none  [on_device(): both = jnp.dot(received, gate_up_all, preferred_element_type=jnp.float32)]
    ppermute x6 -> x0, starting transfers between devices: 3.56 us -> none  [gather_expert(): pieces.append(lax.ppermute(piece, 'cuts', pairs))]
    dot_general x4, matrix products: 15.5 us -> 18.5 us  [the longest x1 7.57 us: on_device(): jnp.einsum('scw,wh->sch', received, gate_up_all, preferred_element_type=j...]
    unnamed x16 -> x12, local copies, waits for them, and re-layouts: 7.96 us -> 7.97 us
  transfers between devices with their start and end apart: 8 -> 4, of which waited for: 4 -> 2; matrix products, arithmetic and copies ran while one was open for 7% -> 40% of each run, Pallas kernels for 0% -> 0%
where the time goes in v2:
time: 201 us; the launch traced here: 200 us
  waiting for transfers between devices  80.3 us (40%)
  matrix products  41.6 us (21%)
  other arithmetic  29.6 us (15%)
  local copies, waits for them, and re-layouts  17.4 us (9%)
  starting transfers between devices  16.3 us (8%)
  between operations  14.9 us (7%)
    all_to_all x1, waiting for transfers between devices, on_device(): lax.all_to_all(outgoing, ('req', 'h'), split_axis=0, concat_axis=0, tiled...  43.9 us
    all_to_all x1, waiting for transfers between devices, on_device(): lax.all_to_all(produced, ('req', 'h'), split_axis=0, concat_axis=0, tiled...  35 us
    sub x1, other arithmetic, attend(): weights = jnp.exp(scores - top)  22.1 us
    all_to_all x1, starting transfers between devices, on_device(): lax.all_to_all(outgoing, ('req', 'h'), split_axis=0, concat_axis=0, tiled...  11.3 us
    dot_general x1, matrix products, attend(): jnp.einsum('tkgd,skd->kgts', query, keys, preferred_element_type=jnp.floa...  10.2 us
    dot_general x1, matrix products, attend(): jnp.einsum('kgts,skd->tkgd', weights, values, preferred_element_type=jnp....  8.42 us
    unnamed x12, local copies, waits for them, and re-layouts  7.97 us
    dot_general x1, matrix products, on_device(): jnp.einsum('scw,wh->sch', received, gate_up_all, preferred_element_type=j...  7.57 us
  transfers between devices with their start and end apart: 4, of which 2 were waited for; matrix products, arithmetic and copies ran while one was open for 40% of the time, Pallas kernels for 0%

profile of v2, /device:TPU:0, one launch (start us, length us, event | category | flops | bytes accessed | tf_op | source)
XLA Modules:
  0.0 200.0 jit_solution(516659859862887635)
XLA Ops:
  7.2 0.0 copy-start
  7.2 0.0 all-gather.5.cloned.1.call-start
  7.2 0.7 all-gather.5.cloned.1.call-update
  7.9 1.1 fusion.25
  9.0 3.1 %fusion.36 = f32[128,2048]{1,0:T(8,128)S(1)} fusion(bf16[1024,2048]{1,0:T(8,128)(2,1)} %param.13, bf16[128,1024]{1,0:T(8,128)(2,1)} %param.12, f32[1024]{0:T(1024)} %param.15, f32[128]{0:T(128)S(1)} %add_rsqrt_fusion.1), kind=kOutput, calls=%fused_computation.50 | convolution fusion | flops 537395200 | bytes 5509632 | tf_op jit(solution)/shard_map/dot_general | solution.py:39
  12.9 0.5 add_convert_fusion.2
  13.4 0.2 copy.38
  13.6 0.1 copy.37
  13.7 0.8 multiply_cosine_fusion
  14.5 0.1 subtract_convert_fusion
  14.6 3.9 %copy.36 = bf16[1,2048,512]{1,2,0:T(8,128)(2,1)} copy(bf16[1,2048,512]{2,1,0:T(8,128)(2,1)} %param.17) | data formatting | bytes 4194304 | tf_op args[5]
  18.6 0.1 copy.35
  18.7 4.0 %copy.34 = bf16[1,2048,512]{1,2,0:T(8,128)(2,1)} copy(bf16[1,2048,512]{2,1,0:T(8,128)(2,1)} %param.18) | data formatting | bytes 4194304 | tf_op args[6]
  22.7 1.8 fusion.19
  24.5 10.2 %fusion.10 = f32[8,2176,128,2]{2,1,3,0:T(8,128)} fusion(bf16[128,8,32]{0,2,1:T(8,128)(2,1)S(1)} %get-tuple-element.7, bf16[128,8,32]{0,2,1:T(8,128)(2,1)S(1)} %get-tuple-element.6, bf16[2048,8,64]{0,2,1:T(8,128)(2,1)} %bitcast.58, bf16[128,8,2,32]{0,3,2,1:T(8,128)(2,1)S(1)} %bitcast.63, bf16[128,8,2,32]{0,3,2,1:T(8,128)(2,1)S(1)} %bitcast.62), kind=kOutput, calls=%fused_computation.16 | convolution fusion | flops 577634304 | bytes 20316160 | tf_op jit(solution)/shard_map/tkgd,skd->kgts/dot_general | solution.py:52
  34.7 22.1 %fusion.53 = (f32[8,2,128]{2,1,0:T(2,128)S(1)}, f32[8,2,128,2176]{2,3,1,0:T(8,128)}) fusion(f32[8,2176,128,2]{2,1,3,0:T(8,128)} %fusion.10, pred[128,2176]{0,1:T(8,128)(4,1)S(1)} %fusion.19), kind=kOutput, calls=%fused_computation.83 | output fusion | flops 26740864 | bytes 35938304 | tf_op jit(solution)/shard_map/sub | solution.py:59
  56.8 8.4 %fusion.18 = bf16[8,64,2,128]{3,1,2,0:T(8,128)(2,1)S(1)} fusion(f32[8,2,128,2176]{2,3,1,0:T(8,128)} %get-tuple-element.11, f32[8,2,128]{2,1,0:T(2,128)S(1)} %get-tuple-element.10, bf16[128,8,64]{0,2,1:T(8,128)(2,1)S(1)} %bitcast.65, bf16[2048,8,64]{0,2,1:T(8,128)(2,1)} %bitcast.59), kind=kOutput, calls=%fused_computation.27 | convolution fusion | flops 583925760 | bytes 20324352 | tf_op jit(solution)/shard_map/kgts,skd->tkgd/dot_general | solution.py:61
  65.3 1.2 multiply_reduce_fusion
  66.5 0.1 convolution_convert_fusion.2
  66.6 2.4 %convolution_convert_fusion.1 = bf16[32,40,1024]{2,1,0:T(8,128)(2,1)} fusion(s32[128,32]{0,1:T(8,128)S(1)} %convolution_convert_fusion.2, pred[128,32]{0,1:T(8,128)(4,1)S(1)} %fusion.46, f32[128,1024]{1,0:T(8,128)S(1)} %get-tuple-element.12, bf16[128,1024]{1,0:T(8,128)(2,1)S(1)} %copy-done.1, f32[1024]{0:T(1024)S(1)} %copy-done.3, f32[128]{0:T(128)S(1)} %add_rsqrt_fusion), kind=kOutput, calls=%fused_computation.24 | convolution fusion | flops 337969152 | bytes 3432960 | tf_op jit(solution)/shard_map/tec,tw->ecw/dot_general | solution.py:102
  69.1 11.3 %all-to-all-start = ((bf16[32,40,1024]{2,1,0:T(8,128)(2,1)}), bf16[32,40,1024]{2,1,0:T(8,128)(2,1)}, u32[]{:S(2)}, u32[]{:S(2)}) async-start(bf16[32,40,1024]{2,1,0:T(8,128)(2,1)} %convolution_convert_fusion.1), calls=%async_computation | async-start | bytes 5242880 | tf_op jit(solution)/shard_map/all_to_all | solution.py:105
  80.3 0.0 all-gather.7.cloned.1.call-start
  80.4 0.7 all-gather.7.cloned.1.call-update
  81.1 43.9 %all-to-all-done = bf16[32,40,1024]{2,1,0:T(8,128)(2,1)} async-done(((bf16[32,40,1024]{2,1,0:T(8,128)(2,1)}), bf16[32,40,1024]{2,1,0:T(8,128)(2,1)}, u32[]{:S(2)}, u32[]{:S(2)}) %all-to-all-start) | async-done | bytes 2621472 | tf_op jit(solution)/shard_map/all_to_all | solution.py:105
  125.0 7.6 %fusion.15 = f32[32,40,1024]{2,1,0:T(8,128)} fusion(bf16[32,40,1024]{2,1,0:T(8,128)(2,1)} %all-to-all-done, bf16[1,1024,1024]{2,1,0:T(8,128)(2,1)} %all-gather.5.cloned.1.call-done), kind=kOutput, calls=%fused_computation.21 | convolution fusion | flops 2684354560 | bytes 9961472 | tf_op jit(solution)/shard_map/scw,wh->sch/dot_general | solution.py:106
  132.6 7.6 %reshape.184 = f32[32,40,4,256]{3,2,1,0:T(4,128)} reshape(f32[32,40,1024]{2,1,0:T(8,128)} %fusion.15) | data formatting | bytes 10485760 | tf_op jit(solution)/shard_map/reshape | solution.py:107
  140.1 3.2 %fusion.7 = bf16[32,40,4,128]{3,2,1,0:T(4,128)(2,1)S(1)} fusion(f32[32,40,4,256]{3,2,1,0:T(4,128)} %reshape.184), kind=kLoop, calls=%fused_computation.11 | loop fusion | flops 3932160 | bytes 6553600 | tf_op jit(solution)/shard_map/convert_element_type | solution.py:108
  143.3 1.4 reshape.185
  144.7 4.7 %convolution_convert_fusion = bf16[32,40,1024]{2,1,0:T(8,128)(2,1)} fusion(bf16[32,40,512]{2,1,0:T(8,128)(2,1)} %reshape.185, bf16[1,512,1024]{2,1,0:T(8,128)(2,1)} %all-gather.7.cloned.1.call-done), kind=kOutput, calls=%fused_computation.23 | convolution fusion | flops 1343488000 | bytes 4980736 | tf_op jit(solution)/shard_map/sch,hw->scw/dot_general | solution.py:110
  149.4 4.9 %all-to-all-start.1 = ((bf16[32,40,1024]{2,1,0:T(8,128)(2,1)}), bf16[32,40,1024]{2,1,0:T(8,128)(2,1)}, u32[]{:S(2)}, u32[]{:S(2)}) async-start(bf16[32,40,1024]{2,1,0:T(8,128)(2,1)} %convolution_convert_fusion), calls=%async_computation.1 | async-start | bytes 5242880 | tf_op jit(solution)/shard_map/all_to_all | solution.py:113
  154.3 35.0 %all-to-all-done.1 = bf16[32,40,1024]{2,1,0:T(8,128)(2,1)} async-done(((bf16[32,40,1024]{2,1,0:T(8,128)(2,1)}), bf16[32,40,1024]{2,1,0:T(8,128)(2,1)}, u32[]{:S(2)}, u32[]{:S(2)}) %all-to-all-start.1) | async-done | bytes 2621472 | tf_op jit(solution)/shard_map/all_to_all | solution.py:113
  189.4 3.8 %fusion.17 = bf16[128,1024]{1,0:T(8,128)(2,1)} fusion(bf16[32,40,1024]{2,1,0:T(8,128)(2,1)} %all-to-all-done.1, f32[128,32]{0,1:T(8,128)S(1)} %select_reduce_fusion, s32[128,32]{0,1:T(8,128)S(1)} %convolution_convert_fusion.2, pred[128,32]{0,1:T(8,128)(4,1)S(1)} %fusion.46), kind=kOutput, calls=%fused_computation.26 | convolution fusion | flops 2013888512 | bytes 2920448 | tf_op jit(solution)/shard_map/tec,ecw->tw/dot_general | solution.py:115
  (22 shorter events, 0.2 us)
Async XLA Ops:
  7.2 58.1 %copy-start = (bf16[1024,1024]{1,0:T(8,128)(2,1)S(1)}, bf16[1024,1024]{1,0:T(8,128)(2,1)}, u32[]{:S(2)}) copy-start(bf16[1024,1024]{1,0:T(8,128)(2,1)} %param.14) | copy-start | bytes 6291460
  7.2 117.8 %all-gather.5.cloned.1.call-start = ((), (), s32[]{:S(2)}) async-start(), calls=%async_computation.2 | async-start | bytes 2621440 | tf_op jit(solution)/shard_map/all_gather | solution.py:82
  56.8 8.5 %copy-start.1 = (bf16[128,1024]{1,0:T(8,128)(2,1)S(1)}, bf16[128,1024]{1,0:T(8,128)(2,1)}, u32[]{:S(2)}) copy-start(bf16[128,1024]{1,0:T(8,128)(2,1)} %param.12) | copy-start | bytes 786436
  65.2 1.3 copy-start.2
  65.2 1.4 copy-start.3
  69.1 55.9 %all-to-all-start = ((bf16[32,40,1024]{2,1,0:T(8,128)(2,1)}), bf16[32,40,1024]{2,1,0:T(8,128)(2,1)}, u32[]{:S(2)}, u32[]{:S(2)}) async-start(bf16[32,40,1024]{2,1,0:T(8,128)(2,1)} %convolution_convert_fusion.1), calls=%async_computation | async-start | bytes 5242880 | tf_op jit(solution)/shard_map/all_to_all | solution.py:105
  80.3 64.4 %all-gather.7.cloned.1.call-start = ((), (), s32[]{:S(2)}) async-start(), calls=%async_computation.3 | async-start | bytes 1310720 | tf_op jit(solution)/shard_map/all_gather | solution.py:83
  149.4 4.9 %copy-start.4 = (f32[128,8]{0,1:T(8,128)S(1)}, f32[128,8]{0,1:T(8,128)}, u32[]{:S(2)}) copy-start(f32[128,8]{0,1:T(8,128)} %param.21) | copy-start | bytes 12292
  149.4 40.0 %all-to-all-start.1 = ((bf16[32,40,1024]{2,1,0:T(8,128)(2,1)}), bf16[32,40,1024]{2,1,0:T(8,128)(2,1)}, u32[]{:S(2)}, u32[]{:S(2)}) async-start(bf16[32,40,1024]{2,1,0:T(8,128)(2,1)} %convolution_convert_fusion), calls=%async_computation.1 | async-start | bytes 5242880 | tf_op jit(solution)/shard_map/all_to_all | solution.py:113
Sparse Core Ops, SparseCore 0:
  9.6 30.4 all-gather.4
  82.8 30.3 all-gather.6

commit v3 on v2

--- a/solution.py
+++ b/solution.py
@@ -2,6 +2,8 @@
 import jax.numpy as jnp
 from jax import lax
 from jax.sharding import PartitionSpec as P
+from jax.experimental import pallas as pl
+from jax.experimental.pallas import tpu as pltpu
 
 HEADS = 16
 KV_HEADS = 8
@@ -30,11 +32,67 @@
     )
 
 
-def attend(tokens, qkv_weight, out_weight, norm_attn, keys_cache, values_cache, length):
+def attention_kernel(length_ref, q_ref, kc_ref, vc_ref, kn_ref, vn_ref, o_ref):
+    length = length_ref[0]
+    span = kc_ref.shape[0]
+    rows = kn_ref.shape[0]
+    kc = kc_ref[...]
+    vc = vc_ref[...]
+    kn = kn_ref[...]
+    vn = vn_ref[...]
+    column = lax.broadcasted_iota(jnp.int32, (rows, span), 1)
+    cache_ok = column < length
+    new_col = lax.broadcasted_iota(jnp.int32, (rows, rows), 1)
+    new_row = lax.broadcasted_iota(jnp.int32, (rows, rows), 0)
+    new_ok = new_col <= new_row
+    contract = (((1,), (1,)), ((), ()))
+    for j in range(q_ref.shape[0]):
+        q = q_ref[j]
+        s = lax.dot_general(q, kc, contract, preferred_element_type=jnp.float32) * 0.015625
+        s = jnp.where(cache_ok, s, -1e30)
+        sn = lax.dot_general(q, kn, contract, preferred_element_type=jnp.float32) * 0.015625
+        sn = jnp.where(new_ok, sn, -1e30)
+        top = jnp.maximum(jnp.max(s, axis=1, keepdims=True), jnp.max(sn, axis=1, keepdims=True))
+        e = jnp.exp(s - top)
+        en = jnp.exp(sn - top)
+        total = jnp.sum(e, axis=1, keepdims=True) + jnp.sum(en, axis=1, keepdims=True)
+        w = (e / total).astype(jnp.bfloat16)
+        wn = (en / total).astype(jnp.bfloat16)
+        o = jnp.dot(w, vc, preferred_element_type=jnp.float32) + jnp.dot(
+            wn, vn, preferred_element_type=jnp.float32
+        )
+        o_ref[j] = o.astype(jnp.bfloat16)
+
+
+def attention_core(length, q_pairs, kc, vc, kn, vn, interpret=False):
+    heads, rows, lanes = q_pairs.shape
+    span = kc.shape[0]
+    pairs = kc.shape[1] // lanes
+    per = heads // pairs
+    return pl.pallas_call(
+        attention_kernel,
+        grid_spec=pltpu.PrefetchScalarGridSpec(
+            num_scalar_prefetch=1,
+            grid=(pairs,),
+            in_specs=[
+                pl.BlockSpec((per, rows, lanes), lambda p, n: (p, 0, 0)),
+                pl.BlockSpec((span, lanes), lambda p, n: (0, p)),
+                pl.BlockSpec((span, lanes), lambda p, n: (0, p)),
+                pl.BlockSpec((rows, lanes), lambda p, n: (0, p)),
+                pl.BlockSpec((rows, lanes), lambda p, n: (0, p)),
+            ],
+            out_specs=pl.BlockSpec((per, rows, lanes), lambda p, n: (p, 0, 0)),
+        ),
+        out_shape=jax.ShapeDtypeStruct((heads, rows, lanes), jnp.bfloat16),
+        interpret=interpret,
+    )(length, q_pairs, kc, vc, kn, vn)
+
+
+def attend(tokens, qkv_weight, out_weight, norm_attn, keys_cache, values_cache, length, interpret=False):
     rows = tokens.shape[0]
-    span = keys_cache.shape[0]
     qwidth = HEADS * HEAD
     kvwidth = KV_HEADS * HEAD
+    lanes = 2 * HEAD
     normed = rms_scale(tokens, norm_attn).astype(jnp.bfloat16)
     mixed = jnp.dot(normed, qkv_weight, preferred_element_type=jnp.float32)
     places = (length + jnp.arange(rows, dtype=jnp.int32)).astype(jnp.float32)
@@ -43,23 +101,24 @@
         mixed[:, qwidth : qwidth + kvwidth].reshape(rows, KV_HEADS, HEAD), places
     ).astype(jnp.bfloat16)
     value_new = mixed[:, qwidth + kvwidth :].astype(jnp.bfloat16)
-    keys = jnp.concatenate([keys_cache, key_new.reshape(rows, kvwidth)], axis=0).reshape(
-        span + rows, KV_HEADS, HEAD
-    )
-    values = jnp.concatenate([values_cache, value_new], axis=0).reshape(span + rows, KV_HEADS, HEAD)
-    query = query.reshape(rows, KV_HEADS, HEADS // KV_HEADS, HEAD)
-    scores = (
-        jnp.einsum("tkgd,skd->kgts", query, keys, preferred_element_type=jnp.float32) * 0.015625
-    )
-    column = jnp.arange(span + rows, dtype=jnp.int32)[None, :]
-    row_index = jnp.arange(rows, dtype=jnp.int32)[:, None]
-    valid = jnp.where(column < span, column < length, column - span <= row_index)
-    scores = jnp.where(valid[None, None], scores, -1e30)
-    top = jnp.max(scores, axis=-1, keepdims=True)
-    weights = jnp.exp(scores - top)
-    weights = (weights / jnp.sum(weights, axis=-1, keepdims=True)).astype(jnp.bfloat16)
-    heads_out = jnp.einsum("kgts,skd->tkgd", weights, values, preferred_element_type=jnp.float32)
-    heads_out = heads_out.astype(jnp.bfloat16).reshape(rows, qwidth)
+    group = HEADS // KV_HEADS
+    half = (jnp.arange(HEADS) // group) % 2
+    lane_half = jnp.arange(lanes) // HEAD
+    doubled = jnp.concatenate([query, query], axis=-1)
+    q_pairs = jnp.where((lane_half[None, :] == half[:, None])[None], doubled, 0)
+    q_pairs = jnp.transpose(q_pairs, (1, 0, 2)).astype(jnp.bfloat16)
+    paired = attention_core(
+        length.reshape(1).astype(jnp.int32),
+        q_pairs,
+        keys_cache,
+        values_cache,
+        key_new.reshape(rows, kvwidth),
+        value_new,
+        interpret=interpret,
+    )
+    split = paired.reshape(HEADS, rows, 2, HEAD)
+    chosen = jnp.where((half == 0)[:, None, None], split[:, :, 0, :], split[:, :, 1, :])
+    heads_out = jnp.transpose(chosen, (1, 0, 2)).reshape(rows, qwidth)
     return jnp.dot(heads_out, out_weight, preferred_element_type=jnp.float32)
 
 
@@ -84,6 +143,7 @@
     branch = attend(
         tokens, qkv_weight, out_weight, norm_attn, keys_cache[0], values_cache[0], lengths[0]
     )
+    branch, gate_up_all, down_all = lax.optimization_barrier((branch, gate_up_all, down_all))
     carried = tokens.astype(jnp.float32) + 0.22 * branch
     normed = rms_scale(carried, norm_expert).astype(jnp.bfloat16)
     rows = tokens.shape[0]
@@ -103,10 +163,12 @@
         "tec,tw->ecw", pick.astype(jnp.bfloat16), normed, preferred_element_type=jnp.float32
     ).astype(jnp.bfloat16)
     received = lax.all_to_all(outgoing, ("req", "h"), split_axis=0, concat_axis=0, tiled=True)
-    both = jnp.einsum("scw,wh->sch", received, gate_up_all, preferred_element_type=jnp.float32)
-    both = both.reshape(both.shape[0], both.shape[1], slices, 2 * width_dev)
-    hidden = (jax.nn.silu(both[..., :width_dev]) * both[..., width_dev:]).astype(jnp.bfloat16)
-    hidden = hidden.reshape(both.shape[0], both.shape[1], slices * width_dev)
+    pieces = gate_up_all.reshape(gate_up_all.shape[0], slices, 2 * width_dev)
+    gate_cols = pieces[..., :width_dev].reshape(gate_up_all.shape[0], slices * width_dev)
+    up_cols = pieces[..., width_dev:].reshape(gate_up_all.shape[0], slices * width_dev)
+    gate = jnp.einsum("scw,wh->sch", received, gate_cols, preferred_element_type=jnp.float32)
+    upper = jnp.einsum("scw,wh->sch", received, up_cols, preferred_element_type=jnp.float32)
+    hidden = (jax.nn.silu(gate) * upper).astype(jnp.bfloat16)
     produced = jnp.einsum(
         "sch,hw->scw", hidden, down_all, preferred_element_type=jnp.float32
     ).astype(jnp.bfloat16)

time: 201 us -> 187 us (0.930)
  other arithmetic: 29.6 us -> 6.29 us
  matrix products: 41.6 us -> 22.4 us
  Pallas kernels: 0 us -> 14.6 us
  waiting for transfers between devices: 80.3 us -> 84.9 us
  local copies, waits for them, and re-layouts: 17.4 us -> 21.3 us
  starting transfers between devices: 16.3 us -> 20.1 us
    sub x2 -> x0, other arithmetic: 22.1 us -> none  [the longest x1 22.1 us: attend(): weights = jnp.exp(scores - top)]
    dot_general x3 -> x1, matrix products: 26.2 us -> 5.08 us  [on_device(): jnp.einsum('scw,wh->sch', received, gate_cols, preferred_element_type=jnp...]
    all_gather x1, waiting for transfers between devices: 0.01 us -> 20.1 us  [on_device(): gate_up_all = lax.all_gather(gate_up[0], 'q', axis=1, tiled=True)]
    all_to_all x1, waiting for transfers between devices: 43.9 us -> 26.2 us  [on_device(): lax.all_to_all(outgoing, ('req', 'h'), split_axis=0, concat_axis=0, tiled...]
    pallas_call x0 -> x1, Pallas kernels: none -> 14.6 us  [attention_core(): pl.pallas_call(attention_kernel, grid_spec=pltpu.PrefetchScalarGridSpec(n...]
    all_to_all x1, starting transfers between devices: 4.94 us -> 10.6 us  [on_device(): lax.all_to_all(produced, ('req', 'h'), split_axis=0, concat_axis=0, tiled...]
    slice x0 -> x2, local copies, waits for them, and re-layouts: none -> 4.09 us  [the longest x1 3.27 us: on_device(): pieces[..., width_dev:].reshape(gate_up_all.shape[0], slices * width_dev)]
    convert_element_type x1 -> x0, other arithmetic: 3.21 us -> none  [on_device(): (jax.nn.silu(both[..., :width_dev]) * both[..., width_dev:]).astype(jnp.b...]
  transfers between devices with their start and end apart: 4 -> 4, of which waited for: 2 -> 3; matrix products, arithmetic and copies ran while one was open for 40% -> 16% of each run, Pallas kernels for 0% -> 8%
where the time goes in v3:
time: 187 us; the launch traced here: 184 us
  waiting for transfers between devices  84.9 us (45%)
  matrix products  22.4 us (12%)
  local copies, waits for them, and re-layouts  21.3 us (11%)
  starting transfers between devices  20.1 us (11%)
  between operations  14.9 us (8%)
  Pallas kernels  14.6 us (8%)
  other arithmetic  6.29 us (3%)
    all_to_all x1, waiting for transfers between devices, on_device(): lax.all_to_all(produced, ('req', 'h'), split_axis=0, concat_axis=0, tiled...  37.2 us
    all_to_all x1, waiting for transfers between devices, on_device(): lax.all_to_all(outgoing, ('req', 'h'), split_axis=0, concat_axis=0, tiled...  26.2 us
    all_gather x1, waiting for transfers between devices, on_device(): gate_up_all = lax.all_gather(gate_up[0], 'q', axis=1, tiled=True)  20.1 us
    pallas_call x1, Pallas kernels, attention_core(): pl.pallas_call(attention_kernel, grid_spec=pltpu.PrefetchScalarGridSpec(n...  14.6 us
    all_to_all x1, starting transfers between devices, on_device(): lax.all_to_all(produced, ('req', 'h'), split_axis=0, concat_axis=0, tiled...  10.6 us
    all_to_all x1, starting transfers between devices, on_device(): lax.all_to_all(outgoing, ('req', 'h'), split_axis=0, concat_axis=0, tiled...  9.35 us
    dot_general x1, matrix products, on_device(): jnp.einsum('sch,hw->scw', hidden, down_all, preferred_element_type=jnp.fl...  7.34 us
    unnamed x18, local copies, waits for them, and re-layouts  5.14 us
  transfers between devices with their start and end apart: 4, of which 3 were waited for; matrix products, arithmetic and copies ran while one was open for 16% of the time, Pallas kernels for 8%

profile of v3, /device:TPU:0, one launch (start us, length us, event | category | flops | bytes accessed | tf_op | source)
XLA Modules:
  0.0 184.5 jit_solution(1584097623459078664)
XLA Ops:
  7.2 0.7 all-gather.7.cloned.1.call-update
  8.0 0.7 all-gather.5.cloned.1.call-update
  8.7 1.1 fusion.6
  9.8 3.1 %fusion.18 = f32[128,2048]{1,0:T(8,128)S(1)} fusion(bf16[1024,2048]{1,0:T(8,128)(2,1)} %param.13, bf16[128,1024]{1,0:T(8,128)(2,1)} %param.12, f32[1024]{0:T(1024)} %param.15, f32[128]{0:T(128)S(1)} %add_rsqrt_fusion.1), kind=kOutput, calls=%fused_computation.29 | convolution fusion | flops 537395200 | bytes 5509632 | tf_op jit(solution)/shard_map/dot_general | solution.py:97
  12.9 1.0 copy-done.2
  13.9 0.7 slice.67.vn_ref
  15.4 0.8 fusion.32
  16.2 1.3 copy.44
  17.5 2.4 %copy.43 = f32[128,16,32]{2,0,1:T(8,128)} copy(f32[128,16,32]{0,2,1:T(8,128)} %get-tuple-element.15) | data formatting | bytes 524288
  20.2 0.5 copy-done.4
  20.8 0.8 copy.40
  21.6 1.0 subtract_convert_fusion.1
  22.7 0.8 copy.41.kn_ref
  23.5 1.5 subtract_convert_fusion
  25.0 1.5 fusion.9.q_ref
  26.5 14.6 %shard_map.131 = bf16[16,128,128]{2,1,0:T(8,128)(2,1)} custom-call(s32[1]{0:T(128)} %copy.45.length_ref, bf16[16,128,128]{2,1,0:T(8,128)(2,1)} %fusion.9.q_ref, bf16[2048,512]{1,0:T(8,128)(2,1)} %bitcast.42, bf16[2048,512]{1,0:T(8,128)(2,1)} %bitcast.43, bf16[128,512]{1,0:T(8,128)(2,1)} %copy.41.kn_ref, bf16[128,512]{1,0:T(8,128)(2,1)} %slice.67.vn_ref), custom_call_target="tpu_custom_call" | custom-call | tf_op jit(solution)/shard_map/pallas_call | solution.py:72
  41.1 1.4 copy.42
  42.8 0.5 fusion.33
  43.3 20.1 %all-gather.5.cloned.1.call-done = bf16[1,1024,1024]{2,1,0:T(8,128)(2,1)} async-done(((bf16[1,1024,256]{2,1,0:T(8,128)(2,1)}), bf16[1,1024,1024]{2,1,0:T(8,128)(2,1)}) %all-gather.5.cloned.1.call-update) | async-done | bytes 2097168 | tf_op jit(solution)/shard_map/all_gather | solution.py:141
  63.4 0.8 multiply_reduce_fusion
  64.2 2.4 %convolution_convert_fusion.1 = bf16[32,40,1024]{2,1,0:T(8,128)(2,1)} fusion(s32[128,32]{0,1:T(8,128)S(1)} %convolution_convert_fusion.2, pred[128,32]{0,1:T(8,128)(4,1)S(1)} %fusion.26, f32[128,1024]{1,0:T(8,128)S(1)} %fusion.33, bf16[128,1024]{1,0:T(8,128)(2,1)S(1)} %copy-done.1, f32[1024]{0:T(1024)S(1)} %copy-done.6, f32[128]{0:T(128)S(1)} %add_rsqrt_fusion), kind=kOutput, calls=%fused_computation.2 | convolution fusion | flops 337969152 | bytes 3432960 | tf_op jit(solution)/shard_map/tec,tw->ecw/dot_general | solution.py:162
  66.7 9.4 %all-to-all-start = ((bf16[32,40,1024]{2,1,0:T(8,128)(2,1)}), bf16[32,40,1024]{2,1,0:T(8,128)(2,1)}, u32[]{:S(2)}, u32[]{:S(2)}) async-start(bf16[32,40,1024]{2,1,0:T(8,128)(2,1)} %convolution_convert_fusion.1), calls=%async_computation | async-start | bytes 5242880 | tf_op jit(solution)/shard_map/all_to_all | solution.py:165
  76.0 4.5 %reshape.202 = bf16[1024,4,256]{2,1,0:T(4,128)(2,1)} reshape(bf16[1024,1024]{1,0:T(8,128)(2,1)} %bitcast.44) | data formatting | bytes 4194304 | tf_op jit(solution)/shard_map/reshape | solution.py:166
  80.6 3.3 %fusion.31 = (bf16[1024,4,128]{2,1,0:T(4,128)(2,1)S(1)}, bf16[1024,4,128]{2,1,0:T(4,128)(2,1)}) fusion(bf16[1024,4,256]{2,1,0:T(4,128)(2,1)} %reshape.202), kind=kLoop, calls=%fused_computation.69 | loop fusion | bytes 4194304 | tf_op jit(solution)/shard_map/slice | solution.py:168
  83.8 2.3 %reshape.208 = bf16[1024,512,1]{1,0,2:T(8,128)(2,1)} reshape(bf16[1024,4,128]{2,1,0:T(4,128)(2,1)} %get-tuple-element.11) | data formatting | bytes 2097152 | tf_op jit(solution)/shard_map/reshape | solution.py:167
  86.1 1.2 reshape.209
  87.3 26.2 %all-to-all-done = bf16[32,40,1024]{2,1,0:T(8,128)(2,1)} async-done(((bf16[32,40,1024]{2,1,0:T(8,128)(2,1)}), bf16[32,40,1024]{2,1,0:T(8,128)(2,1)}, u32[]{:S(2)}, u32[]{:S(2)}) %all-to-all-start) | async-done | bytes 2621472 | tf_op jit(solution)/shard_map/all_to_all | solution.py:165
  113.5 5.1 %fusion.34 = f32[32,40,512]{2,1,0:T(8,128)} fusion(bf16[32,40,1024]{2,1,0:T(8,128)(2,1)} %all-to-all-done, bf16[1024,512,1]{1,0,2:T(8,128)(2,1)} %reshape.208), kind=kOutput, calls=%fused_computation.72 | convolution fusion | flops 1342177280 | bytes 6291456 | tf_op jit(solution)/shard_map/scw,wh->sch/dot_general | solution.py:169
  118.6 7.3 %convolution_convert_fusion = bf16[32,40,1024]{2,1,0:T(8,128)(2,1)} fusion(f32[32,40,512]{2,1,0:T(8,128)} %fusion.34, bf16[32,40,1024]{2,1,0:T(8,128)(2,1)} %all-to-all-done, bf16[1024,512,1]{1,0,2:T(8,128)(2,1)S(1)} %copy-done.3, bf16[512,1024]{1,0:T(8,128)(2,1)} %bitcast.50), kind=kOutput, calls=%fused_computation.1 | convolution fusion | flops 2689597440 | bytes 9961472 | tf_op jit(solution)/shard_map/sch,hw->scw/dot_general | solution.py:172
  126.0 10.6 %all-to-all-start.1 = ((bf16[32,40,1024]{2,1,0:T(8,128)(2,1)}), bf16[32,40,1024]{2,1,0:T(8,128)(2,1)}, u32[]{:S(2)}, u32[]{:S(2)}) async-start(bf16[32,40,1024]{2,1,0:T(8,128)(2,1)} %convolution_convert_fusion), calls=%async_computation.1 | async-start | bytes 5242880 | tf_op jit(solution)/shard_map/all_to_all | solution.py:175
  136.6 37.2 %all-to-all-done.1 = bf16[32,40,1024]{2,1,0:T(8,128)(2,1)} async-done(((bf16[32,40,1024]{2,1,0:T(8,128)(2,1)}), bf16[32,40,1024]{2,1,0:T(8,128)(2,1)}, u32[]{:S(2)}, u32[]{:S(2)}) %all-to-all-start.1) | async-done | bytes 2621472 | tf_op jit(solution)/shard_map/all_to_all | solution.py:175
  173.8 3.8 %fusion = bf16[128,1024]{1,0:T(8,128)(2,1)} fusion(bf16[32,40,1024]{2,1,0:T(8,128)(2,1)} %all-to-all-done.1, f32[128,32]{0,1:T(8,128)S(1)} %select_reduce_fusion, s32[128,32]{0,1:T(8,128)S(1)} %convolution_convert_fusion.2, pred[128,32]{0,1:T(8,128)(4,1)S(1)} %fusion.26), kind=kOutput, calls=%fused_computation.4 | convolution fusion | flops 2013888512 | bytes 2920448 | tf_op jit(solution)/shard_map/tec,ecw->tw/dot_general | solution.py:177
  (37 shorter events, 1.1 us)
Async XLA Ops:
  7.2 35.6 %copy-start = (bf16[1024,1024]{1,0:T(8,128)(2,1)S(1)}, bf16[1024,1024]{1,0:T(8,128)(2,1)}, u32[]{:S(2)}) copy-start(bf16[1024,1024]{1,0:T(8,128)(2,1)} %param.14) | copy-start | bytes 6291460
  7.2 36.1 %all-gather.7.cloned.1.call-start = ((), (), s32[]{:S(2)}) async-start(), calls=%async_computation.3 | async-start | bytes 1310720 | tf_op jit(solution)/shard_map/all_gather | solution.py:142
  7.9 55.5 %all-gather.5.cloned.1.call-start = ((), (), s32[]{:S(2)}) async-start(), calls=%async_computation.2 | async-start | bytes 2621440 | tf_op jit(solution)/shard_map/all_gather | solution.py:141
  12.8 1.0 copy-start.2
  14.5 6.3 %slice-start = ((f32[128,2048]{1,0:T(8,128)}), f32[128,512]{1,0:T(8,128)S(1)}, s32[]{:S(2)}) async-start(f32[128,2048]{1,0:T(8,128)} %copy-done.2), calls=%async_computation.4 | async-start | bytes 524288 | tf_op jit(solution)/shard_map/slice | solution.py:101
  20.1 0.6 copy-start.4
  26.5 16.0 %copy-start.5 = (s32[128,8]{0,1:T(8,128)S(1)}, s32[128,8]{0,1:T(8,128)}, u32[]{:S(2)}) copy-start(s32[128,8]{0,1:T(8,128)} %param.20) | copy-start | bytes 12292
  41.1 22.3 %copy-start.1 = (bf16[128,1024]{1,0:T(8,128)(2,1)S(1)}, bf16[128,1024]{1,0:T(8,128)(2,1)}, u32[]{:S(2)}) copy-start(bf16[128,1024]{1,0:T(8,128)(2,1)} %param.12) | copy-start | bytes 786436
  42.4 21.8 %copy-start.6 = (f32[1024]{0:T(1024)S(1)}, f32[1024]{0:T(1024)}, u32[]{:S(2)}) copy-start(f32[1024]{0:T(1024)} %param.16) | copy-start | bytes 12292
  66.7 46.8 %all-to-all-start = ((bf16[32,40,1024]{2,1,0:T(8,128)(2,1)}), bf16[32,40,1024]{2,1,0:T(8,128)(2,1)}, u32[]{:S(2)}, u32[]{:S(2)}) async-start(bf16[32,40,1024]{2,1,0:T(8,128)(2,1)} %convolution_convert_fusion.1), calls=%async_computation | async-start | bytes 5242880 | tf_op jit(solution)/shard_map/all_to_all | solution.py:165
  87.3 31.3 %copy-start.3 = (bf16[1024,512,1]{1,0,2:T(8,128)(2,1)S(1)}, bf16[1024,512,1]{1,0,2:T(8,128)(2,1)}, u32[]{:S(2)}) copy-start(bf16[1024,512,1]{1,0,2:T(8,128)(2,1)} %reshape.209) | copy-start | bytes 3145732
  126.0 10.7 %copy-start.7 = (f32[128,8]{0,1:T(8,128)S(1)}, f32[128,8]{0,1:T(8,128)}, u32[]{:S(2)}) copy-start(f32[128,8]{0,1:T(8,128)} %param.21) | copy-start | bytes 12292
  126.0 47.8 %all-to-all-start.1 = ((bf16[32,40,1024]{2,1,0:T(8,128)(2,1)}), bf16[32,40,1024]{2,1,0:T(8,128)(2,1)}, u32[]{:S(2)}, u32[]{:S(2)}) async-start(bf16[32,40,1024]{2,1,0:T(8,128)(2,1)} %convolution_convert_fusion), calls=%async_computation.1 | async-start | bytes 5242880 | tf_op jit(solution)/shard_map/all_to_all | solution.py:175
Sparse Core Ops, SparseCore 0:
  9.6 22.6 all-gather.6
  34.0 29.3 all-gather.4

commit v4 on v3

--- a/solution.py
+++ b/solution.py
@@ -34,8 +34,9 @@
 
 def attention_kernel(length_ref, q_ref, kc_ref, vc_ref, kn_ref, vn_ref, o_ref):
     length = length_ref[0]
-    span = kc_ref.shape[0]
+    span, lanes = kc_ref.shape
     rows = kn_ref.shape[0]
+    half = lanes // 2
     kc = kc_ref[...]
     vc = vc_ref[...]
     kn = kn_ref[...]
@@ -45,81 +46,108 @@
     new_col = lax.broadcasted_iota(jnp.int32, (rows, rows), 1)
     new_row = lax.broadcasted_iota(jnp.int32, (rows, rows), 0)
     new_ok = new_col <= new_row
+    low = lax.broadcasted_iota(jnp.int32, (rows, lanes), 1) < half
+    first = q_ref[:, :lanes].astype(jnp.float32)
+    second = q_ref[:, lanes:].astype(jnp.float32)
+    queries = (
+        jnp.where(low, first, 0.0),
+        jnp.where(low, pltpu.roll(first, half, 1), 0.0),
+        jnp.where(low, 0.0, pltpu.roll(second, half, 1)),
+        jnp.where(low, 0.0, second),
+    )
     contract = (((1,), (1,)), ((), ()))
-    for j in range(q_ref.shape[0]):
-        q = q_ref[j]
-        s = lax.dot_general(q, kc, contract, preferred_element_type=jnp.float32) * 0.015625
+    outs = []
+    for q in queries:
+        q = q.astype(jnp.bfloat16)
+        s = lax.dot_general(q, kc, contract, preferred_element_type=jnp.float32)
         s = jnp.where(cache_ok, s, -1e30)
-        sn = lax.dot_general(q, kn, contract, preferred_element_type=jnp.float32) * 0.015625
+        sn = lax.dot_general(q, kn, contract, preferred_element_type=jnp.float32)
         sn = jnp.where(new_ok, sn, -1e30)
         top = jnp.maximum(jnp.max(s, axis=1, keepdims=True), jnp.max(sn, axis=1, keepdims=True))
         e = jnp.exp(s - top)
         en = jnp.exp(sn - top)
         total = jnp.sum(e, axis=1, keepdims=True) + jnp.sum(en, axis=1, keepdims=True)
-        w = (e / total).astype(jnp.bfloat16)
-        wn = (en / total).astype(jnp.bfloat16)
+        inverse = 1.0 / total
+        w = (e * inverse).astype(jnp.bfloat16)
+        wn = (en * inverse).astype(jnp.bfloat16)
         o = jnp.dot(w, vc, preferred_element_type=jnp.float32) + jnp.dot(
             wn, vn, preferred_element_type=jnp.float32
         )
-        o_ref[j] = o.astype(jnp.bfloat16)
-
-
-def attention_core(length, q_pairs, kc, vc, kn, vn, interpret=False):
-    heads, rows, lanes = q_pairs.shape
-    span = kc.shape[0]
-    pairs = kc.shape[1] // lanes
-    per = heads // pairs
+        outs.append(o.astype(jnp.bfloat16).astype(jnp.float32))
+    left = jnp.where(low, outs[0], pltpu.roll(outs[1], half, 1))
+    right = jnp.where(low, pltpu.roll(outs[2], half, 1), outs[3])
+    o_ref[:, :lanes] = left.astype(jnp.bfloat16)
+    o_ref[:, lanes:] = right.astype(jnp.bfloat16)
+
+
+def attention_core(length, query, kc, vc, kn, vn, interpret=False):
+    rows, qwidth = query.shape
+    span, kvwidth = kc.shape
+    lanes = 2 * HEAD
+    pairs = kvwidth // lanes
+    qblock = qwidth // pairs
     return pl.pallas_call(
         attention_kernel,
         grid_spec=pltpu.PrefetchScalarGridSpec(
             num_scalar_prefetch=1,
             grid=(pairs,),
             in_specs=[
-                pl.BlockSpec((per, rows, lanes), lambda p, n: (p, 0, 0)),
+                pl.BlockSpec((rows, qblock), lambda p, n: (0, p)),
                 pl.BlockSpec((span, lanes), lambda p, n: (0, p)),
                 pl.BlockSpec((span, lanes), lambda p, n: (0, p)),
                 pl.BlockSpec((rows, lanes), lambda p, n: (0, p)),
                 pl.BlockSpec((rows, lanes), lambda p, n: (0, p)),
             ],
-            out_specs=pl.BlockSpec((per, rows, lanes), lambda p, n: (p, 0, 0)),
+            out_specs=pl.BlockSpec((rows, qblock), lambda p, n: (0, p)),
         ),
-        out_shape=jax.ShapeDtypeStruct((heads, rows, lanes), jnp.bfloat16),
+        out_shape=jax.ShapeDtypeStruct((rows, qwidth), jnp.bfloat16),
         interpret=interpret,
-    )(length, q_pairs, kc, vc, kn, vn)
+    )(length, query, kc, vc, kn, vn)
+
+
+def rotate_lanes(values, places):
+    half = HEAD // 2
+    freq = 10000.0 ** (-jnp.arange(half, dtype=jnp.float32) / half)
+    angle = places[:, None] * freq[None, :]
+    repeat = values.shape[1] // half
+    cosine = jnp.tile(jnp.cos(angle), (1, repeat))
+    sine = jnp.tile(jnp.sin(angle), (1, repeat))
+    lead = (jnp.arange(values.shape[1]) % HEAD < half)[None, :]
+    partner = jnp.where(lead, jnp.roll(values, -half, axis=1), jnp.roll(values, half, axis=1))
+    return jnp.where(lead, values * cosine - partner * sine, values * cosine + partner * sine)
 
 
 def attend(tokens, qkv_weight, out_weight, norm_attn, keys_cache, values_cache, length, interpret=False):
     rows = tokens.shape[0]
     qwidth = HEADS * HEAD
     kvwidth = KV_HEADS * HEAD
-    lanes = 2 * HEAD
     normed = rms_scale(tokens, norm_attn).astype(jnp.bfloat16)
     mixed = jnp.dot(normed, qkv_weight, preferred_element_type=jnp.float32)
     places = (length + jnp.arange(rows, dtype=jnp.int32)).astype(jnp.float32)
-    query = rotate(mixed[:, :qwidth].reshape(rows, HEADS, HEAD), places).astype(jnp.bfloat16)
-    key_new = rotate(
-        mixed[:, qwidth : qwidth + kvwidth].reshape(rows, KV_HEADS, HEAD), places
-    ).astype(jnp.bfloat16)
+    turned = rotate_lanes(mixed[:, : qwidth + kvwidth], places)
+    query = (turned[:, :qwidth].astype(jnp.bfloat16) * 0.015625).astype(jnp.bfloat16)
+    key_new = turned[:, qwidth:].astype(jnp.bfloat16)
     value_new = mixed[:, qwidth + kvwidth :].astype(jnp.bfloat16)
-    group = HEADS // KV_HEADS
-    half = (jnp.arange(HEADS) // group) % 2
-    lane_half = jnp.arange(lanes) // HEAD
-    doubled = jnp.concatenate([query, query], axis=-1)
-    q_pairs = jnp.where((lane_half[None, :] == half[:, None])[None], doubled, 0)
-    q_pairs = jnp.transpose(q_pairs, (1, 0, 2)).astype(jnp.bfloat16)
-    paired = attention_core(
+    heads_out = attention_core(
         length.reshape(1).astype(jnp.int32),
-        q_pairs,
+        query,
         keys_cache,
         values_cache,
-        key_new.reshape(rows, kvwidth),
+        key_new,
         value_new,
         interpret=interpret,
     )
-    split = paired.reshape(HEADS, rows, 2, HEAD)
-    chosen = jnp.where((half == 0)[:, None, None], split[:, :, 0, :], split[:, :, 1, :])
-    heads_out = jnp.transpose(chosen, (1, 0, 2)).reshape(rows, qwidth)
     return jnp.dot(heads_out, out_weight, preferred_element_type=jnp.float32)
+
+
+def gather_expert(piece):
+    near = lax.ppermute(piece, "q", [(i, i ^ 2) for i in range(4)])
+    return [
+        piece,
+        near,
+        lax.ppermute(piece, "q", [(i, i ^ 1) for i in range(4)]),
+        lax.ppermute(near, "q", [(i, i ^ 1) for i in range(4)]),
+    ]
 
 
 def on_device(
@@ -138,8 +166,8 @@
 ):
     slices = lax.axis_size("q")
     width_dev = down_weight.shape[1]
-    gate_up_all = lax.all_gather(gate_up[0], "q", axis=1, tiled=True)
-    down_all = lax.all_gather(down_weight[0], "q", axis=0, tiled=True)
+    gate_up_all = jnp.concatenate(gather_expert(gate_up[0]), axis=1)
+    down_all = jnp.concatenate(gather_expert(down_weight[0]), axis=0)
     branch = attend(
         tokens, qkv_weight, out_weight, norm_attn, keys_cache[0], values_cache[0], lengths[0]
     )

time: 187 us -> 155 us (0.83)
  waiting for transfers between devices: 84.9 us -> 61.4 us
  between operations: 14.9 us -> 1.43 us
  other arithmetic: 6.29 us -> 10.7 us
  starting transfers between devices: 20.1 us -> 22.2 us
    all_gather x2 -> x0, waiting for transfers between devices: 20.2 us -> none  [the longest x1 20.1 us: on_device(): gate_up_all = lax.all_gather(gate_up[0], 'q', axis=1, tiled=True)]
    another operation x0 -> x4, local copies, waits for them, and re-layouts: none -> 6.53 us  [the longest x2 3.27 us: rotate_lanes(): cosine = jnp.tile(jnp.cos(angle), (1, repeat))]
    unnamed x18 -> x16, local copies, waits for them, and re-layouts: 5.14 us -> 0.04 us
    concatenate x1 -> x2, other arithmetic: 0.01 us -> 5.01 us  [the longest x1 3.04 us: on_device(): gate_up_all = jnp.concatenate(gather_expert(gate_up[0]), axis=1)]
    ppermute x0 -> x6, starting transfers between devices: none -> 3.02 us  [the longest x2 2.11 us: gather_expert(): near = lax.ppermute(piece, 'q', [(i, i ^ 2) for i in range(4)])]
    all_to_all x1, starting transfers between devices: 10.6 us -> 7.97 us  [on_device(): lax.all_to_all(produced, ('req', 'h'), split_axis=0, concat_axis=0, tiled...]
  transfers between devices with their start and end apart: 4 -> 8, of which waited for: 3 -> 2; matrix products, arithmetic and copies ran while one was open for 16% -> 21% of each run, Pallas kernels for 8% -> 9%
where the time goes in v4:
time: 155 us; the launch traced here: 154 us
  waiting for transfers between devices  61.4 us (40%)
  matrix products  23.3 us (15%)
  starting transfers between devices  22.2 us (14%)
  local copies, waits for them, and re-layouts  20.7 us (13%)
  Pallas kernels  14.6 us (9%)
  other arithmetic  10.7 us (7%)
    all_to_all x1, waiting for transfers between devices, on_device(): lax.all_to_all(produced, ('req', 'h'), split_axis=0, concat_axis=0, tiled...  36.2 us
    all_to_all x1, waiting for transfers between devices, on_device(): lax.all_to_all(outgoing, ('req', 'h'), split_axis=0, concat_axis=0, tiled...  25.2 us
    pallas_call x1, Pallas kernels, attention_core(): pl.pallas_call(attention_kernel, grid_spec=pltpu.PrefetchScalarGridSpec(n...  14.6 us
    all_to_all x1, starting transfers between devices, on_device(): lax.all_to_all(outgoing, ('req', 'h'), split_axis=0, concat_axis=0, tiled...  11.2 us
    all_to_all x1, starting transfers between devices, on_device(): lax.all_to_all(produced, ('req', 'h'), split_axis=0, concat_axis=0, tiled...  7.97 us
    dot_general x1, matrix products, on_device(): jnp.einsum('sch,hw->scw', hidden, down_all, preferred_element_type=jnp.fl...  7.44 us
    dot_general x1, matrix products, on_device(): jnp.einsum('scw,wh->sch', received, gate_cols, preferred_element_type=jnp...  5.06 us
    reshape x1, local copies, waits for them, and re-layouts, on_device(): pieces = gate_up_all.reshape(gate_up_all.shape[0], slices, 2 * width_dev)  4.53 us
  transfers between devices with their start and end apart: 8, of which 2 were waited for; matrix products, arithmetic and copies ran while one was open for 21% of the time, Pallas kernels for 9%

profile of v4, /device:TPU:0, one launch (start us, length us, event | category | flops | bytes accessed | tf_op | source)
XLA Modules:
  0.0 154.2 jit_solution(10262464917928950551)
XLA Ops:
  0.6 1.7 %collective-permute-start = (bf16[1024,256]{1,0:T(8,128)(2,1)}, bf16[1024,256]{1,0:T(8,128)(2,1)}, u32[]{:S(2)}, u32[]{:S(2)}) collective-permute-start(bf16[1024,256]{1,0:T(8,128)(2,1)} %bitcast.31), channel_id=1, source_target_pairs={{0,2},{1,3},{2,0},{3,1},{4,6},{5,7},{6,4},{7,5},{8,10},{9,11},{10,... | collective-permute-start | bytes 1572872 | tf_op jit(solution)/shard_map/ppermute | solution.py:144
  2.3 0.4 collective-permute-start.3
  3.0 1.1 fusion.7
  4.1 3.1 %fusion.18 = f32[128,2048]{1,0:T(8,128)S(1)} fusion(bf16[1024,2048]{1,0:T(8,128)(2,1)} %param.13, bf16[128,1024]{1,0:T(8,128)(2,1)} %param.12, f32[1024]{0:T(1024)} %param.15, f32[128]{0:T(128)S(1)} %add_rsqrt_fusion.1), kind=kOutput, calls=%fused_computation.31 | convolution fusion | flops 537395200 | bytes 5509632 | tf_op jit(solution)/shard_map/dot_general | solution.py:125
  7.2 1.4 fusion.34
  8.6 0.6 fusion.26
  10.0 1.0 tile.20
  11.0 2.3 %copy.21 = f32[128,1536]{1,0:T(8,128)} copy(f32[128,1536]{0,1:T(8,128)} %bitcast.27) | data formatting | bytes 1572864 | tf_op jit(solution)/shard_map/tile | solution.py:114
  13.3 1.0 tile.8
  14.3 2.3 %copy.20 = f32[128,1536]{1,0:T(8,128)} copy(f32[128,1536]{0,1:T(8,128)} %bitcast.28) | data formatting | bytes 1572864 | tf_op jit(solution)/shard_map/tile | solution.py:113
  16.6 2.2 %select_convert_fusion = bf16[128,1536]{1,0:T(8,128)(2,1)S(1)} fusion(f32[128,1536]{1,0:T(8,128)} %copy.21, f32[128,1504]{1,0:T(8,128)} %get-tuple-element.11, f32[128,32]{1,0:T(8,128)S(1)} %get-tuple-element.13, f32[128,32]{1,0:T(8,128)S(1)} %get-tuple-element.12, f32[128,1504]{1,0:T(8,128)} %get-tuple-element.10, f32[128,1536]{1,0:T(8,128)} %copy.20, ...), kind=kLoop, calls=%fused_computation.12 | loop fusion | flops 1769472 | bytes 4326912 | tf_op jit(solution)/shard_map/convert.2
  18.8 0.7 slice_multiply_fusion.1.q_ref
  19.6 0.4 collective-permute-start.2
  20.1 0.7 slice.57.kn_ref
  20.8 0.7 slice.66.vn_ref
  21.4 14.6 %shard_map.131 = bf16[128,1024]{1,0:T(8,128)(2,1)} custom-call(s32[1]{0:T(128)} %copy.22.length_ref, bf16[128,1024]{1,0:T(8,128)(2,1)} %slice_multiply_fusion.1.q_ref, bf16[2048,512]{1,0:T(8,128)(2,1)} %bitcast.29, bf16[2048,512]{1,0:T(8,128)(2,1)} %bitcast.30, bf16[128,512]{1,0:T(8,128)(2,1)} %slice.57.kn_ref, bf16[128,512]{1,0:T(8,128)(2,1)} %slice.66.vn_ref), custom_call_target="tpu_custom_call" | custom-call | tf_op jit(solution)/shard_map/pallas_call | solution.py:89
  36.3 1.4 fusion.36
  37.8 2.0 %pad_maximum_fusion.1 = bf16[512,1024]{1,0:T(8,128)(2,1)} fusion(bf16[128,1024]{1,0:T(8,128)(2,1)S(1)} %collective-permute-done.5, bf16[128,1024]{1,0:T(8,128)(2,1)} %collective-permute-done.4, bf16[128,1024]{1,0:T(8,128)(2,1)S(1)} %collective-permute-done.3, bf16[128,1024]{1,0:T(8,128)(2,1)S(1)} %bitcast.36), kind=kLoop, calls=%fused_computation.7 | loop fusion | flops 4194304 | bytes 2097152 | tf_op jit(solution)/shard_map/concatenate | solution.py:170
  39.7 3.0 %pad_maximum_fusion = bf16[1024,1024]{1,0:T(8,128)(2,1)} fusion(bf16[1024,256]{1,0:T(8,128)(2,1)} %collective-permute-done.2, bf16[1024,256]{1,0:T(8,128)(2,1)} %collective-permute-done.1, bf16[1024,256]{1,0:T(8,128)(2,1)} %collective-permute-done, bf16[1024,256]{1,0:T(8,128)(2,1)S(1)} %bitcast.33), kind=kLoop, calls=%fused_computation.1 | loop fusion | flops 8388608 | bytes 4194304 | tf_op jit(solution)/shard_map/concatenate | solution.py:169
  42.8 0.8 multiply_reduce_fusion
  43.6 2.4 %convolution_convert_fusion.1 = bf16[32,40,1024]{2,1,0:T(8,128)(2,1)} fusion(s32[128,32]{0,1:T(8,128)S(1)} %convolution_convert_fusion.2, pred[128,32]{0,1:T(8,128)(4,1)S(1)} %fusion.25, f32[128,1024]{1,0:T(8,128)S(1)} %fusion.36, bf16[128,1024]{1,0:T(8,128)(2,1)S(1)} %copy-done.1, f32[1024]{0:T(1024)S(1)} %copy-done.6, f32[128]{0:T(128)S(1)} %add_rsqrt_fusion), kind=kOutput, calls=%fused_computation.3 | convolution fusion | flops 337969152 | bytes 3432960 | tf_op jit(solution)/shard_map/tec,tw->ecw/dot_general | solution.py:190
  46.0 11.2 %all-to-all-start = ((bf16[32,40,1024]{2,1,0:T(8,128)(2,1)}), bf16[32,40,1024]{2,1,0:T(8,128)(2,1)}, u32[]{:S(2)}, u32[]{:S(2)}) async-start(bf16[32,40,1024]{2,1,0:T(8,128)(2,1)} %convolution_convert_fusion.1), calls=%async_computation | async-start | bytes 5242880 | tf_op jit(solution)/shard_map/all_to_all | solution.py:193
  57.2 4.5 %reshape.116 = bf16[1024,4,256]{2,1,0:T(4,128)(2,1)} reshape(bf16[1024,1024]{1,0:T(8,128)(2,1)} %pad_maximum_fusion) | data formatting | bytes 4194304 | tf_op jit(solution)/shard_map/reshape | solution.py:194
  61.8 3.3 %fusion.33 = (bf16[1024,4,128]{2,1,0:T(4,128)(2,1)S(1)}, bf16[1024,4,128]{2,1,0:T(4,128)(2,1)}) fusion(bf16[1024,4,256]{2,1,0:T(4,128)(2,1)} %reshape.116), kind=kLoop, calls=%fused_computation.58 | loop fusion | bytes 4194304 | tf_op jit(solution)/shard_map/slice | solution.py:196
  65.0 2.2 %reshape.120 = bf16[1024,512,1]{1,0,2:T(8,128)(2,1)} reshape(bf16[1024,4,128]{2,1,0:T(4,128)(2,1)} %get-tuple-element.9) | data formatting | bytes 2097152 | tf_op jit(solution)/shard_map/reshape | solution.py:195
  67.2 1.3 reshape.121
  68.5 25.2 %all-to-all-done = bf16[32,40,1024]{2,1,0:T(8,128)(2,1)} async-done(((bf16[32,40,1024]{2,1,0:T(8,128)(2,1)}), bf16[32,40,1024]{2,1,0:T(8,128)(2,1)}, u32[]{:S(2)}, u32[]{:S(2)}) %all-to-all-start) | async-done | bytes 2621472 | tf_op jit(solution)/shard_map/all_to_all | solution.py:193
  93.7 5.1 %fusion.37 = f32[32,40,512]{2,1,0:T(8,128)} fusion(bf16[32,40,1024]{2,1,0:T(8,128)(2,1)} %all-to-all-done, bf16[1024,512,1]{1,0,2:T(8,128)(2,1)} %reshape.120), kind=kOutput, calls=%fused_computation.62 | convolution fusion | flops 1342177280 | bytes 6291456 | tf_op jit(solution)/shard_map/scw,wh->sch/dot_general | solution.py:197
  98.7 7.4 %convolution_convert_fusion = bf16[32,40,1024]{2,1,0:T(8,128)(2,1)} fusion(f32[32,40,512]{2,1,0:T(8,128)} %fusion.37, bf16[32,40,1024]{2,1,0:T(8,128)(2,1)} %all-to-all-done, bf16[1024,512,1]{1,0,2:T(8,128)(2,1)} %reshape.121, bf16[512,1024]{1,0:T(8,128)(2,1)S(1)} %copy-done.2), kind=kOutput, calls=%fused_computation.2 | convolution fusion | flops 2689597440 | bytes 9961472 | tf_op jit(solution)/shard_map/sch,hw->scw/dot_general | solution.py:200
  106.2 8.0 %all-to-all-start.1 = ((bf16[32,40,1024]{2,1,0:T(8,128)(2,1)}), bf16[32,40,1024]{2,1,0:T(8,128)(2,1)}, u32[]{:S(2)}, u32[]{:S(2)}) async-start(bf16[32,40,1024]{2,1,0:T(8,128)(2,1)} %convolution_convert_fusion), calls=%async_computation.1 | async-start | bytes 5242880 | tf_op jit(solution)/shard_map/all_to_all | solution.py:203
  114.2 36.2 %all-to-all-done.1 = bf16[32,40,1024]{2,1,0:T(8,128)(2,1)} async-done(((bf16[32,40,1024]{2,1,0:T(8,128)(2,1)}), bf16[32,40,1024]{2,1,0:T(8,128)(2,1)}, u32[]{:S(2)}, u32[]{:S(2)}) %all-to-all-start.1) | async-done | bytes 2621472 | tf_op jit(solution)/shard_map/all_to_all | solution.py:203
  150.4 3.8 %fusion = bf16[128,1024]{1,0:T(8,128)(2,1)} fusion(bf16[32,40,1024]{2,1,0:T(8,128)(2,1)} %all-to-all-done.1, f32[128,32]{0,1:T(8,128)S(1)} %select_reduce_fusion, s32[128,32]{0,1:T(8,128)S(1)} %convolution_convert_fusion.2, pred[128,32]{0,1:T(8,128)(4,1)S(1)} %fusion.25), kind=kOutput, calls=%fused_computation.5 | convolution fusion | flops 2013888512 | bytes 2920448 | tf_op jit(solution)/shard_map/tec,ecw->tw/dot_general | solution.py:205
  (34 shorter events, 1.0 us)
Async XLA Ops:
  0.6 35.7 %copy-start = (bf16[1024,1024]{1,0:T(8,128)(2,1)S(1)}, bf16[1024,1024]{1,0:T(8,128)(2,1)}, u32[]{:S(2)}) copy-start(bf16[1024,1024]{1,0:T(8,128)(2,1)} %param.14) | copy-start | bytes 6291460
  0.6 18.9 %collective-permute-start = (bf16[1024,256]{1,0:T(8,128)(2,1)}, bf16[1024,256]{1,0:T(8,128)(2,1)}, u32[]{:S(2)}, u32[]{:S(2)}) collective-permute-start(bf16[1024,256]{1,0:T(8,128)(2,1)} %bitcast.31), channel_id=1, source_target_pairs={{0,2},{1,3},{2,0},{3,1},{4,6},{5,7},{6,4},{7,5},{8,10},{9,11},{10,... | collective-permute-start | bytes 1572872 | tf_op jit(solution)/shard_map/ppermute | solution.py:144
  2.3 37.4 %collective-permute-start.1 = (bf16[1024,256]{1,0:T(8,128)(2,1)}, bf16[1024,256]{1,0:T(8,128)(2,1)}, u32[]{:S(2)}, u32[]{:S(2)}) collective-permute-start(bf16[1024,256]{1,0:T(8,128)(2,1)} %bitcast.32), channel_id=1, source_target_pairs={{0,1},{1,0},{2,3},{3,2},{4,5},{5,4},{6,7},{7,6},{8,9},{9,8},{10,11... | collective-permute-start | bytes 1572872 | tf_op jit(solution)/shard_map/ppermute | solution.py:148
  2.3 33.7 %collective-permute-start.3 = (bf16[128,1024]{1,0:T(8,128)(2,1)}, bf16[128,1024]{1,0:T(8,128)(2,1)S(1)}, u32[]{:S(2)}, u32[]{:S(2)}) collective-permute-start(bf16[128,1024]{1,0:T(8,128)(2,1)} %bitcast.34), channel_id=1, source_target_pairs={{0,2},{1,3},{2,0},{3,1},{4,6},{5,7},{6,4},{7,5},{8,10},{9,11},{10,... | collective-permute-start | bytes 786440 | tf_op jit(solution)/shard_map/ppermute | solution.py:144
  2.8 35.0 %collective-permute-start.4 = (bf16[128,1024]{1,0:T(8,128)(2,1)}, bf16[128,1024]{1,0:T(8,128)(2,1)}, u32[]{:S(2)}, u32[]{:S(2)}) collective-permute-start(bf16[128,1024]{1,0:T(8,128)(2,1)} %bitcast.35), channel_id=1, source_target_pairs={{0,1},{1,0},{2,3},{3,2},{4,5},{5,4},{6,7},{7,6},{8,9},{9,8},{10,11... | collective-permute-start | bytes 786440 | tf_op jit(solution)/shard_map/ppermute | solution.py:148
  16.6 3.0 %copy-start.5 = (s32[128,8]{0,1:T(8,128)S(1)}, s32[128,8]{0,1:T(8,128)}, u32[]{:S(2)}) copy-start(s32[128,8]{0,1:T(8,128)} %param.20) | copy-start | bytes 12292
  19.6 20.2 %collective-permute-start.2 = (bf16[1024,256]{1,0:T(8,128)(2,1)}, bf16[1024,256]{1,0:T(8,128)(2,1)}, u32[]{:S(2)}, u32[]{:S(2)}) collective-permute-start(bf16[1024,256]{1,0:T(8,128)(2,1)} %collective-permute-done), channel_id=1, source_target_pairs={{0,1},{1,0},{2,3},{3,2},{4,5},{5,4},{6,7},{7,6},{8,9},{9,8},{10,11... | collective-permute-start | bytes 1572872 | tf_op jit(solution)/shard_map/ppermute | solution.py:149
  36.0 1.8 %copy-start.4 = (bf16[1,128,1024]{2,1,0:T(8,128)(2,1)S(1)}, bf16[1,128,1024]{2,1,0:T(8,128)(2,1)}, u32[]{:S(2)}) copy-start(bf16[1,128,1024]{2,1,0:T(8,128)(2,1)} %param.23) | copy-start | bytes 786436
  36.0 3.7 %copy-start.3 = (bf16[1,1024,256]{2,1,0:T(8,128)(2,1)S(1)}, bf16[1,1024,256]{2,1,0:T(8,128)(2,1)}, u32[]{:S(2)}) copy-start(bf16[1,1024,256]{2,1,0:T(8,128)(2,1)} %param.22) | copy-start | bytes 1572868
  36.0 1.7 %collective-permute-start.5 = (bf16[128,1024]{1,0:T(8,128)(2,1)S(1)}, bf16[128,1024]{1,0:T(8,128)(2,1)S(1)}, u32[]{:S(2)}, u32[]{:S(2)}) collective-permute-start(bf16[128,1024]{1,0:T(8,128)(2,1)S(1)} %collective-permute-done.3), channel_id=1, source_target_pairs={{0,1},{1,0},{2,3},{3,2},{4,5},{5,4},{6,7},{7,6},{8,9},{9,8},{10,11... | collective-permute-start | bytes 786440 | tf_op jit(solution)/shard_map/ppermute | solution.py:149
  39.7 3.1 %copy-start.1 = (bf16[128,1024]{1,0:T(8,128)(2,1)S(1)}, bf16[128,1024]{1,0:T(8,128)(2,1)}, u32[]{:S(2)}) copy-start(bf16[128,1024]{1,0:T(8,128)(2,1)} %param.12) | copy-start | bytes 786436
  39.7 3.9 %copy-start.6 = (f32[1024]{0:T(1024)S(1)}, f32[1024]{0:T(1024)}, u32[]{:S(2)}) copy-start(f32[1024]{0:T(1024)} %param.16) | copy-start | bytes 12292
  46.0 47.6 %all-to-all-start = ((bf16[32,40,1024]{2,1,0:T(8,128)(2,1)}), bf16[32,40,1024]{2,1,0:T(8,128)(2,1)}, u32[]{:S(2)}, u32[]{:S(2)}) async-start(bf16[32,40,1024]{2,1,0:T(8,128)(2,1)} %convolution_convert_fusion.1), calls=%async_computation | async-start | bytes 5242880 | tf_op jit(solution)/shard_map/all_to_all | solution.py:193
  68.5 30.2 %copy-start.2 = (bf16[512,1024]{1,0:T(8,128)(2,1)S(1)}, bf16[512,1024]{1,0:T(8,128)(2,1)}, u32[]{:S(2)}) copy-start(bf16[512,1024]{1,0:T(8,128)(2,1)} %pad_maximum_fusion.1) | copy-start | bytes 3145732
  106.2 8.0 %copy-start.7 = (f32[128,8]{0,1:T(8,128)S(1)}, f32[128,8]{0,1:T(8,128)}, u32[]{:S(2)}) copy-start(f32[128,8]{0,1:T(8,128)} %param.21) | copy-start | bytes 12292
  106.2 44.2 %all-to-all-start.1 = ((bf16[32,40,1024]{2,1,0:T(8,128)(2,1)}), bf16[32,40,1024]{2,1,0:T(8,128)(2,1)}, u32[]{:S(2)}, u32[]{:S(2)}) async-start(bf16[32,40,1024]{2,1,0:T(8,128)(2,1)} %convolution_convert_fusion), calls=%async_computation.1 | async-start | bytes 5242880 | tf_op jit(solution)/shard_map/all_to_all | solution.py:203

commit v5 on v4

--- a/solution.py
+++ b/solution.py
@@ -32,23 +32,40 @@
     )
 
 
-def attention_kernel(length_ref, q_ref, kc_ref, vc_ref, kn_ref, vn_ref, o_ref):
+def turn(values, cosine, sine, lead, half):
+    partner = jnp.where(
+        lead, pltpu.roll(values, values.shape[1] - half, 1), pltpu.roll(values, half, 1)
+    )
+    return jnp.where(lead, values * cosine - partner * sine, values * cosine + partner * sine)
+
+
+def attention_kernel(length_ref, q_ref, k_ref, v_ref, cos_ref, sin_ref, kc_ref, vc_ref, o_ref):
     length = length_ref[0]
     span, lanes = kc_ref.shape
-    rows = kn_ref.shape[0]
+    rows = k_ref.shape[0]
     half = lanes // 2
+    quarter = HEAD // 2
+    cosine = cos_ref[...]
+    sine = sin_ref[...]
+    lane = lax.broadcasted_iota(jnp.int32, (rows, lanes), 1)
+    lead = lane % HEAD < quarter
+    low = lane < half
     kc = kc_ref[...]
     vc = vc_ref[...]
-    kn = kn_ref[...]
-    vn = vn_ref[...]
+    kn = turn(k_ref[...], cosine, sine, lead, quarter).astype(jnp.bfloat16)
+    vn = v_ref[...].astype(jnp.bfloat16)
     column = lax.broadcasted_iota(jnp.int32, (rows, span), 1)
     cache_ok = column < length
     new_col = lax.broadcasted_iota(jnp.int32, (rows, rows), 1)
     new_row = lax.broadcasted_iota(jnp.int32, (rows, rows), 0)
     new_ok = new_col <= new_row
-    low = lax.broadcasted_iota(jnp.int32, (rows, lanes), 1) < half
-    first = q_ref[:, :lanes].astype(jnp.float32)
-    second = q_ref[:, lanes:].astype(jnp.float32)
+
+    def scaled(values):
+        rotated = turn(values, cosine, sine, lead, quarter).astype(jnp.bfloat16)
+        return (rotated * 0.015625).astype(jnp.bfloat16).astype(jnp.float32)
+
+    first = scaled(q_ref[:, :lanes])
+    second = scaled(q_ref[:, lanes:])
     queries = (
         jnp.where(low, first, 0.0),
         jnp.where(low, pltpu.roll(first, half, 1), 0.0),
@@ -80,12 +97,15 @@
     o_ref[:, lanes:] = right.astype(jnp.bfloat16)
 
 
-def attention_core(length, query, kc, vc, kn, vn, interpret=False):
-    rows, qwidth = query.shape
+def attention_core(length, mixed, cosine, sine, kc, vc, interpret=False):
+    rows = mixed.shape[0]
     span, kvwidth = kc.shape
+    qwidth = HEADS * HEAD
     lanes = 2 * HEAD
     pairs = kvwidth // lanes
     qblock = qwidth // pairs
+    kstart = qwidth // lanes
+    vstart = kstart + pairs
     return pl.pallas_call(
         attention_kernel,
         grid_spec=pltpu.PrefetchScalarGridSpec(
@@ -93,48 +113,37 @@
             grid=(pairs,),
             in_specs=[
                 pl.BlockSpec((rows, qblock), lambda p, n: (0, p)),
+                pl.BlockSpec((rows, lanes), lambda p, n: (0, kstart + p)),
+                pl.BlockSpec((rows, lanes), lambda p, n: (0, vstart + p)),
+                pl.BlockSpec((rows, lanes), lambda p, n: (0, 0)),
+                pl.BlockSpec((rows, lanes), lambda p, n: (0, 0)),
                 pl.BlockSpec((span, lanes), lambda p, n: (0, p)),
                 pl.BlockSpec((span, lanes), lambda p, n: (0, p)),
-                pl.BlockSpec((rows, lanes), lambda p, n: (0, p)),
-                pl.BlockSpec((rows, lanes), lambda p, n: (0, p)),
             ],
             out_specs=pl.BlockSpec((rows, qblock), lambda p, n: (0, p)),
         ),
         out_shape=jax.ShapeDtypeStruct((rows, qwidth), jnp.bfloat16),
         interpret=interpret,
-    )(length, query, kc, vc, kn, vn)
-
-
-def rotate_lanes(values, places):
-    half = HEAD // 2
-    freq = 10000.0 ** (-jnp.arange(half, dtype=jnp.float32) / half)
-    angle = places[:, None] * freq[None, :]
-    repeat = values.shape[1] // half
-    cosine = jnp.tile(jnp.cos(angle), (1, repeat))
-    sine = jnp.tile(jnp.sin(angle), (1, repeat))
-    lead = (jnp.arange(values.shape[1]) % HEAD < half)[None, :]
-    partner = jnp.where(lead, jnp.roll(values, -half, axis=1), jnp.roll(values, half, axis=1))
-    return jnp.where(lead, values * cosine - partner * sine, values * cosine + partner * sine)
+    )(length, mixed, mixed, mixed, cosine, sine, kc, vc)
 
 
 def attend(tokens, qkv_weight, out_weight, norm_attn, keys_cache, values_cache, length, interpret=False):
     rows = tokens.shape[0]
-    qwidth = HEADS * HEAD
-    kvwidth = KV_HEADS * HEAD
+    half = HEAD // 2
     normed = rms_scale(tokens, norm_attn).astype(jnp.bfloat16)
     mixed = jnp.dot(normed, qkv_weight, preferred_element_type=jnp.float32)
     places = (length + jnp.arange(rows, dtype=jnp.int32)).astype(jnp.float32)
-    turned = rotate_lanes(mixed[:, : qwidth + kvwidth], places)
-    query = (turned[:, :qwidth].astype(jnp.bfloat16) * 0.015625).astype(jnp.bfloat16)
-    key_new = turned[:, qwidth:].astype(jnp.bfloat16)
-    value_new = mixed[:, qwidth + kvwidth :].astype(jnp.bfloat16)
+    freq = 10000.0 ** (-jnp.arange(half, dtype=jnp.float32) / half)
+    angle = places[:, None] * freq[None, :]
+    cosine = jnp.tile(jnp.cos(angle), (1, 4))
+    sine = jnp.tile(jnp.sin(angle), (1, 4))
     heads_out = attention_core(
         length.reshape(1).astype(jnp.int32),
-        query,
+        mixed,
+        cosine,
+        sine,
         keys_cache,
         values_cache,
-        key_new,
-        value_new,
         interpret=interpret,
     )
     return jnp.dot(heads_out, out_weight, preferred_element_type=jnp.float32)
@@ -166,12 +175,16 @@
 ):
     slices = lax.axis_size("q")
     width_dev = down_weight.shape[1]
-    gate_up_all = jnp.concatenate(gather_expert(gate_up[0]), axis=1)
-    down_all = jnp.concatenate(gather_expert(down_weight[0]), axis=0)
+    gate_up_parts = gather_expert(gate_up[0])
+    down_parts = gather_expert(down_weight[0])
     branch = attend(
         tokens, qkv_weight, out_weight, norm_attn, keys_cache[0], values_cache[0], lengths[0]
     )
-    branch, gate_up_all, down_all = lax.optimization_barrier((branch, gate_up_all, down_all))
+    branch, gate_up_parts, down_parts = lax.optimization_barrier(
+        (branch, gate_up_parts, down_parts)
+    )
+    gate_up_all = jnp.concatenate(gate_up_parts, axis=1)
+    down_all = jnp.concatenate(down_parts, axis=0)
     carried = tokens.astype(jnp.float32) + 0.22 * branch
     normed = rms_scale(carried, norm_expert).astype(jnp.bfloat16)
     rows = tokens.shape[0]

time: 155 us -> 145 us (0.935)
  local copies, waits for them, and re-layouts: 20.7 us -> 12.7 us
  other arithmetic: 10.7 us -> 5.05 us
  waiting for transfers between devices: 61.4 us -> 64.1 us
    ppermute x2, waiting for transfers between devices: 0.01 us -> 6.77 us  [gather_expert(): near = lax.ppermute(piece, 'q', [(i, i ^ 2) for i in range(4)])]
    another operation x4, local copies, waits for them, and re-layouts: 6.53 us -> 1.48 us  [the longest x2 0.74 us: attend(): sine = jnp.tile(jnp.sin(angle), (1, 4))]
    all_to_all x1, waiting for transfers between devices: 25.2 us -> 22.2 us  [on_device(): lax.all_to_all(outgoing, ('req', 'h'), split_axis=0, concat_axis=0, tiled...]
    slice x4 -> x0, local copies, waits for them, and re-layouts: 2.81 us -> none  [the longest x2 1.47 us: rotate_lanes(): jnp.roll(values, -half, axis=1)]
    another operation x1 -> x0, other arithmetic: 2.22 us -> none
    concatenate x2 -> x1, other arithmetic: 5.01 us -> 2.85 us  [on_device(): gate_up_all = jnp.concatenate(gate_up_parts, axis=1)]
  transfers between devices with their start and end apart: 8 -> 8, of which waited for: 2 -> 3; matrix products, arithmetic and copies ran while one was open for 21% -> 16% of each run, Pallas kernels for 9% -> 10%
where the time goes in v5:
time: 145 us; the launch traced here: 144 us
  waiting for transfers between devices  64.1 us (44%)
  matrix products  24.1 us (17%)
  starting transfers between devices  21.5 us (15%)
  Pallas kernels  15.1 us (10%)
  local copies, waits for them, and re-layouts  12.7 us (9%)
  other arithmetic  5.05 us (3%)
  between operations  1.46 us (1%)
    all_to_all x1, waiting for transfers between devices, on_device(): lax.all_to_all(produced, ('req', 'h'), split_axis=0, concat_axis=0, tiled...  35.2 us
    all_to_all x1, waiting for transfers between devices, on_device(): lax.all_to_all(outgoing, ('req', 'h'), split_axis=0, concat_axis=0, tiled...  22.2 us
    pallas_call x1, Pallas kernels, attention_core(): pl.pallas_call(attention_kernel, grid_spec=pltpu.PrefetchScalarGridSpec(n...  15.1 us
    all_to_all x1, starting transfers between devices, on_device(): lax.all_to_all(outgoing, ('req', 'h'), split_axis=0, concat_axis=0, tiled...  11.3 us
    all_to_all x1, starting transfers between devices, on_device(): lax.all_to_all(produced, ('req', 'h'), split_axis=0, concat_axis=0, tiled...  7.3 us
    dot_general x1, matrix products, on_device(): jnp.einsum('sch,hw->scw', hidden, down_all, preferred_element_type=jnp.fl...  7.23 us
    ppermute x2, waiting for transfers between devices, gather_expert(): near = lax.ppermute(piece, 'q', [(i, i ^ 2) for i in range(4)])  6.77 us
    dot_general x1, matrix products, on_device(): jnp.einsum('scw,wh->sch', received, gate_cols, preferred_element_type=jnp...  5.07 us
  transfers between devices with their start and end apart: 8, of which 3 were waited for; matrix products, arithmetic and copies ran while one was open for 16% of the time, Pallas kernels for 10%

profile of v5, /device:TPU:0, one launch (start us, length us, event | category | flops | bytes accessed | tf_op | source)
XLA Modules:
  0.0 144.1 jit_solution(15726365506251270616)
XLA Ops:
  0.6 0.0 copy-start
  0.6 1.7 %collective-permute-start = (bf16[1024,256]{1,0:T(8,128)(2,1)}, bf16[1024,256]{1,0:T(8,128)(2,1)S(1)}, u32[]{:S(2)}, u32[]{:S(2)}) collective-permute-start(bf16[1024,256]{1,0:T(8,128)(2,1)} %bitcast.29), channel_id=1, source_target_pairs={{0,2},{1,3},{2,0},{3,1},{4,6},{5,7},{6,4},{7,5},{8,10},{9,11},{10,... | collective-permute-start | bytes 1572872 | tf_op jit(solution)/shard_map/ppermute | solution.py:153
  2.3 0.0 collective-permute-start.1
  2.3 0.4 collective-permute-start.3
  2.8 0.2 collective-permute-start.4
  3.6 1.1 fusion.11
  4.7 0.1 multiply_sine_fusion
  4.9 0.0 copy-start.5
  4.9 4.0 %fusion.22.q_ref.k_ref.v_ref = f32[128,2048]{1,0:T(8,128)} fusion(bf16[1024,2048]{1,0:T(8,128)(2,1)} %param.13, bf16[128,1024]{1,0:T(8,128)(2,1)} %param.12, f32[1024]{0:T(1024)} %param.15, f32[128]{0:T(128)S(1)} %add_rsqrt_fusion.1), kind=kOutput, calls=%fused_computation.32 | convolution fusion | flops 537395200 | bytes 5509632 | tf_op jit(solution)/shard_map/dot_general | solution.py:134
  9.0 6.8 %collective-permute-done = bf16[1024,256]{1,0:T(8,128)(2,1)S(1)} collective-permute-done((bf16[1024,256]{1,0:T(8,128)(2,1)}, bf16[1024,256]{1,0:T(8,128)(2,1)S(1)}, u32[]{:S(2)}, u32[]{:S(2)}) %collective-permute-start) | collective-permute-done | bytes 524320 | tf_op jit(solution)/shard_map/ppermute | solution.py:153
  15.7 0.0 collective-permute-start.2
  15.8 0.7 copy.20.cos_ref
  16.5 0.7 copy.21.sin_ref
  17.3 15.1 %shard_map.131 = bf16[128,1024]{1,0:T(8,128)(2,1)} custom-call(s32[1]{0:T(128)} %copy.22.length_ref, f32[128,2048]{1,0:T(8,128)} %fusion.22.q_ref.k_ref.v_ref, f32[128,2048]{1,0:T(8,128)} %fusion.22.q_ref.k_ref.v_ref, f32[128,2048]{1,0:T(8,128)} %fusion.22.q_ref.k_ref.v_ref, f32[128,128]{1,0:T(8,128)} %copy.20.cos_ref, f32[128,128]{1,0:T(8,128)} %copy.21.sin_ref, ...), custom_call_target="tpu_custom_call" | custom-call | tf_op jit(solution)/shard_map/pallas_call | solution.py:109
  32.4 0.1 convolution_convert_fusion.2
  32.5 0.6 collective-permute-start.5
  33.1 1.4 fusion.35
  34.5 0.0 copy-start.10
  34.5 0.9 multiply_reduce_fusion
  35.5 2.4 %convolution_convert_fusion.1 = bf16[32,40,1024]{2,1,0:T(8,128)(2,1)} fusion(s32[128,32]{0,1:T(8,128)S(1)} %convolution_convert_fusion.2, pred[128,32]{0,1:T(8,128)(4,1)S(1)} %fusion.29, f32[128,1024]{1,0:T(8,128)S(1)} %fusion.35, bf16[128,1024]{1,0:T(8,128)(2,1)S(1)} %copy-done.1, f32[1024]{0:T(1024)S(1)} %copy-done.6, f32[128]{0:T(128)S(1)} %add_rsqrt_fusion), kind=kOutput, calls=%fused_computation.3 | convolution fusion | flops 337969152 | bytes 3432960 | tf_op jit(solution)/shard_map/tec,tw->ecw/dot_general | solution.py:203
  37.9 11.3 %all-to-all-start = ((bf16[32,40,1024]{2,1,0:T(8,128)(2,1)}), bf16[32,40,1024]{2,1,0:T(8,128)(2,1)}, u32[]{:S(2)}, u32[]{:S(2)}) async-start(bf16[32,40,1024]{2,1,0:T(8,128)(2,1)} %convolution_convert_fusion.1), calls=%async_computation | async-start | bytes 5242880 | tf_op jit(solution)/shard_map/all_to_all | solution.py:206
  49.3 2.9 %pad_maximum_fusion = bf16[1024,1024]{1,0:T(8,128)(2,1)} fusion(bf16[1024,256]{1,0:T(8,128)(2,1)} %collective-permute-done.2, bf16[1024,256]{1,0:T(8,128)(2,1)} %copy-done.4, bf16[1024,256]{1,0:T(8,128)(2,1)S(1)} %collective-permute-done, bf16[1024,256]{1,0:T(8,128)(2,1)S(1)} %bitcast.31), kind=kLoop, calls=%fused_computation.1 | loop fusion | flops 8388608 | bytes 4194304 | tf_op jit(solution)/shard_map/concatenate | solution.py:186
  52.1 4.5 %reshape.106 = bf16[1024,4,256]{2,1,0:T(4,128)(2,1)} reshape(bf16[1024,1024]{1,0:T(8,128)(2,1)} %pad_maximum_fusion) | data formatting | bytes 4194304 | tf_op jit(solution)/shard_map/reshape | solution.py:207
  56.6 3.2 %fusion.34 = (bf16[1024,4,128]{2,1,0:T(4,128)(2,1)S(1)}, bf16[1024,4,128]{2,1,0:T(4,128)(2,1)}) fusion(bf16[1024,4,256]{2,1,0:T(4,128)(2,1)} %reshape.106), kind=kLoop, calls=%fused_computation.52 | loop fusion | bytes 4194304 | tf_op jit(solution)/shard_map/slice | solution.py:209
  59.9 2.2 %reshape.110 = bf16[1024,512,1]{1,0,2:T(8,128)(2,1)} reshape(bf16[1024,4,128]{2,1,0:T(4,128)(2,1)} %get-tuple-element.21) | data formatting | bytes 2097152 | tf_op jit(solution)/shard_map/reshape | solution.py:208
  62.1 1.2 reshape.111
  63.3 22.2 %all-to-all-done = bf16[32,40,1024]{2,1,0:T(8,128)(2,1)} async-done(((bf16[32,40,1024]{2,1,0:T(8,128)(2,1)}), bf16[32,40,1024]{2,1,0:T(8,128)(2,1)}, u32[]{:S(2)}, u32[]{:S(2)}) %all-to-all-start) | async-done | bytes 2621472 | tf_op jit(solution)/shard_map/all_to_all | solution.py:206
  85.5 5.1 %fusion.36 = f32[32,40,512]{2,1,0:T(8,128)} fusion(bf16[32,40,1024]{2,1,0:T(8,128)(2,1)} %all-to-all-done, bf16[1024,512,1]{1,0,2:T(8,128)(2,1)} %reshape.110), kind=kOutput, calls=%fused_computation.54 | convolution fusion | flops 1342177280 | bytes 6291456 | tf_op jit(solution)/shard_map/scw,wh->sch/dot_general | solution.py:210
  90.6 7.2 %convolution_convert_fusion = bf16[32,40,1024]{2,1,0:T(8,128)(2,1)} fusion(f32[32,40,512]{2,1,0:T(8,128)} %fusion.36, bf16[32,40,1024]{2,1,0:T(8,128)(2,1)} %all-to-all-done, bf16[1024,512,1]{1,0,2:T(8,128)(2,1)S(1)} %copy-done.2, bf16[128,1024]{1,0:T(8,128)(2,1)} %copy-done.10, bf16[128,1024]{1,0:T(8,128)(2,1)} %collective-permute-done.4, ...), kind=kOutput, calls=%fused_computation.2 | convolution fusion | flops 2693791744 | bytes 9961472 | tf_op jit(solution)/shard_map/sch,hw->scw/dot_general | solution.py:213
  97.8 7.3 %all-to-all-start.1 = ((bf16[32,40,1024]{2,1,0:T(8,128)(2,1)}), bf16[32,40,1024]{2,1,0:T(8,128)(2,1)}, u32[]{:S(2)}, u32[]{:S(2)}) async-start(bf16[32,40,1024]{2,1,0:T(8,128)(2,1)} %convolution_convert_fusion), calls=%async_computation.1 | async-start | bytes 5242880 | tf_op jit(solution)/shard_map/all_to_all | solution.py:216
  105.1 35.2 %all-to-all-done.1 = bf16[32,40,1024]{2,1,0:T(8,128)(2,1)} async-done(((bf16[32,40,1024]{2,1,0:T(8,128)(2,1)}), bf16[32,40,1024]{2,1,0:T(8,128)(2,1)}, u32[]{:S(2)}, u32[]{:S(2)}) %all-to-all-start.1) | async-done | bytes 2621472 | tf_op jit(solution)/shard_map/all_to_all | solution.py:216
  140.3 3.8 %fusion = bf16[128,1024]{1,0:T(8,128)(2,1)} fusion(bf16[32,40,1024]{2,1,0:T(8,128)(2,1)} %all-to-all-done.1, f32[128,32]{0,1:T(8,128)S(1)} %select_reduce_fusion, s32[128,32]{0,1:T(8,128)S(1)} %convolution_convert_fusion.2, pred[128,32]{0,1:T(8,128)(4,1)S(1)} %fusion.29), kind=kOutput, calls=%fused_computation.5 | convolution fusion | flops 2013888512 | bytes 2920448 | tf_op jit(solution)/shard_map/tec,ecw->tw/dot_general | solution.py:218
  (32 shorter events, 0.1 us)
Async XLA Ops:
  0.6 32.4 %copy-start = (bf16[1024,1024]{1,0:T(8,128)(2,1)S(1)}, bf16[1024,1024]{1,0:T(8,128)(2,1)}, u32[]{:S(2)}) copy-start(bf16[1024,1024]{1,0:T(8,128)(2,1)} %param.14) | copy-start | bytes 6291460
  0.6 15.1 %collective-permute-start = (bf16[1024,256]{1,0:T(8,128)(2,1)}, bf16[1024,256]{1,0:T(8,128)(2,1)S(1)}, u32[]{:S(2)}, u32[]{:S(2)}) collective-permute-start(bf16[1024,256]{1,0:T(8,128)(2,1)} %bitcast.29), channel_id=1, source_target_pairs={{0,2},{1,3},{2,0},{3,1},{4,6},{5,7},{6,4},{7,5},{8,10},{9,11},{10,... | collective-permute-start | bytes 1572872 | tf_op jit(solution)/shard_map/ppermute | solution.py:153
  2.3 32.1 %collective-permute-start.1 = (bf16[1024,256]{1,0:T(8,128)(2,1)}, bf16[1024,256]{1,0:T(8,128)(2,1)S(1)}, u32[]{:S(2)}, u32[]{:S(2)}) collective-permute-start(bf16[1024,256]{1,0:T(8,128)(2,1)} %bitcast.30), channel_id=1, source_target_pairs={{0,1},{1,0},{2,3},{3,2},{4,5},{5,4},{6,7},{7,6},{8,9},{9,8},{10,11... | collective-permute-start | bytes 1572872 | tf_op jit(solution)/shard_map/ppermute | solution.py:157
  2.3 30.2 %collective-permute-start.3 = (bf16[128,1024]{1,0:T(8,128)(2,1)}, bf16[128,1024]{1,0:T(8,128)(2,1)S(1)}, u32[]{:S(2)}, u32[]{:S(2)}) collective-permute-start(bf16[128,1024]{1,0:T(8,128)(2,1)} %bitcast.34), channel_id=1, source_target_pairs={{0,2},{1,3},{2,0},{3,1},{4,6},{5,7},{6,4},{7,5},{8,10},{9,11},{10,... | collective-permute-start | bytes 786440 | tf_op jit(solution)/shard_map/ppermute | solution.py:153
  2.8 31.7 %collective-permute-start.4 = (bf16[128,1024]{1,0:T(8,128)(2,1)}, bf16[128,1024]{1,0:T(8,128)(2,1)}, u32[]{:S(2)}, u32[]{:S(2)}) collective-permute-start(bf16[128,1024]{1,0:T(8,128)(2,1)} %bitcast.35), channel_id=1, source_target_pairs={{0,1},{1,0},{2,3},{3,2},{4,5},{5,4},{6,7},{7,6},{8,9},{9,8},{10,11... | collective-permute-start | bytes 786440 | tf_op jit(solution)/shard_map/ppermute | solution.py:157
  4.9 10.8 %copy-start.5 = (s32[128,8]{0,1:T(8,128)S(1)}, s32[128,8]{0,1:T(8,128)}, u32[]{:S(2)}) copy-start(s32[128,8]{0,1:T(8,128)} %param.20) | copy-start | bytes 12292
  15.7 18.8 %collective-permute-start.2 = (bf16[1024,256]{1,0:T(8,128)(2,1)S(1)}, bf16[1024,256]{1,0:T(8,128)(2,1)}, u32[]{:S(2)}, u32[]{:S(2)}) collective-permute-start(bf16[1024,256]{1,0:T(8,128)(2,1)S(1)} %collective-permute-done), channel_id=1, source_target_pairs={{0,1},{1,0},{2,3},{3,2},{4,5},{5,4},{6,7},{7,6},{8,9},{9,8},{10,11... | collective-permute-start | bytes 1572872 | tf_op jit(solution)/shard_map/ppermute | solution.py:158
  32.4 2.2 %copy-start.1 = (bf16[128,1024]{1,0:T(8,128)(2,1)S(1)}, bf16[128,1024]{1,0:T(8,128)(2,1)}, u32[]{:S(2)}) copy-start(bf16[128,1024]{1,0:T(8,128)(2,1)} %param.12) | copy-start | bytes 786436
  32.4 3.1 %copy-start.6 = (f32[1024]{0:T(1024)S(1)}, f32[1024]{0:T(1024)}, u32[]{:S(2)}) copy-start(f32[1024]{0:T(1024)} %param.16) | copy-start | bytes 12292
  32.5 5.4 %copy-start.9 = (bf16[128,1024]{1,0:T(8,128)(2,1)}, bf16[128,1024]{1,0:T(8,128)(2,1)S(1)}, u32[]{:S(2)}) copy-start(bf16[128,1024]{1,0:T(8,128)(2,1)S(1)} %collective-permute-done.3) | copy-start | bytes 786436
  32.5 2.0 %collective-permute-start.5 = (bf16[128,1024]{1,0:T(8,128)(2,1)S(1)}, bf16[128,1024]{1,0:T(8,128)(2,1)S(1)}, u32[]{:S(2)}, u32[]{:S(2)}) collective-permute-start(bf16[128,1024]{1,0:T(8,128)(2,1)S(1)} %collective-permute-done.3), channel_id=1, source_target_pairs={{0,1},{1,0},{2,3},{3,2},{4,5},{5,4},{6,7},{7,6},{8,9},{9,8},{10,11... | collective-permute-start | bytes 786440 | tf_op jit(solution)/shard_map/ppermute | solution.py:158
  34.5 1.0 copy-start.4
  34.5 0.9 copy-start.10
  37.9 11.3 %copy-start.3 = (bf16[1,1024,256]{2,1,0:T(8,128)(2,1)S(1)}, bf16[1,1024,256]{2,1,0:T(8,128)(2,1)}, u32[]{:S(2)}) copy-start(bf16[1,1024,256]{2,1,0:T(8,128)(2,1)} %param.22) | copy-start | bytes 1572868
  37.9 47.6 %all-to-all-start = ((bf16[32,40,1024]{2,1,0:T(8,128)(2,1)}), bf16[32,40,1024]{2,1,0:T(8,128)(2,1)}, u32[]{:S(2)}, u32[]{:S(2)}) async-start(bf16[32,40,1024]{2,1,0:T(8,128)(2,1)} %convolution_convert_fusion.1), calls=%async_computation | async-start | bytes 5242880 | tf_op jit(solution)/shard_map/all_to_all | solution.py:206
  63.3 27.2 %copy-start.2 = (bf16[1024,512,1]{1,0,2:T(8,128)(2,1)S(1)}, bf16[1024,512,1]{1,0,2:T(8,128)(2,1)}, u32[]{:S(2)}) copy-start(bf16[1024,512,1]{1,0,2:T(8,128)(2,1)} %reshape.111) | copy-start | bytes 3145732
  63.3 27.2 %copy-start.8 = (bf16[1,128,1024]{2,1,0:T(8,128)(2,1)S(1)}, bf16[1,128,1024]{2,1,0:T(8,128)(2,1)}, u32[]{:S(2)}) copy-start(bf16[1,128,1024]{2,1,0:T(8,128)(2,1)} %param.23) | copy-start | bytes 786436
  97.8 7.3 %copy-start.7 = (f32[128,8]{0,1:T(8,128)S(1)}, f32[128,8]{0,1:T(8,128)}, u32[]{:S(2)}) copy-start(f32[128,8]{0,1:T(8,128)} %param.21) | copy-start | bytes 12292
  97.8 42.5 %all-to-all-start.1 = ((bf16[32,40,1024]{2,1,0:T(8,128)(2,1)}), bf16[32,40,1024]{2,1,0:T(8,128)(2,1)}, u32[]{:S(2)}, u32[]{:S(2)}) async-start(bf16[32,40,1024]{2,1,0:T(8,128)(2,1)} %convolution_convert_fusion), calls=%async_computation.1 | async-start | bytes 5242880 | tf_op jit(solution)/shard_map/all_to_all | solution.py:216

commit v6 on v5

--- a/solution.py
+++ b/solution.py
@@ -149,14 +149,8 @@
     return jnp.dot(heads_out, out_weight, preferred_element_type=jnp.float32)
 
 
-def gather_expert(piece):
-    near = lax.ppermute(piece, "q", [(i, i ^ 2) for i in range(4)])
-    return [
-        piece,
-        near,
-        lax.ppermute(piece, "q", [(i, i ^ 1) for i in range(4)]),
-        lax.ppermute(near, "q", [(i, i ^ 1) for i in range(4)]),
-    ]
+def swap(piece, bit):
+    return lax.ppermute(piece, "q", [(i, i ^ bit) for i in range(lax.axis_size("q"))])
 
 
 def on_device(
@@ -175,19 +169,22 @@
 ):
     slices = lax.axis_size("q")
     width_dev = down_weight.shape[1]
-    gate_up_parts = gather_expert(gate_up[0])
-    down_parts = gather_expert(down_weight[0])
+    own_gu = gate_up[0]
+    own_dw = down_weight[0]
+    far_gu = swap(own_gu, 2)
+    far_dw = swap(own_dw, 2)
+    side_gu = swap(own_gu, 1)
+    side_dw = swap(own_dw, 1)
     branch = attend(
         tokens, qkv_weight, out_weight, norm_attn, keys_cache[0], values_cache[0], lengths[0]
     )
-    branch, gate_up_parts, down_parts = lax.optimization_barrier(
-        (branch, gate_up_parts, down_parts)
-    )
-    gate_up_all = jnp.concatenate(gate_up_parts, axis=1)
-    down_all = jnp.concatenate(down_parts, axis=0)
+    branch, far_gu, far_dw = lax.optimization_barrier((branch, far_gu, far_dw))
+    gate_up_all = jnp.concatenate([own_gu, far_gu, side_gu, swap(far_gu, 1)], axis=1)
+    down_all = jnp.concatenate([own_dw, far_dw, side_dw, swap(far_dw, 1)], axis=0)
     carried = tokens.astype(jnp.float32) + 0.22 * branch
     normed = rms_scale(carried, norm_expert).astype(jnp.bfloat16)
-    rows = tokens.shape[0]
+    rows, width = normed.shape
+    part = width // 2
     capacity = CAPACITY
     hits = routes[:, :, None] == jnp.arange(EXPERTS, dtype=jnp.int32)[None, None, :]
     marks = jnp.any(hits, axis=1)
@@ -200,28 +197,46 @@
     pick = marks[:, :, None] & (
         slot[:, :, None] == jnp.arange(capacity, dtype=jnp.int32)[None, None, :]
     )
+    empty = jnp.zeros_like(pick)
+    pick_lo = jnp.concatenate([pick, empty], axis=2).astype(jnp.bfloat16)
+    pick_hi = jnp.concatenate([empty, pick], axis=2).astype(jnp.bfloat16)
     outgoing = jnp.einsum(
-        "tec,tw->ecw", pick.astype(jnp.bfloat16), normed, preferred_element_type=jnp.float32
-    ).astype(jnp.bfloat16)
-    received = lax.all_to_all(outgoing, ("req", "h"), split_axis=0, concat_axis=0, tiled=True)
+        "ter,tw->erw", pick_lo, normed[:, :part], preferred_element_type=jnp.float32
+    ) + jnp.einsum("ter,tw->erw", pick_hi, normed[:, part:], preferred_element_type=jnp.float32)
+    received = lax.all_to_all(
+        outgoing.astype(jnp.bfloat16), ("req", "h"), split_axis=0, concat_axis=0, tiled=True
+    )
+    joined = jnp.concatenate([received[:, :capacity], received[:, capacity:]], axis=2)
     pieces = gate_up_all.reshape(gate_up_all.shape[0], slices, 2 * width_dev)
     gate_cols = pieces[..., :width_dev].reshape(gate_up_all.shape[0], slices * width_dev)
     up_cols = pieces[..., width_dev:].reshape(gate_up_all.shape[0], slices * width_dev)
-    gate = jnp.einsum("scw,wh->sch", received, gate_cols, preferred_element_type=jnp.float32)
-    upper = jnp.einsum("scw,wh->sch", received, up_cols, preferred_element_type=jnp.float32)
+    gate = jnp.einsum("scw,wh->sch", joined, gate_cols, preferred_element_type=jnp.float32)
+    upper = jnp.einsum("scw,wh->sch", joined, up_cols, preferred_element_type=jnp.float32)
     hidden = (jax.nn.silu(gate) * upper).astype(jnp.bfloat16)
     produced = jnp.einsum(
         "sch,hw->scw", hidden, down_all, preferred_element_type=jnp.float32
     ).astype(jnp.bfloat16)
-    results = lax.all_to_all(produced, ("req", "h"), split_axis=0, concat_axis=0, tiled=True)
+    back = jnp.concatenate([produced[..., :part], produced[..., part:]], axis=1)
+    results = lax.all_to_all(back, ("req", "h"), split_axis=0, concat_axis=0, tiled=True)
     scale = jnp.where(pick, weight[:, :, None], 0.0)
-    mix = jnp.einsum(
-        "tec,ecw->tw",
-        scale,
-        results.astype(jnp.float32),
-        precision=lax.Precision.HIGHEST,
-        preferred_element_type=jnp.float32,
-    )
+    scale_hi = scale.astype(jnp.bfloat16)
+    scale_lo = (scale - scale_hi.astype(jnp.float32)).astype(jnp.bfloat16)
+    zero = jnp.zeros_like(scale_hi)
+
+    def combine(lead, trail):
+        low = jnp.concatenate([lead, zero], axis=2)
+        high = jnp.concatenate([zero, lead], axis=2)
+        low_t = jnp.concatenate([trail, zero], axis=2)
+        high_t = jnp.concatenate([zero, trail], axis=2)
+        first = jnp.einsum("ter,erw->tw", low, results, preferred_element_type=jnp.float32)
+        first = first + jnp.einsum("ter,erw->tw", low_t, results, preferred_element_type=jnp.float32)
+        second = jnp.einsum("ter,erw->tw", high, results, preferred_element_type=jnp.float32)
+        second = second + jnp.einsum(
+            "ter,erw->tw", high_t, results, preferred_element_type=jnp.float32
+        )
+        return jnp.concatenate([first, second], axis=1)
+
+    mix = combine(scale_hi, scale_lo)
     return (branch.astype(jnp.bfloat16), mix.astype(jnp.bfloat16))
 
 

time: 145 us -> 146 us (level)
  local copies, waits for them, and re-layouts: 12.7 us -> 8.38 us
  matrix products: 24.1 us -> 28.4 us
  waiting for transfers between devices: 64.1 us -> 66.9 us
  starting transfers between devices: 21.5 us -> 19.1 us
    reshape x3 -> x0, local copies, waits for them, and re-layouts: 7.96 us -> none  [the longest x1 4.53 us: on_device(): pieces = gate_up_all.reshape(gate_up_all.shape[0], slices, 2 * width_dev)]
    all_to_all x2, waiting for transfers between devices: 57.3 us -> 65.3 us  [the longest x1 34.3 us: on_device(): lax.all_to_all(back, ('req', 'h'), split_axis=0, concat_axis=0, tiled=True)]
    ppermute x6, waiting for transfers between devices: 6.78 us -> 1.65 us  [swap(): lax.ppermute(piece, 'q', [(i, i ^ bit) for i in range(lax.axis_size('q'))])]
    dot_general x3 -> x7, matrix products: 11.3 us -> 15.4 us  [the longest x1 3.12 us: on_device(): jnp.einsum('scw,wh->sch', joined, gate_cols, preferred_element_type=jnp.f...]
    slice x0 -> x2, local copies, waits for them, and re-layouts: none -> 3.87 us  [the longest x1 1.98 us: on_device(): received[:, :capacity]]
    all_to_all x2, starting transfers between devices: 18.6 us -> 15.9 us  [the longest x1 11 us: on_device(): lax.all_to_all(outgoing.astype(jnp.bfloat16), ('req', 'h'), split_axis=0,...]
    slice x1, local copies, waits for them, and re-layouts: 3.24 us -> 1.58 us  [on_device(): pieces[..., width_dev:].reshape(gate_up_all.shape[0], slices * width_dev)]
  transfers between devices with their start and end apart: 8 -> 8, of which waited for: 3 -> 4; matrix products, arithmetic and copies ran while one was open for 16% -> 11% of each run, Pallas kernels for 10% -> 10%
where the time goes in v6:
time: 146 us; the launch traced here: 145 us
  waiting for transfers between devices  66.9 us (46%)
  matrix products  28.4 us (19%)
  starting transfers between devices  19.1 us (13%)
  Pallas kernels  15.1 us (10%)
  local copies, waits for them, and re-layouts  8.38 us (6%)
  other arithmetic  5.64 us (4%)
  between operations  1.53 us (1%)
    all_to_all x1, waiting for transfers between devices, on_device(): lax.all_to_all(back, ('req', 'h'), split_axis=0, concat_axis=0, tiled=True)  34.3 us
    all_to_all x1, waiting for transfers between devices, on_device(): lax.all_to_all(outgoing.astype(jnp.bfloat16), ('req', 'h'), split_axis=0,...  31 us
    pallas_call x1, Pallas kernels, attention_core(): pl.pallas_call(attention_kernel, grid_spec=pltpu.PrefetchScalarGridSpec(n...  15.1 us
    all_to_all x1, starting transfers between devices, on_device(): lax.all_to_all(outgoing.astype(jnp.bfloat16), ('req', 'h'), split_axis=0,...  11 us
    dot_general x1, matrix products, on_device(): jnp.einsum('sch,hw->scw', hidden, down_all, preferred_element_type=jnp.fl...  7.29 us
    all_to_all x1, starting transfers between devices, on_device(): lax.all_to_all(back, ('req', 'h'), split_axis=0, concat_axis=0, tiled=True)  4.94 us
    dot_general x1, matrix products, attend(): mixed = jnp.dot(normed, qkv_weight, preferred_element_type=jnp.float32)  4.09 us
    ppermute x6, starting transfers between devices, swap(): lax.ppermute(piece, 'q', [(i, i ^ bit) for i in range(lax.axis_size('q'))])  3.2 us
  transfers between devices with their start and end apart: 8, of which 4 were waited for; matrix products, arithmetic and copies ran while one was open for 11% of the time, Pallas kernels for 10%

profile of v6, /device:TPU:0, one launch (start us, length us, event | category | flops | bytes accessed | tf_op | source)
XLA Modules:
  0.0 145.1 jit_solution(17247623379343830064)
XLA Ops:
  0.6 1.4 copy.26
  2.0 1.7 %collective-permute-start = (bf16[1024,256]{0,1:T(8,128)(2,1)S(1)}, bf16[1024,256]{0,1:T(8,128)(2,1)S(1)}, u32[]{:S(2)}, u32[]{:S(2)}) collective-permute-start(bf16[1024,256]{0,1:T(8,128)(2,1)S(1)} %bitcast.56), channel_id=1, source_target_pairs={{0,2},{1,3},{2,0},{3,1},{4,6},{5,7},{6,4},{7,5},{8,10},{9,11},{10,... | collective-permute-start | bytes 1572872 | tf_op jit(solution)/shard_map/ppermute | solution.py:153
  3.7 0.4 collective-permute-start.1
  5.0 0.7 copy.24.cos_ref
  5.7 0.7 copy.25.sin_ref
  6.5 1.1 fusion.20
  7.5 4.1 %fusion.23.q_ref.k_ref.v_ref = f32[128,2048]{1,0:T(8,128)} fusion(bf16[1024,2048]{1,0:T(8,128)(2,1)} %param.13, bf16[128,1024]{1,0:T(8,128)(2,1)} %param.12, f32[1024]{0:T(1024)} %param.15, f32[128]{0:T(128)S(1)} %add_rsqrt_fusion.1), kind=kOutput, calls=%fused_computation.43 | convolution fusion | flops 537395200 | bytes 5509632 | tf_op jit(solution)/shard_map/dot_general | solution.py:134
  11.6 15.1 %shard_map.131 = bf16[128,1024]{1,0:T(8,128)(2,1)} custom-call(s32[1]{0:T(128)} %copy.33.length_ref, f32[128,2048]{1,0:T(8,128)} %fusion.23.q_ref.k_ref.v_ref, f32[128,2048]{1,0:T(8,128)} %fusion.23.q_ref.k_ref.v_ref, f32[128,2048]{1,0:T(8,128)} %fusion.23.q_ref.k_ref.v_ref, f32[128,128]{1,0:T(8,128)} %copy.24.cos_ref, f32[128,128]{1,0:T(8,128)} %copy.25.sin_ref, ...), custom_call_target="tpu_custom_call" | custom-call | tf_op jit(solution)/shard_map/pallas_call | solution.py:109
  26.8 1.4 fusion.41
  28.8 0.8 multiply_convert_fusion.1
  29.6 0.8 fusion.2
  30.4 2.3 %add_convert_fusion = bf16[32,80,512]{2,1,0:T(8,128)(2,1)} fusion(f32[32,80,512]{2,1,0:T(8,128)S(1)} %fusion.2, pred[128,32,40]{0,2,1:T(8,128)(4,1)S(1)} %fusion.19, bf16[128,1024]{1,0:T(8,128)(2,1)S(1)} %get-tuple-element.14), kind=kOutput, calls=%fused_computation | convolution fusion | flops 338165760 | bytes 8159232 | tf_op jit(solution)/shard_map/ter,tw->erw/dot_general | solution.py:205
  32.8 11.0 %all-to-all-start = ((bf16[32,80,512]{2,1,0:T(8,128)(2,1)}), bf16[32,80,512]{2,1,0:T(8,128)(2,1)}, u32[]{:S(2)}, u32[]{:S(2)}) async-start(bf16[32,80,512]{2,1,0:T(8,128)(2,1)} %add_convert_fusion), calls=%async_computation | async-start | bytes 5242880 | tf_op jit(solution)/shard_map/all_to_all | solution.py:206
  43.9 0.5 collective-permute-start.3
  44.5 0.4 collective-permute-start.5
  44.9 0.9 collective-permute-done.2
  45.8 0.7 collective-permute-done.3
  46.5 0.3 pad_maximum_fusion.2
  46.8 1.6 %fusion.40 = (bf16[1024,4,128]{0,2,1:T(8,128)(2,1)}, bf16[1024,4,128]{0,2,1:T(8,128)(2,1)}) fusion(bf16[1024,4,256]{0,2,1:T(8,128)(2,1)S(1)} %pad_maximum_fusion.2), kind=kLoop, calls=%fused_computation.70 | loop fusion | bytes 4194304 | tf_op jit(solution)/shard_map/slice | solution.py:212
  48.4 31.0 %all-to-all-done = bf16[32,80,512]{2,1,0:T(8,128)(2,1)} async-done(((bf16[32,80,512]{2,1,0:T(8,128)(2,1)}), bf16[32,80,512]{2,1,0:T(8,128)(2,1)}, u32[]{:S(2)}, u32[]{:S(2)}) %all-to-all-start) | async-done | bytes 2621472 | tf_op jit(solution)/shard_map/all_to_all | solution.py:206
  79.4 2.0 %fusion.39 = (bf16[32,40,512]{2,1,0:T(8,128)(2,1)S(1)}, bf16[32,40,512]{2,1,0:T(8,128)(2,1)S(1)}) fusion(bf16[32,80,512]{2,1,0:T(8,128)(2,1)} %all-to-all-done), kind=kLoop, calls=%fused_computation.69 | loop fusion | bytes 5242880 | tf_op jit(solution)/shard_map/slice | solution.py:209
  81.4 3.1 %fusion = f32[32,40,512]{2,1,0:T(8,128)} fusion(bf16[1024,512,1]{0,1,2:T(8,128)(2,1)S(1)} %bitcast.60, bf16[32,40,512]{2,1,0:T(8,128)(2,1)S(1)} %get-tuple-element.11, bf16[32,40,512]{2,1,0:T(8,128)(2,1)S(1)} %get-tuple-element.10), kind=kOutput, calls=%fused_computation.6 | convolution fusion | flops 1347420160 | bytes 6291456 | tf_op jit(solution)/shard_map/scw,wh->sch/dot_general | solution.py:213
  84.5 7.3 %convolution_convert_fusion = bf16[32,40,1024]{2,1,0:T(8,128)(2,1)} fusion(f32[32,40,512]{2,1,0:T(8,128)} %fusion, bf16[1024,512,1]{0,1,2:T(8,128)(2,1)} %bitcast.59, bf16[32,40,512]{2,1,0:T(8,128)(2,1)} %copy-done.2, bf16[32,40,512]{2,1,0:T(8,128)(2,1)S(1)} %get-tuple-element.10, bf16[128,1024]{1,0:T(8,128)(2,1)} %collective-permute-done.5, ...), kind=kOutput, calls=%fused_computation.5 | convolution fusion | flops 2699034624 | bytes 9961472 | tf_op jit(solution)/shard_map/sch,hw->scw/dot_general | solution.py:216
  91.8 1.9 %fusion.38 = (bf16[32,40,512]{2,1,0:T(8,128)(2,1)S(1)}, bf16[32,40,512]{2,1,0:T(8,128)(2,1)S(1)}) fusion(bf16[32,40,1024]{2,1,0:T(8,128)(2,1)} %convolution_convert_fusion), kind=kLoop, calls=%fused_computation.68 | loop fusion | bytes 5242880 | tf_op jit(solution)/shard_map/slice | solution.py:219
  93.7 1.9 %pad_maximum_fusion.1 = bf16[32,80,512]{2,1,0:T(8,128)(2,1)} fusion(bf16[32,40,512]{2,1,0:T(8,128)(2,1)S(1)} %get-tuple-element.9, bf16[32,40,512]{2,1,0:T(8,128)(2,1)S(1)} %get-tuple-element.8), kind=kLoop, calls=%fused_computation.2 | loop fusion | flops 5242880 | bytes 5242880 | tf_op jit(solution)/shard_map/concatenate | solution.py:219
  95.6 4.9 %all-to-all-start.1 = ((bf16[32,80,512]{2,1,0:T(8,128)(2,1)}), bf16[32,80,512]{2,1,0:T(8,128)(2,1)}, u32[]{:S(2)}, u32[]{:S(2)}) async-start(bf16[32,80,512]{2,1,0:T(8,128)(2,1)} %pad_maximum_fusion.1), calls=%async_computation.1 | async-start | bytes 5242880 | tf_op jit(solution)/shard_map/all_to_all | solution.py:220
  101.0 34.3 %all-to-all-done.1 = bf16[32,80,512]{2,1,0:T(8,128)(2,1)} async-done(((bf16[32,80,512]{2,1,0:T(8,128)(2,1)}), bf16[32,80,512]{2,1,0:T(8,128)(2,1)}, u32[]{:S(2)}, u32[]{:S(2)}) %all-to-all-start.1) | async-done | bytes 2621472 | tf_op jit(solution)/shard_map/all_to_all | solution.py:220
  135.2 2.3 %convolution_bitcast_fusion.2 = f32[128,512]{1,0:T(8,128)S(1)} fusion(bf16[32,80,512]{2,1,0:T(8,128)(2,1)} %all-to-all-done.1, bf16[128,32,40]{0,2,1:T(8,128)(2,1)S(1)} %fusion.14), kind=kOutput, calls=%fused_computation.12 | convolution fusion | flops 335544320 | bytes 3211264 | tf_op jit(solution)/shard_map/ter,erw->tw/dot_general | solution.py:232
  137.5 2.3 %convolution_bitcast_fusion = f32[128,512]{1,0:T(8,128)S(1)} fusion(bf16[32,80,512]{2,1,0:T(8,128)(2,1)} %all-to-all-done.1, bf16[128,32,40]{0,2,1:T(8,128)(2,1)S(1)} %fusion.14), kind=kOutput, calls=%fused_computation.10 | convolution fusion | flops 335544320 | bytes 3211264 | tf_op jit(solution)/shard_map/ter,erw->tw/dot_general | solution.py:234
  139.8 2.3 %fusion.7 = bf16[128,512]{1,0:T(8,128)(2,1)S(1)} fusion(f32[128,512]{1,0:T(8,128)S(1)} %convolution_bitcast_fusion.2, bf16[32,80,512]{2,1,0:T(8,128)(2,1)} %all-to-all-done.1, bf16[128,32,40]{0,2,1:T(8,128)(2,1)S(1)} %select_convert_fusion), kind=kOutput, calls=%fused_computation.17 | convolution fusion | flops 335675392 | bytes 3342336 | tf_op jit(solution)/shard_map/ter,erw->tw/dot_general | solution.py:231
  142.1 2.3 %fusion.6 = bf16[128,512]{1,0:T(8,128)(2,1)S(1)} fusion(f32[128,512]{1,0:T(8,128)S(1)} %convolution_bitcast_fusion, bf16[32,80,512]{2,1,0:T(8,128)(2,1)} %all-to-all-done.1, bf16[128,32,40]{0,2,1:T(8,128)(2,1)S(1)} %select_convert_fusion), kind=kOutput, calls=%fused_computation.16 | convolution fusion | flops 335675392 | bytes 3342336 | tf_op jit(solution)/shard_map/ter,erw->tw/dot_general | solution.py:233
  144.4 0.7 pad_maximum_fusion.7
  (34 shorter events, 1.3 us)
Async XLA Ops:
  0.6 26.1 %copy-start = (bf16[1024,1024]{1,0:T(8,128)(2,1)S(1)}, bf16[1024,1024]{1,0:T(8,128)(2,1)}, u32[]{:S(2)}) copy-start(bf16[1024,1024]{1,0:T(8,128)(2,1)} %param.14) | copy-start | bytes 6291460
  2.0 26.5 %collective-permute-start = (bf16[1024,256]{0,1:T(8,128)(2,1)S(1)}, bf16[1024,256]{0,1:T(8,128)(2,1)S(1)}, u32[]{:S(2)}, u32[]{:S(2)}) collective-permute-start(bf16[1024,256]{0,1:T(8,128)(2,1)S(1)} %bitcast.56), channel_id=1, source_target_pairs={{0,2},{1,3},{2,0},{3,1},{4,6},{5,7},{6,4},{7,5},{8,10},{9,11},{10,... | collective-permute-start | bytes 1572872 | tf_op jit(solution)/shard_map/ppermute | solution.py:153
  3.7 24.8 %collective-permute-start.1 = (bf16[128,1024]{1,0:T(8,128)(2,1)}, bf16[128,1024]{1,0:T(8,128)(2,1)}, u32[]{:S(2)}, u32[]{:S(2)}) collective-permute-start(bf16[128,1024]{1,0:T(8,128)(2,1)} %bitcast.6), channel_id=1, source_target_pairs={{0,2},{1,3},{2,0},{3,1},{4,6},{5,7},{6,4},{7,5},{8,10},{9,11},{10,... | collective-permute-start | bytes 786440 | tf_op jit(solution)/shard_map/ppermute | solution.py:153
  26.8 1.5 %copy-start.4 = (s32[128,8]{0,1:T(8,128)S(1)}, s32[128,8]{0,1:T(8,128)}, u32[]{:S(2)}) copy-start(s32[128,8]{0,1:T(8,128)} %param.20) | copy-start | bytes 12292
  26.8 1.8 %copy-start.1 = (bf16[128,1024]{1,0:T(8,128)(2,1)S(1)}, bf16[128,1024]{1,0:T(8,128)(2,1)}, u32[]{:S(2)}) copy-start(bf16[128,1024]{1,0:T(8,128)(2,1)} %param.12) | copy-start | bytes 786436
  26.8 2.0 %copy-start.5 = (f32[1024]{0:T(1024)S(1)}, f32[1024]{0:T(1024)}, u32[]{:S(2)}) copy-start(f32[1024]{0:T(1024)} %param.16) | copy-start | bytes 12292
  32.8 46.6 %all-to-all-start = ((bf16[32,80,512]{2,1,0:T(8,128)(2,1)}), bf16[32,80,512]{2,1,0:T(8,128)(2,1)}, u32[]{:S(2)}, u32[]{:S(2)}) async-start(bf16[32,80,512]{2,1,0:T(8,128)(2,1)} %add_convert_fusion), calls=%async_computation | async-start | bytes 5242880 | tf_op jit(solution)/shard_map/all_to_all | solution.py:206
  43.8 2.0 %collective-permute-start.2 = (bf16[1024,256]{0,1:T(8,128)(2,1)S(1)}, bf16[1024,256]{0,1:T(8,128)(2,1)S(1)}, u32[]{:S(2)}, u32[]{:S(2)}) collective-permute-start(bf16[1024,256]{0,1:T(8,128)(2,1)S(1)} %bitcast.57), channel_id=1, source_target_pairs={{0,1},{1,0},{2,3},{3,2},{4,5},{5,4},{6,7},{7,6},{8,9},{9,8},{10,11... | collective-permute-start | bytes 1572872 | tf_op jit(solution)/shard_map/ppermute | solution.py:153
  43.9 2.6 %collective-permute-start.3 = (bf16[1024,256]{0,1:T(8,128)(2,1)S(1)}, bf16[1024,256]{0,1:T(8,128)(2,1)S(1)}, u32[]{:S(2)}, u32[]{:S(2)}) collective-permute-start(bf16[1024,256]{0,1:T(8,128)(2,1)S(1)} %collective-permute-done), channel_id=1, source_target_pairs={{0,1},{1,0},{2,3},{3,2},{4,5},{5,4},{6,7},{7,6},{8,9},{9,8},{10,11... | collective-permute-start | bytes 1572872 | tf_op jit(solution)/shard_map/ppermute | solution.py:153
  44.4 40.2 %collective-permute-start.4 = (bf16[128,1024]{1,0:T(8,128)(2,1)}, bf16[128,1024]{1,0:T(8,128)(2,1)}, u32[]{:S(2)}, u32[]{:S(2)}) collective-permute-start(bf16[128,1024]{1,0:T(8,128)(2,1)} %bitcast.6), channel_id=1, source_target_pairs={{0,1},{1,0},{2,3},{3,2},{4,5},{5,4},{6,7},{7,6},{8,9},{9,8},{10,11... | collective-permute-start | bytes 786440 | tf_op jit(solution)/shard_map/ppermute | solution.py:153
  44.5 40.1 %collective-permute-start.5 = (bf16[128,1024]{1,0:T(8,128)(2,1)}, bf16[128,1024]{1,0:T(8,128)(2,1)}, u32[]{:S(2)}, u32[]{:S(2)}) collective-permute-start(bf16[128,1024]{1,0:T(8,128)(2,1)} %collective-permute-done.1), channel_id=1, source_target_pairs={{0,1},{1,0},{2,3},{3,2},{4,5},{5,4},{6,7},{7,6},{8,9},{9,8},{10,11... | collective-permute-start | bytes 786440 | tf_op jit(solution)/shard_map/ppermute | solution.py:153
  79.4 2.0 %copy-start.3 = (bf16[1024,4,128]{0,2,1:T(8,128)(2,1)S(1)}, bf16[1024,4,128]{0,2,1:T(8,128)(2,1)}, u32[]{:S(2)}) copy-start(bf16[1024,4,128]{0,2,1:T(8,128)(2,1)} %get-tuple-element.13) | copy-start | bytes 3145732
  81.4 3.2 %copy-start.2 = (bf16[32,40,512]{2,1,0:T(8,128)(2,1)}, bf16[32,40,512]{2,1,0:T(8,128)(2,1)S(1)}, u32[]{:S(2)}) copy-start(bf16[32,40,512]{2,1,0:T(8,128)(2,1)S(1)} %get-tuple-element.11) | copy-start | bytes 3932164
  95.6 5.0 %copy-start.6 = (f32[128,8]{0,1:T(8,128)S(1)}, f32[128,8]{0,1:T(8,128)}, u32[]{:S(2)}) copy-start(f32[128,8]{0,1:T(8,128)} %param.21) | copy-start | bytes 12292
  95.6 39.6 %all-to-all-start.1 = ((bf16[32,80,512]{2,1,0:T(8,128)(2,1)}), bf16[32,80,512]{2,1,0:T(8,128)(2,1)}, u32[]{:S(2)}, u32[]{:S(2)}) async-start(bf16[32,80,512]{2,1,0:T(8,128)(2,1)} %pad_maximum_fusion.1), calls=%async_computation.1 | async-start | bytes 5242880 | tf_op jit(solution)/shard_map/all_to_all | solution.py:220

commit v7 on v6

--- a/solution.py
+++ b/solution.py
@@ -219,24 +219,14 @@
     back = jnp.concatenate([produced[..., :part], produced[..., part:]], axis=1)
     results = lax.all_to_all(back, ("req", "h"), split_axis=0, concat_axis=0, tiled=True)
     scale = jnp.where(pick, weight[:, :, None], 0.0)
-    scale_hi = scale.astype(jnp.bfloat16)
-    scale_lo = (scale - scale_hi.astype(jnp.float32)).astype(jnp.bfloat16)
-    zero = jnp.zeros_like(scale_hi)
-
-    def combine(lead, trail):
-        low = jnp.concatenate([lead, zero], axis=2)
-        high = jnp.concatenate([zero, lead], axis=2)
-        low_t = jnp.concatenate([trail, zero], axis=2)
-        high_t = jnp.concatenate([zero, trail], axis=2)
-        first = jnp.einsum("ter,erw->tw", low, results, preferred_element_type=jnp.float32)
-        first = first + jnp.einsum("ter,erw->tw", low_t, results, preferred_element_type=jnp.float32)
-        second = jnp.einsum("ter,erw->tw", high, results, preferred_element_type=jnp.float32)
-        second = second + jnp.einsum(
-            "ter,erw->tw", high_t, results, preferred_element_type=jnp.float32
-        )
-        return jnp.concatenate([first, second], axis=1)
-
-    mix = combine(scale_hi, scale_lo)
+    output = jnp.concatenate([results[:, :capacity], results[:, capacity:]], axis=2)
+    mix = jnp.einsum(
+        "tec,ecw->tw",
+        scale,
+        output.astype(jnp.float32),
+        precision=lax.Precision.HIGHEST,
+        preferred_element_type=jnp.float32,
+    )
     return (branch.astype(jnp.bfloat16), mix.astype(jnp.bfloat16))
 
 

time: 146 us -> 140 us (0.959)
  matrix products: 28.4 us -> 21.3 us
  local copies, waits for them, and re-layouts: 8.38 us -> 10.2 us
    dot_general x4 -> x1, matrix products: 9.11 us -> 2.11 us  [on_device(): jnp.einsum('tec,ecw->tw', scale, output.astype(jnp.float32), precision=la...]
    slice x0 -> x1, local copies, waits for them, and re-layouts: none -> 1.89 us  [on_device(): results[:, :capacity]]
  transfers between devices with their start and end apart: 8 -> 8, of which waited for: 4 -> 4; matrix products, arithmetic and copies ran while one was open for 11% -> 11% of each run, Pallas kernels for 10% -> 11%
where the time goes in v7:
time: 140 us; the launch traced here: 139 us
  waiting for transfers between devices  67.3 us (48%)
  matrix products  21.3 us (15%)
  starting transfers between devices  19.2 us (14%)
  Pallas kernels  15.1 us (11%)
  local copies, waits for them, and re-layouts  10.2 us (7%)
  other arithmetic  4.53 us (3%)
  between operations  1.49 us (1%)
    all_to_all x1, waiting for transfers between devices, on_device(): lax.all_to_all(back, ('req', 'h'), split_axis=0, concat_axis=0, tiled=True)  34.6 us
    all_to_all x1, waiting for transfers between devices, on_device(): lax.all_to_all(outgoing.astype(jnp.bfloat16), ('req', 'h'), split_axis=0,...  31 us
    pallas_call x1, Pallas kernels, attention_core(): pl.pallas_call(attention_kernel, grid_spec=pltpu.PrefetchScalarGridSpec(n...  15.1 us
    all_to_all x1, starting transfers between devices, on_device(): lax.all_to_all(outgoing.astype(jnp.bfloat16), ('req', 'h'), split_axis=0,...  11 us
    dot_general x1, matrix products, on_device(): jnp.einsum('sch,hw->scw', hidden, down_all, preferred_element_type=jnp.fl...  7.29 us
    all_to_all x1, starting transfers between devices, on_device(): lax.all_to_all(back, ('req', 'h'), split_axis=0, concat_axis=0, tiled=True)  4.94 us
    dot_general x1, matrix products, attend(): mixed = jnp.dot(normed, qkv_weight, preferred_element_type=jnp.float32)  4.09 us
    ppermute x6, starting transfers between devices, swap(): lax.ppermute(piece, 'q', [(i, i ^ bit) for i in range(lax.axis_size('q'))])  3.2 us
  transfers between devices with their start and end apart: 8, of which 4 were waited for; matrix products, arithmetic and copies ran while one was open for 11% of the time, Pallas kernels for 11%

profile of v7, /device:TPU:0, one launch (start us, length us, event | category | flops | bytes accessed | tf_op | source)
XLA Modules:
  0.0 139.2 jit_solution(16875483701898329535)
XLA Ops:
  0.6 1.4 %copy.26 = bf16[1,1024,256]{1,2,0:T(8,128)(2,1)S(1)} copy(bf16[1,1024,256]{2,1,0:T(8,128)(2,1)} %param.22) | data formatting | bytes 1048576 | tf_op args[10]
  2.0 1.7 %collective-permute-start = (bf16[1024,256]{0,1:T(8,128)(2,1)S(1)}, bf16[1024,256]{0,1:T(8,128)(2,1)S(1)}, u32[]{:S(2)}, u32[]{:S(2)}) collective-permute-start(bf16[1024,256]{0,1:T(8,128)(2,1)S(1)} %bitcast.40), channel_id=1, source_target_pairs={{0,2},{1,3},{2,0},{3,1},{4,6},{5,7},{6,4},{7,5},{8,10},{9,11},{10,... | collective-permute-start | bytes 1572872 | tf_op jit(solution)/shard_map/ppermute | solution.py:153
  3.7 0.4 collective-permute-start.1
  4.8 0.1 multiply_sine_fusion
  5.0 0.7 copy.24.cos_ref
  5.7 0.7 copy.25.sin_ref
  6.4 1.1 fusion.22
  7.5 4.1 %fusion.27.q_ref.k_ref.v_ref = f32[128,2048]{1,0:T(8,128)} fusion(bf16[1024,2048]{1,0:T(8,128)(2,1)} %param.13, bf16[128,1024]{1,0:T(8,128)(2,1)} %param.12, f32[1024]{0:T(1024)} %param.15, f32[128]{0:T(128)S(1)} %add_rsqrt_fusion.1), kind=kOutput, calls=%fused_computation.37 | convolution fusion | flops 537395200 | bytes 5509632 | tf_op jit(solution)/shard_map/dot_general | solution.py:134
  11.6 15.1 %shard_map.131 = bf16[128,1024]{1,0:T(8,128)(2,1)} custom-call(s32[1]{0:T(128)} %copy.33.length_ref, f32[128,2048]{1,0:T(8,128)} %fusion.27.q_ref.k_ref.v_ref, f32[128,2048]{1,0:T(8,128)} %fusion.27.q_ref.k_ref.v_ref, f32[128,2048]{1,0:T(8,128)} %fusion.27.q_ref.k_ref.v_ref, f32[128,128]{1,0:T(8,128)} %copy.24.cos_ref, f32[128,128]{1,0:T(8,128)} %copy.25.sin_ref, ...), custom_call_target="tpu_custom_call" | custom-call | tf_op jit(solution)/shard_map/pallas_call | solution.py:109
  26.8 1.4 %fusion.45 = f32[128,1024]{1,0:T(8,128)S(1)} fusion(bf16[128,1024]{1,0:T(8,128)(2,1)} %shard_map.131, bf16[1024,1024]{1,0:T(8,128)(2,1)S(1)} %copy-done), kind=kOutput, calls=%fused_computation.63 | convolution fusion | flops 268435456 | bytes 2883584 | tf_op jit(solution)/shard_map/dot_general | solution.py:149
  28.4 0.2 fusion.21
  28.6 0.2 multiply_reduce_fusion
  28.8 0.8 multiply_convert_fusion.1
  29.6 0.8 fusion.6
  30.4 2.3 %add_convert_fusion = bf16[32,80,512]{2,1,0:T(8,128)(2,1)} fusion(f32[32,80,512]{2,1,0:T(8,128)S(1)} %fusion.6, pred[128,32,40]{0,2,1:T(8,128)(4,1)S(1)} %fusion.21, bf16[128,1024]{1,0:T(8,128)(2,1)S(1)} %get-tuple-element.16), kind=kOutput, calls=%fused_computation | convolution fusion | flops 338165760 | bytes 8159232 | tf_op jit(solution)/shard_map/ter,tw->erw/dot_general | solution.py:205
  32.7 11.0 %all-to-all-start = ((bf16[32,80,512]{2,1,0:T(8,128)(2,1)}), bf16[32,80,512]{2,1,0:T(8,128)(2,1)}, u32[]{:S(2)}, u32[]{:S(2)}) async-start(bf16[32,80,512]{2,1,0:T(8,128)(2,1)} %add_convert_fusion), calls=%async_computation | async-start | bytes 5242880 | tf_op jit(solution)/shard_map/all_to_all | solution.py:206
  43.9 0.5 collective-permute-start.3
  44.4 0.4 collective-permute-start.5
  44.9 0.9 collective-permute-done.2
  45.8 0.7 collective-permute-done.3
  46.5 0.3 pad_maximum_fusion.2
  46.8 1.6 %fusion.44 = (bf16[1024,4,128]{0,2,1:T(8,128)(2,1)}, bf16[1024,4,128]{0,2,1:T(8,128)(2,1)}) fusion(bf16[1024,4,256]{0,2,1:T(8,128)(2,1)S(1)} %pad_maximum_fusion.2), kind=kLoop, calls=%fused_computation.62 | loop fusion | bytes 4194304 | tf_op jit(solution)/shard_map/slice | solution.py:212
  48.3 31.0 %all-to-all-done = bf16[32,80,512]{2,1,0:T(8,128)(2,1)} async-done(((bf16[32,80,512]{2,1,0:T(8,128)(2,1)}), bf16[32,80,512]{2,1,0:T(8,128)(2,1)}, u32[]{:S(2)}, u32[]{:S(2)}) %all-to-all-start) | async-done | bytes 2621472 | tf_op jit(solution)/shard_map/all_to_all | solution.py:206
  79.4 2.0 %fusion.43 = (bf16[32,40,512]{2,1,0:T(8,128)(2,1)S(1)}, bf16[32,40,512]{2,1,0:T(8,128)(2,1)S(1)}) fusion(bf16[32,80,512]{2,1,0:T(8,128)(2,1)} %all-to-all-done), kind=kLoop, calls=%fused_computation.61 | loop fusion | bytes 5242880 | tf_op jit(solution)/shard_map/slice | solution.py:209
  81.4 3.1 %fusion.4 = f32[32,40,512]{2,1,0:T(8,128)} fusion(bf16[1024,512,1]{0,1,2:T(8,128)(2,1)S(1)} %bitcast.44, bf16[32,40,512]{2,1,0:T(8,128)(2,1)S(1)} %get-tuple-element.13, bf16[32,40,512]{2,1,0:T(8,128)(2,1)S(1)} %get-tuple-element.12), kind=kOutput, calls=%fused_computation.10 | convolution fusion | flops 1347420160 | bytes 6291456 | tf_op jit(solution)/shard_map/scw,wh->sch/dot_general | solution.py:213
  84.5 7.3 %convolution_convert_fusion = bf16[32,40,1024]{2,1,0:T(8,128)(2,1)} fusion(f32[32,40,512]{2,1,0:T(8,128)} %fusion.4, bf16[1024,512,1]{0,1,2:T(8,128)(2,1)} %bitcast.43, bf16[32,40,512]{2,1,0:T(8,128)(2,1)} %copy-done.2, bf16[32,40,512]{2,1,0:T(8,128)(2,1)S(1)} %get-tuple-element.12, bf16[128,1024]{1,0:T(8,128)(2,1)} %collective-permute-done.5, ...), kind=kOutput, calls=%fused_computation.9 | convolution fusion | flops 2699034624 | bytes 9961472 | tf_op jit(solution)/shard_map/sch,hw->scw/dot_general | solution.py:216
  91.8 1.9 %fusion.42 = (bf16[32,40,512]{2,1,0:T(8,128)(2,1)S(1)}, bf16[32,40,512]{2,1,0:T(8,128)(2,1)S(1)}) fusion(bf16[32,40,1024]{2,1,0:T(8,128)(2,1)} %convolution_convert_fusion), kind=kLoop, calls=%fused_computation.60 | loop fusion | bytes 5242880 | tf_op jit(solution)/shard_map/slice | solution.py:219
  93.7 1.9 %pad_maximum_fusion.1 = bf16[32,80,512]{2,1,0:T(8,128)(2,1)} fusion(bf16[32,40,512]{2,1,0:T(8,128)(2,1)S(1)} %get-tuple-element.11, bf16[32,40,512]{2,1,0:T(8,128)(2,1)S(1)} %get-tuple-element.10), kind=kLoop, calls=%fused_computation.2 | loop fusion | flops 5242880 | bytes 5242880 | tf_op jit(solution)/shard_map/concatenate | solution.py:219
  95.6 4.9 %all-to-all-start.1 = ((bf16[32,80,512]{2,1,0:T(8,128)(2,1)}), bf16[32,80,512]{2,1,0:T(8,128)(2,1)}, u32[]{:S(2)}, u32[]{:S(2)}) async-start(bf16[32,80,512]{2,1,0:T(8,128)(2,1)} %pad_maximum_fusion.1), calls=%async_computation.1 | async-start | bytes 5242880 | tf_op jit(solution)/shard_map/all_to_all | solution.py:220
  100.6 34.6 %all-to-all-done.1 = bf16[32,80,512]{2,1,0:T(8,128)(2,1)} async-done(((bf16[32,80,512]{2,1,0:T(8,128)(2,1)}), bf16[32,80,512]{2,1,0:T(8,128)(2,1)}, u32[]{:S(2)}, u32[]{:S(2)}) %all-to-all-start.1) | async-done | bytes 2621472 | tf_op jit(solution)/shard_map/all_to_all | solution.py:220
  135.2 1.9 %fusion.41 = (bf16[32,40,512]{2,1,0:T(8,128)(2,1)S(1)}, bf16[32,40,512]{2,1,0:T(8,128)(2,1)S(1)}) fusion(bf16[32,80,512]{2,1,0:T(8,128)(2,1)} %all-to-all-done.1), kind=kLoop, calls=%fused_computation.59 | loop fusion | bytes 5242880 | tf_op jit(solution)/shard_map/slice | solution.py:222
  137.1 2.1 %fusion.11 = bf16[128,1024]{1,0:T(8,128)(2,1)} fusion(bf16[32,40,512]{2,1,0:T(8,128)(2,1)S(1)} %get-tuple-element.9, bf16[32,40,512]{2,1,0:T(8,128)(2,1)S(1)} %get-tuple-element.8, f32[128,32]{0,1:T(8,128)S(1)} %select_reduce_fusion, s32[128,32]{0,1:T(8,128)S(1)} %convolution_convert_fusion.1, pred[128,32]{0,1:T(8,128)(4,1)S(1)} %fusion.31), kind=kOutput, calls=%fused_computation.15 | convolution fusion | flops 2019131392 | bytes 2920448 | tf_op jit(solution)/shard_map/tec,ecw->tw/dot_general | solution.py:223
  (29 shorter events, 0.5 us)
Async XLA Ops:
  0.6 26.1 %copy-start = (bf16[1024,1024]{1,0:T(8,128)(2,1)S(1)}, bf16[1024,1024]{1,0:T(8,128)(2,1)}, u32[]{:S(2)}) copy-start(bf16[1024,1024]{1,0:T(8,128)(2,1)} %param.14) | copy-start | bytes 6291460
  2.0 26.5 %collective-permute-start = (bf16[1024,256]{0,1:T(8,128)(2,1)S(1)}, bf16[1024,256]{0,1:T(8,128)(2,1)S(1)}, u32[]{:S(2)}, u32[]{:S(2)}) collective-permute-start(bf16[1024,256]{0,1:T(8,128)(2,1)S(1)} %bitcast.40), channel_id=1, source_target_pairs={{0,2},{1,3},{2,0},{3,1},{4,6},{5,7},{6,4},{7,5},{8,10},{9,11},{10,... | collective-permute-start | bytes 1572872 | tf_op jit(solution)/shard_map/ppermute | solution.py:153
  3.7 24.8 %collective-permute-start.1 = (bf16[128,1024]{1,0:T(8,128)(2,1)}, bf16[128,1024]{1,0:T(8,128)(2,1)}, u32[]{:S(2)}, u32[]{:S(2)}) collective-permute-start(bf16[128,1024]{1,0:T(8,128)(2,1)} %bitcast.6), channel_id=1, source_target_pairs={{0,2},{1,3},{2,0},{3,1},{4,6},{5,7},{6,4},{7,5},{8,10},{9,11},{10,... | collective-permute-start | bytes 786440 | tf_op jit(solution)/shard_map/ppermute | solution.py:153
  26.7 1.5 %copy-start.4 = (s32[128,8]{0,1:T(8,128)S(1)}, s32[128,8]{0,1:T(8,128)}, u32[]{:S(2)}) copy-start(s32[128,8]{0,1:T(8,128)} %param.20) | copy-start | bytes 12292
  26.7 1.8 %copy-start.1 = (bf16[128,1024]{1,0:T(8,128)(2,1)S(1)}, bf16[128,1024]{1,0:T(8,128)(2,1)}, u32[]{:S(2)}) copy-start(bf16[128,1024]{1,0:T(8,128)(2,1)} %param.12) | copy-start | bytes 786436
  26.7 2.0 %copy-start.5 = (f32[1024]{0:T(1024)S(1)}, f32[1024]{0:T(1024)}, u32[]{:S(2)}) copy-start(f32[1024]{0:T(1024)} %param.16) | copy-start | bytes 12292
  32.7 46.6 %all-to-all-start = ((bf16[32,80,512]{2,1,0:T(8,128)(2,1)}), bf16[32,80,512]{2,1,0:T(8,128)(2,1)}, u32[]{:S(2)}, u32[]{:S(2)}) async-start(bf16[32,80,512]{2,1,0:T(8,128)(2,1)} %add_convert_fusion), calls=%async_computation | async-start | bytes 5242880 | tf_op jit(solution)/shard_map/all_to_all | solution.py:206
  43.8 2.0 %collective-permute-start.2 = (bf16[1024,256]{0,1:T(8,128)(2,1)S(1)}, bf16[1024,256]{0,1:T(8,128)(2,1)S(1)}, u32[]{:S(2)}, u32[]{:S(2)}) collective-permute-start(bf16[1024,256]{0,1:T(8,128)(2,1)S(1)} %bitcast.41), channel_id=1, source_target_pairs={{0,1},{1,0},{2,3},{3,2},{4,5},{5,4},{6,7},{7,6},{8,9},{9,8},{10,11... | collective-permute-start | bytes 1572872 | tf_op jit(solution)/shard_map/ppermute | solution.py:153
  43.9 2.6 %collective-permute-start.3 = (bf16[1024,256]{0,1:T(8,128)(2,1)S(1)}, bf16[1024,256]{0,1:T(8,128)(2,1)S(1)}, u32[]{:S(2)}, u32[]{:S(2)}) collective-permute-start(bf16[1024,256]{0,1:T(8,128)(2,1)S(1)} %collective-permute-done), channel_id=1, source_target_pairs={{0,1},{1,0},{2,3},{3,2},{4,5},{5,4},{6,7},{7,6},{8,9},{9,8},{10,11... | collective-permute-start | bytes 1572872 | tf_op jit(solution)/shard_map/ppermute | solution.py:153
  44.4 40.2 %collective-permute-start.4 = (bf16[128,1024]{1,0:T(8,128)(2,1)}, bf16[128,1024]{1,0:T(8,128)(2,1)}, u32[]{:S(2)}, u32[]{:S(2)}) collective-permute-start(bf16[128,1024]{1,0:T(8,128)(2,1)} %bitcast.6), channel_id=1, source_target_pairs={{0,1},{1,0},{2,3},{3,2},{4,5},{5,4},{6,7},{7,6},{8,9},{9,8},{10,11... | collective-permute-start | bytes 786440 | tf_op jit(solution)/shard_map/ppermute | solution.py:153
  44.4 40.1 %collective-permute-start.5 = (bf16[128,1024]{1,0:T(8,128)(2,1)}, bf16[128,1024]{1,0:T(8,128)(2,1)}, u32[]{:S(2)}, u32[]{:S(2)}) collective-permute-start(bf16[128,1024]{1,0:T(8,128)(2,1)} %collective-permute-done.1), channel_id=1, source_target_pairs={{0,1},{1,0},{2,3},{3,2},{4,5},{5,4},{6,7},{7,6},{8,9},{9,8},{10,11... | collective-permute-start | bytes 786440 | tf_op jit(solution)/shard_map/ppermute | solution.py:153
  79.4 2.0 %copy-start.3 = (bf16[1024,4,128]{0,2,1:T(8,128)(2,1)S(1)}, bf16[1024,4,128]{0,2,1:T(8,128)(2,1)}, u32[]{:S(2)}) copy-start(bf16[1024,4,128]{0,2,1:T(8,128)(2,1)} %get-tuple-element.15) | copy-start | bytes 3145732
  81.4 3.2 %copy-start.2 = (bf16[32,40,512]{2,1,0:T(8,128)(2,1)}, bf16[32,40,512]{2,1,0:T(8,128)(2,1)S(1)}, u32[]{:S(2)}) copy-start(bf16[32,40,512]{2,1,0:T(8,128)(2,1)S(1)} %get-tuple-element.13) | copy-start | bytes 3932164
  95.6 5.0 %copy-start.6 = (f32[128,8]{0,1:T(8,128)S(1)}, f32[128,8]{0,1:T(8,128)}, u32[]{:S(2)}) copy-start(f32[128,8]{0,1:T(8,128)} %param.21) | copy-start | bytes 12292
  95.6 39.6 %all-to-all-start.1 = ((bf16[32,80,512]{2,1,0:T(8,128)(2,1)}), bf16[32,80,512]{2,1,0:T(8,128)(2,1)}, u32[]{:S(2)}, u32[]{:S(2)}) async-start(bf16[32,80,512]{2,1,0:T(8,128)(2,1)} %pad_maximum_fusion.1), calls=%async_computation.1 | async-start | bytes 5242880 | tf_op jit(solution)/shard_map/all_to_all | solution.py:220

commit v8 on v7

--- a/solution.py
+++ b/solution.py
@@ -39,7 +39,9 @@
     return jnp.where(lead, values * cosine - partner * sine, values * cosine + partner * sine)
 
 
-def attention_kernel(length_ref, q_ref, k_ref, v_ref, cos_ref, sin_ref, kc_ref, vc_ref, o_ref):
+def attention_kernel(
+    length_ref, q_ref, k_ref, v_ref, cos_ref, sin_ref, kc_ref, vc_ref, o_ref, s_ref, sn_ref, w_ref, wn_ref
+):
     length = length_ref[0]
     span, lanes = kc_ref.shape
     rows = k_ref.shape[0]
@@ -54,12 +56,6 @@
     vc = vc_ref[...]
     kn = turn(k_ref[...], cosine, sine, lead, quarter).astype(jnp.bfloat16)
     vn = v_ref[...].astype(jnp.bfloat16)
-    column = lax.broadcasted_iota(jnp.int32, (rows, span), 1)
-    cache_ok = column < length
-    new_col = lax.broadcasted_iota(jnp.int32, (rows, rows), 1)
-    new_row = lax.broadcasted_iota(jnp.int32, (rows, rows), 0)
-    new_ok = new_col <= new_row
-
     def scaled(values):
         rotated = turn(values, cosine, sine, lead, quarter).astype(jnp.bfloat16)
         return (rotated * 0.015625).astype(jnp.bfloat16).astype(jnp.float32)
@@ -73,22 +69,34 @@
         jnp.where(low, 0.0, second),
     )
     contract = (((1,), (1,)), ((), ()))
+    chunk = 16
     outs = []
     for q in queries:
         q = q.astype(jnp.bfloat16)
-        s = lax.dot_general(q, kc, contract, preferred_element_type=jnp.float32)
-        s = jnp.where(cache_ok, s, -1e30)
-        sn = lax.dot_general(q, kn, contract, preferred_element_type=jnp.float32)
-        sn = jnp.where(new_ok, sn, -1e30)
-        top = jnp.maximum(jnp.max(s, axis=1, keepdims=True), jnp.max(sn, axis=1, keepdims=True))
-        e = jnp.exp(s - top)
-        en = jnp.exp(sn - top)
-        total = jnp.sum(e, axis=1, keepdims=True) + jnp.sum(en, axis=1, keepdims=True)
-        inverse = 1.0 / total
-        w = (e * inverse).astype(jnp.bfloat16)
-        wn = (en * inverse).astype(jnp.bfloat16)
-        o = jnp.dot(w, vc, preferred_element_type=jnp.float32) + jnp.dot(
-            wn, vn, preferred_element_type=jnp.float32
+        s_ref[...] = lax.dot_general(q, kc, contract, preferred_element_type=jnp.float32)
+        sn_ref[...] = lax.dot_general(q, kn, contract, preferred_element_type=jnp.float32)
+
+        def normalize(i, carry):
+            at = pl.ds(pl.multiple_of(i * chunk, chunk), chunk)
+            column = lax.broadcasted_iota(jnp.int32, (chunk, span), 1)
+            s = jnp.where(column < length, s_ref[at, :], -1e30)
+            new_col = lax.broadcasted_iota(jnp.int32, (chunk, rows), 1)
+            new_row = lax.broadcasted_iota(jnp.int32, (chunk, rows), 0) + i * chunk
+            sn = jnp.where(new_col <= new_row, sn_ref[at, :], -1e30)
+            top = jnp.maximum(
+                jnp.max(s, axis=1, keepdims=True), jnp.max(sn, axis=1, keepdims=True)
+            )
+            e = jnp.exp(s - top)
+            en = jnp.exp(sn - top)
+            total = jnp.sum(e, axis=1, keepdims=True) + jnp.sum(en, axis=1, keepdims=True)
+            inverse = 1.0 / total
+            w_ref[at, :] = (e * inverse).astype(jnp.bfloat16)
+            wn_ref[at, :] = (en * inverse).astype(jnp.bfloat16)
+            return carry
+
+        lax.fori_loop(0, rows // chunk, normalize, 0)
+        o = jnp.dot(w_ref[...], vc, preferred_element_type=jnp.float32) + jnp.dot(
+            wn_ref[...], vn, preferred_element_type=jnp.float32
         )
         outs.append(o.astype(jnp.bfloat16).astype(jnp.float32))
     left = jnp.where(low, outs[0], pltpu.roll(outs[1], half, 1))
@@ -121,6 +129,12 @@
                 pl.BlockSpec((span, lanes), lambda p, n: (0, p)),
             ],
             out_specs=pl.BlockSpec((rows, qblock), lambda p, n: (0, p)),
+            scratch_shapes=[
+                pltpu.VMEM((rows, span), jnp.float32),
+                pltpu.VMEM((rows, rows), jnp.float32),
+                pltpu.VMEM((rows, span), jnp.bfloat16),
+                pltpu.VMEM((rows, rows), jnp.bfloat16),
+            ],
         ),
         out_shape=jax.ShapeDtypeStruct((rows, qwidth), jnp.bfloat16),
         interpret=interpret,

time: 140 us -> 163 us (1.16)
  Pallas kernels: 15.1 us -> 37.8 us
    pallas_call x1, Pallas kernels: 15.1 us -> 37.8 us  [attention_core(): pl.pallas_call(attention_kernel, grid_spec=pltpu.PrefetchScalarGridSpec(n...]
  transfers between devices with their start and end apart: 8 -> 8, of which waited for: 4 -> 4; matrix products, arithmetic and copies ran while one was open for 11% -> 10% of each run, Pallas kernels for 11% -> 23%
where the time goes in v8:
time: 163 us; the launch traced here: 162 us
  waiting for transfers between devices  67.4 us (41%)
  Pallas kernels  37.8 us (23%)
  matrix products  21.3 us (13%)
  starting transfers between devices  19.2 us (12%)
  local copies, waits for them, and re-layouts  10.2 us (6%)
  other arithmetic  4.53 us (3%)
    pallas_call x1, Pallas kernels, attention_core(): pl.pallas_call(attention_kernel, grid_spec=pltpu.PrefetchScalarGridSpec(n...  37.8 us
    all_to_all x1, waiting for transfers between devices, on_device(): lax.all_to_all(back, ('req', 'h'), split_axis=0, concat_axis=0, tiled=True)  34.7 us
    all_to_all x1, waiting for transfers between devices, on_device(): lax.all_to_all(outgoing.astype(jnp.bfloat16), ('req', 'h'), split_axis=0,...  31.1 us
    all_to_all x1, starting transfers between devices, on_device(): lax.all_to_all(outgoing.astype(jnp.bfloat16), ('req', 'h'), split_axis=0,...  11 us
    dot_general x1, matrix products, on_device(): jnp.einsum('sch,hw->scw', hidden, down_all, preferred_element_type=jnp.fl...  7.29 us
    all_to_all x1, starting transfers between devices, on_device(): lax.all_to_all(back, ('req', 'h'), split_axis=0, concat_axis=0, tiled=True)  4.94 us
    dot_general x1, matrix products, attend(): mixed = jnp.dot(normed, qkv_weight, preferred_element_type=jnp.float32)  4.09 us
  transfers between devices with their start and end apart: 8, of which 4 were waited for; matrix products, arithmetic and copies ran while one was open for 10% of the time, Pallas kernels for 23%

profile of v8, /device:TPU:0, one launch (start us, length us, event | category | flops | bytes accessed | tf_op | source)
XLA Modules:
  0.0 161.9 jit_solution(4397226481906043349)
XLA Ops:
  0.6 1.4 copy.26
  2.0 1.7 %collective-permute-start = (bf16[1024,256]{0,1:T(8,128)(2,1)S(1)}, bf16[1024,256]{0,1:T(8,128)(2,1)S(1)}, u32[]{:S(2)}, u32[]{:S(2)}) collective-permute-start(bf16[1024,256]{0,1:T(8,128)(2,1)S(1)} %bitcast.40), channel_id=1, source_target_pairs={{0,2},{1,3},{2,0},{3,1},{4,6},{5,7},{6,4},{7,5},{8,10},{9,11},{10,... | collective-permute-start | bytes 1572872 | tf_op jit(solution)/shard_map/ppermute | solution.py:167
  3.7 0.4 collective-permute-start.1
  4.8 0.1 multiply_sine_fusion
  5.0 0.7 copy.24.cos_ref
  5.7 0.7 copy.25.sin_ref
  6.4 1.1 fusion.22
  7.5 4.1 %fusion.27.q_ref.k_ref.v_ref = f32[128,2048]{1,0:T(8,128)} fusion(bf16[1024,2048]{1,0:T(8,128)(2,1)} %param.13, bf16[128,1024]{1,0:T(8,128)(2,1)} %param.12, f32[1024]{0:T(1024)} %param.15, f32[128]{0:T(128)S(1)} %add_rsqrt_fusion.1), kind=kOutput, calls=%fused_computation.37 | convolution fusion | flops 537395200 | bytes 5509632 | tf_op jit(solution)/shard_map/dot_general | solution.py:148
  11.6 37.8 %shard_map.131 = bf16[128,1024]{1,0:T(8,128)(2,1)} custom-call(s32[1]{0:T(128)} %copy.33.length_ref, f32[128,2048]{1,0:T(8,128)} %fusion.27.q_ref.k_ref.v_ref, f32[128,2048]{1,0:T(8,128)} %fusion.27.q_ref.k_ref.v_ref, f32[128,2048]{1,0:T(8,128)} %fusion.27.q_ref.k_ref.v_ref, f32[128,128]{1,0:T(8,128)} %copy.24.cos_ref, f32[128,128]{1,0:T(8,128)} %copy.25.sin_ref, ...), custom_call_target="tpu_custom_call" | custom-call | tf_op jit(solution)/shard_map/pallas_call | solution.py:117
  49.4 1.4 fusion.45
  51.1 0.2 fusion.21
  51.3 0.2 multiply_reduce_fusion
  51.5 0.8 multiply_convert_fusion.1
  52.2 0.8 fusion.6
  53.1 2.3 %add_convert_fusion = bf16[32,80,512]{2,1,0:T(8,128)(2,1)} fusion(f32[32,80,512]{2,1,0:T(8,128)S(1)} %fusion.6, pred[128,32,40]{0,2,1:T(8,128)(4,1)S(1)} %fusion.21, bf16[128,1024]{1,0:T(8,128)(2,1)S(1)} %get-tuple-element.16), kind=kOutput, calls=%fused_computation | convolution fusion | flops 338165760 | bytes 8159232 | tf_op jit(solution)/shard_map/ter,tw->erw/dot_general | solution.py:219
  55.4 11.0 %all-to-all-start = ((bf16[32,80,512]{2,1,0:T(8,128)(2,1)}), bf16[32,80,512]{2,1,0:T(8,128)(2,1)}, u32[]{:S(2)}, u32[]{:S(2)}) async-start(bf16[32,80,512]{2,1,0:T(8,128)(2,1)} %add_convert_fusion), calls=%async_computation | async-start | bytes 5242880 | tf_op jit(solution)/shard_map/all_to_all | solution.py:220
  66.5 0.5 collective-permute-start.3
  67.1 0.4 collective-permute-start.5
  67.5 0.9 collective-permute-done.2
  68.4 0.7 collective-permute-done.3
  69.2 0.3 pad_maximum_fusion.2
  69.5 1.6 fusion.44
  71.0 31.1 %all-to-all-done = bf16[32,80,512]{2,1,0:T(8,128)(2,1)} async-done(((bf16[32,80,512]{2,1,0:T(8,128)(2,1)}), bf16[32,80,512]{2,1,0:T(8,128)(2,1)}, u32[]{:S(2)}, u32[]{:S(2)}) %all-to-all-start) | async-done | bytes 2621472 | tf_op jit(solution)/shard_map/all_to_all | solution.py:220
  102.1 2.0 %fusion.43 = (bf16[32,40,512]{2,1,0:T(8,128)(2,1)S(1)}, bf16[32,40,512]{2,1,0:T(8,128)(2,1)S(1)}) fusion(bf16[32,80,512]{2,1,0:T(8,128)(2,1)} %all-to-all-done), kind=kLoop, calls=%fused_computation.61 | loop fusion | bytes 5242880 | tf_op jit(solution)/shard_map/slice | solution.py:223
  104.1 3.1 %fusion.4 = f32[32,40,512]{2,1,0:T(8,128)} fusion(bf16[1024,512,1]{0,1,2:T(8,128)(2,1)S(1)} %bitcast.44, bf16[32,40,512]{2,1,0:T(8,128)(2,1)S(1)} %get-tuple-element.13, bf16[32,40,512]{2,1,0:T(8,128)(2,1)S(1)} %get-tuple-element.12), kind=kOutput, calls=%fused_computation.10 | convolution fusion | flops 1347420160 | bytes 6291456 | tf_op jit(solution)/shard_map/scw,wh->sch/dot_general | solution.py:227
  107.2 7.3 %convolution_convert_fusion = bf16[32,40,1024]{2,1,0:T(8,128)(2,1)} fusion(f32[32,40,512]{2,1,0:T(8,128)} %fusion.4, bf16[1024,512,1]{0,1,2:T(8,128)(2,1)} %bitcast.43, bf16[32,40,512]{2,1,0:T(8,128)(2,1)} %copy-done.2, bf16[32,40,512]{2,1,0:T(8,128)(2,1)S(1)} %get-tuple-element.12, bf16[128,1024]{1,0:T(8,128)(2,1)} %collective-permute-done.5, ...), kind=kOutput, calls=%fused_computation.9 | convolution fusion | flops 2699034624 | bytes 9961472 | tf_op jit(solution)/shard_map/sch,hw->scw/dot_general | solution.py:230
  114.5 1.9 %fusion.42 = (bf16[32,40,512]{2,1,0:T(8,128)(2,1)S(1)}, bf16[32,40,512]{2,1,0:T(8,128)(2,1)S(1)}) fusion(bf16[32,40,1024]{2,1,0:T(8,128)(2,1)} %convolution_convert_fusion), kind=kLoop, calls=%fused_computation.60 | loop fusion | bytes 5242880 | tf_op jit(solution)/shard_map/slice | solution.py:233
  116.4 1.9 %pad_maximum_fusion.1 = bf16[32,80,512]{2,1,0:T(8,128)(2,1)} fusion(bf16[32,40,512]{2,1,0:T(8,128)(2,1)S(1)} %get-tuple-element.11, bf16[32,40,512]{2,1,0:T(8,128)(2,1)S(1)} %get-tuple-element.10), kind=kLoop, calls=%fused_computation.2 | loop fusion | flops 5242880 | bytes 5242880 | tf_op jit(solution)/shard_map/concatenate | solution.py:233
  118.3 4.9 %all-to-all-start.1 = ((bf16[32,80,512]{2,1,0:T(8,128)(2,1)}), bf16[32,80,512]{2,1,0:T(8,128)(2,1)}, u32[]{:S(2)}, u32[]{:S(2)}) async-start(bf16[32,80,512]{2,1,0:T(8,128)(2,1)} %pad_maximum_fusion.1), calls=%async_computation.1 | async-start | bytes 5242880 | tf_op jit(solution)/shard_map/all_to_all | solution.py:234
  123.3 34.7 %all-to-all-done.1 = bf16[32,80,512]{2,1,0:T(8,128)(2,1)} async-done(((bf16[32,80,512]{2,1,0:T(8,128)(2,1)}), bf16[32,80,512]{2,1,0:T(8,128)(2,1)}, u32[]{:S(2)}, u32[]{:S(2)}) %all-to-all-start.1) | async-done | bytes 2621472 | tf_op jit(solution)/shard_map/all_to_all | solution.py:234
  157.9 1.9 %fusion.41 = (bf16[32,40,512]{2,1,0:T(8,128)(2,1)S(1)}, bf16[32,40,512]{2,1,0:T(8,128)(2,1)S(1)}) fusion(bf16[32,80,512]{2,1,0:T(8,128)(2,1)} %all-to-all-done.1), kind=kLoop, calls=%fused_computation.59 | loop fusion | bytes 5242880 | tf_op jit(solution)/shard_map/slice | solution.py:236
  159.8 2.1 %fusion.11 = bf16[128,1024]{1,0:T(8,128)(2,1)} fusion(bf16[32,40,512]{2,1,0:T(8,128)(2,1)S(1)} %get-tuple-element.9, bf16[32,40,512]{2,1,0:T(8,128)(2,1)S(1)} %get-tuple-element.8, f32[128,32]{0,1:T(8,128)S(1)} %select_reduce_fusion, s32[128,32]{0,1:T(8,128)S(1)} %convolution_convert_fusion.1, pred[128,32]{0,1:T(8,128)(4,1)S(1)} %fusion.31), kind=kOutput, calls=%fused_computation.15 | convolution fusion | flops 2019131392 | bytes 2920448 | tf_op jit(solution)/shard_map/tec,ecw->tw/dot_general | solution.py:237
  (29 shorter events, 0.5 us)
Async XLA Ops:
  0.6 48.8 %copy-start = (bf16[1024,1024]{1,0:T(8,128)(2,1)S(1)}, bf16[1024,1024]{1,0:T(8,128)(2,1)}, u32[]{:S(2)}) copy-start(bf16[1024,1024]{1,0:T(8,128)(2,1)} %param.14) | copy-start | bytes 6291460
  2.0 49.2 %collective-permute-start = (bf16[1024,256]{0,1:T(8,128)(2,1)S(1)}, bf16[1024,256]{0,1:T(8,128)(2,1)S(1)}, u32[]{:S(2)}, u32[]{:S(2)}) collective-permute-start(bf16[1024,256]{0,1:T(8,128)(2,1)S(1)} %bitcast.40), channel_id=1, source_target_pairs={{0,2},{1,3},{2,0},{3,1},{4,6},{5,7},{6,4},{7,5},{8,10},{9,11},{10,... | collective-permute-start | bytes 1572872 | tf_op jit(solution)/shard_map/ppermute | solution.py:167
  3.7 47.5 %collective-permute-start.1 = (bf16[128,1024]{1,0:T(8,128)(2,1)}, bf16[128,1024]{1,0:T(8,128)(2,1)}, u32[]{:S(2)}, u32[]{:S(2)}) collective-permute-start(bf16[128,1024]{1,0:T(8,128)(2,1)} %bitcast.6), channel_id=1, source_target_pairs={{0,2},{1,3},{2,0},{3,1},{4,6},{5,7},{6,4},{7,5},{8,10},{9,11},{10,... | collective-permute-start | bytes 786440 | tf_op jit(solution)/shard_map/ppermute | solution.py:167
  49.4 1.5 copy-start.4
  49.4 1.8 %copy-start.1 = (bf16[128,1024]{1,0:T(8,128)(2,1)S(1)}, bf16[128,1024]{1,0:T(8,128)(2,1)}, u32[]{:S(2)}) copy-start(bf16[128,1024]{1,0:T(8,128)(2,1)} %param.12) | copy-start | bytes 786436
  49.4 2.0 %copy-start.5 = (f32[1024]{0:T(1024)S(1)}, f32[1024]{0:T(1024)}, u32[]{:S(2)}) copy-start(f32[1024]{0:T(1024)} %param.16) | copy-start | bytes 12292
  55.4 46.7 %all-to-all-start = ((bf16[32,80,512]{2,1,0:T(8,128)(2,1)}), bf16[32,80,512]{2,1,0:T(8,128)(2,1)}, u32[]{:S(2)}, u32[]{:S(2)}) async-start(bf16[32,80,512]{2,1,0:T(8,128)(2,1)} %add_convert_fusion), calls=%async_computation | async-start | bytes 5242880 | tf_op jit(solution)/shard_map/all_to_all | solution.py:220
  66.4 2.0 %collective-permute-start.2 = (bf16[1024,256]{0,1:T(8,128)(2,1)S(1)}, bf16[1024,256]{0,1:T(8,128)(2,1)S(1)}, u32[]{:S(2)}, u32[]{:S(2)}) collective-permute-start(bf16[1024,256]{0,1:T(8,128)(2,1)S(1)} %bitcast.41), channel_id=1, source_target_pairs={{0,1},{1,0},{2,3},{3,2},{4,5},{5,4},{6,7},{7,6},{8,9},{9,8},{10,11... | collective-permute-start | bytes 1572872 | tf_op jit(solution)/shard_map/ppermute | solution.py:167
  66.5 2.6 %collective-permute-start.3 = (bf16[1024,256]{0,1:T(8,128)(2,1)S(1)}, bf16[1024,256]{0,1:T(8,128)(2,1)S(1)}, u32[]{:S(2)}, u32[]{:S(2)}) collective-permute-start(bf16[1024,256]{0,1:T(8,128)(2,1)S(1)} %collective-permute-done), channel_id=1, source_target_pairs={{0,1},{1,0},{2,3},{3,2},{4,5},{5,4},{6,7},{7,6},{8,9},{9,8},{10,11... | collective-permute-start | bytes 1572872 | tf_op jit(solution)/shard_map/ppermute | solution.py:167
  67.0 40.2 %collective-permute-start.4 = (bf16[128,1024]{1,0:T(8,128)(2,1)}, bf16[128,1024]{1,0:T(8,128)(2,1)}, u32[]{:S(2)}, u32[]{:S(2)}) collective-permute-start(bf16[128,1024]{1,0:T(8,128)(2,1)} %bitcast.6), channel_id=1, source_target_pairs={{0,1},{1,0},{2,3},{3,2},{4,5},{5,4},{6,7},{7,6},{8,9},{9,8},{10,11... | collective-permute-start | bytes 786440 | tf_op jit(solution)/shard_map/ppermute | solution.py:167
  67.1 40.1 %collective-permute-start.5 = (bf16[128,1024]{1,0:T(8,128)(2,1)}, bf16[128,1024]{1,0:T(8,128)(2,1)}, u32[]{:S(2)}, u32[]{:S(2)}) collective-permute-start(bf16[128,1024]{1,0:T(8,128)(2,1)} %collective-permute-done.1), channel_id=1, source_target_pairs={{0,1},{1,0},{2,3},{3,2},{4,5},{5,4},{6,7},{7,6},{8,9},{9,8},{10,11... | collective-permute-start | bytes 786440 | tf_op jit(solution)/shard_map/ppermute | solution.py:167
  102.1 2.0 %copy-start.3 = (bf16[1024,4,128]{0,2,1:T(8,128)(2,1)S(1)}, bf16[1024,4,128]{0,2,1:T(8,128)(2,1)}, u32[]{:S(2)}) copy-start(bf16[1024,4,128]{0,2,1:T(8,128)(2,1)} %get-tuple-element.15) | copy-start | bytes 3145732
  104.1 3.2 %copy-start.2 = (bf16[32,40,512]{2,1,0:T(8,128)(2,1)}, bf16[32,40,512]{2,1,0:T(8,128)(2,1)S(1)}, u32[]{:S(2)}) copy-start(bf16[32,40,512]{2,1,0:T(8,128)(2,1)S(1)} %get-tuple-element.13) | copy-start | bytes 3932164
  118.3 5.0 %copy-start.6 = (f32[128,8]{0,1:T(8,128)S(1)}, f32[128,8]{0,1:T(8,128)}, u32[]{:S(2)}) copy-start(f32[128,8]{0,1:T(8,128)} %param.21) | copy-start | bytes 12292
  118.3 39.7 %all-to-all-start.1 = ((bf16[32,80,512]{2,1,0:T(8,128)(2,1)}), bf16[32,80,512]{2,1,0:T(8,128)(2,1)}, u32[]{:S(2)}, u32[]{:S(2)}) async-start(bf16[32,80,512]{2,1,0:T(8,128)(2,1)} %pad_maximum_fusion.1), calls=%async_computation.1 | async-start | bytes 5242880 | tf_op jit(solution)/shard_map/all_to_all | solution.py:234

commit v9 on v7

--- a/solution.py
+++ b/solution.py
@@ -54,12 +54,6 @@
     vc = vc_ref[...]
     kn = turn(k_ref[...], cosine, sine, lead, quarter).astype(jnp.bfloat16)
     vn = v_ref[...].astype(jnp.bfloat16)
-    column = lax.broadcasted_iota(jnp.int32, (rows, span), 1)
-    cache_ok = column < length
-    new_col = lax.broadcasted_iota(jnp.int32, (rows, rows), 1)
-    new_row = lax.broadcasted_iota(jnp.int32, (rows, rows), 0)
-    new_ok = new_col <= new_row
-
     def scaled(values):
         rotated = turn(values, cosine, sine, lead, quarter).astype(jnp.bfloat16)
         return (rotated * 0.015625).astype(jnp.bfloat16).astype(jnp.float32)
@@ -73,24 +67,29 @@
         jnp.where(low, 0.0, second),
     )
     contract = (((1,), (1,)), ((), ()))
-    outs = []
-    for q in queries:
-        q = q.astype(jnp.bfloat16)
-        s = lax.dot_general(q, kc, contract, preferred_element_type=jnp.float32)
-        s = jnp.where(cache_ok, s, -1e30)
-        sn = lax.dot_general(q, kn, contract, preferred_element_type=jnp.float32)
-        sn = jnp.where(new_ok, sn, -1e30)
-        top = jnp.maximum(jnp.max(s, axis=1, keepdims=True), jnp.max(sn, axis=1, keepdims=True))
-        e = jnp.exp(s - top)
-        en = jnp.exp(sn - top)
-        total = jnp.sum(e, axis=1, keepdims=True) + jnp.sum(en, axis=1, keepdims=True)
-        inverse = 1.0 / total
-        w = (e * inverse).astype(jnp.bfloat16)
-        wn = (en * inverse).astype(jnp.bfloat16)
-        o = jnp.dot(w, vc, preferred_element_type=jnp.float32) + jnp.dot(
-            wn, vn, preferred_element_type=jnp.float32
-        )
-        outs.append(o.astype(jnp.bfloat16).astype(jnp.float32))
+    stacked = jnp.concatenate(queries, axis=0).astype(jnp.bfloat16)
+    tall = stacked.shape[0]
+    column = lax.broadcasted_iota(jnp.int32, (tall, span), 1)
+    cache_ok = column < length
+    new_col = lax.broadcasted_iota(jnp.int32, (tall, rows), 1)
+    new_row = lax.broadcasted_iota(jnp.int32, (tall, rows), 0) % rows
+    new_ok = new_col <= new_row
+    s = lax.dot_general(stacked, kc, contract, preferred_element_type=jnp.float32)
+    s = jnp.where(cache_ok, s, -1e30)
+    sn = lax.dot_general(stacked, kn, contract, preferred_element_type=jnp.float32)
+    sn = jnp.where(new_ok, sn, -1e30)
+    top = jnp.maximum(jnp.max(s, axis=1, keepdims=True), jnp.max(sn, axis=1, keepdims=True))
+    e = jnp.exp(s - top)
+    en = jnp.exp(sn - top)
+    total = jnp.sum(e, axis=1, keepdims=True) + jnp.sum(en, axis=1, keepdims=True)
+    inverse = 1.0 / total
+    w = (e * inverse).astype(jnp.bfloat16)
+    wn = (en * inverse).astype(jnp.bfloat16)
+    o = jnp.dot(w, vc, preferred_element_type=jnp.float32) + jnp.dot(
+        wn, vn, preferred_element_type=jnp.float32
+    )
+    o = o.astype(jnp.bfloat16).astype(jnp.float32)
+    outs = [o[j * rows : (j + 1) * rows] for j in range(len(queries))]
     left = jnp.where(low, outs[0], pltpu.roll(outs[1], half, 1))
     right = jnp.where(low, pltpu.roll(outs[2], half, 1), outs[3])
     o_ref[:, :lanes] = left.astype(jnp.bfloat16)

time: 140 us -> 141 us (level)
  no operation moved by 1% of the time
where the time goes in v9:
time: 141 us; the launch traced here: 140 us
  waiting for transfers between devices  67.3 us (48%)
  matrix products  21.3 us (15%)
  starting transfers between devices  19.2 us (14%)
  Pallas kernels  15.6 us (11%)
  local copies, waits for them, and re-layouts  10.2 us (7%)
  other arithmetic  4.53 us (3%)
  between operations  1.49 us (1%)
    all_to_all x1, waiting for transfers between devices, on_device(): lax.all_to_all(back, ('req', 'h'), split_axis=0, concat_axis=0, tiled=True)  34.6 us
    all_to_all x1, waiting for transfers between devices, on_device(): lax.all_to_all(outgoing.astype(jnp.bfloat16), ('req', 'h'), split_axis=0,...  31.1 us
    pallas_call x1, Pallas kernels, attention_core(): pl.pallas_call(attention_kernel, grid_spec=pltpu.PrefetchScalarGridSpec(n...  15.6 us
    all_to_all x1, starting transfers between devices, on_device(): lax.all_to_all(outgoing.astype(jnp.bfloat16), ('req', 'h'), split_axis=0,...  11 us
    dot_general x1, matrix products, on_device(): jnp.einsum('sch,hw->scw', hidden, down_all, preferred_element_type=jnp.fl...  7.29 us
    all_to_all x1, starting transfers between devices, on_device(): lax.all_to_all(back, ('req', 'h'), split_axis=0, concat_axis=0, tiled=True)  4.94 us
    dot_general x1, matrix products, attend(): mixed = jnp.dot(normed, qkv_weight, preferred_element_type=jnp.float32)  4.09 us
    ppermute x6, starting transfers between devices, swap(): lax.ppermute(piece, 'q', [(i, i ^ bit) for i in range(lax.axis_size('q'))])  3.2 us
  transfers between devices with their start and end apart: 8, of which 4 were waited for; matrix products, arithmetic and copies ran while one was open for 11% of the time, Pallas kernels for 11%

profile of v9, /device:TPU:0, one launch (start us, length us, event | category | flops | bytes accessed | tf_op | source)
XLA Modules:
  0.0 139.7 jit_solution(6825182728431018767)
XLA Ops:
  0.6 1.4 copy.26
  2.0 1.7 %collective-permute-start = (bf16[1024,256]{0,1:T(8,128)(2,1)S(1)}, bf16[1024,256]{0,1:T(8,128)(2,1)S(1)}, u32[]{:S(2)}, u32[]{:S(2)}) collective-permute-start(bf16[1024,256]{0,1:T(8,128)(2,1)S(1)} %bitcast.40), channel_id=1, source_target_pairs={{0,2},{1,3},{2,0},{3,1},{4,6},{5,7},{6,4},{7,5},{8,10},{9,11},{10,... | collective-permute-start | bytes 1572872 | tf_op jit(solution)/shard_map/ppermute | solution.py:152
  3.7 0.4 collective-permute-start.1
  4.8 0.1 multiply_sine_fusion
  5.0 0.7 copy.24.cos_ref
  5.7 0.7 copy.25.sin_ref
  6.4 1.1 fusion.22
  7.5 4.1 %fusion.27.q_ref.k_ref.v_ref = f32[128,2048]{1,0:T(8,128)} fusion(bf16[1024,2048]{1,0:T(8,128)(2,1)} %param.13, bf16[128,1024]{1,0:T(8,128)(2,1)} %param.12, f32[1024]{0:T(1024)} %param.15, f32[128]{0:T(128)S(1)} %add_rsqrt_fusion.1), kind=kOutput, calls=%fused_computation.37 | convolution fusion | flops 537395200 | bytes 5509632 | tf_op jit(solution)/shard_map/dot_general | solution.py:133
  11.6 15.6 %shard_map.131 = bf16[128,1024]{1,0:T(8,128)(2,1)} custom-call(s32[1]{0:T(128)} %copy.33.length_ref, f32[128,2048]{1,0:T(8,128)} %fusion.27.q_ref.k_ref.v_ref, f32[128,2048]{1,0:T(8,128)} %fusion.27.q_ref.k_ref.v_ref, f32[128,2048]{1,0:T(8,128)} %fusion.27.q_ref.k_ref.v_ref, f32[128,128]{1,0:T(8,128)} %copy.24.cos_ref, f32[128,128]{1,0:T(8,128)} %copy.25.sin_ref, ...), custom_call_target="tpu_custom_call" | custom-call | tf_op jit(solution)/shard_map/pallas_call | solution.py:108
  27.2 1.4 %fusion.45 = f32[128,1024]{1,0:T(8,128)S(1)} fusion(bf16[128,1024]{1,0:T(8,128)(2,1)} %shard_map.131, bf16[1024,1024]{1,0:T(8,128)(2,1)S(1)} %copy-done), kind=kOutput, calls=%fused_computation.63 | convolution fusion | flops 268435456 | bytes 2883584 | tf_op jit(solution)/shard_map/dot_general | solution.py:148
  28.8 0.2 fusion.21
  29.0 0.2 multiply_reduce_fusion
  29.2 0.8 multiply_convert_fusion.1
  30.0 0.8 fusion.6
  30.9 2.3 %add_convert_fusion = bf16[32,80,512]{2,1,0:T(8,128)(2,1)} fusion(f32[32,80,512]{2,1,0:T(8,128)S(1)} %fusion.6, pred[128,32,40]{0,2,1:T(8,128)(4,1)S(1)} %fusion.21, bf16[128,1024]{1,0:T(8,128)(2,1)S(1)} %get-tuple-element.16), kind=kOutput, calls=%fused_computation | convolution fusion | flops 338165760 | bytes 8159232 | tf_op jit(solution)/shard_map/ter,tw->erw/dot_general | solution.py:204
  33.2 11.0 %all-to-all-start = ((bf16[32,80,512]{2,1,0:T(8,128)(2,1)}), bf16[32,80,512]{2,1,0:T(8,128)(2,1)}, u32[]{:S(2)}, u32[]{:S(2)}) async-start(bf16[32,80,512]{2,1,0:T(8,128)(2,1)} %add_convert_fusion), calls=%async_computation | async-start | bytes 5242880 | tf_op jit(solution)/shard_map/all_to_all | solution.py:205
  44.3 0.5 collective-permute-start.3
  44.9 0.4 collective-permute-start.5
  45.3 0.9 collective-permute-done.2
  46.2 0.7 collective-permute-done.3
  47.0 0.3 pad_maximum_fusion.2
  47.2 1.6 %fusion.44 = (bf16[1024,4,128]{0,2,1:T(8,128)(2,1)}, bf16[1024,4,128]{0,2,1:T(8,128)(2,1)}) fusion(bf16[1024,4,256]{0,2,1:T(8,128)(2,1)S(1)} %pad_maximum_fusion.2), kind=kLoop, calls=%fused_computation.62 | loop fusion | bytes 4194304 | tf_op jit(solution)/shard_map/slice | solution.py:211
  48.8 31.1 %all-to-all-done = bf16[32,80,512]{2,1,0:T(8,128)(2,1)} async-done(((bf16[32,80,512]{2,1,0:T(8,128)(2,1)}), bf16[32,80,512]{2,1,0:T(8,128)(2,1)}, u32[]{:S(2)}, u32[]{:S(2)}) %all-to-all-start) | async-done | bytes 2621472 | tf_op jit(solution)/shard_map/all_to_all | solution.py:205
  79.8 2.0 %fusion.43 = (bf16[32,40,512]{2,1,0:T(8,128)(2,1)S(1)}, bf16[32,40,512]{2,1,0:T(8,128)(2,1)S(1)}) fusion(bf16[32,80,512]{2,1,0:T(8,128)(2,1)} %all-to-all-done), kind=kLoop, calls=%fused_computation.61 | loop fusion | bytes 5242880 | tf_op jit(solution)/shard_map/slice | solution.py:208
  81.9 3.1 %fusion.4 = f32[32,40,512]{2,1,0:T(8,128)} fusion(bf16[1024,512,1]{0,1,2:T(8,128)(2,1)S(1)} %bitcast.44, bf16[32,40,512]{2,1,0:T(8,128)(2,1)S(1)} %get-tuple-element.13, bf16[32,40,512]{2,1,0:T(8,128)(2,1)S(1)} %get-tuple-element.12), kind=kOutput, calls=%fused_computation.10 | convolution fusion | flops 1347420160 | bytes 6291456 | tf_op jit(solution)/shard_map/scw,wh->sch/dot_general | solution.py:212
  85.0 7.3 %convolution_convert_fusion = bf16[32,40,1024]{2,1,0:T(8,128)(2,1)} fusion(f32[32,40,512]{2,1,0:T(8,128)} %fusion.4, bf16[1024,512,1]{0,1,2:T(8,128)(2,1)} %bitcast.43, bf16[32,40,512]{2,1,0:T(8,128)(2,1)} %copy-done.2, bf16[32,40,512]{2,1,0:T(8,128)(2,1)S(1)} %get-tuple-element.12, bf16[128,1024]{1,0:T(8,128)(2,1)} %collective-permute-done.5, ...), kind=kOutput, calls=%fused_computation.9 | convolution fusion | flops 2699034624 | bytes 9961472 | tf_op jit(solution)/shard_map/sch,hw->scw/dot_general | solution.py:215
  92.3 1.9 %fusion.42 = (bf16[32,40,512]{2,1,0:T(8,128)(2,1)S(1)}, bf16[32,40,512]{2,1,0:T(8,128)(2,1)S(1)}) fusion(bf16[32,40,1024]{2,1,0:T(8,128)(2,1)} %convolution_convert_fusion), kind=kLoop, calls=%fused_computation.60 | loop fusion | bytes 5242880 | tf_op jit(solution)/shard_map/slice | solution.py:218
  94.2 1.9 %pad_maximum_fusion.1 = bf16[32,80,512]{2,1,0:T(8,128)(2,1)} fusion(bf16[32,40,512]{2,1,0:T(8,128)(2,1)S(1)} %get-tuple-element.11, bf16[32,40,512]{2,1,0:T(8,128)(2,1)S(1)} %get-tuple-element.10), kind=kLoop, calls=%fused_computation.2 | loop fusion | flops 5242880 | bytes 5242880 | tf_op jit(solution)/shard_map/concatenate | solution.py:218
  96.0 4.9 %all-to-all-start.1 = ((bf16[32,80,512]{2,1,0:T(8,128)(2,1)}), bf16[32,80,512]{2,1,0:T(8,128)(2,1)}, u32[]{:S(2)}, u32[]{:S(2)}) async-start(bf16[32,80,512]{2,1,0:T(8,128)(2,1)} %pad_maximum_fusion.1), calls=%async_computation.1 | async-start | bytes 5242880 | tf_op jit(solution)/shard_map/all_to_all | solution.py:219
  101.0 34.6 %all-to-all-done.1 = bf16[32,80,512]{2,1,0:T(8,128)(2,1)} async-done(((bf16[32,80,512]{2,1,0:T(8,128)(2,1)}), bf16[32,80,512]{2,1,0:T(8,128)(2,1)}, u32[]{:S(2)}, u32[]{:S(2)}) %all-to-all-start.1) | async-done | bytes 2621472 | tf_op jit(solution)/shard_map/all_to_all | solution.py:219
  135.7 1.9 %fusion.41 = (bf16[32,40,512]{2,1,0:T(8,128)(2,1)S(1)}, bf16[32,40,512]{2,1,0:T(8,128)(2,1)S(1)}) fusion(bf16[32,80,512]{2,1,0:T(8,128)(2,1)} %all-to-all-done.1), kind=kLoop, calls=%fused_computation.59 | loop fusion | bytes 5242880 | tf_op jit(solution)/shard_map/slice | solution.py:221
  137.6 2.1 %fusion.11 = bf16[128,1024]{1,0:T(8,128)(2,1)} fusion(bf16[32,40,512]{2,1,0:T(8,128)(2,1)S(1)} %get-tuple-element.9, bf16[32,40,512]{2,1,0:T(8,128)(2,1)S(1)} %get-tuple-element.8, f32[128,32]{0,1:T(8,128)S(1)} %select_reduce_fusion, s32[128,32]{0,1:T(8,128)S(1)} %convolution_convert_fusion.1, pred[128,32]{0,1:T(8,128)(4,1)S(1)} %fusion.31), kind=kOutput, calls=%fused_computation.15 | convolution fusion | flops 2019131392 | bytes 2920448 | tf_op jit(solution)/shard_map/tec,ecw->tw/dot_general | solution.py:222
  (29 shorter events, 0.5 us)
Async XLA Ops:
  0.6 26.6 %copy-start = (bf16[1024,1024]{1,0:T(8,128)(2,1)S(1)}, bf16[1024,1024]{1,0:T(8,128)(2,1)}, u32[]{:S(2)}) copy-start(bf16[1024,1024]{1,0:T(8,128)(2,1)} %param.14) | copy-start | bytes 6291460
  2.0 27.0 %collective-permute-start = (bf16[1024,256]{0,1:T(8,128)(2,1)S(1)}, bf16[1024,256]{0,1:T(8,128)(2,1)S(1)}, u32[]{:S(2)}, u32[]{:S(2)}) collective-permute-start(bf16[1024,256]{0,1:T(8,128)(2,1)S(1)} %bitcast.40), channel_id=1, source_target_pairs={{0,2},{1,3},{2,0},{3,1},{4,6},{5,7},{6,4},{7,5},{8,10},{9,11},{10,... | collective-permute-start | bytes 1572872 | tf_op jit(solution)/shard_map/ppermute | solution.py:152
  3.7 25.3 %collective-permute-start.1 = (bf16[128,1024]{1,0:T(8,128)(2,1)}, bf16[128,1024]{1,0:T(8,128)(2,1)}, u32[]{:S(2)}, u32[]{:S(2)}) collective-permute-start(bf16[128,1024]{1,0:T(8,128)(2,1)} %bitcast.6), channel_id=1, source_target_pairs={{0,2},{1,3},{2,0},{3,1},{4,6},{5,7},{6,4},{7,5},{8,10},{9,11},{10,... | collective-permute-start | bytes 786440 | tf_op jit(solution)/shard_map/ppermute | solution.py:152
  27.2 1.5 %copy-start.4 = (s32[128,8]{0,1:T(8,128)S(1)}, s32[128,8]{0,1:T(8,128)}, u32[]{:S(2)}) copy-start(s32[128,8]{0,1:T(8,128)} %param.20) | copy-start | bytes 12292
  27.2 1.8 %copy-start.1 = (bf16[128,1024]{1,0:T(8,128)(2,1)S(1)}, bf16[128,1024]{1,0:T(8,128)(2,1)}, u32[]{:S(2)}) copy-start(bf16[128,1024]{1,0:T(8,128)(2,1)} %param.12) | copy-start | bytes 786436
  27.2 2.0 %copy-start.5 = (f32[1024]{0:T(1024)S(1)}, f32[1024]{0:T(1024)}, u32[]{:S(2)}) copy-start(f32[1024]{0:T(1024)} %param.16) | copy-start | bytes 12292
  33.2 46.6 %all-to-all-start = ((bf16[32,80,512]{2,1,0:T(8,128)(2,1)}), bf16[32,80,512]{2,1,0:T(8,128)(2,1)}, u32[]{:S(2)}, u32[]{:S(2)}) async-start(bf16[32,80,512]{2,1,0:T(8,128)(2,1)} %add_convert_fusion), calls=%async_computation | async-start | bytes 5242880 | tf_op jit(solution)/shard_map/all_to_all | solution.py:205
  44.2 2.0 %collective-permute-start.2 = (bf16[1024,256]{0,1:T(8,128)(2,1)S(1)}, bf16[1024,256]{0,1:T(8,128)(2,1)S(1)}, u32[]{:S(2)}, u32[]{:S(2)}) collective-permute-start(bf16[1024,256]{0,1:T(8,128)(2,1)S(1)} %bitcast.41), channel_id=1, source_target_pairs={{0,1},{1,0},{2,3},{3,2},{4,5},{5,4},{6,7},{7,6},{8,9},{9,8},{10,11... | collective-permute-start | bytes 1572872 | tf_op jit(solution)/shard_map/ppermute | solution.py:152
  44.3 2.6 %collective-permute-start.3 = (bf16[1024,256]{0,1:T(8,128)(2,1)S(1)}, bf16[1024,256]{0,1:T(8,128)(2,1)S(1)}, u32[]{:S(2)}, u32[]{:S(2)}) collective-permute-start(bf16[1024,256]{0,1:T(8,128)(2,1)S(1)} %collective-permute-done), channel_id=1, source_target_pairs={{0,1},{1,0},{2,3},{3,2},{4,5},{5,4},{6,7},{7,6},{8,9},{9,8},{10,11... | collective-permute-start | bytes 1572872 | tf_op jit(solution)/shard_map/ppermute | solution.py:152
  44.8 40.2 %collective-permute-start.4 = (bf16[128,1024]{1,0:T(8,128)(2,1)}, bf16[128,1024]{1,0:T(8,128)(2,1)}, u32[]{:S(2)}, u32[]{:S(2)}) collective-permute-start(bf16[128,1024]{1,0:T(8,128)(2,1)} %bitcast.6), channel_id=1, source_target_pairs={{0,1},{1,0},{2,3},{3,2},{4,5},{5,4},{6,7},{7,6},{8,9},{9,8},{10,11... | collective-permute-start | bytes 786440 | tf_op jit(solution)/shard_map/ppermute | solution.py:152
  44.9 40.1 %collective-permute-start.5 = (bf16[128,1024]{1,0:T(8,128)(2,1)}, bf16[128,1024]{1,0:T(8,128)(2,1)}, u32[]{:S(2)}, u32[]{:S(2)}) collective-permute-start(bf16[128,1024]{1,0:T(8,128)(2,1)} %collective-permute-done.1), channel_id=1, source_target_pairs={{0,1},{1,0},{2,3},{3,2},{4,5},{5,4},{6,7},{7,6},{8,9},{9,8},{10,11... | collective-permute-start | bytes 786440 | tf_op jit(solution)/shard_map/ppermute | solution.py:152
  79.8 2.0 %copy-start.3 = (bf16[1024,4,128]{0,2,1:T(8,128)(2,1)S(1)}, bf16[1024,4,128]{0,2,1:T(8,128)(2,1)}, u32[]{:S(2)}) copy-start(bf16[1024,4,128]{0,2,1:T(8,128)(2,1)} %get-tuple-element.15) | copy-start | bytes 3145732
  81.8 3.2 %copy-start.2 = (bf16[32,40,512]{2,1,0:T(8,128)(2,1)}, bf16[32,40,512]{2,1,0:T(8,128)(2,1)S(1)}, u32[]{:S(2)}) copy-start(bf16[32,40,512]{2,1,0:T(8,128)(2,1)S(1)} %get-tuple-element.13) | copy-start | bytes 3932164
  96.0 5.0 %copy-start.6 = (f32[128,8]{0,1:T(8,128)S(1)}, f32[128,8]{0,1:T(8,128)}, u32[]{:S(2)}) copy-start(f32[128,8]{0,1:T(8,128)} %param.21) | copy-start | bytes 12292
  96.0 39.6 %all-to-all-start.1 = ((bf16[32,80,512]{2,1,0:T(8,128)(2,1)}), bf16[32,80,512]{2,1,0:T(8,128)(2,1)}, u32[]{:S(2)}, u32[]{:S(2)}) async-start(bf16[32,80,512]{2,1,0:T(8,128)(2,1)} %pad_maximum_fusion.1), calls=%async_computation.1 | async-start | bytes 5242880 | tf_op jit(solution)/shard_map/all_to_all | solution.py:219

commit v10 on v7

--- a/solution.py
+++ b/solution.py
@@ -133,10 +133,11 @@
     normed = rms_scale(tokens, norm_attn).astype(jnp.bfloat16)
     mixed = jnp.dot(normed, qkv_weight, preferred_element_type=jnp.float32)
     places = (length + jnp.arange(rows, dtype=jnp.int32)).astype(jnp.float32)
-    freq = 10000.0 ** (-jnp.arange(half, dtype=jnp.float32) / half)
+    index = (jnp.arange(2 * HEAD, dtype=jnp.int32) % half).astype(jnp.float32)
+    freq = 10000.0 ** (-index / half)
     angle = places[:, None] * freq[None, :]
-    cosine = jnp.tile(jnp.cos(angle), (1, 4))
-    sine = jnp.tile(jnp.sin(angle), (1, 4))
+    cosine = jnp.cos(angle)
+    sine = jnp.sin(angle)
     heads_out = attention_core(
         length.reshape(1).astype(jnp.int32),
         mixed,
@@ -210,9 +211,14 @@
     pieces = gate_up_all.reshape(gate_up_all.shape[0], slices, 2 * width_dev)
     gate_cols = pieces[..., :width_dev].reshape(gate_up_all.shape[0], slices * width_dev)
     up_cols = pieces[..., width_dev:].reshape(gate_up_all.shape[0], slices * width_dev)
-    gate = jnp.einsum("scw,wh->sch", joined, gate_cols, preferred_element_type=jnp.float32)
-    upper = jnp.einsum("scw,wh->sch", joined, up_cols, preferred_element_type=jnp.float32)
-    hidden = (jax.nn.silu(gate) * upper).astype(jnp.bfloat16)
+    both = jnp.einsum(
+        "scw,wh->sch",
+        joined,
+        jnp.concatenate([gate_cols, up_cols], axis=1),
+        preferred_element_type=jnp.float32,
+    )
+    inner = slices * width_dev
+    hidden = (jax.nn.silu(both[..., :inner]) * both[..., inner:]).astype(jnp.bfloat16)
     produced = jnp.einsum(
         "sch,hw->scw", hidden, down_all, preferred_element_type=jnp.float32
     ).astype(jnp.bfloat16)

time: 140 us -> 132 us (0.943)
  matrix products: 21.3 us -> 16.6 us
  local copies, waits for them, and re-layouts: 10.2 us -> 5.76 us
    dot_general x1, matrix products: 7.29 us -> 2.74 us  [on_device(): jnp.einsum('sch,hw->scw', hidden, down_all, preferred_element_type=jnp.fl...]
    slice x1, local copies, waits for them, and re-layouts: 1.89 us -> 0.21 us  [on_device(): back = jnp.concatenate([produced[..., :part], produced[..., part:]], axis=1)]
    slice x1 -> x0, local copies, waits for them, and re-layouts: 1.56 us -> none  [on_device(): pieces[..., width_dev:].reshape(gate_up_all.shape[0], slices * width_dev)]
    another operation x4 -> x0, local copies, waits for them, and re-layouts: 1.46 us -> none  [the longest x2 0.74 us: attend(): cosine = jnp.tile(jnp.cos(angle), (1, 4))]
  transfers between devices with their start and end apart: 8 -> 8, of which waited for: 4 -> 4; matrix products, arithmetic and copies ran while one was open for 11% -> 11% of each run, Pallas kernels for 11% -> 12%
where the time goes in v10:
time: 132 us; the launch traced here: 131 us
  waiting for transfers between devices  67.3 us (51%)
  starting transfers between devices  19.3 us (15%)
  matrix products  16.6 us (13%)
  Pallas kernels  15.1 us (11%)
  local copies, waits for them, and re-layouts  5.76 us (4%)
  other arithmetic  5.36 us (4%)
  between operations  1.53 us (1%)
    all_to_all x1, waiting for transfers between devices, on_device(): lax.all_to_all(back, ('req', 'h'), split_axis=0, concat_axis=0, tiled=True)  34.7 us
    all_to_all x1, waiting for transfers between devices, on_device(): lax.all_to_all(outgoing.astype(jnp.bfloat16), ('req', 'h'), split_axis=0,...  31 us
    pallas_call x1, Pallas kernels, attention_core(): pl.pallas_call(attention_kernel, grid_spec=pltpu.PrefetchScalarGridSpec(n...  15.1 us
    all_to_all x1, starting transfers between devices, on_device(): lax.all_to_all(outgoing.astype(jnp.bfloat16), ('req', 'h'), split_axis=0,...  11.1 us
    all_to_all x1, starting transfers between devices, on_device(): lax.all_to_all(back, ('req', 'h'), split_axis=0, concat_axis=0, tiled=True)  4.94 us
    dot_general x1, matrix products, attend(): mixed = jnp.dot(normed, qkv_weight, preferred_element_type=jnp.float32)  4.05 us
    ppermute x6, starting transfers between devices, swap(): lax.ppermute(piece, 'q', [(i, i ^ bit) for i in range(lax.axis_size('q'))])  3.2 us
    dot_general x1, matrix products, on_device(): jnp.einsum('scw,wh->sch', joined, jnp.concatenate([gate_cols, up_cols], a...  2.91 us
  transfers between devices with their start and end apart: 8, of which 4 were waited for; matrix products, arithmetic and copies ran while one was open for 11% of the time, Pallas kernels for 12%

profile of v10, /device:TPU:0, one launch (start us, length us, event | category | flops | bytes accessed | tf_op | source)
XLA Modules:
  0.0 130.9 jit_solution(3226356578927747386)
XLA Ops:
  0.6 1.7 %collective-permute-start = (bf16[1024,256]{1,0:T(8,128)(2,1)}, bf16[1024,256]{1,0:T(8,128)(2,1)S(1)}, u32[]{:S(2)}, u32[]{:S(2)}) collective-permute-start(bf16[1024,256]{1,0:T(8,128)(2,1)} %bitcast.40), channel_id=1, source_target_pairs={{0,2},{1,3},{2,0},{3,1},{4,6},{5,7},{6,4},{7,5},{8,10},{9,11},{10,... | collective-permute-start | bytes 1572872 | tf_op jit(solution)/shard_map/ppermute | solution.py:154
  2.3 0.4 collective-permute-start.1
  3.4 1.1 fusion.29
  4.5 1.0 multiply_sine_fusion
  5.5 4.1 %fusion.34.q_ref.k_ref.v_ref = f32[128,2048]{1,0:T(8,128)} fusion(bf16[1024,2048]{1,0:T(8,128)(2,1)} %param.13, bf16[128,1024]{1,0:T(8,128)(2,1)} %param.12, f32[1024]{0:T(1024)} %param.15, f32[128]{0:T(128)S(1)} %add_rsqrt_fusion.1), kind=kOutput, calls=%fused_computation.47 | convolution fusion | flops 537395200 | bytes 5509632 | tf_op jit(solution)/shard_map/dot_general | solution.py:134
  9.5 15.1 %shard_map.131 = bf16[128,1024]{1,0:T(8,128)(2,1)} custom-call(s32[1]{0:T(128)} %copy.24.length_ref, f32[128,2048]{1,0:T(8,128)} %fusion.34.q_ref.k_ref.v_ref, f32[128,2048]{1,0:T(8,128)} %fusion.34.q_ref.k_ref.v_ref, f32[128,2048]{1,0:T(8,128)} %fusion.34.q_ref.k_ref.v_ref, f32[128,128]{1,0:T(8,128)} %get-tuple-element.19.cos_ref, ...), custom_call_target="tpu_custom_call" | custom-call | tf_op jit(solution)/shard_map/pallas_call | solution.py:109
  24.6 1.4 %fusion.54 = f32[128,1024]{1,0:T(8,128)S(1)} fusion(bf16[128,1024]{1,0:T(8,128)(2,1)} %shard_map.131, bf16[1024,1024]{1,0:T(8,128)(2,1)S(1)} %copy-done), kind=kOutput, calls=%fused_computation.76 | convolution fusion | flops 268435456 | bytes 2883584 | tf_op jit(solution)/shard_map/dot_general | solution.py:150
  26.1 0.1 convolution_convert_fusion.1
  26.3 0.2 fusion.28
  26.5 0.2 multiply_reduce_fusion
  26.7 0.8 multiply_convert_fusion
  27.5 0.8 fusion.13
  28.3 2.4 %add_convert_fusion = bf16[32,80,512]{2,1,0:T(8,128)(2,1)} fusion(f32[32,80,512]{2,1,0:T(8,128)S(1)} %fusion.13, pred[128,32,40]{0,2,1:T(8,128)(4,1)S(1)} %fusion.28, bf16[128,1024]{1,0:T(8,128)(2,1)S(1)} %get-tuple-element.16), kind=kOutput, calls=%fused_computation | convolution fusion | flops 338165760 | bytes 8159232 | tf_op jit(solution)/shard_map/ter,tw->erw/dot_general | solution.py:206
  30.7 11.1 %all-to-all-start = ((bf16[32,80,512]{2,1,0:T(8,128)(2,1)}), bf16[32,80,512]{2,1,0:T(8,128)(2,1)}, u32[]{:S(2)}, u32[]{:S(2)}) async-start(bf16[32,80,512]{2,1,0:T(8,128)(2,1)} %add_convert_fusion), calls=%async_computation | async-start | bytes 5242880 | tf_op jit(solution)/shard_map/all_to_all | solution.py:207
  41.9 0.5 collective-permute-start.3
  42.4 0.1 collective-permute-start.4
  42.5 0.4 collective-permute-start.5
  42.9 0.9 collective-permute-done.2
  43.8 0.7 collective-permute-done.3
  44.6 0.3 pad_maximum_fusion.1
  44.8 0.4 slice_bitcast_fusion.1
  45.2 1.2 copy_bitcast_fusion
  46.4 31.0 %all-to-all-done = bf16[32,80,512]{2,1,0:T(8,128)(2,1)} async-done(((bf16[32,80,512]{2,1,0:T(8,128)(2,1)}), bf16[32,80,512]{2,1,0:T(8,128)(2,1)}, u32[]{:S(2)}, u32[]{:S(2)}) %all-to-all-start) | async-done | bytes 2621472 | tf_op jit(solution)/shard_map/all_to_all | solution.py:207
  77.5 2.0 %fusion.53 = (bf16[32,40,512]{2,1,0:T(8,128)(2,1)S(1)}, bf16[32,40,512]{2,1,0:T(8,128)(2,1)S(1)}) fusion(bf16[32,80,512]{2,1,0:T(8,128)(2,1)} %all-to-all-done), kind=kLoop, calls=%fused_computation.75 | loop fusion | bytes 5242880 | tf_op jit(solution)/shard_map/slice | solution.py:210
  79.5 2.9 %fusion.1 = f32[32,40,1024]{2,1,0:T(8,128)S(1)} fusion(bf16[32,40,512]{2,1,0:T(8,128)(2,1)S(1)} %get-tuple-element.13, bf16[32,40,512]{2,1,0:T(8,128)(2,1)S(1)} %get-tuple-element.12, bf16[1024,512]{1,0:T(8,128)(2,1)S(1)} %get-tuple-element.20, bf16[1024,512]{1,0:T(8,128)(2,1)S(1)} %copy-done.2), kind=kOutput, calls=%fused_computation.3 | convolution fusion | flops 2693791744 | bytes 9961472 | tf_op jit(solution)/shard_map/scw,wh->sch/dot_general | solution.py:214
  82.4 2.7 %convolution_convert_fusion = bf16[32,40,1024]{2,1,0:T(8,128)(2,1)S(1)} fusion(f32[32,40,1024]{2,1,0:T(8,128)S(1)} %fusion.1, bf16[128,1024]{1,0:T(8,128)(2,1)} %collective-permute-done.5, bf16[128,1024]{1,0:T(8,128)(2,1)} %collective-permute-done.4, bf16[128,1024]{1,0:T(8,128)(2,1)S(1)} %copy-done.9, bf16[128,1024]{1,0:T(8,128)(2,1)S(1)} %bitcast.48), kind=kOutput, calls=%fused_computation.16 | convolution fusion | flops 1351614464 | bytes 8912896 | tf_op jit(solution)/shard_map/sch,hw->scw/dot_general | solution.py:222
  85.2 0.2 fusion.52
  85.4 1.9 %pad_maximum_fusion = bf16[32,80,512]{2,1,0:T(8,128)(2,1)} fusion(bf16[32,40,512]{2,1,0:T(8,128)(2,1)S(1)} %get-tuple-element.11, bf16[32,40,512]{2,1,0:T(8,128)(2,1)S(1)} %get-tuple-element.10), kind=kLoop, calls=%fused_computation.7 | loop fusion | flops 5242880 | bytes 5242880 | tf_op jit(solution)/shard_map/concatenate | solution.py:225
  87.3 4.9 %all-to-all-start.1 = ((bf16[32,80,512]{2,1,0:T(8,128)(2,1)}), bf16[32,80,512]{2,1,0:T(8,128)(2,1)}, u32[]{:S(2)}, u32[]{:S(2)}) async-start(bf16[32,80,512]{2,1,0:T(8,128)(2,1)} %pad_maximum_fusion), calls=%async_computation.1 | async-start | bytes 5242880 | tf_op jit(solution)/shard_map/all_to_all | solution.py:226
  92.2 34.7 %all-to-all-done.1 = bf16[32,80,512]{2,1,0:T(8,128)(2,1)} async-done(((bf16[32,80,512]{2,1,0:T(8,128)(2,1)}), bf16[32,80,512]{2,1,0:T(8,128)(2,1)}, u32[]{:S(2)}, u32[]{:S(2)}) %all-to-all-start.1) | async-done | bytes 2621472 | tf_op jit(solution)/shard_map/all_to_all | solution.py:226
  126.9 1.9 %fusion.51 = (bf16[32,40,512]{2,1,0:T(8,128)(2,1)S(1)}, bf16[32,40,512]{2,1,0:T(8,128)(2,1)S(1)}) fusion(bf16[32,80,512]{2,1,0:T(8,128)(2,1)} %all-to-all-done.1), kind=kLoop, calls=%fused_computation.73 | loop fusion | bytes 5242880 | tf_op jit(solution)/shard_map/slice | solution.py:228
  128.8 2.1 %fusion.18 = bf16[128,1024]{1,0:T(8,128)(2,1)} fusion(bf16[32,40,512]{2,1,0:T(8,128)(2,1)S(1)} %get-tuple-element.9, bf16[32,40,512]{2,1,0:T(8,128)(2,1)S(1)} %get-tuple-element.8, f32[128,32]{0,1:T(8,128)S(1)} %select_reduce_fusion, s32[128,32]{0,1:T(8,128)S(1)} %convolution_convert_fusion.1, pred[128,32]{0,1:T(8,128)(4,1)S(1)} %fusion.38), kind=kOutput, calls=%fused_computation.21 | convolution fusion | flops 2019131392 | bytes 2920448 | tf_op jit(solution)/shard_map/tec,ecw->tw/dot_general | solution.py:229
  (31 shorter events, 0.2 us)
Async XLA Ops:
  0.6 24.0 %copy-start = (bf16[1024,1024]{1,0:T(8,128)(2,1)S(1)}, bf16[1024,1024]{1,0:T(8,128)(2,1)}, u32[]{:S(2)}) copy-start(bf16[1024,1024]{1,0:T(8,128)(2,1)} %param.14) | copy-start | bytes 6291460
  0.6 25.8 %collective-permute-start = (bf16[1024,256]{1,0:T(8,128)(2,1)}, bf16[1024,256]{1,0:T(8,128)(2,1)S(1)}, u32[]{:S(2)}, u32[]{:S(2)}) collective-permute-start(bf16[1024,256]{1,0:T(8,128)(2,1)} %bitcast.40), channel_id=1, source_target_pairs={{0,2},{1,3},{2,0},{3,1},{4,6},{5,7},{6,4},{7,5},{8,10},{9,11},{10,... | collective-permute-start | bytes 1572872 | tf_op jit(solution)/shard_map/ppermute | solution.py:154
  2.3 24.1 %collective-permute-start.1 = (bf16[128,1024]{1,0:T(8,128)(2,1)}, bf16[128,1024]{1,0:T(8,128)(2,1)S(1)}, u32[]{:S(2)}, u32[]{:S(2)}) collective-permute-start(bf16[128,1024]{1,0:T(8,128)(2,1)} %bitcast.46), channel_id=1, source_target_pairs={{0,2},{1,3},{2,0},{3,1},{4,6},{5,7},{6,4},{7,5},{8,10},{9,11},{10,... | collective-permute-start | bytes 786440 | tf_op jit(solution)/shard_map/ppermute | solution.py:154
  24.6 1.5 %copy-start.4 = (s32[128,8]{0,1:T(8,128)S(1)}, s32[128,8]{0,1:T(8,128)}, u32[]{:S(2)}) copy-start(s32[128,8]{0,1:T(8,128)} %param.20) | copy-start | bytes 12292
  24.6 1.8 %copy-start.1 = (bf16[128,1024]{1,0:T(8,128)(2,1)S(1)}, bf16[128,1024]{1,0:T(8,128)(2,1)}, u32[]{:S(2)}) copy-start(bf16[128,1024]{1,0:T(8,128)(2,1)} %param.12) | copy-start | bytes 786436
  24.6 2.0 %copy-start.5 = (f32[1024]{0:T(1024)S(1)}, f32[1024]{0:T(1024)}, u32[]{:S(2)}) copy-start(f32[1024]{0:T(1024)} %param.16) | copy-start | bytes 12292
  26.4 1.8 %copy-start.8 = (bf16[128,1024]{1,0:T(8,128)(2,1)}, bf16[128,1024]{1,0:T(8,128)(2,1)S(1)}, u32[]{:S(2)}) copy-start(bf16[128,1024]{1,0:T(8,128)(2,1)S(1)} %collective-permute-done.1) | copy-start | bytes 786436
  30.7 11.2 %copy-start.3 = (bf16[1,1024,256]{2,1,0:T(8,128)(2,1)S(1)}, bf16[1,1024,256]{2,1,0:T(8,128)(2,1)}, u32[]{:S(2)}) copy-start(bf16[1,1024,256]{2,1,0:T(8,128)(2,1)} %param.22) | copy-start | bytes 1572868
  30.7 11.8 %copy-start.7 = (bf16[1,128,1024]{2,1,0:T(8,128)(2,1)S(1)}, bf16[1,128,1024]{2,1,0:T(8,128)(2,1)}, u32[]{:S(2)}) copy-start(bf16[1,128,1024]{2,1,0:T(8,128)(2,1)} %param.23) | copy-start | bytes 786436
  30.7 46.8 %all-to-all-start = ((bf16[32,80,512]{2,1,0:T(8,128)(2,1)}), bf16[32,80,512]{2,1,0:T(8,128)(2,1)}, u32[]{:S(2)}, u32[]{:S(2)}) async-start(bf16[32,80,512]{2,1,0:T(8,128)(2,1)} %add_convert_fusion), calls=%async_computation | async-start | bytes 5242880 | tf_op jit(solution)/shard_map/all_to_all | solution.py:207
  41.8 2.0 %collective-permute-start.2 = (bf16[1024,256]{1,0:T(8,128)(2,1)S(1)}, bf16[1024,256]{1,0:T(8,128)(2,1)S(1)}, u32[]{:S(2)}, u32[]{:S(2)}) collective-permute-start(bf16[1024,256]{1,0:T(8,128)(2,1)S(1)} %bitcast.41), channel_id=1, source_target_pairs={{0,1},{1,0},{2,3},{3,2},{4,5},{5,4},{6,7},{7,6},{8,9},{9,8},{10,11... | collective-permute-start | bytes 1572872 | tf_op jit(solution)/shard_map/ppermute | solution.py:154
  41.9 2.6 %collective-permute-start.3 = (bf16[1024,256]{1,0:T(8,128)(2,1)S(1)}, bf16[1024,256]{1,0:T(8,128)(2,1)S(1)}, u32[]{:S(2)}, u32[]{:S(2)}) collective-permute-start(bf16[1024,256]{1,0:T(8,128)(2,1)S(1)} %collective-permute-done), channel_id=1, source_target_pairs={{0,1},{1,0},{2,3},{3,2},{4,5},{5,4},{6,7},{7,6},{8,9},{9,8},{10,11... | collective-permute-start | bytes 1572872 | tf_op jit(solution)/shard_map/ppermute | solution.py:154
  42.4 40.0 %collective-permute-start.4 = (bf16[128,1024]{1,0:T(8,128)(2,1)S(1)}, bf16[128,1024]{1,0:T(8,128)(2,1)}, u32[]{:S(2)}, u32[]{:S(2)}) collective-permute-start(bf16[128,1024]{1,0:T(8,128)(2,1)S(1)} %bitcast.47), channel_id=1, source_target_pairs={{0,1},{1,0},{2,3},{3,2},{4,5},{5,4},{6,7},{7,6},{8,9},{9,8},{10,11... | collective-permute-start | bytes 786440 | tf_op jit(solution)/shard_map/ppermute | solution.py:154
  42.5 39.9 %collective-permute-start.5 = (bf16[128,1024]{1,0:T(8,128)(2,1)}, bf16[128,1024]{1,0:T(8,128)(2,1)}, u32[]{:S(2)}, u32[]{:S(2)}) collective-permute-start(bf16[128,1024]{1,0:T(8,128)(2,1)} %copy-done.8), channel_id=1, source_target_pairs={{0,1},{1,0},{2,3},{3,2},{4,5},{5,4},{6,7},{7,6},{8,9},{9,8},{10,11... | collective-permute-start | bytes 786440 | tf_op jit(solution)/shard_map/ppermute | solution.py:154
  77.5 2.0 %copy-start.2 = (bf16[1024,512]{1,0:T(8,128)(2,1)S(1)}, bf16[1024,512]{1,0:T(8,128)(2,1)}, u32[]{:S(2)}) copy-start(bf16[1024,512]{1,0:T(8,128)(2,1)} %get-tuple-element.21) | copy-start | bytes 3145732
  79.5 2.9 %copy-start.9 = (bf16[128,1024]{1,0:T(8,128)(2,1)S(1)}, bf16[128,1024]{1,0:T(8,128)(2,1)}, u32[]{:S(2)}) copy-start(bf16[128,1024]{1,0:T(8,128)(2,1)} %copy-done.8) | copy-start | bytes 786436
  87.3 4.9 %copy-start.6 = (f32[128,8]{0,1:T(8,128)S(1)}, f32[128,8]{0,1:T(8,128)}, u32[]{:S(2)}) copy-start(f32[128,8]{0,1:T(8,128)} %param.21) | copy-start | bytes 12292
  87.3 39.7 %all-to-all-start.1 = ((bf16[32,80,512]{2,1,0:T(8,128)(2,1)}), bf16[32,80,512]{2,1,0:T(8,128)(2,1)}, u32[]{:S(2)}, u32[]{:S(2)}) async-start(bf16[32,80,512]{2,1,0:T(8,128)(2,1)} %pad_maximum_fusion), calls=%async_computation.1 | async-start | bytes 5242880 | tf_op jit(solution)/shard_map/all_to_all | solution.py:226

commit v11 on v10

--- a/solution.py
+++ b/solution.py
@@ -202,8 +202,11 @@
     pick_lo = jnp.concatenate([pick, empty], axis=2).astype(jnp.bfloat16)
     pick_hi = jnp.concatenate([empty, pick], axis=2).astype(jnp.bfloat16)
     outgoing = jnp.einsum(
-        "ter,tw->erw", pick_lo, normed[:, :part], preferred_element_type=jnp.float32
-    ) + jnp.einsum("ter,tw->erw", pick_hi, normed[:, part:], preferred_element_type=jnp.float32)
+        "ter,tw->erw",
+        jnp.concatenate([pick_lo, pick_hi], axis=0),
+        jnp.concatenate([normed[:, :part], normed[:, part:]], axis=0),
+        preferred_element_type=jnp.float32,
+    )
     received = lax.all_to_all(
         outgoing.astype(jnp.bfloat16), ("req", "h"), split_axis=0, concat_axis=0, tiled=True
     )
@@ -225,14 +228,18 @@
     back = jnp.concatenate([produced[..., :part], produced[..., part:]], axis=1)
     results = lax.all_to_all(back, ("req", "h"), split_axis=0, concat_axis=0, tiled=True)
     scale = jnp.where(pick, weight[:, :, None], 0.0)
-    output = jnp.concatenate([results[:, :capacity], results[:, capacity:]], axis=2)
-    mix = jnp.einsum(
-        "tec,ecw->tw",
-        scale,
-        output.astype(jnp.float32),
-        precision=lax.Precision.HIGHEST,
-        preferred_element_type=jnp.float32,
-    )
+    wide = results.astype(jnp.float32)
+    halves = [
+        jnp.einsum(
+            "tec,ecw->tw",
+            scale,
+            piece,
+            precision=lax.Precision.HIGHEST,
+            preferred_element_type=jnp.float32,
+        )
+        for piece in (wide[:, :capacity], wide[:, capacity:])
+    ]
+    mix = jnp.concatenate(halves, axis=1)
     return (branch.astype(jnp.bfloat16), mix.astype(jnp.bfloat16))
 
 

time: 132 us -> 132 us (level)
  local copies, waits for them, and re-layouts: 5.76 us -> 3.89 us
  matrix products: 16.6 us -> 18 us
    slice x1, local copies, waits for them, and re-layouts: 1.89 us -> 0.02 us  [on_device(): normed[:, :part]]
    dot_general x3, matrix products: 5.29 us -> 6.68 us  [the longest x2 4.3 us: on_device(): jnp.einsum('tec,ecw->tw', scale, piece, precision=lax.Precision.HIGHEST,...]
where the time goes in v11:
time: 132 us; the launch traced here: 131 us
  waiting for transfers between devices  67.3 us (51%)
  starting transfers between devices  19.3 us (15%)
  matrix products  18 us (14%)
  Pallas kernels  15.1 us (11%)
  other arithmetic  6.09 us (5%)
  local copies, waits for them, and re-layouts  3.89 us (3%)
  between operations  1.53 us (1%)
    all_to_all x1, waiting for transfers between devices, on_device(): lax.all_to_all(back, ('req', 'h'), split_axis=0, concat_axis=0, tiled=True)  34.7 us
    all_to_all x1, waiting for transfers between devices, on_device(): lax.all_to_all(outgoing.astype(jnp.bfloat16), ('req', 'h'), split_axis=0,...  31 us
    pallas_call x1, Pallas kernels, attention_core(): pl.pallas_call(attention_kernel, grid_spec=pltpu.PrefetchScalarGridSpec(n...  15.1 us
    all_to_all x1, starting transfers between devices, on_device(): lax.all_to_all(outgoing.astype(jnp.bfloat16), ('req', 'h'), split_axis=0,...  11.1 us
    all_to_all x1, starting transfers between devices, on_device(): lax.all_to_all(back, ('req', 'h'), split_axis=0, concat_axis=0, tiled=True)  4.94 us
    dot_general x2, matrix products, on_device(): jnp.einsum('tec,ecw->tw', scale, piece, precision=lax.Precision.HIGHEST,...  4.3 us
    dot_general x1, matrix products, attend(): mixed = jnp.dot(normed, qkv_weight, preferred_element_type=jnp.float32)  4.05 us
    ppermute x6, starting transfers between devices, swap(): lax.ppermute(piece, 'q', [(i, i ^ bit) for i in range(lax.axis_size('q'))])  3.2 us
  transfers between devices with their start and end apart: 8, of which 4 were waited for; matrix products, arithmetic and copies ran while one was open for 11% of the time, Pallas kernels for 12%

profile of v11, /device:TPU:0, one launch (start us, length us, event | category | flops | bytes accessed | tf_op | source)
XLA Modules:
  0.0 131.2 jit_solution(8314722639164033155)
XLA Ops:
  0.6 1.7 %collective-permute-start = (bf16[1024,256]{1,0:T(8,128)(2,1)}, bf16[1024,256]{1,0:T(8,128)(2,1)S(1)}, u32[]{:S(2)}, u32[]{:S(2)}) collective-permute-start(bf16[1024,256]{1,0:T(8,128)(2,1)} %bitcast.41), channel_id=1, source_target_pairs={{0,2},{1,3},{2,0},{3,1},{4,6},{5,7},{6,4},{7,5},{8,10},{9,11},{10,... | collective-permute-start | bytes 1572872 | tf_op jit(solution)/shard_map/ppermute | solution.py:154
  2.3 0.4 collective-permute-start.1
  3.4 1.1 fusion.36
  4.5 1.0 multiply_sine_fusion
  5.5 4.1 %fusion.43.q_ref.k_ref.v_ref = f32[128,2048]{1,0:T(8,128)} fusion(bf16[1024,2048]{1,0:T(8,128)(2,1)} %param.13, bf16[128,1024]{1,0:T(8,128)(2,1)} %param.12, f32[1024]{0:T(1024)} %param.15, f32[128]{0:T(128)S(1)} %add_rsqrt_fusion.1), kind=kOutput, calls=%fused_computation.52 | convolution fusion | flops 537395200 | bytes 5509632 | tf_op jit(solution)/shard_map/dot_general | solution.py:134
  9.5 15.1 %shard_map.131 = bf16[128,1024]{1,0:T(8,128)(2,1)} custom-call(s32[1]{0:T(128)} %copy.24.length_ref, f32[128,2048]{1,0:T(8,128)} %fusion.43.q_ref.k_ref.v_ref, f32[128,2048]{1,0:T(8,128)} %fusion.43.q_ref.k_ref.v_ref, f32[128,2048]{1,0:T(8,128)} %fusion.43.q_ref.k_ref.v_ref, f32[128,128]{1,0:T(8,128)} %get-tuple-element.19.cos_ref, ...), custom_call_target="tpu_custom_call" | custom-call | tf_op jit(solution)/shard_map/pallas_call | solution.py:109
  24.6 1.4 %fusion.66 = f32[128,1024]{1,0:T(8,128)S(1)} fusion(bf16[128,1024]{1,0:T(8,128)(2,1)} %shard_map.131, bf16[1024,1024]{1,0:T(8,128)(2,1)S(1)} %copy-done), kind=kOutput, calls=%fused_computation.83 | convolution fusion | flops 268435456 | bytes 2883584 | tf_op jit(solution)/shard_map/dot_general | solution.py:150
  26.1 0.1 convolution_convert_fusion.1
  26.3 0.2 fusion.35
  26.5 0.2 multiply_reduce_fusion
  26.7 0.8 multiply_convert_fusion
  27.5 2.4 %fusion.9 = bf16[32,80,512]{2,1,0:T(8,128)(2,1)} fusion(pred[128,32,40]{0,2,1:T(8,128)(4,1)S(1)} %fusion.35, bf16[128,512]{1,0:T(8,128)(2,1)S(1)} %get-tuple-element.17, bf16[128,512]{1,0:T(8,128)(2,1)S(1)} %get-tuple-element.16), kind=kOutput, calls=%fused_computation.14 | convolution fusion | flops 673579008 | bytes 3047424 | tf_op jit(solution)/shard_map/ter,tw->erw/dot_general | solution.py:204
  29.9 11.1 %all-to-all-start = ((bf16[32,80,512]{2,1,0:T(8,128)(2,1)}), bf16[32,80,512]{2,1,0:T(8,128)(2,1)}, u32[]{:S(2)}, u32[]{:S(2)}) async-start(bf16[32,80,512]{2,1,0:T(8,128)(2,1)} %fusion.9), calls=%async_computation | async-start | bytes 5242880 | tf_op jit(solution)/shard_map/all_to_all | solution.py:210
  41.1 0.5 collective-permute-start.3
  41.6 0.1 collective-permute-start.4
  41.7 0.4 collective-permute-start.5
  42.1 0.9 collective-permute-done.2
  43.0 0.7 collective-permute-done.3
  43.8 0.3 pad_maximum_fusion.1
  44.0 0.4 slice_bitcast_fusion.1
  44.4 1.2 copy_bitcast_fusion
  45.7 31.0 %all-to-all-done = bf16[32,80,512]{2,1,0:T(8,128)(2,1)} async-done(((bf16[32,80,512]{2,1,0:T(8,128)(2,1)}), bf16[32,80,512]{2,1,0:T(8,128)(2,1)}, u32[]{:S(2)}, u32[]{:S(2)}) %all-to-all-start) | async-done | bytes 2621472 | tf_op jit(solution)/shard_map/all_to_all | solution.py:210
  76.7 2.0 %fusion.64 = (bf16[32,40,512]{2,1,0:T(8,128)(2,1)S(1)}, bf16[32,40,512]{2,1,0:T(8,128)(2,1)S(1)}) fusion(bf16[32,80,512]{2,1,0:T(8,128)(2,1)} %all-to-all-done), kind=kLoop, calls=%fused_computation.81 | loop fusion | bytes 5242880 | tf_op jit(solution)/shard_map/slice | solution.py:213
  78.7 2.9 %fusion.1 = f32[32,40,1024]{2,1,0:T(8,128)S(1)} fusion(bf16[32,40,512]{2,1,0:T(8,128)(2,1)S(1)} %get-tuple-element.11, bf16[32,40,512]{2,1,0:T(8,128)(2,1)S(1)} %get-tuple-element.10, bf16[1024,512]{1,0:T(8,128)(2,1)S(1)} %get-tuple-element.20, bf16[1024,512]{1,0:T(8,128)(2,1)S(1)} %copy-done.2), kind=kOutput, calls=%fused_computation.2 | convolution fusion | flops 2693791744 | bytes 9961472 | tf_op jit(solution)/shard_map/scw,wh->sch/dot_general | solution.py:217
  81.6 2.7 %convolution_convert_fusion = bf16[32,40,1024]{2,1,0:T(8,128)(2,1)S(1)} fusion(f32[32,40,1024]{2,1,0:T(8,128)S(1)} %fusion.1, bf16[128,1024]{1,0:T(8,128)(2,1)} %collective-permute-done.5, bf16[128,1024]{1,0:T(8,128)(2,1)} %collective-permute-done.4, bf16[128,1024]{1,0:T(8,128)(2,1)S(1)} %copy-done.9, bf16[128,1024]{1,0:T(8,128)(2,1)S(1)} %bitcast.49), kind=kOutput, calls=%fused_computation.15 | convolution fusion | flops 1351614464 | bytes 8912896 | tf_op jit(solution)/shard_map/sch,hw->scw/dot_general | solution.py:225
  84.4 0.2 fusion.63
  84.6 1.9 %pad_maximum_fusion = bf16[32,80,512]{2,1,0:T(8,128)(2,1)} fusion(bf16[32,40,512]{2,1,0:T(8,128)(2,1)S(1)} %get-tuple-element.9, bf16[32,40,512]{2,1,0:T(8,128)(2,1)S(1)} %get-tuple-element.8), kind=kLoop, calls=%fused_computation.6 | loop fusion | flops 5242880 | bytes 5242880 | tf_op jit(solution)/shard_map/concatenate | solution.py:228
  86.5 4.9 %all-to-all-start.1 = ((bf16[32,80,512]{2,1,0:T(8,128)(2,1)}), bf16[32,80,512]{2,1,0:T(8,128)(2,1)}, u32[]{:S(2)}, u32[]{:S(2)}) async-start(bf16[32,80,512]{2,1,0:T(8,128)(2,1)} %pad_maximum_fusion), calls=%async_computation.1 | async-start | bytes 5242880 | tf_op jit(solution)/shard_map/all_to_all | solution.py:229
  91.5 34.7 %all-to-all-done.1 = bf16[32,80,512]{2,1,0:T(8,128)(2,1)} async-done(((bf16[32,80,512]{2,1,0:T(8,128)(2,1)}), bf16[32,80,512]{2,1,0:T(8,128)(2,1)}, u32[]{:S(2)}, u32[]{:S(2)}) %all-to-all-start.1) | async-done | bytes 2621472 | tf_op jit(solution)/shard_map/all_to_all | solution.py:229
  126.1 2.1 %fusion.21 = bf16[128,512]{1,0:T(8,128)(2,1)S(1)} fusion(bf16[32,80,512]{2,1,0:T(8,128)(2,1)} %all-to-all-done.1, f32[128,32]{0,1:T(8,128)S(1)} %select_reduce_fusion, s32[128,32]{0,1:T(8,128)S(1)} %convolution_convert_fusion.1, pred[128,32]{0,1:T(8,128)(4,1)S(1)} %fusion.49), kind=kOutput, calls=%fused_computation.22 | convolution fusion | flops 1007190016 | bytes 1478656 | tf_op jit(solution)/shard_map/tec,ecw->tw/dot_general | solution.py:233
  128.3 2.2 %fusion.24 = bf16[128,512]{1,0:T(8,128)(2,1)S(1)} fusion(bf16[32,80,512]{2,1,0:T(8,128)(2,1)} %all-to-all-done.1, f32[128,32]{0,1:T(8,128)S(1)} %select_reduce_fusion, s32[128,32]{0,1:T(8,128)S(1)} %convolution_convert_fusion.1, pred[128,32]{0,1:T(8,128)(4,1)S(1)} %fusion.49), kind=kOutput, calls=%fused_computation.23 | convolution fusion | flops 1007190016 | bytes 1478656 | tf_op jit(solution)/shard_map/tec,ecw->tw/dot_general | solution.py:233
  130.5 0.7 pad_maximum_fusion.2
  (32 shorter events, 0.3 us)
Async XLA Ops:
  0.6 24.0 %copy-start = (bf16[1024,1024]{1,0:T(8,128)(2,1)S(1)}, bf16[1024,1024]{1,0:T(8,128)(2,1)}, u32[]{:S(2)}) copy-start(bf16[1024,1024]{1,0:T(8,128)(2,1)} %param.14) | copy-start | bytes 6291460
  0.6 25.8 %collective-permute-start = (bf16[1024,256]{1,0:T(8,128)(2,1)}, bf16[1024,256]{1,0:T(8,128)(2,1)S(1)}, u32[]{:S(2)}, u32[]{:S(2)}) collective-permute-start(bf16[1024,256]{1,0:T(8,128)(2,1)} %bitcast.41), channel_id=1, source_target_pairs={{0,2},{1,3},{2,0},{3,1},{4,6},{5,7},{6,4},{7,5},{8,10},{9,11},{10,... | collective-permute-start | bytes 1572872 | tf_op jit(solution)/shard_map/ppermute | solution.py:154
  2.3 24.1 %collective-permute-start.1 = (bf16[128,1024]{1,0:T(8,128)(2,1)}, bf16[128,1024]{1,0:T(8,128)(2,1)S(1)}, u32[]{:S(2)}, u32[]{:S(2)}) collective-permute-start(bf16[128,1024]{1,0:T(8,128)(2,1)} %bitcast.47), channel_id=1, source_target_pairs={{0,2},{1,3},{2,0},{3,1},{4,6},{5,7},{6,4},{7,5},{8,10},{9,11},{10,... | collective-permute-start | bytes 786440 | tf_op jit(solution)/shard_map/ppermute | solution.py:154
  24.6 1.5 %copy-start.4 = (s32[128,8]{0,1:T(8,128)S(1)}, s32[128,8]{0,1:T(8,128)}, u32[]{:S(2)}) copy-start(s32[128,8]{0,1:T(8,128)} %param.20) | copy-start | bytes 12292
  24.6 1.8 %copy-start.1 = (bf16[128,1024]{1,0:T(8,128)(2,1)S(1)}, bf16[128,1024]{1,0:T(8,128)(2,1)}, u32[]{:S(2)}) copy-start(bf16[128,1024]{1,0:T(8,128)(2,1)} %param.12) | copy-start | bytes 786436
  24.6 2.0 %copy-start.5 = (f32[1024]{0:T(1024)S(1)}, f32[1024]{0:T(1024)}, u32[]{:S(2)}) copy-start(f32[1024]{0:T(1024)} %param.16) | copy-start | bytes 12292
  26.4 1.0 copy-start.8
  29.9 11.2 %copy-start.3 = (bf16[1,1024,256]{2,1,0:T(8,128)(2,1)S(1)}, bf16[1,1024,256]{2,1,0:T(8,128)(2,1)}, u32[]{:S(2)}) copy-start(bf16[1,1024,256]{2,1,0:T(8,128)(2,1)} %param.22) | copy-start | bytes 1572868
  29.9 11.8 %copy-start.7 = (bf16[1,128,1024]{2,1,0:T(8,128)(2,1)S(1)}, bf16[1,128,1024]{2,1,0:T(8,128)(2,1)}, u32[]{:S(2)}) copy-start(bf16[1,128,1024]{2,1,0:T(8,128)(2,1)} %param.23) | copy-start | bytes 786436
  29.9 46.8 %all-to-all-start = ((bf16[32,80,512]{2,1,0:T(8,128)(2,1)}), bf16[32,80,512]{2,1,0:T(8,128)(2,1)}, u32[]{:S(2)}, u32[]{:S(2)}) async-start(bf16[32,80,512]{2,1,0:T(8,128)(2,1)} %fusion.9), calls=%async_computation | async-start | bytes 5242880 | tf_op jit(solution)/shard_map/all_to_all | solution.py:210
  41.0 2.0 %collective-permute-start.2 = (bf16[1024,256]{1,0:T(8,128)(2,1)S(1)}, bf16[1024,256]{1,0:T(8,128)(2,1)S(1)}, u32[]{:S(2)}, u32[]{:S(2)}) collective-permute-start(bf16[1024,256]{1,0:T(8,128)(2,1)S(1)} %bitcast.42), channel_id=1, source_target_pairs={{0,1},{1,0},{2,3},{3,2},{4,5},{5,4},{6,7},{7,6},{8,9},{9,8},{10,11... | collective-permute-start | bytes 1572872 | tf_op jit(solution)/shard_map/ppermute | solution.py:154
  41.1 2.6 %collective-permute-start.3 = (bf16[1024,256]{1,0:T(8,128)(2,1)S(1)}, bf16[1024,256]{1,0:T(8,128)(2,1)S(1)}, u32[]{:S(2)}, u32[]{:S(2)}) collective-permute-start(bf16[1024,256]{1,0:T(8,128)(2,1)S(1)} %collective-permute-done), channel_id=1, source_target_pairs={{0,1},{1,0},{2,3},{3,2},{4,5},{5,4},{6,7},{7,6},{8,9},{9,8},{10,11... | collective-permute-start | bytes 1572872 | tf_op jit(solution)/shard_map/ppermute | solution.py:154
  41.6 40.0 %collective-permute-start.4 = (bf16[128,1024]{1,0:T(8,128)(2,1)S(1)}, bf16[128,1024]{1,0:T(8,128)(2,1)}, u32[]{:S(2)}, u32[]{:S(2)}) collective-permute-start(bf16[128,1024]{1,0:T(8,128)(2,1)S(1)} %bitcast.48), channel_id=1, source_target_pairs={{0,1},{1,0},{2,3},{3,2},{4,5},{5,4},{6,7},{7,6},{8,9},{9,8},{10,11... | collective-permute-start | bytes 786440 | tf_op jit(solution)/shard_map/ppermute | solution.py:154
  41.7 39.9 %collective-permute-start.5 = (bf16[128,1024]{1,0:T(8,128)(2,1)}, bf16[128,1024]{1,0:T(8,128)(2,1)}, u32[]{:S(2)}, u32[]{:S(2)}) collective-permute-start(bf16[128,1024]{1,0:T(8,128)(2,1)} %copy-done.8), channel_id=1, source_target_pairs={{0,1},{1,0},{2,3},{3,2},{4,5},{5,4},{6,7},{7,6},{8,9},{9,8},{10,11... | collective-permute-start | bytes 786440 | tf_op jit(solution)/shard_map/ppermute | solution.py:154
  76.7 2.0 %copy-start.2 = (bf16[1024,512]{1,0:T(8,128)(2,1)S(1)}, bf16[1024,512]{1,0:T(8,128)(2,1)}, u32[]{:S(2)}) copy-start(bf16[1024,512]{1,0:T(8,128)(2,1)} %get-tuple-element.21) | copy-start | bytes 3145732
  78.7 2.9 %copy-start.9 = (bf16[128,1024]{1,0:T(8,128)(2,1)S(1)}, bf16[128,1024]{1,0:T(8,128)(2,1)}, u32[]{:S(2)}) copy-start(bf16[128,1024]{1,0:T(8,128)(2,1)} %copy-done.8) | copy-start | bytes 786436
  86.5 4.9 %copy-start.6 = (f32[128,8]{0,1:T(8,128)S(1)}, f32[128,8]{0,1:T(8,128)}, u32[]{:S(2)}) copy-start(f32[128,8]{0,1:T(8,128)} %param.21) | copy-start | bytes 12292
  86.5 39.7 %all-to-all-start.1 = ((bf16[32,80,512]{2,1,0:T(8,128)(2,1)}), bf16[32,80,512]{2,1,0:T(8,128)(2,1)}, u32[]{:S(2)}, u32[]{:S(2)}) async-start(bf16[32,80,512]{2,1,0:T(8,128)(2,1)} %pad_maximum_fusion), calls=%async_computation.1 | async-start | bytes 5242880 | tf_op jit(solution)/shard_map/all_to_all | solution.py:229

commit v12 on v10

--- a/solution.py
+++ b/solution.py
@@ -90,11 +90,19 @@
         o = jnp.dot(w, vc, preferred_element_type=jnp.float32) + jnp.dot(
             wn, vn, preferred_element_type=jnp.float32
         )
-        outs.append(o.astype(jnp.bfloat16).astype(jnp.float32))
-    left = jnp.where(low, outs[0], pltpu.roll(outs[1], half, 1))
-    right = jnp.where(low, pltpu.roll(outs[2], half, 1), outs[3])
-    o_ref[:, :lanes] = left.astype(jnp.bfloat16)
-    o_ref[:, lanes:] = right.astype(jnp.bfloat16)
+        o = o.astype(jnp.bfloat16).astype(jnp.float32)
+        j = len(outs)
+        outs.append(j)
+        place = slice(0, lanes) if j < 2 else slice(lanes, 2 * lanes)
+        if j % 2 == 0:
+            o_ref[:, place] = o.astype(jnp.bfloat16)
+        else:
+            kept = o_ref[:, place].astype(jnp.float32)
+            if j == 1:
+                merged = jnp.where(low, kept, pltpu.roll(o, half, 1))
+            else:
+                merged = jnp.where(low, pltpu.roll(kept, half, 1), o)
+            o_ref[:, place] = merged.astype(jnp.bfloat16)
 
 
 def attention_core(length, mixed, cosine, sine, kc, vc, interpret=False):
@@ -202,8 +210,11 @@
     pick_lo = jnp.concatenate([pick, empty], axis=2).astype(jnp.bfloat16)
     pick_hi = jnp.concatenate([empty, pick], axis=2).astype(jnp.bfloat16)
     outgoing = jnp.einsum(
-        "ter,tw->erw", pick_lo, normed[:, :part], preferred_element_type=jnp.float32
-    ) + jnp.einsum("ter,tw->erw", pick_hi, normed[:, part:], preferred_element_type=jnp.float32)
+        "ter,tw->erw",
+        jnp.concatenate([pick_lo, pick_hi], axis=0),
+        jnp.concatenate([normed[:, :part], normed[:, part:]], axis=0),
+        preferred_element_type=jnp.float32,
+    )
     received = lax.all_to_all(
         outgoing.astype(jnp.bfloat16), ("req", "h"), split_axis=0, concat_axis=0, tiled=True
     )

time: 132 us -> 131 us (level)
    dot_general x2 -> x1, matrix products: 3.18 us -> 2.37 us  [on_device(): jnp.einsum('ter,tw->erw', jnp.concatenate([pick_lo, pick_hi], axis=0), jn...]
where the time goes in v12:
time: 131 us; the launch traced here: 130 us
  waiting for transfers between devices  67.3 us (51%)
  starting transfers between devices  19.3 us (15%)
  matrix products  15.8 us (12%)
  Pallas kernels  15.1 us (12%)
  local copies, waits for them, and re-layouts  5.79 us (4%)
  other arithmetic  5.37 us (4%)
  between operations  1.52 us (1%)
    all_to_all x1, waiting for transfers between devices, on_device(): lax.all_to_all(back, ('req', 'h'), split_axis=0, concat_axis=0, tiled=True)  34.7 us
    all_to_all x1, waiting for transfers between devices, on_device(): lax.all_to_all(outgoing.astype(jnp.bfloat16), ('req', 'h'), split_axis=0,...  31 us
    pallas_call x1, Pallas kernels, attention_core(): pl.pallas_call(attention_kernel, grid_spec=pltpu.PrefetchScalarGridSpec(n...  15.1 us
    all_to_all x1, starting transfers between devices, on_device(): lax.all_to_all(outgoing.astype(jnp.bfloat16), ('req', 'h'), split_axis=0,...  11.1 us
    all_to_all x1, starting transfers between devices, on_device(): lax.all_to_all(back, ('req', 'h'), split_axis=0, concat_axis=0, tiled=True)  4.95 us
    dot_general x1, matrix products, attend(): mixed = jnp.dot(normed, qkv_weight, preferred_element_type=jnp.float32)  4.05 us
    ppermute x6, starting transfers between devices, swap(): lax.ppermute(piece, 'q', [(i, i ^ bit) for i in range(lax.axis_size('q'))])  3.2 us
    dot_general x1, matrix products, on_device(): jnp.einsum('scw,wh->sch', joined, jnp.concatenate([gate_cols, up_cols], a...  2.91 us
  transfers between devices with their start and end apart: 8, of which 4 were waited for; matrix products, arithmetic and copies ran while one was open for 11% of the time, Pallas kernels for 12%

profile of v12, /device:TPU:0, one launch (start us, length us, event | category | flops | bytes accessed | tf_op | source)
XLA Modules:
  0.0 130.1 jit_solution(17209936121374986874)
XLA Ops:
  0.6 1.7 %collective-permute-start = (bf16[1024,256]{1,0:T(8,128)(2,1)}, bf16[1024,256]{1,0:T(8,128)(2,1)S(1)}, u32[]{:S(2)}, u32[]{:S(2)}) collective-permute-start(bf16[1024,256]{1,0:T(8,128)(2,1)} %bitcast.37), channel_id=1, source_target_pairs={{0,2},{1,3},{2,0},{3,1},{4,6},{5,7},{6,4},{7,5},{8,10},{9,11},{10,... | collective-permute-start | bytes 1572872 | tf_op jit(solution)/shard_map/ppermute | solution.py:162
  2.3 0.4 collective-permute-start.1
  3.4 1.1 fusion.29
  4.5 1.0 multiply_sine_fusion
  5.5 4.0 %fusion.34.q_ref.k_ref.v_ref = f32[128,2048]{1,0:T(8,128)} fusion(bf16[1024,2048]{1,0:T(8,128)(2,1)} %param.13, bf16[128,1024]{1,0:T(8,128)(2,1)} %param.12, f32[1024]{0:T(1024)} %param.15, f32[128]{0:T(128)S(1)} %add_rsqrt_fusion.1), kind=kOutput, calls=%fused_computation.47 | convolution fusion | flops 537395200 | bytes 5509632 | tf_op jit(solution)/shard_map/dot_general | solution.py:142
  9.5 15.1 %shard_map.131 = bf16[128,1024]{1,0:T(8,128)(2,1)} custom-call(s32[1]{0:T(128)} %copy.24.length_ref, f32[128,2048]{1,0:T(8,128)} %fusion.34.q_ref.k_ref.v_ref, f32[128,2048]{1,0:T(8,128)} %fusion.34.q_ref.k_ref.v_ref, f32[128,2048]{1,0:T(8,128)} %fusion.34.q_ref.k_ref.v_ref, f32[128,128]{1,0:T(8,128)} %get-tuple-element.21.cos_ref, ...), custom_call_target="tpu_custom_call" | custom-call | tf_op jit(solution)/shard_map/pallas_call | solution.py:117
  24.7 1.4 %fusion.57 = f32[128,1024]{1,0:T(8,128)S(1)} fusion(bf16[128,1024]{1,0:T(8,128)(2,1)} %shard_map.131, bf16[1024,1024]{1,0:T(8,128)(2,1)S(1)} %copy-done), kind=kOutput, calls=%fused_computation.78 | convolution fusion | flops 268435456 | bytes 2883584 | tf_op jit(solution)/shard_map/dot_general | solution.py:158
  26.2 0.1 convolution_convert_fusion.1
  26.3 0.2 fusion.28
  26.5 0.2 multiply_reduce_fusion
  26.7 0.8 multiply_convert_fusion
  27.5 2.4 %fusion.13 = bf16[32,80,512]{2,1,0:T(8,128)(2,1)} fusion(pred[128,32,40]{0,2,1:T(8,128)(4,1)S(1)} %fusion.28, bf16[128,512]{1,0:T(8,128)(2,1)S(1)} %get-tuple-element.19, bf16[128,512]{1,0:T(8,128)(2,1)S(1)} %get-tuple-element.18), kind=kOutput, calls=%fused_computation.18 | convolution fusion | flops 673579008 | bytes 3047424 | tf_op jit(solution)/shard_map/ter,tw->erw/dot_general | solution.py:212
  29.9 11.1 %all-to-all-start = ((bf16[32,80,512]{2,1,0:T(8,128)(2,1)}), bf16[32,80,512]{2,1,0:T(8,128)(2,1)}, u32[]{:S(2)}, u32[]{:S(2)}) async-start(bf16[32,80,512]{2,1,0:T(8,128)(2,1)} %fusion.13), calls=%async_computation | async-start | bytes 5242880 | tf_op jit(solution)/shard_map/all_to_all | solution.py:218
  41.0 0.1 collective-permute-start.2
  41.1 0.5 collective-permute-start.3
  41.6 0.1 collective-permute-start.4
  41.7 0.4 collective-permute-start.5
  42.2 0.9 collective-permute-done.2
  43.0 0.7 collective-permute-done.3
  43.8 0.3 pad_maximum_fusion.1
  44.1 0.4 slice_bitcast_fusion.1
  44.4 1.2 copy_bitcast_fusion
  45.7 31.0 %all-to-all-done = bf16[32,80,512]{2,1,0:T(8,128)(2,1)} async-done(((bf16[32,80,512]{2,1,0:T(8,128)(2,1)}), bf16[32,80,512]{2,1,0:T(8,128)(2,1)}, u32[]{:S(2)}, u32[]{:S(2)}) %all-to-all-start) | async-done | bytes 2621472 | tf_op jit(solution)/shard_map/all_to_all | solution.py:218
  76.7 2.0 %fusion.55 = (bf16[32,40,512]{2,1,0:T(8,128)(2,1)S(1)}, bf16[32,40,512]{2,1,0:T(8,128)(2,1)S(1)}) fusion(bf16[32,80,512]{2,1,0:T(8,128)(2,1)} %all-to-all-done), kind=kLoop, calls=%fused_computation.76 | loop fusion | bytes 5242880 | tf_op jit(solution)/shard_map/slice | solution.py:221
  78.7 2.9 %fusion.1 = f32[32,40,1024]{2,1,0:T(8,128)S(1)} fusion(bf16[32,40,512]{2,1,0:T(8,128)(2,1)S(1)} %get-tuple-element.13, bf16[32,40,512]{2,1,0:T(8,128)(2,1)S(1)} %get-tuple-element.12, bf16[1024,512]{1,0:T(8,128)(2,1)S(1)} %get-tuple-element.22, bf16[1024,512]{1,0:T(8,128)(2,1)S(1)} %copy-done.2), kind=kOutput, calls=%fused_computation.2 | convolution fusion | flops 2693791744 | bytes 9961472 | tf_op jit(solution)/shard_map/scw,wh->sch/dot_general | solution.py:225
  81.6 2.7 %convolution_convert_fusion = bf16[32,40,1024]{2,1,0:T(8,128)(2,1)S(1)} fusion(f32[32,40,1024]{2,1,0:T(8,128)S(1)} %fusion.1, bf16[128,1024]{1,0:T(8,128)(2,1)} %collective-permute-done.5, bf16[128,1024]{1,0:T(8,128)(2,1)} %collective-permute-done.4, bf16[128,1024]{1,0:T(8,128)(2,1)S(1)} %copy-done.9, bf16[128,1024]{1,0:T(8,128)(2,1)S(1)} %bitcast.45), kind=kOutput, calls=%fused_computation.19 | convolution fusion | flops 1351614464 | bytes 8912896 | tf_op jit(solution)/shard_map/sch,hw->scw/dot_general | solution.py:233
  84.4 0.2 fusion.54
  84.6 1.9 %pad_maximum_fusion = bf16[32,80,512]{2,1,0:T(8,128)(2,1)} fusion(bf16[32,40,512]{2,1,0:T(8,128)(2,1)S(1)} %get-tuple-element.11, bf16[32,40,512]{2,1,0:T(8,128)(2,1)S(1)} %get-tuple-element.10), kind=kLoop, calls=%fused_computation.6 | loop fusion | flops 5242880 | bytes 5242880 | tf_op jit(solution)/shard_map/concatenate | solution.py:236
  86.5 4.9 %all-to-all-start.1 = ((bf16[32,80,512]{2,1,0:T(8,128)(2,1)}), bf16[32,80,512]{2,1,0:T(8,128)(2,1)}, u32[]{:S(2)}, u32[]{:S(2)}) async-start(bf16[32,80,512]{2,1,0:T(8,128)(2,1)} %pad_maximum_fusion), calls=%async_computation.1 | async-start | bytes 5242880 | tf_op jit(solution)/shard_map/all_to_all | solution.py:237
  91.5 34.7 %all-to-all-done.1 = bf16[32,80,512]{2,1,0:T(8,128)(2,1)} async-done(((bf16[32,80,512]{2,1,0:T(8,128)(2,1)}), bf16[32,80,512]{2,1,0:T(8,128)(2,1)}, u32[]{:S(2)}, u32[]{:S(2)}) %all-to-all-start.1) | async-done | bytes 2621472 | tf_op jit(solution)/shard_map/all_to_all | solution.py:237
  126.1 1.9 %fusion.53 = (bf16[32,40,512]{2,1,0:T(8,128)(2,1)S(1)}, bf16[32,40,512]{2,1,0:T(8,128)(2,1)S(1)}) fusion(bf16[32,80,512]{2,1,0:T(8,128)(2,1)} %all-to-all-done.1), kind=kLoop, calls=%fused_computation.74 | loop fusion | bytes 5242880 | tf_op jit(solution)/shard_map/slice | solution.py:239
  128.0 2.1 %fusion.18 = bf16[128,1024]{1,0:T(8,128)(2,1)} fusion(bf16[32,40,512]{2,1,0:T(8,128)(2,1)S(1)} %get-tuple-element.9, bf16[32,40,512]{2,1,0:T(8,128)(2,1)S(1)} %get-tuple-element.8, f32[128,32]{0,1:T(8,128)S(1)} %select_reduce_fusion, s32[128,32]{0,1:T(8,128)S(1)} %convolution_convert_fusion.1, pred[128,32]{0,1:T(8,128)(4,1)S(1)} %fusion.40), kind=kOutput, calls=%fused_computation.21 | convolution fusion | flops 2019131392 | bytes 2920448 | tf_op jit(solution)/shard_map/tec,ecw->tw/dot_general | solution.py:240
  (31 shorter events, 0.2 us)
Async XLA Ops:
  0.6 24.0 %copy-start = (bf16[1024,1024]{1,0:T(8,128)(2,1)S(1)}, bf16[1024,1024]{1,0:T(8,128)(2,1)}, u32[]{:S(2)}) copy-start(bf16[1024,1024]{1,0:T(8,128)(2,1)} %param.14) | copy-start | bytes 6291460
  0.6 25.8 %collective-permute-start = (bf16[1024,256]{1,0:T(8,128)(2,1)}, bf16[1024,256]{1,0:T(8,128)(2,1)S(1)}, u32[]{:S(2)}, u32[]{:S(2)}) collective-permute-start(bf16[1024,256]{1,0:T(8,128)(2,1)} %bitcast.37), channel_id=1, source_target_pairs={{0,2},{1,3},{2,0},{3,1},{4,6},{5,7},{6,4},{7,5},{8,10},{9,11},{10,... | collective-permute-start | bytes 1572872 | tf_op jit(solution)/shard_map/ppermute | solution.py:162
  2.3 24.1 %collective-permute-start.1 = (bf16[128,1024]{1,0:T(8,128)(2,1)}, bf16[128,1024]{1,0:T(8,128)(2,1)S(1)}, u32[]{:S(2)}, u32[]{:S(2)}) collective-permute-start(bf16[128,1024]{1,0:T(8,128)(2,1)} %bitcast.43), channel_id=1, source_target_pairs={{0,2},{1,3},{2,0},{3,1},{4,6},{5,7},{6,4},{7,5},{8,10},{9,11},{10,... | collective-permute-start | bytes 786440 | tf_op jit(solution)/shard_map/ppermute | solution.py:162
  24.6 1.5 %copy-start.4 = (s32[128,8]{0,1:T(8,128)S(1)}, s32[128,8]{0,1:T(8,128)}, u32[]{:S(2)}) copy-start(s32[128,8]{0,1:T(8,128)} %param.20) | copy-start | bytes 12292
  24.6 1.9 %copy-start.1 = (bf16[128,1024]{1,0:T(8,128)(2,1)S(1)}, bf16[128,1024]{1,0:T(8,128)(2,1)}, u32[]{:S(2)}) copy-start(bf16[128,1024]{1,0:T(8,128)(2,1)} %param.12) | copy-start | bytes 786436
  24.7 2.0 %copy-start.5 = (f32[1024]{0:T(1024)S(1)}, f32[1024]{0:T(1024)}, u32[]{:S(2)}) copy-start(f32[1024]{0:T(1024)} %param.16) | copy-start | bytes 12292
  26.5 1.0 copy-start.8
  29.9 11.2 %copy-start.3 = (bf16[1,1024,256]{2,1,0:T(8,128)(2,1)S(1)}, bf16[1,1024,256]{2,1,0:T(8,128)(2,1)}, u32[]{:S(2)}) copy-start(bf16[1,1024,256]{2,1,0:T(8,128)(2,1)} %param.22) | copy-start | bytes 1572868
  29.9 11.8 %copy-start.7 = (bf16[1,128,1024]{2,1,0:T(8,128)(2,1)S(1)}, bf16[1,128,1024]{2,1,0:T(8,128)(2,1)}, u32[]{:S(2)}) copy-start(bf16[1,128,1024]{2,1,0:T(8,128)(2,1)} %param.23) | copy-start | bytes 786436
  29.9 46.8 %all-to-all-start = ((bf16[32,80,512]{2,1,0:T(8,128)(2,1)}), bf16[32,80,512]{2,1,0:T(8,128)(2,1)}, u32[]{:S(2)}, u32[]{:S(2)}) async-start(bf16[32,80,512]{2,1,0:T(8,128)(2,1)} %fusion.13), calls=%async_computation | async-start | bytes 5242880 | tf_op jit(solution)/shard_map/all_to_all | solution.py:218
  41.0 2.0 %collective-permute-start.2 = (bf16[1024,256]{1,0:T(8,128)(2,1)S(1)}, bf16[1024,256]{1,0:T(8,128)(2,1)S(1)}, u32[]{:S(2)}, u32[]{:S(2)}) collective-permute-start(bf16[1024,256]{1,0:T(8,128)(2,1)S(1)} %bitcast.38), channel_id=1, source_target_pairs={{0,1},{1,0},{2,3},{3,2},{4,5},{5,4},{6,7},{7,6},{8,9},{9,8},{10,11... | collective-permute-start | bytes 1572872 | tf_op jit(solution)/shard_map/ppermute | solution.py:162
  41.1 2.6 %collective-permute-start.3 = (bf16[1024,256]{1,0:T(8,128)(2,1)S(1)}, bf16[1024,256]{1,0:T(8,128)(2,1)S(1)}, u32[]{:S(2)}, u32[]{:S(2)}) collective-permute-start(bf16[1024,256]{1,0:T(8,128)(2,1)S(1)} %collective-permute-done), channel_id=1, source_target_pairs={{0,1},{1,0},{2,3},{3,2},{4,5},{5,4},{6,7},{7,6},{8,9},{9,8},{10,11... | collective-permute-start | bytes 1572872 | tf_op jit(solution)/shard_map/ppermute | solution.py:162
  41.6 40.0 %collective-permute-start.4 = (bf16[128,1024]{1,0:T(8,128)(2,1)S(1)}, bf16[128,1024]{1,0:T(8,128)(2,1)}, u32[]{:S(2)}, u32[]{:S(2)}) collective-permute-start(bf16[128,1024]{1,0:T(8,128)(2,1)S(1)} %bitcast.44), channel_id=1, source_target_pairs={{0,1},{1,0},{2,3},{3,2},{4,5},{5,4},{6,7},{7,6},{8,9},{9,8},{10,11... | collective-permute-start | bytes 786440 | tf_op jit(solution)/shard_map/ppermute | solution.py:162
  41.7 39.9 %collective-permute-start.5 = (bf16[128,1024]{1,0:T(8,128)(2,1)}, bf16[128,1024]{1,0:T(8,128)(2,1)}, u32[]{:S(2)}, u32[]{:S(2)}) collective-permute-start(bf16[128,1024]{1,0:T(8,128)(2,1)} %copy-done.8), channel_id=1, source_target_pairs={{0,1},{1,0},{2,3},{3,2},{4,5},{5,4},{6,7},{7,6},{8,9},{9,8},{10,11... | collective-permute-start | bytes 786440 | tf_op jit(solution)/shard_map/ppermute | solution.py:162
  76.7 2.0 %copy-start.2 = (bf16[1024,512]{1,0:T(8,128)(2,1)S(1)}, bf16[1024,512]{1,0:T(8,128)(2,1)}, u32[]{:S(2)}) copy-start(bf16[1024,512]{1,0:T(8,128)(2,1)} %get-tuple-element.23) | copy-start | bytes 3145732
  78.7 2.9 %copy-start.9 = (bf16[128,1024]{1,0:T(8,128)(2,1)S(1)}, bf16[128,1024]{1,0:T(8,128)(2,1)}, u32[]{:S(2)}) copy-start(bf16[128,1024]{1,0:T(8,128)(2,1)} %copy-done.8) | copy-start | bytes 786436
  86.5 5.0 %copy-start.6 = (f32[128,8]{0,1:T(8,128)S(1)}, f32[128,8]{0,1:T(8,128)}, u32[]{:S(2)}) copy-start(f32[128,8]{0,1:T(8,128)} %param.21) | copy-start | bytes 12292
  86.5 39.7 %all-to-all-start.1 = ((bf16[32,80,512]{2,1,0:T(8,128)(2,1)}), bf16[32,80,512]{2,1,0:T(8,128)(2,1)}, u32[]{:S(2)}, u32[]{:S(2)}) async-start(bf16[32,80,512]{2,1,0:T(8,128)(2,1)} %pad_maximum_fusion), calls=%async_computation.1 | async-start | bytes 5242880 | tf_op jit(solution)/shard_map/all_to_all | solution.py:237

commit v13 on v12

--- a/solution.py
+++ b/solution.py
@@ -39,7 +39,9 @@
     return jnp.where(lead, values * cosine - partner * sine, values * cosine + partner * sine)
 
 
-def attention_kernel(length_ref, q_ref, k_ref, v_ref, cos_ref, sin_ref, kc_ref, vc_ref, o_ref):
+def attention_kernel(
+    length_ref, q_ref, k_ref, v_ref, cos_ref, sin_ref, kc_ref, vc_ref, o_ref, s_ref, sn_ref, w_ref, wn_ref
+):
     length = length_ref[0]
     span, lanes = kc_ref.shape
     rows = k_ref.shape[0]
@@ -54,12 +56,6 @@
     vc = vc_ref[...]
     kn = turn(k_ref[...], cosine, sine, lead, quarter).astype(jnp.bfloat16)
     vn = v_ref[...].astype(jnp.bfloat16)
-    column = lax.broadcasted_iota(jnp.int32, (rows, span), 1)
-    cache_ok = column < length
-    new_col = lax.broadcasted_iota(jnp.int32, (rows, rows), 1)
-    new_row = lax.broadcasted_iota(jnp.int32, (rows, rows), 0)
-    new_ok = new_col <= new_row
-
     def scaled(values):
         rotated = turn(values, cosine, sine, lead, quarter).astype(jnp.bfloat16)
         return (rotated * 0.015625).astype(jnp.bfloat16).astype(jnp.float32)
@@ -73,22 +69,30 @@
         jnp.where(low, 0.0, second),
     )
     contract = (((1,), (1,)), ((), ()))
+    chunk = 32
     outs = []
     for q in queries:
         q = q.astype(jnp.bfloat16)
-        s = lax.dot_general(q, kc, contract, preferred_element_type=jnp.float32)
-        s = jnp.where(cache_ok, s, -1e30)
-        sn = lax.dot_general(q, kn, contract, preferred_element_type=jnp.float32)
-        sn = jnp.where(new_ok, sn, -1e30)
-        top = jnp.maximum(jnp.max(s, axis=1, keepdims=True), jnp.max(sn, axis=1, keepdims=True))
-        e = jnp.exp(s - top)
-        en = jnp.exp(sn - top)
-        total = jnp.sum(e, axis=1, keepdims=True) + jnp.sum(en, axis=1, keepdims=True)
-        inverse = 1.0 / total
-        w = (e * inverse).astype(jnp.bfloat16)
-        wn = (en * inverse).astype(jnp.bfloat16)
-        o = jnp.dot(w, vc, preferred_element_type=jnp.float32) + jnp.dot(
-            wn, vn, preferred_element_type=jnp.float32
+        s_ref[...] = lax.dot_general(q, kc, contract, preferred_element_type=jnp.float32)
+        sn_ref[...] = lax.dot_general(q, kn, contract, preferred_element_type=jnp.float32)
+        for i in range(rows // chunk):
+            at = slice(i * chunk, (i + 1) * chunk)
+            column = lax.broadcasted_iota(jnp.int32, (chunk, span), 1)
+            s = jnp.where(column < length, s_ref[at, :], -1e30)
+            new_col = lax.broadcasted_iota(jnp.int32, (chunk, rows), 1)
+            new_row = lax.broadcasted_iota(jnp.int32, (chunk, rows), 0) + i * chunk
+            sn = jnp.where(new_col <= new_row, sn_ref[at, :], -1e30)
+            top = jnp.maximum(
+                jnp.max(s, axis=1, keepdims=True), jnp.max(sn, axis=1, keepdims=True)
+            )
+            e = jnp.exp(s - top)
+            en = jnp.exp(sn - top)
+            total = jnp.sum(e, axis=1, keepdims=True) + jnp.sum(en, axis=1, keepdims=True)
+            inverse = 1.0 / total
+            w_ref[at, :] = (e * inverse).astype(jnp.bfloat16)
+            wn_ref[at, :] = (en * inverse).astype(jnp.bfloat16)
+        o = jnp.dot(w_ref[...], vc, preferred_element_type=jnp.float32) + jnp.dot(
+            wn_ref[...], vn, preferred_element_type=jnp.float32
         )
         o = o.astype(jnp.bfloat16).astype(jnp.float32)
         j = len(outs)
@@ -129,6 +133,12 @@
                 pl.BlockSpec((span, lanes), lambda p, n: (0, p)),
             ],
             out_specs=pl.BlockSpec((rows, qblock), lambda p, n: (0, p)),
+            scratch_shapes=[
+                pltpu.VMEM((rows, span), jnp.float32),
+                pltpu.VMEM((rows, rows), jnp.float32),
+                pltpu.VMEM((rows, span), jnp.bfloat16),
+                pltpu.VMEM((rows, rows), jnp.bfloat16),
+            ],
         ),
         out_shape=jax.ShapeDtypeStruct((rows, qwidth), jnp.bfloat16),
         interpret=interpret,

time: 131 us -> 131 us (level)
  no operation moved by 1% of the time
where the time goes in v13:
time: 131 us; the launch traced here: 130 us
  waiting for transfers between devices  67.3 us (51%)
  starting transfers between devices  19.3 us (15%)
  matrix products  15.8 us (12%)
  Pallas kernels  15.2 us (12%)
  local copies, waits for them, and re-layouts  5.79 us (4%)
  other arithmetic  5.37 us (4%)
  between operations  1.52 us (1%)
    all_to_all x1, waiting for transfers between devices, on_device(): lax.all_to_all(back, ('req', 'h'), split_axis=0, concat_axis=0, tiled=True)  34.6 us
    all_to_all x1, waiting for transfers between devices, on_device(): lax.all_to_all(outgoing.astype(jnp.bfloat16), ('req', 'h'), split_axis=0,...  31 us
    pallas_call x1, Pallas kernels, attention_core(): pl.pallas_call(attention_kernel, grid_spec=pltpu.PrefetchScalarGridSpec(n...  15.2 us
    all_to_all x1, starting transfers between devices, on_device(): lax.all_to_all(outgoing.astype(jnp.bfloat16), ('req', 'h'), split_axis=0,...  11.2 us
    all_to_all x1, starting transfers between devices, on_device(): lax.all_to_all(back, ('req', 'h'), split_axis=0, concat_axis=0, tiled=True)  4.95 us
    dot_general x1, matrix products, attend(): mixed = jnp.dot(normed, qkv_weight, preferred_element_type=jnp.float32)  4.05 us
    ppermute x6, starting transfers between devices, swap(): lax.ppermute(piece, 'q', [(i, i ^ bit) for i in range(lax.axis_size('q'))])  3.2 us
    dot_general x1, matrix products, on_device(): jnp.einsum('scw,wh->sch', joined, jnp.concatenate([gate_cols, up_cols], a...  2.91 us
  transfers between devices with their start and end apart: 8, of which 4 were waited for; matrix products, arithmetic and copies ran while one was open for 11% of the time, Pallas kernels for 12%

profile of v13, /device:TPU:0, one launch (start us, length us, event | category | flops | bytes accessed | tf_op | source)
XLA Modules:
  0.0 130.2 jit_solution(8926874786365031230)
XLA Ops:
  0.6 1.7 %collective-permute-start = (bf16[1024,256]{1,0:T(8,128)(2,1)}, bf16[1024,256]{1,0:T(8,128)(2,1)S(1)}, u32[]{:S(2)}, u32[]{:S(2)}) collective-permute-start(bf16[1024,256]{1,0:T(8,128)(2,1)} %bitcast.37), channel_id=1, source_target_pairs={{0,2},{1,3},{2,0},{3,1},{4,6},{5,7},{6,4},{7,5},{8,10},{9,11},{10,... | collective-permute-start | bytes 1572872 | tf_op jit(solution)/shard_map/ppermute | solution.py:172
  2.3 0.4 collective-permute-start.1
  3.4 1.1 fusion.29
  4.5 1.0 multiply_sine_fusion
  5.5 4.0 %fusion.34.q_ref.k_ref.v_ref = f32[128,2048]{1,0:T(8,128)} fusion(bf16[1024,2048]{1,0:T(8,128)(2,1)} %param.13, bf16[128,1024]{1,0:T(8,128)(2,1)} %param.12, f32[1024]{0:T(1024)} %param.15, f32[128]{0:T(128)S(1)} %add_rsqrt_fusion.1), kind=kOutput, calls=%fused_computation.47 | convolution fusion | flops 537395200 | bytes 5509632 | tf_op jit(solution)/shard_map/dot_general | solution.py:152
  9.5 15.2 %shard_map.131 = bf16[128,1024]{1,0:T(8,128)(2,1)} custom-call(s32[1]{0:T(128)} %copy.24.length_ref, f32[128,2048]{1,0:T(8,128)} %fusion.34.q_ref.k_ref.v_ref, f32[128,2048]{1,0:T(8,128)} %fusion.34.q_ref.k_ref.v_ref, f32[128,2048]{1,0:T(8,128)} %fusion.34.q_ref.k_ref.v_ref, f32[128,128]{1,0:T(8,128)} %get-tuple-element.21.cos_ref, ...), custom_call_target="tpu_custom_call" | custom-call | tf_op jit(solution)/shard_map/pallas_call | solution.py:121
  24.7 1.4 %fusion.57 = f32[128,1024]{1,0:T(8,128)S(1)} fusion(bf16[128,1024]{1,0:T(8,128)(2,1)} %shard_map.131, bf16[1024,1024]{1,0:T(8,128)(2,1)S(1)} %copy-done), kind=kOutput, calls=%fused_computation.78 | convolution fusion | flops 268435456 | bytes 2883584 | tf_op jit(solution)/shard_map/dot_general | solution.py:168
  26.2 0.1 convolution_convert_fusion.1
  26.4 0.2 fusion.28
  26.6 0.2 multiply_reduce_fusion
  26.8 0.8 multiply_convert_fusion
  27.6 2.4 %fusion.13 = bf16[32,80,512]{2,1,0:T(8,128)(2,1)} fusion(pred[128,32,40]{0,2,1:T(8,128)(4,1)S(1)} %fusion.28, bf16[128,512]{1,0:T(8,128)(2,1)S(1)} %get-tuple-element.19, bf16[128,512]{1,0:T(8,128)(2,1)S(1)} %get-tuple-element.18), kind=kOutput, calls=%fused_computation.18 | convolution fusion | flops 673579008 | bytes 3047424 | tf_op jit(solution)/shard_map/ter,tw->erw/dot_general | solution.py:222
  30.0 11.2 %all-to-all-start = ((bf16[32,80,512]{2,1,0:T(8,128)(2,1)}), bf16[32,80,512]{2,1,0:T(8,128)(2,1)}, u32[]{:S(2)}, u32[]{:S(2)}) async-start(bf16[32,80,512]{2,1,0:T(8,128)(2,1)} %fusion.13), calls=%async_computation | async-start | bytes 5242880 | tf_op jit(solution)/shard_map/all_to_all | solution.py:228
  41.1 0.1 collective-permute-start.2
  41.2 0.5 collective-permute-start.3
  41.7 0.1 collective-permute-start.4
  41.8 0.4 collective-permute-start.5
  42.2 0.9 collective-permute-done.2
  43.1 0.7 collective-permute-done.3
  43.9 0.3 pad_maximum_fusion.1
  44.1 0.4 slice_bitcast_fusion.1
  44.5 1.2 copy_bitcast_fusion
  45.8 31.0 %all-to-all-done = bf16[32,80,512]{2,1,0:T(8,128)(2,1)} async-done(((bf16[32,80,512]{2,1,0:T(8,128)(2,1)}), bf16[32,80,512]{2,1,0:T(8,128)(2,1)}, u32[]{:S(2)}, u32[]{:S(2)}) %all-to-all-start) | async-done | bytes 2621472 | tf_op jit(solution)/shard_map/all_to_all | solution.py:228
  76.7 2.0 %fusion.55 = (bf16[32,40,512]{2,1,0:T(8,128)(2,1)S(1)}, bf16[32,40,512]{2,1,0:T(8,128)(2,1)S(1)}) fusion(bf16[32,80,512]{2,1,0:T(8,128)(2,1)} %all-to-all-done), kind=kLoop, calls=%fused_computation.76 | loop fusion | bytes 5242880 | tf_op jit(solution)/shard_map/slice | solution.py:231
  78.8 2.9 %fusion.1 = f32[32,40,1024]{2,1,0:T(8,128)S(1)} fusion(bf16[32,40,512]{2,1,0:T(8,128)(2,1)S(1)} %get-tuple-element.13, bf16[32,40,512]{2,1,0:T(8,128)(2,1)S(1)} %get-tuple-element.12, bf16[1024,512]{1,0:T(8,128)(2,1)S(1)} %get-tuple-element.22, bf16[1024,512]{1,0:T(8,128)(2,1)S(1)} %copy-done.2), kind=kOutput, calls=%fused_computation.2 | convolution fusion | flops 2693791744 | bytes 9961472 | tf_op jit(solution)/shard_map/scw,wh->sch/dot_general | solution.py:235
  81.7 2.7 %convolution_convert_fusion = bf16[32,40,1024]{2,1,0:T(8,128)(2,1)S(1)} fusion(f32[32,40,1024]{2,1,0:T(8,128)S(1)} %fusion.1, bf16[128,1024]{1,0:T(8,128)(2,1)} %collective-permute-done.5, bf16[128,1024]{1,0:T(8,128)(2,1)} %collective-permute-done.4, bf16[128,1024]{1,0:T(8,128)(2,1)S(1)} %copy-done.9, bf16[128,1024]{1,0:T(8,128)(2,1)S(1)} %bitcast.45), kind=kOutput, calls=%fused_computation.19 | convolution fusion | flops 1351614464 | bytes 8912896 | tf_op jit(solution)/shard_map/sch,hw->scw/dot_general | solution.py:243
  84.5 0.2 fusion.54
  84.7 1.9 %pad_maximum_fusion = bf16[32,80,512]{2,1,0:T(8,128)(2,1)} fusion(bf16[32,40,512]{2,1,0:T(8,128)(2,1)S(1)} %get-tuple-element.11, bf16[32,40,512]{2,1,0:T(8,128)(2,1)S(1)} %get-tuple-element.10), kind=kLoop, calls=%fused_computation.6 | loop fusion | flops 5242880 | bytes 5242880 | tf_op jit(solution)/shard_map/concatenate | solution.py:246
  86.6 4.9 %all-to-all-start.1 = ((bf16[32,80,512]{2,1,0:T(8,128)(2,1)}), bf16[32,80,512]{2,1,0:T(8,128)(2,1)}, u32[]{:S(2)}, u32[]{:S(2)}) async-start(bf16[32,80,512]{2,1,0:T(8,128)(2,1)} %pad_maximum_fusion), calls=%async_computation.1 | async-start | bytes 5242880 | tf_op jit(solution)/shard_map/all_to_all | solution.py:247
  91.5 34.6 %all-to-all-done.1 = bf16[32,80,512]{2,1,0:T(8,128)(2,1)} async-done(((bf16[32,80,512]{2,1,0:T(8,128)(2,1)}), bf16[32,80,512]{2,1,0:T(8,128)(2,1)}, u32[]{:S(2)}, u32[]{:S(2)}) %all-to-all-start.1) | async-done | bytes 2621472 | tf_op jit(solution)/shard_map/all_to_all | solution.py:247
  126.2 1.9 %fusion.53 = (bf16[32,40,512]{2,1,0:T(8,128)(2,1)S(1)}, bf16[32,40,512]{2,1,0:T(8,128)(2,1)S(1)}) fusion(bf16[32,80,512]{2,1,0:T(8,128)(2,1)} %all-to-all-done.1), kind=kLoop, calls=%fused_computation.74 | loop fusion | bytes 5242880 | tf_op jit(solution)/shard_map/slice | solution.py:249
  128.1 2.1 %fusion.18 = bf16[128,1024]{1,0:T(8,128)(2,1)} fusion(bf16[32,40,512]{2,1,0:T(8,128)(2,1)S(1)} %get-tuple-element.9, bf16[32,40,512]{2,1,0:T(8,128)(2,1)S(1)} %get-tuple-element.8, f32[128,32]{0,1:T(8,128)S(1)} %select_reduce_fusion, s32[128,32]{0,1:T(8,128)S(1)} %convolution_convert_fusion.1, pred[128,32]{0,1:T(8,128)(4,1)S(1)} %fusion.40), kind=kOutput, calls=%fused_computation.21 | convolution fusion | flops 2019131392 | bytes 2920448 | tf_op jit(solution)/shard_map/tec,ecw->tw/dot_general | solution.py:250
  (31 shorter events, 0.2 us)
Async XLA Ops:
  0.6 24.1 %copy-start = (bf16[1024,1024]{1,0:T(8,128)(2,1)S(1)}, bf16[1024,1024]{1,0:T(8,128)(2,1)}, u32[]{:S(2)}) copy-start(bf16[1024,1024]{1,0:T(8,128)(2,1)} %param.14) | copy-start | bytes 6291460
  0.6 25.9 %collective-permute-start = (bf16[1024,256]{1,0:T(8,128)(2,1)}, bf16[1024,256]{1,0:T(8,128)(2,1)S(1)}, u32[]{:S(2)}, u32[]{:S(2)}) collective-permute-start(bf16[1024,256]{1,0:T(8,128)(2,1)} %bitcast.37), channel_id=1, source_target_pairs={{0,2},{1,3},{2,0},{3,1},{4,6},{5,7},{6,4},{7,5},{8,10},{9,11},{10,... | collective-permute-start | bytes 1572872 | tf_op jit(solution)/shard_map/ppermute | solution.py:172
  2.3 24.2 %collective-permute-start.1 = (bf16[128,1024]{1,0:T(8,128)(2,1)}, bf16[128,1024]{1,0:T(8,128)(2,1)S(1)}, u32[]{:S(2)}, u32[]{:S(2)}) collective-permute-start(bf16[128,1024]{1,0:T(8,128)(2,1)} %bitcast.43), channel_id=1, source_target_pairs={{0,2},{1,3},{2,0},{3,1},{4,6},{5,7},{6,4},{7,5},{8,10},{9,11},{10,... | collective-permute-start | bytes 786440 | tf_op jit(solution)/shard_map/ppermute | solution.py:172
  24.7 1.5 %copy-start.4 = (s32[128,8]{0,1:T(8,128)S(1)}, s32[128,8]{0,1:T(8,128)}, u32[]{:S(2)}) copy-start(s32[128,8]{0,1:T(8,128)} %param.20) | copy-start | bytes 12292
  24.7 1.8 %copy-start.1 = (bf16[128,1024]{1,0:T(8,128)(2,1)S(1)}, bf16[128,1024]{1,0:T(8,128)(2,1)}, u32[]{:S(2)}) copy-start(bf16[128,1024]{1,0:T(8,128)(2,1)} %param.12) | copy-start | bytes 786436
  24.7 2.0 %copy-start.5 = (f32[1024]{0:T(1024)S(1)}, f32[1024]{0:T(1024)}, u32[]{:S(2)}) copy-start(f32[1024]{0:T(1024)} %param.16) | copy-start | bytes 12292
  26.5 1.0 copy-start.8
  30.0 11.2 %copy-start.3 = (bf16[1,1024,256]{2,1,0:T(8,128)(2,1)S(1)}, bf16[1,1024,256]{2,1,0:T(8,128)(2,1)}, u32[]{:S(2)}) copy-start(bf16[1,1024,256]{2,1,0:T(8,128)(2,1)} %param.22) | copy-start | bytes 1572868
  30.0 11.8 %copy-start.7 = (bf16[1,128,1024]{2,1,0:T(8,128)(2,1)S(1)}, bf16[1,128,1024]{2,1,0:T(8,128)(2,1)}, u32[]{:S(2)}) copy-start(bf16[1,128,1024]{2,1,0:T(8,128)(2,1)} %param.23) | copy-start | bytes 786436
  30.0 46.8 %all-to-all-start = ((bf16[32,80,512]{2,1,0:T(8,128)(2,1)}), bf16[32,80,512]{2,1,0:T(8,128)(2,1)}, u32[]{:S(2)}, u32[]{:S(2)}) async-start(bf16[32,80,512]{2,1,0:T(8,128)(2,1)} %fusion.13), calls=%async_computation | async-start | bytes 5242880 | tf_op jit(solution)/shard_map/all_to_all | solution.py:228
  41.1 2.0 %collective-permute-start.2 = (bf16[1024,256]{1,0:T(8,128)(2,1)S(1)}, bf16[1024,256]{1,0:T(8,128)(2,1)S(1)}, u32[]{:S(2)}, u32[]{:S(2)}) collective-permute-start(bf16[1024,256]{1,0:T(8,128)(2,1)S(1)} %bitcast.38), channel_id=1, source_target_pairs={{0,1},{1,0},{2,3},{3,2},{4,5},{5,4},{6,7},{7,6},{8,9},{9,8},{10,11... | collective-permute-start | bytes 1572872 | tf_op jit(solution)/shard_map/ppermute | solution.py:172
  41.2 2.6 %collective-permute-start.3 = (bf16[1024,256]{1,0:T(8,128)(2,1)S(1)}, bf16[1024,256]{1,0:T(8,128)(2,1)S(1)}, u32[]{:S(2)}, u32[]{:S(2)}) collective-permute-start(bf16[1024,256]{1,0:T(8,128)(2,1)S(1)} %collective-permute-done), channel_id=1, source_target_pairs={{0,1},{1,0},{2,3},{3,2},{4,5},{5,4},{6,7},{7,6},{8,9},{9,8},{10,11... | collective-permute-start | bytes 1572872 | tf_op jit(solution)/shard_map/ppermute | solution.py:172
  41.7 40.0 %collective-permute-start.4 = (bf16[128,1024]{1,0:T(8,128)(2,1)S(1)}, bf16[128,1024]{1,0:T(8,128)(2,1)}, u32[]{:S(2)}, u32[]{:S(2)}) collective-permute-start(bf16[128,1024]{1,0:T(8,128)(2,1)S(1)} %bitcast.44), channel_id=1, source_target_pairs={{0,1},{1,0},{2,3},{3,2},{4,5},{5,4},{6,7},{7,6},{8,9},{9,8},{10,11... | collective-permute-start | bytes 786440 | tf_op jit(solution)/shard_map/ppermute | solution.py:172
  41.8 39.9 %collective-permute-start.5 = (bf16[128,1024]{1,0:T(8,128)(2,1)}, bf16[128,1024]{1,0:T(8,128)(2,1)}, u32[]{:S(2)}, u32[]{:S(2)}) collective-permute-start(bf16[128,1024]{1,0:T(8,128)(2,1)} %copy-done.8), channel_id=1, source_target_pairs={{0,1},{1,0},{2,3},{3,2},{4,5},{5,4},{6,7},{7,6},{8,9},{9,8},{10,11... | collective-permute-start | bytes 786440 | tf_op jit(solution)/shard_map/ppermute | solution.py:172
  76.7 2.0 %copy-start.2 = (bf16[1024,512]{1,0:T(8,128)(2,1)S(1)}, bf16[1024,512]{1,0:T(8,128)(2,1)}, u32[]{:S(2)}) copy-start(bf16[1024,512]{1,0:T(8,128)(2,1)} %get-tuple-element.23) | copy-start | bytes 3145732
  78.8 2.9 %copy-start.9 = (bf16[128,1024]{1,0:T(8,128)(2,1)S(1)}, bf16[128,1024]{1,0:T(8,128)(2,1)}, u32[]{:S(2)}) copy-start(bf16[128,1024]{1,0:T(8,128)(2,1)} %copy-done.8) | copy-start | bytes 786436
  86.6 5.0 %copy-start.6 = (f32[128,8]{0,1:T(8,128)S(1)}, f32[128,8]{0,1:T(8,128)}, u32[]{:S(2)}) copy-start(f32[128,8]{0,1:T(8,128)} %param.21) | copy-start | bytes 12292
  86.6 39.6 %all-to-all-start.1 = ((bf16[32,80,512]{2,1,0:T(8,128)(2,1)}), bf16[32,80,512]{2,1,0:T(8,128)(2,1)}, u32[]{:S(2)}, u32[]{:S(2)}) async-start(bf16[32,80,512]{2,1,0:T(8,128)(2,1)} %pad_maximum_fusion), calls=%async_computation.1 | async-start | bytes 5242880 | tf_op jit(solution)/shard_map/all_to_all | solution.py:247

commit v14 on v12

--- a/solution.py
+++ b/solution.py
@@ -233,14 +233,12 @@
     produced = jnp.einsum(
         "sch,hw->scw", hidden, down_all, preferred_element_type=jnp.float32
     ).astype(jnp.bfloat16)
-    back = jnp.concatenate([produced[..., :part], produced[..., part:]], axis=1)
-    results = lax.all_to_all(back, ("req", "h"), split_axis=0, concat_axis=0, tiled=True)
+    results = lax.all_to_all(produced, ("req", "h"), split_axis=0, concat_axis=0, tiled=True)
     scale = jnp.where(pick, weight[:, :, None], 0.0)
-    output = jnp.concatenate([results[:, :capacity], results[:, capacity:]], axis=2)
     mix = jnp.einsum(
         "tec,ecw->tw",
         scale,
-        output.astype(jnp.float32),
+        results.astype(jnp.float32),
         precision=lax.Precision.HIGHEST,
         preferred_element_type=jnp.float32,
     )

time: 131 us -> 130 us (level)
  matrix products: 15.8 us -> 19 us
  local copies, waits for them, and re-layouts: 5.79 us -> 3.69 us
  other arithmetic: 5.37 us -> 3.49 us
    slice x2 -> x0, local copies, waits for them, and re-layouts: 2.1 us -> none  [the longest x1 1.89 us: on_device(): results[:, :capacity]]
    concatenate x1 -> x0, other arithmetic: 1.87 us -> none  [on_device(): back = jnp.concatenate([produced[..., :part], produced[..., part:]], axis=1)]
    dot_general x1, matrix products: 2.11 us -> 3.82 us  [on_device(): jnp.einsum('tec,ecw->tw', scale, results.astype(jnp.float32), precision=l...]
    dot_general x1, matrix products: 2.74 us -> 4.25 us  [on_device(): jnp.einsum('sch,hw->scw', hidden, down_all, preferred_element_type=jnp.fl...]
where the time goes in v14:
time: 130 us; the launch traced here: 129 us
  waiting for transfers between devices  67.3 us (52%)
  starting transfers between devices  19.3 us (15%)
  matrix products  19 us (15%)
  Pallas kernels  15.1 us (12%)
  local copies, waits for them, and re-layouts  3.69 us (3%)
  other arithmetic  3.49 us (3%)
  between operations  1.51 us (1%)
    all_to_all x1, waiting for transfers between devices, on_device(): lax.all_to_all(produced, ('req', 'h'), split_axis=0, concat_axis=0, tiled...  34.7 us
    all_to_all x1, waiting for transfers between devices, on_device(): lax.all_to_all(outgoing.astype(jnp.bfloat16), ('req', 'h'), split_axis=0,...  31 us
    pallas_call x1, Pallas kernels, attention_core(): pl.pallas_call(attention_kernel, grid_spec=pltpu.PrefetchScalarGridSpec(n...  15.1 us
    all_to_all x1, starting transfers between devices, on_device(): lax.all_to_all(outgoing.astype(jnp.bfloat16), ('req', 'h'), split_axis=0,...  11.1 us
    all_to_all x1, starting transfers between devices, on_device(): lax.all_to_all(produced, ('req', 'h'), split_axis=0, concat_axis=0, tiled...  4.93 us
    dot_general x1, matrix products, on_device(): jnp.einsum('sch,hw->scw', hidden, down_all, preferred_element_type=jnp.fl...  4.25 us
    dot_general x1, matrix products, attend(): mixed = jnp.dot(normed, qkv_weight, preferred_element_type=jnp.float32)  4.05 us
    dot_general x1, matrix products, on_device(): jnp.einsum('tec,ecw->tw', scale, results.astype(jnp.float32), precision=l...  3.82 us
  transfers between devices with their start and end apart: 8, of which 4 were waited for; matrix products, arithmetic and copies ran while one was open for 11% of the time, Pallas kernels for 12%

profile of v14, /device:TPU:0, one launch (start us, length us, event | category | flops | bytes accessed | tf_op | source)
XLA Modules:
  0.0 129.4 jit_solution(16029416647490668197)
XLA Ops:
  0.6 0.0 copy-start
  0.6 1.7 %collective-permute-start = (bf16[1024,256]{1,0:T(8,128)(2,1)}, bf16[1024,256]{1,0:T(8,128)(2,1)S(1)}, u32[]{:S(2)}, u32[]{:S(2)}) collective-permute-start(bf16[1024,256]{1,0:T(8,128)(2,1)} %bitcast.38), channel_id=1, source_target_pairs={{0,2},{1,3},{2,0},{3,1},{4,6},{5,7},{6,4},{7,5},{8,10},{9,11},{10,... | collective-permute-start | bytes 1572872 | tf_op jit(solution)/shard_map/ppermute | solution.py:162
  2.3 0.4 collective-permute-start.1
  3.4 1.1 fusion.20
  4.5 1.0 multiply_sine_fusion
  5.5 4.1 %fusion.25.q_ref.k_ref.v_ref = f32[128,2048]{1,0:T(8,128)} fusion(bf16[1024,2048]{1,0:T(8,128)(2,1)} %param.13, bf16[128,1024]{1,0:T(8,128)(2,1)} %param.12, f32[1024]{0:T(1024)} %param.15, f32[128]{0:T(128)S(1)} %add_rsqrt_fusion.1), kind=kOutput, calls=%fused_computation.42 | convolution fusion | flops 537395200 | bytes 5509632 | tf_op jit(solution)/shard_map/dot_general | solution.py:142
  9.5 15.1 %shard_map.131 = bf16[128,1024]{1,0:T(8,128)(2,1)} custom-call(s32[1]{0:T(128)} %copy.24.length_ref, f32[128,2048]{1,0:T(8,128)} %fusion.25.q_ref.k_ref.v_ref, f32[128,2048]{1,0:T(8,128)} %fusion.25.q_ref.k_ref.v_ref, f32[128,2048]{1,0:T(8,128)} %fusion.25.q_ref.k_ref.v_ref, f32[128,128]{1,0:T(8,128)} %get-tuple-element.17.cos_ref, ...), custom_call_target="tpu_custom_call" | custom-call | tf_op jit(solution)/shard_map/pallas_call | solution.py:117
  24.7 1.4 %fusion.45 = f32[128,1024]{1,0:T(8,128)S(1)} fusion(bf16[128,1024]{1,0:T(8,128)(2,1)} %shard_map.131, bf16[1024,1024]{1,0:T(8,128)(2,1)S(1)} %copy-done), kind=kOutput, calls=%fused_computation.70 | convolution fusion | flops 268435456 | bytes 2883584 | tf_op jit(solution)/shard_map/dot_general | solution.py:158
  26.2 0.1 convolution_convert_fusion.1
  26.3 0.2 fusion.19
  26.5 0.0 copy-start.8
  26.5 0.2 multiply_reduce_fusion
  26.7 0.8 multiply_convert_fusion
  27.5 2.4 %fusion.9 = bf16[32,80,512]{2,1,0:T(8,128)(2,1)} fusion(pred[128,32,40]{0,2,1:T(8,128)(4,1)S(1)} %fusion.19, bf16[128,512]{1,0:T(8,128)(2,1)S(1)} %get-tuple-element.15, bf16[128,512]{1,0:T(8,128)(2,1)S(1)} %get-tuple-element.14), kind=kOutput, calls=%fused_computation.13 | convolution fusion | flops 673579008 | bytes 3047424 | tf_op jit(solution)/shard_map/ter,tw->erw/dot_general | solution.py:212
  29.9 11.1 %all-to-all-start = ((bf16[32,80,512]{2,1,0:T(8,128)(2,1)}), bf16[32,80,512]{2,1,0:T(8,128)(2,1)}, u32[]{:S(2)}, u32[]{:S(2)}) async-start(bf16[32,80,512]{2,1,0:T(8,128)(2,1)} %fusion.9), calls=%async_computation | async-start | bytes 5242880 | tf_op jit(solution)/shard_map/all_to_all | solution.py:218
  41.1 0.1 collective-permute-start.2
  41.1 0.5 collective-permute-start.3
  41.6 0.1 collective-permute-start.4
  41.7 0.4 collective-permute-start.5
  42.2 0.9 collective-permute-done.2
  43.0 0.7 collective-permute-done.3
  43.8 0.3 pad_maximum_fusion
  44.1 0.4 slice_bitcast_fusion.1
  44.4 1.2 copy_bitcast_fusion
  45.7 31.0 %all-to-all-done = bf16[32,80,512]{2,1,0:T(8,128)(2,1)} async-done(((bf16[32,80,512]{2,1,0:T(8,128)(2,1)}), bf16[32,80,512]{2,1,0:T(8,128)(2,1)}, u32[]{:S(2)}, u32[]{:S(2)}) %all-to-all-start) | async-done | bytes 2621472 | tf_op jit(solution)/shard_map/all_to_all | solution.py:218
  76.7 2.0 %fusion.43 = (bf16[32,40,512]{2,1,0:T(8,128)(2,1)S(1)}, bf16[32,40,512]{2,1,0:T(8,128)(2,1)S(1)}) fusion(bf16[32,80,512]{2,1,0:T(8,128)(2,1)} %all-to-all-done), kind=kLoop, calls=%fused_computation.68 | loop fusion | bytes 5242880 | tf_op jit(solution)/shard_map/slice | solution.py:221
  78.7 0.0 copy-done.2
  78.7 2.9 %fusion.1 = f32[32,40,1024]{2,1,0:T(8,128)S(1)} fusion(bf16[32,40,512]{2,1,0:T(8,128)(2,1)S(1)} %get-tuple-element.9, bf16[32,40,512]{2,1,0:T(8,128)(2,1)S(1)} %get-tuple-element.8, bf16[1024,512]{1,0:T(8,128)(2,1)S(1)} %get-tuple-element.18, bf16[1024,512]{1,0:T(8,128)(2,1)S(1)} %copy-done.2), kind=kOutput, calls=%fused_computation.2 | convolution fusion | flops 2693791744 | bytes 9961472 | tf_op jit(solution)/shard_map/scw,wh->sch/dot_general | solution.py:225
  81.6 4.3 %convolution_convert_fusion = bf16[32,40,1024]{2,1,0:T(8,128)(2,1)} fusion(f32[32,40,1024]{2,1,0:T(8,128)S(1)} %fusion.1, bf16[128,1024]{1,0:T(8,128)(2,1)} %collective-permute-done.5, bf16[128,1024]{1,0:T(8,128)(2,1)} %collective-permute-done.4, bf16[128,1024]{1,0:T(8,128)(2,1)S(1)} %copy-done.9, bf16[128,1024]{1,0:T(8,128)(2,1)S(1)} %bitcast.46), kind=kOutput, calls=%fused_computation.14 | convolution fusion | flops 1351614464 | bytes 8912896 | tf_op jit(solution)/shard_map/sch,hw->scw/dot_general | solution.py:233
  85.9 4.9 %all-to-all-start.1 = ((bf16[32,40,1024]{2,1,0:T(8,128)(2,1)}), bf16[32,40,1024]{2,1,0:T(8,128)(2,1)}, u32[]{:S(2)}, u32[]{:S(2)}) async-start(bf16[32,40,1024]{2,1,0:T(8,128)(2,1)} %convolution_convert_fusion), calls=%async_computation.1 | async-start | bytes 5242880 | tf_op jit(solution)/shard_map/all_to_all | solution.py:236
  90.9 34.7 %all-to-all-done.1 = bf16[32,40,1024]{2,1,0:T(8,128)(2,1)} async-done(((bf16[32,40,1024]{2,1,0:T(8,128)(2,1)}), bf16[32,40,1024]{2,1,0:T(8,128)(2,1)}, u32[]{:S(2)}, u32[]{:S(2)}) %all-to-all-start.1) | async-done | bytes 2621472 | tf_op jit(solution)/shard_map/all_to_all | solution.py:236
  125.6 3.8 %fusion.11 = bf16[128,1024]{1,0:T(8,128)(2,1)} fusion(bf16[32,40,1024]{2,1,0:T(8,128)(2,1)} %all-to-all-done.1, f32[128,32]{0,1:T(8,128)S(1)} %select_reduce_fusion, s32[128,32]{0,1:T(8,128)S(1)} %convolution_convert_fusion.1, pred[128,32]{0,1:T(8,128)(4,1)S(1)} %fusion.31), kind=kOutput, calls=%fused_computation.16 | convolution fusion | flops 2013888512 | bytes 2920448 | tf_op jit(solution)/shard_map/tec,ecw->tw/dot_general | solution.py:238
  (28 shorter events, 0.1 us)
Async XLA Ops:
  0.6 24.0 %copy-start = (bf16[1024,1024]{1,0:T(8,128)(2,1)S(1)}, bf16[1024,1024]{1,0:T(8,128)(2,1)}, u32[]{:S(2)}) copy-start(bf16[1024,1024]{1,0:T(8,128)(2,1)} %param.14) | copy-start | bytes 6291460
  0.6 25.8 %collective-permute-start = (bf16[1024,256]{1,0:T(8,128)(2,1)}, bf16[1024,256]{1,0:T(8,128)(2,1)S(1)}, u32[]{:S(2)}, u32[]{:S(2)}) collective-permute-start(bf16[1024,256]{1,0:T(8,128)(2,1)} %bitcast.38), channel_id=1, source_target_pairs={{0,2},{1,3},{2,0},{3,1},{4,6},{5,7},{6,4},{7,5},{8,10},{9,11},{10,... | collective-permute-start | bytes 1572872 | tf_op jit(solution)/shard_map/ppermute | solution.py:162
  2.3 24.1 %collective-permute-start.1 = (bf16[128,1024]{1,0:T(8,128)(2,1)}, bf16[128,1024]{1,0:T(8,128)(2,1)S(1)}, u32[]{:S(2)}, u32[]{:S(2)}) collective-permute-start(bf16[128,1024]{1,0:T(8,128)(2,1)} %bitcast.44), channel_id=1, source_target_pairs={{0,2},{1,3},{2,0},{3,1},{4,6},{5,7},{6,4},{7,5},{8,10},{9,11},{10,... | collective-permute-start | bytes 786440 | tf_op jit(solution)/shard_map/ppermute | solution.py:162
  24.6 1.5 %copy-start.4 = (s32[128,8]{0,1:T(8,128)S(1)}, s32[128,8]{0,1:T(8,128)}, u32[]{:S(2)}) copy-start(s32[128,8]{0,1:T(8,128)} %param.20) | copy-start | bytes 12292
  24.6 1.9 %copy-start.1 = (bf16[128,1024]{1,0:T(8,128)(2,1)S(1)}, bf16[128,1024]{1,0:T(8,128)(2,1)}, u32[]{:S(2)}) copy-start(bf16[128,1024]{1,0:T(8,128)(2,1)} %param.12) | copy-start | bytes 786436
  24.7 2.0 %copy-start.5 = (f32[1024]{0:T(1024)S(1)}, f32[1024]{0:T(1024)}, u32[]{:S(2)}) copy-start(f32[1024]{0:T(1024)} %param.16) | copy-start | bytes 12292
  26.5 1.0 copy-start.8
  29.9 11.2 %copy-start.3 = (bf16[1,1024,256]{2,1,0:T(8,128)(2,1)S(1)}, bf16[1,1024,256]{2,1,0:T(8,128)(2,1)}, u32[]{:S(2)}) copy-start(bf16[1,1024,256]{2,1,0:T(8,128)(2,1)} %param.22) | copy-start | bytes 1572868
  29.9 11.8 %copy-start.7 = (bf16[1,128,1024]{2,1,0:T(8,128)(2,1)S(1)}, bf16[1,128,1024]{2,1,0:T(8,128)(2,1)}, u32[]{:S(2)}) copy-start(bf16[1,128,1024]{2,1,0:T(8,128)(2,1)} %param.23) | copy-start | bytes 786436
  29.9 46.8 %all-to-all-start = ((bf16[32,80,512]{2,1,0:T(8,128)(2,1)}), bf16[32,80,512]{2,1,0:T(8,128)(2,1)}, u32[]{:S(2)}, u32[]{:S(2)}) async-start(bf16[32,80,512]{2,1,0:T(8,128)(2,1)} %fusion.9), calls=%async_computation | async-start | bytes 5242880 | tf_op jit(solution)/shard_map/all_to_all | solution.py:218
  41.1 2.0 %collective-permute-start.2 = (bf16[1024,256]{1,0:T(8,128)(2,1)S(1)}, bf16[1024,256]{1,0:T(8,128)(2,1)S(1)}, u32[]{:S(2)}, u32[]{:S(2)}) collective-permute-start(bf16[1024,256]{1,0:T(8,128)(2,1)S(1)} %bitcast.39), channel_id=1, source_target_pairs={{0,1},{1,0},{2,3},{3,2},{4,5},{5,4},{6,7},{7,6},{8,9},{9,8},{10,11... | collective-permute-start | bytes 1572872 | tf_op jit(solution)/shard_map/ppermute | solution.py:162
  41.1 2.6 %collective-permute-start.3 = (bf16[1024,256]{1,0:T(8,128)(2,1)S(1)}, bf16[1024,256]{1,0:T(8,128)(2,1)S(1)}, u32[]{:S(2)}, u32[]{:S(2)}) collective-permute-start(bf16[1024,256]{1,0:T(8,128)(2,1)S(1)} %collective-permute-done), channel_id=1, source_target_pairs={{0,1},{1,0},{2,3},{3,2},{4,5},{5,4},{6,7},{7,6},{8,9},{9,8},{10,11... | collective-permute-start | bytes 1572872 | tf_op jit(solution)/shard_map/ppermute | solution.py:162
  41.6 40.0 %collective-permute-start.4 = (bf16[128,1024]{1,0:T(8,128)(2,1)S(1)}, bf16[128,1024]{1,0:T(8,128)(2,1)}, u32[]{:S(2)}, u32[]{:S(2)}) collective-permute-start(bf16[128,1024]{1,0:T(8,128)(2,1)S(1)} %bitcast.45), channel_id=1, source_target_pairs={{0,1},{1,0},{2,3},{3,2},{4,5},{5,4},{6,7},{7,6},{8,9},{9,8},{10,11... | collective-permute-start | bytes 786440 | tf_op jit(solution)/shard_map/ppermute | solution.py:162
  41.7 39.9 %collective-permute-start.5 = (bf16[128,1024]{1,0:T(8,128)(2,1)}, bf16[128,1024]{1,0:T(8,128)(2,1)}, u32[]{:S(2)}, u32[]{:S(2)}) collective-permute-start(bf16[128,1024]{1,0:T(8,128)(2,1)} %copy-done.8), channel_id=1, source_target_pairs={{0,1},{1,0},{2,3},{3,2},{4,5},{5,4},{6,7},{7,6},{8,9},{9,8},{10,11... | collective-permute-start | bytes 786440 | tf_op jit(solution)/shard_map/ppermute | solution.py:162
  76.7 2.0 %copy-start.2 = (bf16[1024,512]{1,0:T(8,128)(2,1)S(1)}, bf16[1024,512]{1,0:T(8,128)(2,1)}, u32[]{:S(2)}) copy-start(bf16[1024,512]{1,0:T(8,128)(2,1)} %get-tuple-element.19) | copy-start | bytes 3145732
  78.7 2.9 %copy-start.9 = (bf16[128,1024]{1,0:T(8,128)(2,1)S(1)}, bf16[128,1024]{1,0:T(8,128)(2,1)}, u32[]{:S(2)}) copy-start(bf16[128,1024]{1,0:T(8,128)(2,1)} %copy-done.8) | copy-start | bytes 786436
  85.9 4.9 %copy-start.6 = (f32[128,8]{0,1:T(8,128)S(1)}, f32[128,8]{0,1:T(8,128)}, u32[]{:S(2)}) copy-start(f32[128,8]{0,1:T(8,128)} %param.21) | copy-start | bytes 12292
  85.9 39.7 %all-to-all-start.1 = ((bf16[32,40,1024]{2,1,0:T(8,128)(2,1)}), bf16[32,40,1024]{2,1,0:T(8,128)(2,1)}, u32[]{:S(2)}, u32[]{:S(2)}) async-start(bf16[32,40,1024]{2,1,0:T(8,128)(2,1)} %convolution_convert_fusion), calls=%async_computation.1 | async-start | bytes 5242880 | tf_op jit(solution)/shard_map/all_to_all | solution.py:236

commit v15 on v14

--- a/solution.py
+++ b/solution.py
@@ -193,7 +193,6 @@
     carried = tokens.astype(jnp.float32) + 0.22 * branch
     normed = rms_scale(carried, norm_expert).astype(jnp.bfloat16)
     rows, width = normed.shape
-    part = width // 2
     capacity = CAPACITY
     hits = routes[:, :, None] == jnp.arange(EXPERTS, dtype=jnp.int32)[None, None, :]
     marks = jnp.any(hits, axis=1)
@@ -206,19 +205,10 @@
     pick = marks[:, :, None] & (
         slot[:, :, None] == jnp.arange(capacity, dtype=jnp.int32)[None, None, :]
     )
-    empty = jnp.zeros_like(pick)
-    pick_lo = jnp.concatenate([pick, empty], axis=2).astype(jnp.bfloat16)
-    pick_hi = jnp.concatenate([empty, pick], axis=2).astype(jnp.bfloat16)
     outgoing = jnp.einsum(
-        "ter,tw->erw",
-        jnp.concatenate([pick_lo, pick_hi], axis=0),
-        jnp.concatenate([normed[:, :part], normed[:, part:]], axis=0),
-        preferred_element_type=jnp.float32,
-    )
-    received = lax.all_to_all(
-        outgoing.astype(jnp.bfloat16), ("req", "h"), split_axis=0, concat_axis=0, tiled=True
-    )
-    joined = jnp.concatenate([received[:, :capacity], received[:, capacity:]], axis=2)
+        "tec,tw->ecw", pick.astype(jnp.bfloat16), normed, preferred_element_type=jnp.float32
+    ).astype(jnp.bfloat16)
+    joined = lax.all_to_all(outgoing, ("req", "h"), split_axis=0, concat_axis=0, tiled=True)
     pieces = gate_up_all.reshape(gate_up_all.shape[0], slices, 2 * width_dev)
     gate_cols = pieces[..., :width_dev].reshape(gate_up_all.shape[0], slices * width_dev)
     up_cols = pieces[..., width_dev:].reshape(gate_up_all.shape[0], slices * width_dev)

time: 130 us -> 130 us (level)
  matrix products: 19 us -> 21.1 us
  local copies, waits for them, and re-layouts: 3.69 us -> 1.64 us
    dot_general x1, matrix products: 2.91 us -> 4.96 us  [on_device(): jnp.einsum('scw,wh->sch', joined, jnp.concatenate([gate_cols, up_cols], a...]
    slice x2 -> x0, local copies, waits for them, and re-layouts: 2.01 us -> none  [the longest x1 1.99 us: on_device(): received[:, :capacity]]
where the time goes in v15:
time: 130 us; the launch traced here: 129 us
  waiting for transfers between devices  67.3 us (52%)
  matrix products  21.1 us (16%)
  starting transfers between devices  19.3 us (15%)
  Pallas kernels  15.1 us (12%)
  other arithmetic  3.18 us (2%)
  local copies, waits for them, and re-layouts  1.64 us (1%)
  between operations  1.45 us (1%)
    all_to_all x1, waiting for transfers between devices, on_device(): lax.all_to_all(produced, ('req', 'h'), split_axis=0, concat_axis=0, tiled...  34.6 us
    all_to_all x1, waiting for transfers between devices, on_device(): lax.all_to_all(outgoing, ('req', 'h'), split_axis=0, concat_axis=0, tiled...  31 us
    pallas_call x1, Pallas kernels, attention_core(): pl.pallas_call(attention_kernel, grid_spec=pltpu.PrefetchScalarGridSpec(n...  15.1 us
    all_to_all x1, starting transfers between devices, on_device(): lax.all_to_all(outgoing, ('req', 'h'), split_axis=0, concat_axis=0, tiled...  11.2 us
    dot_general x1, matrix products, on_device(): jnp.einsum('scw,wh->sch', joined, jnp.concatenate([gate_cols, up_cols], a...  4.96 us
    all_to_all x1, starting transfers between devices, on_device(): lax.all_to_all(produced, ('req', 'h'), split_axis=0, concat_axis=0, tiled...  4.94 us
    dot_general x1, matrix products, on_device(): jnp.einsum('sch,hw->scw', hidden, down_all, preferred_element_type=jnp.fl...  4.27 us
    dot_general x1, matrix products, attend(): mixed = jnp.dot(normed, qkv_weight, preferred_element_type=jnp.float32)  4.05 us
  transfers between devices with their start and end apart: 8, of which 4 were waited for; matrix products, arithmetic and copies ran while one was open for 11% of the time, Pallas kernels for 12%

profile of v15, /device:TPU:0, one launch (start us, length us, event | category | flops | bytes accessed | tf_op | source)
XLA Modules:
  0.0 129.0 jit_solution(1967070144813534002)
XLA Ops:
  0.6 0.0 copy-start
  0.6 1.7 %collective-permute-start = (bf16[1024,256]{1,0:T(8,128)(2,1)}, bf16[1024,256]{1,0:T(8,128)(2,1)S(1)}, u32[]{:S(2)}, u32[]{:S(2)}) collective-permute-start(bf16[1024,256]{1,0:T(8,128)(2,1)} %bitcast.39), channel_id=1, source_target_pairs={{0,2},{1,3},{2,0},{3,1},{4,6},{5,7},{6,4},{7,5},{8,10},{9,11},{10,... | collective-permute-start | bytes 1572872 | tf_op jit(solution)/shard_map/ppermute | solution.py:162
  2.3 0.4 collective-permute-start.1
  3.4 1.1 fusion.16
  4.5 1.0 multiply_sine_fusion
  5.5 4.1 %fusion.27.q_ref.k_ref.v_ref = f32[128,2048]{1,0:T(8,128)} fusion(bf16[1024,2048]{1,0:T(8,128)(2,1)} %param.13, bf16[128,1024]{1,0:T(8,128)(2,1)} %param.12, f32[1024]{0:T(1024)} %param.15, f32[128]{0:T(128)S(1)} %add_rsqrt_fusion.1), kind=kOutput, calls=%fused_computation.41 | convolution fusion | flops 537395200 | bytes 5509632 | tf_op jit(solution)/shard_map/dot_general | solution.py:142
  9.6 15.1 %shard_map.131 = bf16[128,1024]{1,0:T(8,128)(2,1)} custom-call(s32[1]{0:T(128)} %copy.24.length_ref, f32[128,2048]{1,0:T(8,128)} %fusion.27.q_ref.k_ref.v_ref, f32[128,2048]{1,0:T(8,128)} %fusion.27.q_ref.k_ref.v_ref, f32[128,2048]{1,0:T(8,128)} %fusion.27.q_ref.k_ref.v_ref, f32[128,128]{1,0:T(8,128)} %get-tuple-element.13.cos_ref, ...), custom_call_target="tpu_custom_call" | custom-call | tf_op jit(solution)/shard_map/pallas_call | solution.py:117
  24.7 0.1 convolution_convert_fusion.2
  24.8 1.4 %fusion.44 = f32[128,1024]{1,0:T(8,128)S(1)} fusion(bf16[128,1024]{1,0:T(8,128)(2,1)} %shard_map.131, bf16[1024,1024]{1,0:T(8,128)(2,1)S(1)} %copy-done), kind=kOutput, calls=%fused_computation.66 | convolution fusion | flops 268435456 | bytes 2883584 | tf_op jit(solution)/shard_map/dot_general | solution.py:158
  26.2 0.0 collective-permute-done.1
  26.2 0.0 copy-start.7
  26.3 0.0 collective-permute-done
  26.3 0.8 multiply_reduce_fusion
  27.1 2.4 %convolution_convert_fusion.1 = bf16[32,40,1024]{2,1,0:T(8,128)(2,1)} fusion(s32[128,32]{0,1:T(8,128)S(1)} %convolution_convert_fusion.2, pred[128,32]{0,1:T(8,128)(4,1)S(1)} %fusion.34, f32[128,1024]{1,0:T(8,128)S(1)} %fusion.44, bf16[128,1024]{1,0:T(8,128)(2,1)S(1)} %copy-done.1, f32[1024]{0:T(1024)S(1)} %copy-done.4, f32[128]{0:T(128)S(1)} %add_rsqrt_fusion), kind=kOutput, calls=%fused_computation.8 | convolution fusion | flops 337969152 | bytes 3432960 | tf_op jit(solution)/shard_map/tec,tw->ecw/dot_general | solution.py:208
  29.5 11.2 %all-to-all-start = ((bf16[32,40,1024]{2,1,0:T(8,128)(2,1)}), bf16[32,40,1024]{2,1,0:T(8,128)(2,1)}, u32[]{:S(2)}, u32[]{:S(2)}) async-start(bf16[32,40,1024]{2,1,0:T(8,128)(2,1)} %convolution_convert_fusion.1), calls=%async_computation | async-start | bytes 5242880 | tf_op jit(solution)/shard_map/all_to_all | solution.py:211
  40.7 0.1 collective-permute-start.2
  40.8 0.5 collective-permute-start.3
  41.3 0.1 collective-permute-start.4
  41.4 0.4 collective-permute-start.5
  41.8 0.9 collective-permute-done.2
  42.7 0.7 collective-permute-done.3
  43.5 0.3 pad_maximum_fusion
  43.7 0.4 slice_bitcast_fusion.1
  44.1 1.2 copy_bitcast_fusion
  45.3 31.0 %all-to-all-done = bf16[32,40,1024]{2,1,0:T(8,128)(2,1)} async-done(((bf16[32,40,1024]{2,1,0:T(8,128)(2,1)}), bf16[32,40,1024]{2,1,0:T(8,128)(2,1)}, u32[]{:S(2)}, u32[]{:S(2)}) %all-to-all-start) | async-done | bytes 2621472 | tf_op jit(solution)/shard_map/all_to_all | solution.py:211
  76.3 5.0 %fusion.1 = f32[32,40,1024]{2,1,0:T(8,128)S(1)} fusion(bf16[32,40,1024]{2,1,0:T(8,128)(2,1)} %all-to-all-done, bf16[1024,512]{1,0:T(8,128)(2,1)S(1)} %get-tuple-element.14, bf16[1024,512]{1,0:T(8,128)(2,1)} %get-tuple-element.15), kind=kOutput, calls=%fused_computation.4 | convolution fusion | flops 2688548864 | bytes 9961472 | tf_op jit(solution)/shard_map/scw,wh->sch/dot_general | solution.py:215
  81.3 0.0 collective-permute-done.4
  81.3 0.0 collective-permute-done.5
  81.3 4.3 %convolution_convert_fusion = bf16[32,40,1024]{2,1,0:T(8,128)(2,1)} fusion(f32[32,40,1024]{2,1,0:T(8,128)S(1)} %fusion.1, bf16[128,1024]{1,0:T(8,128)(2,1)} %collective-permute-done.5, bf16[128,1024]{1,0:T(8,128)(2,1)} %collective-permute-done.4, bf16[128,1024]{1,0:T(8,128)(2,1)S(1)} %copy-done.8, bf16[128,1024]{1,0:T(8,128)(2,1)S(1)} %bitcast.47), kind=kOutput, calls=%fused_computation.7 | convolution fusion | flops 1351614464 | bytes 8912896 | tf_op jit(solution)/shard_map/sch,hw->scw/dot_general | solution.py:223
  85.6 4.9 %all-to-all-start.1 = ((bf16[32,40,1024]{2,1,0:T(8,128)(2,1)}), bf16[32,40,1024]{2,1,0:T(8,128)(2,1)}, u32[]{:S(2)}, u32[]{:S(2)}) async-start(bf16[32,40,1024]{2,1,0:T(8,128)(2,1)} %convolution_convert_fusion), calls=%async_computation.1 | async-start | bytes 5242880 | tf_op jit(solution)/shard_map/all_to_all | solution.py:226
  90.6 34.6 %all-to-all-done.1 = bf16[32,40,1024]{2,1,0:T(8,128)(2,1)} async-done(((bf16[32,40,1024]{2,1,0:T(8,128)(2,1)}), bf16[32,40,1024]{2,1,0:T(8,128)(2,1)}, u32[]{:S(2)}, u32[]{:S(2)}) %all-to-all-start.1) | async-done | bytes 2621472 | tf_op jit(solution)/shard_map/all_to_all | solution.py:226
  125.2 3.8 %fusion.5 = bf16[128,1024]{1,0:T(8,128)(2,1)} fusion(bf16[32,40,1024]{2,1,0:T(8,128)(2,1)} %all-to-all-done.1, f32[128,32]{0,1:T(8,128)S(1)} %select_reduce_fusion, s32[128,32]{0,1:T(8,128)S(1)} %convolution_convert_fusion.2, pred[128,32]{0,1:T(8,128)(4,1)S(1)} %fusion.34), kind=kOutput, calls=%fused_computation.10 | convolution fusion | flops 2013888512 | bytes 2920448 | tf_op jit(solution)/shard_map/tec,ecw->tw/dot_general | solution.py:228
  (22 shorter events, 0.1 us)
Async XLA Ops:
  0.6 24.2 %copy-start = (bf16[1024,1024]{1,0:T(8,128)(2,1)S(1)}, bf16[1024,1024]{1,0:T(8,128)(2,1)}, u32[]{:S(2)}) copy-start(bf16[1024,1024]{1,0:T(8,128)(2,1)} %param.14) | copy-start | bytes 6291460
  0.6 25.6 %collective-permute-start = (bf16[1024,256]{1,0:T(8,128)(2,1)}, bf16[1024,256]{1,0:T(8,128)(2,1)S(1)}, u32[]{:S(2)}, u32[]{:S(2)}) collective-permute-start(bf16[1024,256]{1,0:T(8,128)(2,1)} %bitcast.39), channel_id=1, source_target_pairs={{0,2},{1,3},{2,0},{3,1},{4,6},{5,7},{6,4},{7,5},{8,10},{9,11},{10,... | collective-permute-start | bytes 1572872 | tf_op jit(solution)/shard_map/ppermute | solution.py:162
  2.3 23.9 %collective-permute-start.1 = (bf16[128,1024]{1,0:T(8,128)(2,1)}, bf16[128,1024]{1,0:T(8,128)(2,1)S(1)}, u32[]{:S(2)}, u32[]{:S(2)}) collective-permute-start(bf16[128,1024]{1,0:T(8,128)(2,1)} %bitcast.45), channel_id=1, source_target_pairs={{0,2},{1,3},{2,0},{3,1},{4,6},{5,7},{6,4},{7,5},{8,10},{9,11},{10,... | collective-permute-start | bytes 786440 | tf_op jit(solution)/shard_map/ppermute | solution.py:162
  5.5 4.1 %copy-start.3 = (s32[128,8]{0,1:T(8,128)S(1)}, s32[128,8]{0,1:T(8,128)}, u32[]{:S(2)}) copy-start(s32[128,8]{0,1:T(8,128)} %param.20) | copy-start | bytes 12292
  24.7 1.6 %copy-start.1 = (bf16[128,1024]{1,0:T(8,128)(2,1)S(1)}, bf16[128,1024]{1,0:T(8,128)(2,1)}, u32[]{:S(2)}) copy-start(bf16[128,1024]{1,0:T(8,128)(2,1)} %param.12) | copy-start | bytes 786436
  24.7 2.4 %copy-start.4 = (f32[1024]{0:T(1024)S(1)}, f32[1024]{0:T(1024)}, u32[]{:S(2)}) copy-start(f32[1024]{0:T(1024)} %param.16) | copy-start | bytes 12292
  26.2 0.8 copy-start.7
  29.5 11.2 %copy-start.2 = (bf16[1,1024,256]{2,1,0:T(8,128)(2,1)S(1)}, bf16[1,1024,256]{2,1,0:T(8,128)(2,1)}, u32[]{:S(2)}) copy-start(bf16[1,1024,256]{2,1,0:T(8,128)(2,1)} %param.22) | copy-start | bytes 1572868
  29.5 11.8 %copy-start.6 = (bf16[1,128,1024]{2,1,0:T(8,128)(2,1)S(1)}, bf16[1,128,1024]{2,1,0:T(8,128)(2,1)}, u32[]{:S(2)}) copy-start(bf16[1,128,1024]{2,1,0:T(8,128)(2,1)} %param.23) | copy-start | bytes 786436
  29.5 46.8 %all-to-all-start = ((bf16[32,40,1024]{2,1,0:T(8,128)(2,1)}), bf16[32,40,1024]{2,1,0:T(8,128)(2,1)}, u32[]{:S(2)}, u32[]{:S(2)}) async-start(bf16[32,40,1024]{2,1,0:T(8,128)(2,1)} %convolution_convert_fusion.1), calls=%async_computation | async-start | bytes 5242880 | tf_op jit(solution)/shard_map/all_to_all | solution.py:211
  40.7 2.0 %collective-permute-start.2 = (bf16[1024,256]{1,0:T(8,128)(2,1)S(1)}, bf16[1024,256]{1,0:T(8,128)(2,1)S(1)}, u32[]{:S(2)}, u32[]{:S(2)}) collective-permute-start(bf16[1024,256]{1,0:T(8,128)(2,1)S(1)} %bitcast.40), channel_id=1, source_target_pairs={{0,1},{1,0},{2,3},{3,2},{4,5},{5,4},{6,7},{7,6},{8,9},{9,8},{10,11... | collective-permute-start | bytes 1572872 | tf_op jit(solution)/shard_map/ppermute | solution.py:162
  40.8 2.6 %collective-permute-start.3 = (bf16[1024,256]{1,0:T(8,128)(2,1)S(1)}, bf16[1024,256]{1,0:T(8,128)(2,1)S(1)}, u32[]{:S(2)}, u32[]{:S(2)}) collective-permute-start(bf16[1024,256]{1,0:T(8,128)(2,1)S(1)} %collective-permute-done), channel_id=1, source_target_pairs={{0,1},{1,0},{2,3},{3,2},{4,5},{5,4},{6,7},{7,6},{8,9},{9,8},{10,11... | collective-permute-start | bytes 1572872 | tf_op jit(solution)/shard_map/ppermute | solution.py:162
  41.3 40.0 %collective-permute-start.4 = (bf16[128,1024]{1,0:T(8,128)(2,1)S(1)}, bf16[128,1024]{1,0:T(8,128)(2,1)}, u32[]{:S(2)}, u32[]{:S(2)}) collective-permute-start(bf16[128,1024]{1,0:T(8,128)(2,1)S(1)} %bitcast.46), channel_id=1, source_target_pairs={{0,1},{1,0},{2,3},{3,2},{4,5},{5,4},{6,7},{7,6},{8,9},{9,8},{10,11... | collective-permute-start | bytes 786440 | tf_op jit(solution)/shard_map/ppermute | solution.py:162
  41.4 39.9 %collective-permute-start.5 = (bf16[128,1024]{1,0:T(8,128)(2,1)}, bf16[128,1024]{1,0:T(8,128)(2,1)}, u32[]{:S(2)}, u32[]{:S(2)}) collective-permute-start(bf16[128,1024]{1,0:T(8,128)(2,1)} %copy-done.7), channel_id=1, source_target_pairs={{0,1},{1,0},{2,3},{3,2},{4,5},{5,4},{6,7},{7,6},{8,9},{9,8},{10,11... | collective-permute-start | bytes 786440 | tf_op jit(solution)/shard_map/ppermute | solution.py:162
  76.3 5.0 %copy-start.8 = (bf16[128,1024]{1,0:T(8,128)(2,1)S(1)}, bf16[128,1024]{1,0:T(8,128)(2,1)}, u32[]{:S(2)}) copy-start(bf16[128,1024]{1,0:T(8,128)(2,1)} %copy-done.7) | copy-start | bytes 786436
  85.6 5.0 %copy-start.5 = (f32[128,8]{0,1:T(8,128)S(1)}, f32[128,8]{0,1:T(8,128)}, u32[]{:S(2)}) copy-start(f32[128,8]{0,1:T(8,128)} %param.21) | copy-start | bytes 12292
  85.6 39.6 %all-to-all-start.1 = ((bf16[32,40,1024]{2,1,0:T(8,128)(2,1)}), bf16[32,40,1024]{2,1,0:T(8,128)(2,1)}, u32[]{:S(2)}, u32[]{:S(2)}) async-start(bf16[32,40,1024]{2,1,0:T(8,128)(2,1)} %convolution_convert_fusion), calls=%async_computation.1 | async-start | bytes 5242880 | tf_op jit(solution)/shard_map/all_to_all | solution.py:226

commit v16 on v15

--- a/solution.py
+++ b/solution.py
@@ -229,7 +229,7 @@
         "tec,ecw->tw",
         scale,
         results.astype(jnp.float32),
-        precision=lax.Precision.HIGHEST,
+        precision=lax.Precision.HIGH,
         preferred_element_type=jnp.float32,
     )
     return (branch.astype(jnp.bfloat16), mix.astype(jnp.bfloat16))

time: 130 us -> 130 us (level)
  no operation moved by 1% of the time
where the time goes in v16:
time: 130 us; the launch traced here: 129 us
  waiting for transfers between devices  67.3 us (52%)
  matrix products  20.7 us (16%)
  starting transfers between devices  19.3 us (15%)
  Pallas kernels  15.1 us (12%)
  other arithmetic  3.18 us (2%)
  local copies, waits for them, and re-layouts  1.64 us (1%)
  between operations  1.45 us (1%)
    all_to_all x1, waiting for transfers between devices, on_device(): lax.all_to_all(produced, ('req', 'h'), split_axis=0, concat_axis=0, tiled...  34.6 us
    all_to_all x1, waiting for transfers between devices, on_device(): lax.all_to_all(outgoing, ('req', 'h'), split_axis=0, concat_axis=0, tiled...  31 us
    pallas_call x1, Pallas kernels, attention_core(): pl.pallas_call(attention_kernel, grid_spec=pltpu.PrefetchScalarGridSpec(n...  15.1 us
    all_to_all x1, starting transfers between devices, on_device(): lax.all_to_all(outgoing, ('req', 'h'), split_axis=0, concat_axis=0, tiled...  11.2 us
    dot_general x1, matrix products, on_device(): jnp.einsum('scw,wh->sch', joined, jnp.concatenate([gate_cols, up_cols], a...  4.96 us
    all_to_all x1, starting transfers between devices, on_device(): lax.all_to_all(produced, ('req', 'h'), split_axis=0, concat_axis=0, tiled...  4.94 us
    dot_general x1, matrix products, on_device(): jnp.einsum('sch,hw->scw', hidden, down_all, preferred_element_type=jnp.fl...  4.27 us
    dot_general x1, matrix products, attend(): mixed = jnp.dot(normed, qkv_weight, preferred_element_type=jnp.float32)  4.05 us
  transfers between devices with their start and end apart: 8, of which 4 were waited for; matrix products, arithmetic and copies ran while one was open for 11% of the time, Pallas kernels for 12%

profile of v16, /device:TPU:0, one launch (start us, length us, event | category | flops | bytes accessed | tf_op | source)
XLA Modules:
  0.0 128.6 jit_solution(4604419883399977675)
XLA Ops:
  0.6 0.0 copy-start
  0.6 1.7 %collective-permute-start = (bf16[1024,256]{1,0:T(8,128)(2,1)}, bf16[1024,256]{1,0:T(8,128)(2,1)S(1)}, u32[]{:S(2)}, u32[]{:S(2)}) collective-permute-start(bf16[1024,256]{1,0:T(8,128)(2,1)} %bitcast.39), channel_id=1, source_target_pairs={{0,2},{1,3},{2,0},{3,1},{4,6},{5,7},{6,4},{7,5},{8,10},{9,11},{10,... | collective-permute-start | bytes 1572872 | tf_op jit(solution)/shard_map/ppermute | solution.py:162
  2.3 0.4 collective-permute-start.1
  3.4 1.1 fusion.16
  4.5 1.0 multiply_sine_fusion
  5.5 4.1 %fusion.27.q_ref.k_ref.v_ref = f32[128,2048]{1,0:T(8,128)} fusion(bf16[1024,2048]{1,0:T(8,128)(2,1)} %param.13, bf16[128,1024]{1,0:T(8,128)(2,1)} %param.12, f32[1024]{0:T(1024)} %param.15, f32[128]{0:T(128)S(1)} %add_rsqrt_fusion.1), kind=kOutput, calls=%fused_computation.41 | convolution fusion | flops 537395200 | bytes 5509632 | tf_op jit(solution)/shard_map/dot_general | solution.py:142
  9.6 15.1 %shard_map.131 = bf16[128,1024]{1,0:T(8,128)(2,1)} custom-call(s32[1]{0:T(128)} %copy.24.length_ref, f32[128,2048]{1,0:T(8,128)} %fusion.27.q_ref.k_ref.v_ref, f32[128,2048]{1,0:T(8,128)} %fusion.27.q_ref.k_ref.v_ref, f32[128,2048]{1,0:T(8,128)} %fusion.27.q_ref.k_ref.v_ref, f32[128,128]{1,0:T(8,128)} %get-tuple-element.13.cos_ref, ...), custom_call_target="tpu_custom_call" | custom-call | tf_op jit(solution)/shard_map/pallas_call | solution.py:117
  24.7 0.1 convolution_convert_fusion.2
  24.8 1.4 %fusion.44 = f32[128,1024]{1,0:T(8,128)S(1)} fusion(bf16[128,1024]{1,0:T(8,128)(2,1)} %shard_map.131, bf16[1024,1024]{1,0:T(8,128)(2,1)S(1)} %copy-done), kind=kOutput, calls=%fused_computation.66 | convolution fusion | flops 268435456 | bytes 2883584 | tf_op jit(solution)/shard_map/dot_general | solution.py:158
  26.2 0.0 collective-permute-done.1
  26.2 0.0 copy-start.7
  26.3 0.0 collective-permute-done
  26.3 0.8 multiply_reduce_fusion
  27.1 2.4 %convolution_convert_fusion.1 = bf16[32,40,1024]{2,1,0:T(8,128)(2,1)} fusion(s32[128,32]{0,1:T(8,128)S(1)} %convolution_convert_fusion.2, pred[128,32]{0,1:T(8,128)(4,1)S(1)} %fusion.34, f32[128,1024]{1,0:T(8,128)S(1)} %fusion.44, bf16[128,1024]{1,0:T(8,128)(2,1)S(1)} %copy-done.1, f32[1024]{0:T(1024)S(1)} %copy-done.4, f32[128]{0:T(128)S(1)} %add_rsqrt_fusion), kind=kOutput, calls=%fused_computation.8 | convolution fusion | flops 337969152 | bytes 3432960 | tf_op jit(solution)/shard_map/tec,tw->ecw/dot_general | solution.py:208
  29.5 11.2 %all-to-all-start = ((bf16[32,40,1024]{2,1,0:T(8,128)(2,1)}), bf16[32,40,1024]{2,1,0:T(8,128)(2,1)}, u32[]{:S(2)}, u32[]{:S(2)}) async-start(bf16[32,40,1024]{2,1,0:T(8,128)(2,1)} %convolution_convert_fusion.1), calls=%async_computation | async-start | bytes 5242880 | tf_op jit(solution)/shard_map/all_to_all | solution.py:211
  40.7 0.1 collective-permute-start.2
  40.8 0.5 collective-permute-start.3
  41.3 0.1 collective-permute-start.4
  41.4 0.4 collective-permute-start.5
  41.8 0.9 collective-permute-done.2
  42.7 0.7 collective-permute-done.3
  43.5 0.3 pad_maximum_fusion
  43.7 0.4 slice_bitcast_fusion.1
  44.1 1.2 copy_bitcast_fusion
  45.3 31.0 %all-to-all-done = bf16[32,40,1024]{2,1,0:T(8,128)(2,1)} async-done(((bf16[32,40,1024]{2,1,0:T(8,128)(2,1)}), bf16[32,40,1024]{2,1,0:T(8,128)(2,1)}, u32[]{:S(2)}, u32[]{:S(2)}) %all-to-all-start) | async-done | bytes 2621472 | tf_op jit(solution)/shard_map/all_to_all | solution.py:211
  76.3 5.0 %fusion.1 = f32[32,40,1024]{2,1,0:T(8,128)S(1)} fusion(bf16[32,40,1024]{2,1,0:T(8,128)(2,1)} %all-to-all-done, bf16[1024,512]{1,0:T(8,128)(2,1)S(1)} %get-tuple-element.14, bf16[1024,512]{1,0:T(8,128)(2,1)} %get-tuple-element.15), kind=kOutput, calls=%fused_computation.4 | convolution fusion | flops 2688548864 | bytes 9961472 | tf_op jit(solution)/shard_map/scw,wh->sch/dot_general | solution.py:215
  81.3 0.0 collective-permute-done.4
  81.3 0.0 collective-permute-done.5
  81.3 4.3 %convolution_convert_fusion = bf16[32,40,1024]{2,1,0:T(8,128)(2,1)} fusion(f32[32,40,1024]{2,1,0:T(8,128)S(1)} %fusion.1, bf16[128,1024]{1,0:T(8,128)(2,1)} %collective-permute-done.5, bf16[128,1024]{1,0:T(8,128)(2,1)} %collective-permute-done.4, bf16[128,1024]{1,0:T(8,128)(2,1)S(1)} %copy-done.8, bf16[128,1024]{1,0:T(8,128)(2,1)S(1)} %bitcast.47), kind=kOutput, calls=%fused_computation.7 | convolution fusion | flops 1351614464 | bytes 8912896 | tf_op jit(solution)/shard_map/sch,hw->scw/dot_general | solution.py:223
  85.6 4.9 %all-to-all-start.1 = ((bf16[32,40,1024]{2,1,0:T(8,128)(2,1)}), bf16[32,40,1024]{2,1,0:T(8,128)(2,1)}, u32[]{:S(2)}, u32[]{:S(2)}) async-start(bf16[32,40,1024]{2,1,0:T(8,128)(2,1)} %convolution_convert_fusion), calls=%async_computation.1 | async-start | bytes 5242880 | tf_op jit(solution)/shard_map/all_to_all | solution.py:226
  90.6 34.6 %all-to-all-done.1 = bf16[32,40,1024]{2,1,0:T(8,128)(2,1)} async-done(((bf16[32,40,1024]{2,1,0:T(8,128)(2,1)}), bf16[32,40,1024]{2,1,0:T(8,128)(2,1)}, u32[]{:S(2)}, u32[]{:S(2)}) %all-to-all-start.1) | async-done | bytes 2621472 | tf_op jit(solution)/shard_map/all_to_all | solution.py:226
  125.2 3.4 %fusion.5 = bf16[128,1024]{1,0:T(8,128)(2,1)} fusion(bf16[32,40,1024]{2,1,0:T(8,128)(2,1)} %all-to-all-done.1, f32[128,32]{0,1:T(8,128)S(1)} %select_reduce_fusion, s32[128,32]{0,1:T(8,128)S(1)} %convolution_convert_fusion.2, pred[128,32]{0,1:T(8,128)(4,1)S(1)} %fusion.34), kind=kOutput, calls=%fused_computation.10 | convolution fusion | flops 1007255552 | bytes 2920448 | tf_op jit(solution)/shard_map/tec,ecw->tw/dot_general | solution.py:228
  (22 shorter events, 0.1 us)
Async XLA Ops:
  0.6 24.2 %copy-start = (bf16[1024,1024]{1,0:T(8,128)(2,1)S(1)}, bf16[1024,1024]{1,0:T(8,128)(2,1)}, u32[]{:S(2)}) copy-start(bf16[1024,1024]{1,0:T(8,128)(2,1)} %param.14) | copy-start | bytes 6291460
  0.6 25.6 %collective-permute-start = (bf16[1024,256]{1,0:T(8,128)(2,1)}, bf16[1024,256]{1,0:T(8,128)(2,1)S(1)}, u32[]{:S(2)}, u32[]{:S(2)}) collective-permute-start(bf16[1024,256]{1,0:T(8,128)(2,1)} %bitcast.39), channel_id=1, source_target_pairs={{0,2},{1,3},{2,0},{3,1},{4,6},{5,7},{6,4},{7,5},{8,10},{9,11},{10,... | collective-permute-start | bytes 1572872 | tf_op jit(solution)/shard_map/ppermute | solution.py:162
  2.3 23.9 %collective-permute-start.1 = (bf16[128,1024]{1,0:T(8,128)(2,1)}, bf16[128,1024]{1,0:T(8,128)(2,1)S(1)}, u32[]{:S(2)}, u32[]{:S(2)}) collective-permute-start(bf16[128,1024]{1,0:T(8,128)(2,1)} %bitcast.45), channel_id=1, source_target_pairs={{0,2},{1,3},{2,0},{3,1},{4,6},{5,7},{6,4},{7,5},{8,10},{9,11},{10,... | collective-permute-start | bytes 786440 | tf_op jit(solution)/shard_map/ppermute | solution.py:162
  5.5 4.1 %copy-start.3 = (s32[128,8]{0,1:T(8,128)S(1)}, s32[128,8]{0,1:T(8,128)}, u32[]{:S(2)}) copy-start(s32[128,8]{0,1:T(8,128)} %param.20) | copy-start | bytes 12292
  24.7 1.6 %copy-start.1 = (bf16[128,1024]{1,0:T(8,128)(2,1)S(1)}, bf16[128,1024]{1,0:T(8,128)(2,1)}, u32[]{:S(2)}) copy-start(bf16[128,1024]{1,0:T(8,128)(2,1)} %param.12) | copy-start | bytes 786436
  24.7 2.4 %copy-start.4 = (f32[1024]{0:T(1024)S(1)}, f32[1024]{0:T(1024)}, u32[]{:S(2)}) copy-start(f32[1024]{0:T(1024)} %param.16) | copy-start | bytes 12292
  26.2 0.8 copy-start.7
  29.5 11.2 %copy-start.2 = (bf16[1,1024,256]{2,1,0:T(8,128)(2,1)S(1)}, bf16[1,1024,256]{2,1,0:T(8,128)(2,1)}, u32[]{:S(2)}) copy-start(bf16[1,1024,256]{2,1,0:T(8,128)(2,1)} %param.22) | copy-start | bytes 1572868
  29.5 11.8 %copy-start.6 = (bf16[1,128,1024]{2,1,0:T(8,128)(2,1)S(1)}, bf16[1,128,1024]{2,1,0:T(8,128)(2,1)}, u32[]{:S(2)}) copy-start(bf16[1,128,1024]{2,1,0:T(8,128)(2,1)} %param.23) | copy-start | bytes 786436
  29.5 46.8 %all-to-all-start = ((bf16[32,40,1024]{2,1,0:T(8,128)(2,1)}), bf16[32,40,1024]{2,1,0:T(8,128)(2,1)}, u32[]{:S(2)}, u32[]{:S(2)}) async-start(bf16[32,40,1024]{2,1,0:T(8,128)(2,1)} %convolution_convert_fusion.1), calls=%async_computation | async-start | bytes 5242880 | tf_op jit(solution)/shard_map/all_to_all | solution.py:211
  40.7 2.0 %collective-permute-start.2 = (bf16[1024,256]{1,0:T(8,128)(2,1)S(1)}, bf16[1024,256]{1,0:T(8,128)(2,1)S(1)}, u32[]{:S(2)}, u32[]{:S(2)}) collective-permute-start(bf16[1024,256]{1,0:T(8,128)(2,1)S(1)} %bitcast.40), channel_id=1, source_target_pairs={{0,1},{1,0},{2,3},{3,2},{4,5},{5,4},{6,7},{7,6},{8,9},{9,8},{10,11... | collective-permute-start | bytes 1572872 | tf_op jit(solution)/shard_map/ppermute | solution.py:162
  40.8 2.6 %collective-permute-start.3 = (bf16[1024,256]{1,0:T(8,128)(2,1)S(1)}, bf16[1024,256]{1,0:T(8,128)(2,1)S(1)}, u32[]{:S(2)}, u32[]{:S(2)}) collective-permute-start(bf16[1024,256]{1,0:T(8,128)(2,1)S(1)} %collective-permute-done), channel_id=1, source_target_pairs={{0,1},{1,0},{2,3},{3,2},{4,5},{5,4},{6,7},{7,6},{8,9},{9,8},{10,11... | collective-permute-start | bytes 1572872 | tf_op jit(solution)/shard_map/ppermute | solution.py:162
  41.3 40.0 %collective-permute-start.4 = (bf16[128,1024]{1,0:T(8,128)(2,1)S(1)}, bf16[128,1024]{1,0:T(8,128)(2,1)}, u32[]{:S(2)}, u32[]{:S(2)}) collective-permute-start(bf16[128,1024]{1,0:T(8,128)(2,1)S(1)} %bitcast.46), channel_id=1, source_target_pairs={{0,1},{1,0},{2,3},{3,2},{4,5},{5,4},{6,7},{7,6},{8,9},{9,8},{10,11... | collective-permute-start | bytes 786440 | tf_op jit(solution)/shard_map/ppermute | solution.py:162
  41.4 39.9 %collective-permute-start.5 = (bf16[128,1024]{1,0:T(8,128)(2,1)}, bf16[128,1024]{1,0:T(8,128)(2,1)}, u32[]{:S(2)}, u32[]{:S(2)}) collective-permute-start(bf16[128,1024]{1,0:T(8,128)(2,1)} %copy-done.7), channel_id=1, source_target_pairs={{0,1},{1,0},{2,3},{3,2},{4,5},{5,4},{6,7},{7,6},{8,9},{9,8},{10,11... | collective-permute-start | bytes 786440 | tf_op jit(solution)/shard_map/ppermute | solution.py:162
  76.3 5.0 %copy-start.8 = (bf16[128,1024]{1,0:T(8,128)(2,1)S(1)}, bf16[128,1024]{1,0:T(8,128)(2,1)}, u32[]{:S(2)}) copy-start(bf16[128,1024]{1,0:T(8,128)(2,1)} %copy-done.7) | copy-start | bytes 786436
  85.6 5.0 %copy-start.5 = (f32[128,8]{0,1:T(8,128)S(1)}, f32[128,8]{0,1:T(8,128)}, u32[]{:S(2)}) copy-start(f32[128,8]{0,1:T(8,128)} %param.21) | copy-start | bytes 12292
  85.6 39.6 %all-to-all-start.1 = ((bf16[32,40,1024]{2,1,0:T(8,128)(2,1)}), bf16[32,40,1024]{2,1,0:T(8,128)(2,1)}, u32[]{:S(2)}, u32[]{:S(2)}) async-start(bf16[32,40,1024]{2,1,0:T(8,128)(2,1)} %convolution_convert_fusion), calls=%async_computation.1 | async-start | bytes 5242880 | tf_op jit(solution)/shard_map/all_to_all | solution.py:226

commit v17 on v16

--- a/solution.py
+++ b/solution.py
@@ -182,12 +182,14 @@
     own_dw = down_weight[0]
     far_gu = swap(own_gu, 2)
     far_dw = swap(own_dw, 2)
+    branch = attend(
+        tokens, qkv_weight, out_weight, norm_attn, keys_cache[0], values_cache[0], lengths[0]
+    )
+    branch, far_gu, far_dw, own_gu, own_dw = lax.optimization_barrier(
+        (branch, far_gu, far_dw, own_gu, own_dw)
+    )
     side_gu = swap(own_gu, 1)
     side_dw = swap(own_dw, 1)
-    branch = attend(
-        tokens, qkv_weight, out_weight, norm_attn, keys_cache[0], values_cache[0], lengths[0]
-    )
-    branch, far_gu, far_dw = lax.optimization_barrier((branch, far_gu, far_dw))
     gate_up_all = jnp.concatenate([own_gu, far_gu, side_gu, swap(far_gu, 1)], axis=1)
     down_all = jnp.concatenate([own_dw, far_dw, side_dw, swap(far_dw, 1)], axis=0)
     carried = tokens.astype(jnp.float32) + 0.22 * branch

time: 130 us -> 130 us (level)
  waiting for transfers between devices: 67.3 us -> 59.3 us
  local copies, waits for them, and re-layouts: 1.64 us -> 8.24 us
  other arithmetic: 3.18 us -> 4.56 us
    all_to_all x1, waiting for transfers between devices: 31 us -> 23 us  [on_device(): lax.all_to_all(outgoing, ('req', 'h'), split_axis=0, concat_axis=0, tiled...]
    reshape x0 -> x1, local copies, waits for them, and re-layouts: none -> 4.53 us  [on_device(): pieces = gate_up_all.reshape(gate_up_all.shape[0], slices, 2 * width_dev)]
    slice x0 -> x1, local copies, waits for them, and re-layouts: none -> 2.26 us  [on_device(): pieces[..., :width_dev].reshape(gate_up_all.shape[0], slices * width_dev)]
    concatenate x1, other arithmetic: 0.26 us -> 1.64 us  [on_device(): jnp.concatenate([own_gu, far_gu, side_gu, swap(far_gu, 1)], axis=1)]
  transfers between devices with their start and end apart: 8 -> 8, of which waited for: 4 -> 4; matrix products, arithmetic and copies ran while one was open for 11% -> 17% of each run, Pallas kernels for 12% -> 12%
where the time goes in v17:
time: 130 us; the launch traced here: 129 us
  waiting for transfers between devices  59.3 us (46%)
  matrix products  20.7 us (16%)
  starting transfers between devices  19.3 us (15%)
  Pallas kernels  15.1 us (12%)
  local copies, waits for them, and re-layouts  8.24 us (6%)
  other arithmetic  4.56 us (4%)
  between operations  1.44 us (1%)
    all_to_all x1, waiting for transfers between devices, on_device(): lax.all_to_all(produced, ('req', 'h'), split_axis=0, concat_axis=0, tiled...  34.6 us
    all_to_all x1, waiting for transfers between devices, on_device(): lax.all_to_all(outgoing, ('req', 'h'), split_axis=0, concat_axis=0, tiled...  23 us
    pallas_call x1, Pallas kernels, attention_core(): pl.pallas_call(attention_kernel, grid_spec=pltpu.PrefetchScalarGridSpec(n...  15.1 us
    all_to_all x1, starting transfers between devices, on_device(): lax.all_to_all(outgoing, ('req', 'h'), split_axis=0, concat_axis=0, tiled...  11.2 us
    dot_general x1, matrix products, on_device(): jnp.einsum('scw,wh->sch', joined, jnp.concatenate([gate_cols, up_cols], a...  4.96 us
    all_to_all x1, starting transfers between devices, on_device(): lax.all_to_all(produced, ('req', 'h'), split_axis=0, concat_axis=0, tiled...  4.94 us
    reshape x1, local copies, waits for them, and re-layouts, on_device(): pieces = gate_up_all.reshape(gate_up_all.shape[0], slices, 2 * width_dev)  4.53 us
    dot_general x1, matrix products, on_device(): jnp.einsum('sch,hw->scw', hidden, down_all, preferred_element_type=jnp.fl...  4.27 us
  transfers between devices with their start and end apart: 8, of which 4 were waited for; matrix products, arithmetic and copies ran while one was open for 17% of the time, Pallas kernels for 12%

profile of v17, /device:TPU:0, one launch (start us, length us, event | category | flops | bytes accessed | tf_op | source)
XLA Modules:
  0.0 128.6 jit_solution(4745624260971346621)
XLA Ops:
  0.6 0.0 copy-start
  0.6 1.7 %collective-permute-start = (bf16[1024,256]{1,0:T(8,128)(2,1)}, bf16[1024,256]{1,0:T(8,128)(2,1)S(1)}, u32[]{:S(2)}, u32[]{:S(2)}) collective-permute-start(bf16[1024,256]{1,0:T(8,128)(2,1)} %bitcast.35), channel_id=1, source_target_pairs={{0,2},{1,3},{2,0},{3,1},{4,6},{5,7},{6,4},{7,5},{8,10},{9,11},{10,... | collective-permute-start | bytes 1572872 | tf_op jit(solution)/shard_map/ppermute | solution.py:162
  2.3 0.4 collective-permute-start.1
  3.4 1.1 fusion.16
  4.5 1.0 multiply_sine_fusion
  5.5 4.1 %fusion.27.q_ref.k_ref.v_ref = f32[128,2048]{1,0:T(8,128)} fusion(bf16[1024,2048]{1,0:T(8,128)(2,1)} %param.13, bf16[128,1024]{1,0:T(8,128)(2,1)} %param.12, f32[1024]{0:T(1024)} %param.15, f32[128]{0:T(128)S(1)} %add_rsqrt_fusion.1), kind=kOutput, calls=%fused_computation.39 | convolution fusion | flops 537395200 | bytes 5509632 | tf_op jit(solution)/shard_map/dot_general | solution.py:142
  9.6 15.1 %shard_map.131 = bf16[128,1024]{1,0:T(8,128)(2,1)} custom-call(s32[1]{0:T(128)} %copy.20.length_ref, f32[128,2048]{1,0:T(8,128)} %fusion.27.q_ref.k_ref.v_ref, f32[128,2048]{1,0:T(8,128)} %fusion.27.q_ref.k_ref.v_ref, f32[128,2048]{1,0:T(8,128)} %fusion.27.q_ref.k_ref.v_ref, f32[128,128]{1,0:T(8,128)} %get-tuple-element.17.cos_ref, ...), custom_call_target="tpu_custom_call" | custom-call | tf_op jit(solution)/shard_map/pallas_call | solution.py:117
  24.7 0.1 convolution_convert_fusion.2
  24.8 1.4 %fusion.45 = f32[128,1024]{1,0:T(8,128)S(1)} fusion(bf16[128,1024]{1,0:T(8,128)(2,1)} %shard_map.131, bf16[1024,1024]{1,0:T(8,128)(2,1)S(1)} %copy-done), kind=kOutput, calls=%fused_computation.65 | convolution fusion | flops 268435456 | bytes 2883584 | tf_op jit(solution)/shard_map/dot_general | solution.py:158
  26.2 0.0 collective-permute-done.1
  26.2 0.0 copy-start.7
  26.3 0.0 collective-permute-done
  26.3 0.8 multiply_reduce_fusion
  27.1 2.4 %convolution_convert_fusion.1 = bf16[32,40,1024]{2,1,0:T(8,128)(2,1)} fusion(s32[128,32]{0,1:T(8,128)S(1)} %convolution_convert_fusion.2, pred[128,32]{0,1:T(8,128)(4,1)S(1)} %fusion.34, f32[128,1024]{1,0:T(8,128)S(1)} %fusion.45, bf16[128,1024]{1,0:T(8,128)(2,1)S(1)} %copy-done.1, f32[1024]{0:T(1024)S(1)} %copy-done.4, f32[128]{0:T(128)S(1)} %add_rsqrt_fusion), kind=kOutput, calls=%fused_computation.8 | convolution fusion | flops 337969152 | bytes 3432960 | tf_op jit(solution)/shard_map/tec,tw->ecw/dot_general | solution.py:210
  29.5 11.2 %all-to-all-start = ((bf16[32,40,1024]{2,1,0:T(8,128)(2,1)}), bf16[32,40,1024]{2,1,0:T(8,128)(2,1)}, u32[]{:S(2)}, u32[]{:S(2)}) async-start(bf16[32,40,1024]{2,1,0:T(8,128)(2,1)} %convolution_convert_fusion.1), calls=%async_computation | async-start | bytes 5242880 | tf_op jit(solution)/shard_map/all_to_all | solution.py:213
  40.7 0.1 collective-permute-start.3
  40.8 0.5 collective-permute-start.2
  41.3 0.1 collective-permute-start.5
  41.4 0.4 collective-permute-start.4
  41.8 0.9 collective-permute-done.3
  42.7 0.7 collective-permute-done.2
  43.4 1.6 %pad_maximum_fusion = bf16[1024,1024]{1,0:T(8,128)(2,1)} fusion(bf16[1024,256]{1,0:T(8,128)(2,1)S(1)} %collective-permute-done.3, bf16[1024,256]{1,0:T(8,128)(2,1)S(1)} %collective-permute-done.2, bf16[1024,256]{1,0:T(8,128)(2,1)S(1)} %collective-permute-done, bf16[1024,256]{1,0:T(8,128)(2,1)S(1)} %bitcast.37), kind=kLoop, calls=%fused_computation.2 | loop fusion | flops 8388608 | bytes 4194304 | tf_op jit(solution)/shard_map/concatenate | solution.py:193
  45.1 4.5 %reshape.54 = bf16[1024,4,256]{2,1,0:T(4,128)(2,1)} reshape(bf16[1024,1024]{1,0:T(8,128)(2,1)} %pad_maximum_fusion) | data formatting | bytes 4194304 | tf_op jit(solution)/shard_map/reshape | solution.py:214
  49.6 2.3 %fusion.44 = (bf16[1024,4,128]{2,1,0:T(4,128)(2,1)S(1)}, bf16[1024,4,128]{2,1,0:T(4,128)(2,1)S(1)}) fusion(bf16[1024,4,256]{2,1,0:T(4,128)(2,1)} %reshape.54), kind=kLoop, calls=%fused_computation.64 | loop fusion | bytes 4194304 | tf_op jit(solution)/shard_map/slice | solution.py:215
  51.9 1.4 %copy_bitcast_fusion = (bf16[1024,512]{1,0:T(8,128)(2,1)S(1)}, bf16[1024,512]{1,0:T(8,128)(2,1)}) fusion(bf16[128,8,4,128]{3,2,1,0:T(4,128)(2,1)S(1)} %bitcast.32, bf16[128,8,4,128]{3,2,1,0:T(4,128)(2,1)S(1)} %bitcast.31), kind=kLoop, calls=%fused_computation.12 | loop fusion | bytes 4194304 | tf_op jit(solution)/shard_map/reshape | solution.py:216
  53.3 23.0 %all-to-all-done = bf16[32,40,1024]{2,1,0:T(8,128)(2,1)} async-done(((bf16[32,40,1024]{2,1,0:T(8,128)(2,1)}), bf16[32,40,1024]{2,1,0:T(8,128)(2,1)}, u32[]{:S(2)}, u32[]{:S(2)}) %all-to-all-start) | async-done | bytes 2621472 | tf_op jit(solution)/shard_map/all_to_all | solution.py:213
  76.3 5.0 %fusion.1 = f32[32,40,1024]{2,1,0:T(8,128)S(1)} fusion(bf16[32,40,1024]{2,1,0:T(8,128)(2,1)} %all-to-all-done, bf16[1024,512]{1,0:T(8,128)(2,1)S(1)} %get-tuple-element.18, bf16[1024,512]{1,0:T(8,128)(2,1)} %get-tuple-element.19), kind=kOutput, calls=%fused_computation.4 | convolution fusion | flops 2688548864 | bytes 9961472 | tf_op jit(solution)/shard_map/scw,wh->sch/dot_general | solution.py:217
  81.3 0.0 collective-permute-done.4
  81.3 4.3 %convolution_convert_fusion = bf16[32,40,1024]{2,1,0:T(8,128)(2,1)} fusion(f32[32,40,1024]{2,1,0:T(8,128)S(1)} %fusion.1, bf16[128,1024]{1,0:T(8,128)(2,1)} %collective-permute-done.5, bf16[128,1024]{1,0:T(8,128)(2,1)} %collective-permute-done.4, bf16[128,1024]{1,0:T(8,128)(2,1)S(1)} %copy-done.8, bf16[128,1024]{1,0:T(8,128)(2,1)S(1)} %bitcast.40), kind=kOutput, calls=%fused_computation.7 | convolution fusion | flops 1351614464 | bytes 8912896 | tf_op jit(solution)/shard_map/sch,hw->scw/dot_general | solution.py:225
  85.6 4.9 %all-to-all-start.1 = ((bf16[32,40,1024]{2,1,0:T(8,128)(2,1)}), bf16[32,40,1024]{2,1,0:T(8,128)(2,1)}, u32[]{:S(2)}, u32[]{:S(2)}) async-start(bf16[32,40,1024]{2,1,0:T(8,128)(2,1)} %convolution_convert_fusion), calls=%async_computation.1 | async-start | bytes 5242880 | tf_op jit(solution)/shard_map/all_to_all | solution.py:228
  90.6 34.6 %all-to-all-done.1 = bf16[32,40,1024]{2,1,0:T(8,128)(2,1)} async-done(((bf16[32,40,1024]{2,1,0:T(8,128)(2,1)}), bf16[32,40,1024]{2,1,0:T(8,128)(2,1)}, u32[]{:S(2)}, u32[]{:S(2)}) %all-to-all-start.1) | async-done | bytes 2621472 | tf_op jit(solution)/shard_map/all_to_all | solution.py:228
  125.2 3.4 %fusion.5 = bf16[128,1024]{1,0:T(8,128)(2,1)} fusion(bf16[32,40,1024]{2,1,0:T(8,128)(2,1)} %all-to-all-done.1, f32[128,32]{0,1:T(8,128)S(1)} %select_reduce_fusion, s32[128,32]{0,1:T(8,128)S(1)} %convolution_convert_fusion.2, pred[128,32]{0,1:T(8,128)(4,1)S(1)} %fusion.34), kind=kOutput, calls=%fused_computation.10 | convolution fusion | flops 1007255552 | bytes 2920448 | tf_op jit(solution)/shard_map/tec,ecw->tw/dot_general | solution.py:230
  (23 shorter events, 0.1 us)
Async XLA Ops:
  0.6 24.2 %copy-start = (bf16[1024,1024]{1,0:T(8,128)(2,1)S(1)}, bf16[1024,1024]{1,0:T(8,128)(2,1)}, u32[]{:S(2)}) copy-start(bf16[1024,1024]{1,0:T(8,128)(2,1)} %param.14) | copy-start | bytes 6291460
  0.6 25.6 %collective-permute-start = (bf16[1024,256]{1,0:T(8,128)(2,1)}, bf16[1024,256]{1,0:T(8,128)(2,1)S(1)}, u32[]{:S(2)}, u32[]{:S(2)}) collective-permute-start(bf16[1024,256]{1,0:T(8,128)(2,1)} %bitcast.35), channel_id=1, source_target_pairs={{0,2},{1,3},{2,0},{3,1},{4,6},{5,7},{6,4},{7,5},{8,10},{9,11},{10,... | collective-permute-start | bytes 1572872 | tf_op jit(solution)/shard_map/ppermute | solution.py:162
  2.3 23.9 %collective-permute-start.1 = (bf16[128,1024]{1,0:T(8,128)(2,1)}, bf16[128,1024]{1,0:T(8,128)(2,1)S(1)}, u32[]{:S(2)}, u32[]{:S(2)}) collective-permute-start(bf16[128,1024]{1,0:T(8,128)(2,1)} %bitcast.38), channel_id=1, source_target_pairs={{0,2},{1,3},{2,0},{3,1},{4,6},{5,7},{6,4},{7,5},{8,10},{9,11},{10,... | collective-permute-start | bytes 786440 | tf_op jit(solution)/shard_map/ppermute | solution.py:162
  5.5 4.1 %copy-start.3 = (s32[128,8]{0,1:T(8,128)S(1)}, s32[128,8]{0,1:T(8,128)}, u32[]{:S(2)}) copy-start(s32[128,8]{0,1:T(8,128)} %param.20) | copy-start | bytes 12292
  24.7 1.6 %copy-start.1 = (bf16[128,1024]{1,0:T(8,128)(2,1)S(1)}, bf16[128,1024]{1,0:T(8,128)(2,1)}, u32[]{:S(2)}) copy-start(bf16[128,1024]{1,0:T(8,128)(2,1)} %param.12) | copy-start | bytes 786436
  24.7 2.4 %copy-start.4 = (f32[1024]{0:T(1024)S(1)}, f32[1024]{0:T(1024)}, u32[]{:S(2)}) copy-start(f32[1024]{0:T(1024)} %param.16) | copy-start | bytes 12292
  26.2 0.8 copy-start.7
  29.5 11.3 %copy-start.2 = (bf16[1,1024,256]{2,1,0:T(8,128)(2,1)S(1)}, bf16[1,1024,256]{2,1,0:T(8,128)(2,1)}, u32[]{:S(2)}) copy-start(bf16[1,1024,256]{2,1,0:T(8,128)(2,1)} %param.22) | copy-start | bytes 1572868
  29.5 11.9 %copy-start.6 = (bf16[1,128,1024]{2,1,0:T(8,128)(2,1)S(1)}, bf16[1,128,1024]{2,1,0:T(8,128)(2,1)}, u32[]{:S(2)}) copy-start(bf16[1,128,1024]{2,1,0:T(8,128)(2,1)} %param.23) | copy-start | bytes 786436
  29.5 46.8 %all-to-all-start = ((bf16[32,40,1024]{2,1,0:T(8,128)(2,1)}), bf16[32,40,1024]{2,1,0:T(8,128)(2,1)}, u32[]{:S(2)}, u32[]{:S(2)}) async-start(bf16[32,40,1024]{2,1,0:T(8,128)(2,1)} %convolution_convert_fusion.1), calls=%async_computation | async-start | bytes 5242880 | tf_op jit(solution)/shard_map/all_to_all | solution.py:213
  40.7 2.0 %collective-permute-start.3 = (bf16[1024,256]{1,0:T(8,128)(2,1)S(1)}, bf16[1024,256]{1,0:T(8,128)(2,1)S(1)}, u32[]{:S(2)}, u32[]{:S(2)}) collective-permute-start(bf16[1024,256]{1,0:T(8,128)(2,1)S(1)} %collective-permute-done), channel_id=1, source_target_pairs={{0,1},{1,0},{2,3},{3,2},{4,5},{5,4},{6,7},{7,6},{8,9},{9,8},{10,11... | collective-permute-start | bytes 1572872 | tf_op jit(solution)/shard_map/ppermute | solution.py:162
  40.8 2.6 %collective-permute-start.2 = (bf16[1024,256]{1,0:T(8,128)(2,1)S(1)}, bf16[1024,256]{1,0:T(8,128)(2,1)S(1)}, u32[]{:S(2)}, u32[]{:S(2)}) collective-permute-start(bf16[1024,256]{1,0:T(8,128)(2,1)S(1)} %bitcast.36), channel_id=1, source_target_pairs={{0,1},{1,0},{2,3},{3,2},{4,5},{5,4},{6,7},{7,6},{8,9},{9,8},{10,11... | collective-permute-start | bytes 1572872 | tf_op jit(solution)/shard_map/ppermute | solution.py:162
  41.3 40.0 %collective-permute-start.5 = (bf16[128,1024]{1,0:T(8,128)(2,1)}, bf16[128,1024]{1,0:T(8,128)(2,1)}, u32[]{:S(2)}, u32[]{:S(2)}) collective-permute-start(bf16[128,1024]{1,0:T(8,128)(2,1)} %copy-done.7), channel_id=1, source_target_pairs={{0,1},{1,0},{2,3},{3,2},{4,5},{5,4},{6,7},{7,6},{8,9},{9,8},{10,11... | collective-permute-start | bytes 786440 | tf_op jit(solution)/shard_map/ppermute | solution.py:162
  41.4 39.9 %collective-permute-start.4 = (bf16[128,1024]{1,0:T(8,128)(2,1)S(1)}, bf16[128,1024]{1,0:T(8,128)(2,1)}, u32[]{:S(2)}, u32[]{:S(2)}) collective-permute-start(bf16[128,1024]{1,0:T(8,128)(2,1)S(1)} %bitcast.39), channel_id=1, source_target_pairs={{0,1},{1,0},{2,3},{3,2},{4,5},{5,4},{6,7},{7,6},{8,9},{9,8},{10,11... | collective-permute-start | bytes 786440 | tf_op jit(solution)/shard_map/ppermute | solution.py:162
  76.3 5.0 %copy-start.8 = (bf16[128,1024]{1,0:T(8,128)(2,1)S(1)}, bf16[128,1024]{1,0:T(8,128)(2,1)}, u32[]{:S(2)}) copy-start(bf16[128,1024]{1,0:T(8,128)(2,1)} %copy-done.7) | copy-start | bytes 786436
  85.6 5.0 %copy-start.5 = (f32[128,8]{0,1:T(8,128)S(1)}, f32[128,8]{0,1:T(8,128)}, u32[]{:S(2)}) copy-start(f32[128,8]{0,1:T(8,128)} %param.21) | copy-start | bytes 12292
  85.6 39.6 %all-to-all-start.1 = ((bf16[32,40,1024]{2,1,0:T(8,128)(2,1)}), bf16[32,40,1024]{2,1,0:T(8,128)(2,1)}, u32[]{:S(2)}, u32[]{:S(2)}) async-start(bf16[32,40,1024]{2,1,0:T(8,128)(2,1)} %convolution_convert_fusion), calls=%async_computation.1 | async-start | bytes 5242880 | tf_op jit(solution)/shard_map/all_to_all | solution.py:228
